TPU v7x, 512 devices: a whole 4x4x16 slice. The times are simulated.
512 devices in a mesh: dp: 16 (over y, x_hi, core), tensor: 32 (over x_lo, z).
Axes of the slice: x: 4 (x_hi: 2, x_lo: 2; x = x_hi * 2 + x_lo), y: 4, z: 16, core: 2. Of those that a mesh axis runs over, the one named last changes fastest.
Arguments:
- loader_rows: bfloat16 [16, 32, 32, 4096], P('dp', 'tensor'), may hold values from -23 to 23
- row_counts: int32 [16, 32], P('dp', 'tensor'), may hold values from 0 to 32
- row_targets: int32 [16, 32, 32], P('dp', 'tensor'), may hold values from 0 to 255, as said below
- gate_weight: bfloat16 [4096, 16384], P('dp', 'tensor'), may hold values from -0.09375 to 0.09375
- up_weight: bfloat16 [4096, 16384], P('dp', 'tensor'), may hold values from -0.09375 to 0.09375
- down_weight: bfloat16 [16384, 4096], P('tensor'), may hold values from -0.046875 to 0.046875
Outputs:
- layer_out: bfloat16 [8192, 4096], P(('dp', 'tensor'))
Inputs may be any that keep to these rules, and one draw needn't show every extreme that they name: `row_targets`: among the first row_counts[d, t] slots of replica d and tensor index t, a value v names row v % 16 of the rows of tensor index t on replica v // 16; over all replicas each such row is named exactly once, and no device names more than 2 rows of one replica. Slots past the count hold arbitrary values of the same range.
All inputs are finite; a program needn't handle non-finite values.
Results may differ from a plain program's by a relative error of at most 0.0095.
Values may be sent and summed in bfloat16 or wider, within the bound.
No kernel may reach another device: no remote copies, remote signals or barrier semaphores. Data moves between devices by JAX's collectives and lax.ppermute only.
A program may use at most 64 MiB of HBM per device.

v0:
```python
import jax
import jax.numpy as jnp
from jax import lax
from jax.sharding import PartitionSpec as P

ROWS_GRP = 512


def swiglu(inputs, gate_full, up_full):
    gate_act = jnp.dot(inputs, gate_full, preferred_element_type=jnp.float32)
    up_act = jnp.dot(inputs, up_full, preferred_element_type=jnp.float32)
    return (jax.nn.silu(gate_act) * up_act).astype(jnp.bfloat16)


def normalize(row_block):
    wide_rows = row_block.astype(jnp.float32)
    return (
        wide_rows * lax.rsqrt(jnp.mean(wide_rows * wide_rows, axis=1, keepdims=True) + 1e-05)
    ).astype(jnp.bfloat16)


def rounded_term(hidden_part, weights):
    partial_sum = jnp.dot(hidden_part, weights, preferred_element_type=jnp.float32)
    return lax.optimization_barrier(partial_sum.astype(jnp.bfloat16)).astype(jnp.float32)


def per_device(loader_rows, row_counts, row_targets, gate_weight, up_weight, down_weight):
    dp_count = lax.axis_size("dp")
    tp_count = lax.axis_size("tensor")
    slot_rows = loader_rows[0, 0]
    slot_targets = row_targets[0, 0]
    live_count = row_counts[0, 0]
    slot_count = slot_rows.shape[0]
    feature_count = slot_rows.shape[1]
    per_peer = slot_count // dp_count
    shard_rows = ROWS_GRP // tp_count
    slot_index = jnp.arange(slot_count, dtype=jnp.int32)
    is_live = slot_index < live_count
    peer_index = slot_targets // shard_rows
    row_place = slot_targets % shard_rows
    peer_hot = (
        (peer_index[:, None] == jnp.arange(dp_count, dtype=jnp.int32)[None, :]) & is_live[:, None]
    ).astype(jnp.int32)
    earlier = jnp.cumsum(peer_hot, axis=0) - peer_hot
    slot_rank = jnp.sum(earlier * peer_hot, axis=1)
    send_slot = peer_index * per_peer + slot_rank
    pick_matrix = (send_slot[None, :] == slot_index[:, None]) & is_live[None, :]
    outgoing = jnp.dot(
        pick_matrix.astype(jnp.bfloat16), slot_rows, preferred_element_type=jnp.float32
    ).astype(jnp.bfloat16)
    out_place = jnp.sum(jnp.where(pick_matrix, row_place[None, :] + 1, 0), axis=1) - 1
    arrived, arrived_place = (
        lax.all_to_all(
            outgoing.reshape(dp_count, per_peer, feature_count),
            "dp",
            split_axis=0,
            concat_axis=0,
            tiled=True,
        ),
        lax.all_to_all(
            out_place.reshape(dp_count, per_peer), "dp", split_axis=0, concat_axis=0, tiled=True
        ),
    )
    land_matrix = (
        arrived_place.reshape(slot_count)[None, :]
        == jnp.arange(shard_rows, dtype=jnp.int32)[:, None]
    ).astype(jnp.bfloat16)
    local_batch = jnp.dot(
        land_matrix, arrived.reshape(slot_count, feature_count), preferred_element_type=jnp.float32
    ).astype(jnp.bfloat16)
    gate_full, up_full = (
        lax.all_gather(gate_weight, "dp", axis=0, tiled=True),
        lax.all_gather(up_weight, "dp", axis=0, tiled=True),
    )
    travelling = normalize(local_batch)
    hidden = swiglu(lax.all_gather(travelling, "tensor", axis=0, tiled=True), gate_full, up_full)
    summed = lax.psum_scatter(
        rounded_term(hidden, down_weight).astype(jnp.bfloat16),
        "tensor",
        scatter_dimension=0,
        tiled=True,
    ).astype(jnp.float32)
    return (local_batch.astype(jnp.float32) + summed).astype(jnp.bfloat16)


def solution(mesh):
    placed = (
        P("dp", "tensor", None, None),
        P("dp", "tensor"),
        P("dp", "tensor", None),
        P("dp", "tensor"),
        P("dp", "tensor"),
        P("tensor", None),
    )
    return jax.shard_map(
        per_device, mesh=mesh, in_specs=placed, out_specs=P(("dp", "tensor"), None), check_vma=False
    )
```

profile of v0, /device:TPU:24, one launch (start us, length us, event | category | flops | bytes accessed | tf_op | source)
XLA Modules:
  0.0 452.0 jit_solution(375960735694573083)
XLA Ops:
  6.5 0.7 all-gather.6.cloned.1.call-update
  7.9 0.7 fusion.11
  8.7 0.2 select_reduce_fusion.1
  8.9 0.1 select_reduce_fusion
  9.0 0.7 sub.18
  9.7 8.9 %all-to-all-start = ((s32[16,1,2]{2,1,0:T(1,128)}), s32[16,1,2]{2,1,0:T(1,128)S(1)}, u32[]{:S(2)}, u32[]{:S(2)}) async-start(s32[16,1,2]{2,1,0:T(1,128)} %bitcast.2), calls=%async_computation | async-start | bytes 16384 | tf_op jit(solution)/shard_map/all_to_all | solution.py:60
  18.7 0.2 convolution_convert_fusion.1
  18.9 0.9 reshape.123
  19.8 4.4 all-to-all-done
  24.1 5.5 %all-to-all-start.1 = ((bf16[16,2,4096]{2,1,0:T(2,128)(2,1)}), bf16[16,2,4096]{2,1,0:T(2,128)(2,1)S(1)}, u32[]{:S(2)}, u32[]{:S(2)}) async-start(bf16[16,2,4096]{2,1,0:T(2,128)(2,1)} %reshape.123), calls=%async_computation.1 | async-start | bytes 524288 | tf_op jit(solution)/shard_map/all_to_all | solution.py:53
  29.7 0.5 broadcast.157
  30.2 0.7 reduce.3
  30.9 6.0 %all-to-all-done.1 = bf16[16,2,4096]{2,1,0:T(2,128)(2,1)S(1)} async-done(((bf16[16,2,4096]{2,1,0:T(2,128)(2,1)}), bf16[16,2,4096]{2,1,0:T(2,128)(2,1)S(1)}, u32[]{:S(2)}, u32[]{:S(2)}) %all-to-all-start.1) | async-done | bytes 262176 | tf_op jit(solution)/shard_map/all_to_all | solution.py:53
  36.9 0.1 reshape.124
  37.0 0.3 multiply_reduce_fusion
  37.3 0.7 multiply_convert_fusion
  38.1 0.7 all-gather.8.cloned.1.call-update
  38.8 45.4 %all-gather.6.cloned.1.call-done = bf16[4096,512]{1,0:T(8,128)(2,1)} async-done(((bf16[256,512]{1,0:T(8,128)(2,1)}), bf16[4096,512]{1,0:T(8,128)(2,1)}) %all-gather.6.cloned.1.call-update) | async-done | bytes 4194320 | tf_op jit(solution)/shard_map/all_gather | solution.py:72
  84.2 139.9 %all-gather.4.cloned.1.call-done = bf16[512,4096]{1,0:T(8,128)(2,1)} async-done(((bf16[16,4096]{1,0:T(8,128)(2,1)}), bf16[512,4096]{1,0:T(8,128)(2,1)}) %all-gather.4.cloned.1.call-update) | async-done | bytes 4194320 | tf_op jit(solution)/shard_map/all_gather | solution.py:76
  224.2 5.8 %fusion.13 = f32[512,512]{1,0:T(8,128)S(1)} fusion(bf16[512,4096]{1,0:T(8,128)(2,1)} %all-gather.4.cloned.1.call-done, bf16[4096,512]{1,0:T(8,128)(2,1)} %all-gather.6.cloned.1.call-done), kind=kOutput, calls=%fused_computation.34 | convolution fusion | flops 2147483648 | bytes 9437184 | tf_op jit(solution)/shard_map/dot_general | solution.py:10
  230.0 59.2 %all-gather.8.cloned.1.call-done = bf16[4096,512]{1,0:T(8,128)(2,1)} async-done(((bf16[256,512]{1,0:T(8,128)(2,1)}), bf16[4096,512]{1,0:T(8,128)(2,1)}) %all-gather.8.cloned.1.call-update) | async-done | bytes 4194320 | tf_op jit(solution)/shard_map/all_gather | solution.py:73
  289.2 11.2 %convolution_convert_fusion = bf16[512,4096]{1,0:T(8,128)(2,1)} fusion(bf16[512,4096]{1,0:T(8,128)(2,1)} %param.11, bf16[512,4096]{1,0:T(8,128)(2,1)} %all-gather.4.cloned.1.call-done, bf16[4096,512]{1,0:T(8,128)(2,1)} %all-gather.8.cloned.1.call-done, f32[512,512]{1,0:T(8,128)S(1)} %fusion.13), kind=kOutput, calls=%fused_computation | convolution fusion | flops 4298637312 | bytes 17825792 | tf_op jit(solution)/shard_map/dot_general | solution.py:23
  300.4 143.4 %reduce-scatter.2.cloned.1.call-done = bf16[16,4096]{1,0:T(8,128)(2,1)} async-done(((bf16[512,4096]{1,0:T(8,128)(2,1)}), bf16[16,4096]{1,0:T(8,128)(2,1)}) %reduce-scatter.2.cloned.1.call-update) | async-done | bytes 131088 | tf_op jit(solution)/shard_map/reduce_scatter | solution.py:77
  443.8 1.6 add_convert_fusion
  (15 shorter events, 0.4 us)
Async XLA Ops:
  6.5 12.1 %copy-start = (bf16[1,1,32,4096]{3,2,1,0:T(8,128)(2,1)S(1)}, bf16[1,1,32,4096]{3,2,1,0:T(8,128)(2,1)}, u32[]{:S(2)}) copy-start(bf16[1,1,32,4096]{3,2,1,0:T(8,128)(2,1)} %param.6) | copy-start | bytes 786436
  6.5 77.7 %all-gather.6.cloned.1.call-start = ((), (), s32[]{:S(2)}) async-start(), calls=%async_computation.4 | async-start | bytes 4456448 | tf_op jit(solution)/shard_map/all_gather | solution.py:72
  9.7 14.4 %all-to-all-start = ((s32[16,1,2]{2,1,0:T(1,128)}), s32[16,1,2]{2,1,0:T(1,128)S(1)}, u32[]{:S(2)}, u32[]{:S(2)}) async-start(s32[16,1,2]{2,1,0:T(1,128)} %bitcast.2), calls=%async_computation | async-start | bytes 16384 | tf_op jit(solution)/shard_map/all_to_all | solution.py:60
  24.1 12.8 %all-to-all-start.1 = ((bf16[16,2,4096]{2,1,0:T(2,128)(2,1)}), bf16[16,2,4096]{2,1,0:T(2,128)(2,1)S(1)}, u32[]{:S(2)}, u32[]{:S(2)}) async-start(bf16[16,2,4096]{2,1,0:T(2,128)(2,1)} %reshape.123), calls=%async_computation.1 | async-start | bytes 524288 | tf_op jit(solution)/shard_map/all_to_all | solution.py:53
  29.6 194.6 %all-gather.4.cloned.1.call-start = ((), (), s32[]{:S(2)}) async-start(), calls=%async_computation.3 | async-start | bytes 4325376 | tf_op jit(solution)/shard_map/all_gather | solution.py:76
  38.1 251.1 %all-gather.8.cloned.1.call-start = ((), (), s32[]{:S(2)}) async-start(), calls=%async_computation.5 | async-start | bytes 4456448 | tf_op jit(solution)/shard_map/all_gather | solution.py:73
  38.8 405.0 %reduce-scatter.2.cloned.1.call-start = ((), (), s32[]{:S(2)}) async-start(), calls=%async_computation.6 | async-start | bytes 4325376 | tf_op jit(solution)/shard_map/reduce_scatter | solution.py:77
Sparse Core Ops, SparseCore 0:
  10.7 73.5 all-gather.5
  86.3 137.8 all-gather.3
  227.5 61.6 all-gather.7
  300.5 143.2 reduce-scatter.1
where the time goes:
time: 452 us
  waiting for transfers between devices  400 us (88%)
  matrix products  17.5 us (4%)
  starting transfers between devices  14.5 us (3%)
  between operations  13.8 us (3%)
    reduce_scatter x1, waiting for transfers between devices, per_device(): lax.psum_scatter(rounded_term(hidden, down_weight).astype(jnp.bfloat16),...  143 us
    all_gather x1, waiting for transfers between devices, per_device(): lax.all_gather(travelling, 'tensor', axis=0, tiled=True)  140 us
    all_gather x1, waiting for transfers between devices, per_device(): lax.all_gather(up_weight, 'dp', axis=0, tiled=True)  59.2 us
    all_gather x1, waiting for transfers between devices, per_device(): lax.all_gather(gate_weight, 'dp', axis=0, tiled=True)  45.4 us
    dot_general x1, matrix products, rounded_term(): jnp.dot(hidden_part, weights, preferred_element_type=jnp.float32)  11.2 us
  transfers between devices with their start and end apart: 6, of which 6 were waited for; matrix products, arithmetic and copies ran while one was open for 2% of the time, Pallas kernels for 0%

commit v1 on v0

--- a/solution.py
+++ b/solution.py
@@ -4,12 +4,38 @@
 from jax.sharding import PartitionSpec as P
 
 ROWS_GRP = 512
-
-
-def swiglu(inputs, gate_full, up_full):
-    gate_act = jnp.dot(inputs, gate_full, preferred_element_type=jnp.float32)
-    up_act = jnp.dot(inputs, up_full, preferred_element_type=jnp.float32)
-    return (jax.nn.silu(gate_act) * up_act).astype(jnp.bfloat16)
+DP_SUB = (4, 2, 2)
+TP_SUB = (2, 16)
+
+
+def dp_perm(move):
+    ny, nx, nc = DP_SUB
+    pairs = []
+    for y in range(ny):
+        for x in range(nx):
+            for c in range(nc):
+                ty, tx, tc = move(y, x, c)
+                pairs.append((y * nx * nc + x * nc + c, (ty % ny) * nx * nc + (tx % nx) * nc + tc % nc))
+    return pairs
+
+
+def tp_perm(move):
+    nl, nz = TP_SUB
+    pairs = []
+    for l in range(nl):
+        for z in range(nz):
+            tl, tz = move(l, z)
+            pairs.append((l * nz + z, (tl % nl) * nz + tz % nz))
+    return pairs
+
+
+DP_Y_FWD = dp_perm(lambda y, x, c: (y + 1, x, c))
+DP_Y_BWD = dp_perm(lambda y, x, c: (y - 1, x, c))
+DP_X_SWAP = dp_perm(lambda y, x, c: (y, x + 1, c))
+DP_C_SWAP = dp_perm(lambda y, x, c: (y, x, c + 1))
+TP_L_SWAP = tp_perm(lambda l, z: (l + 1, z))
+TP_Z_FWD = tp_perm(lambda l, z: (l, z + 1))
+TP_Z_BWD = tp_perm(lambda l, z: (l, z - 1))
 
 
 def normalize(row_block):
@@ -19,9 +45,43 @@
     ).astype(jnp.bfloat16)
 
 
-def rounded_term(hidden_part, weights):
-    partial_sum = jnp.dot(hidden_part, weights, preferred_element_type=jnp.float32)
-    return lax.optimization_barrier(partial_sum.astype(jnp.bfloat16)).astype(jnp.float32)
+def y_ring(chunks, key_of):
+    out = dict(chunks)
+    stacked = jnp.stack([chunks[k] for k in sorted(chunks)])
+    keys = sorted(chunks)
+    fwd = stacked
+    for s in range(2):
+        fwd = lax.ppermute(fwd, "dp", DP_Y_FWD)
+        for i, k in enumerate(keys):
+            out[key_of(k, DP_SUB[0] - 1 - s)] = fwd[i]
+    bwd = lax.ppermute(stacked, "dp", DP_Y_BWD)
+    for i, k in enumerate(keys):
+        out[key_of(k, 1)] = bwd[i]
+    return out
+
+
+def swap(chunks, perm, key_of):
+    out = dict(chunks)
+    keys = sorted(chunks)
+    got = lax.ppermute(jnp.stack([chunks[k] for k in keys]), "dp", perm)
+    for i, k in enumerate(keys):
+        out[key_of(k)] = got[i]
+    return out
+
+
+def gather_weight(piece, y_first):
+    set_y = lambda k, v: (v, k[1], k[2])
+    set_x = lambda k: (k[0], 1, k[2])
+    set_c = lambda k: (k[0], k[1], 1)
+    chunks = {(0, 0, 0): piece}
+    if y_first:
+        chunks = y_ring(chunks, set_y)
+        chunks = swap(chunks, DP_X_SWAP, set_x)
+    else:
+        chunks = swap(chunks, DP_X_SWAP, set_x)
+        chunks = y_ring(chunks, set_y)
+    chunks = swap(chunks, DP_C_SWAP, set_c)
+    return chunks
 
 
 def per_device(loader_rows, row_counts, row_targets, gate_weight, up_weight, down_weight):
@@ -68,19 +128,64 @@
     local_batch = jnp.dot(
         land_matrix, arrived.reshape(slot_count, feature_count), preferred_element_type=jnp.float32
     ).astype(jnp.bfloat16)
-    gate_full, up_full = (
-        lax.all_gather(gate_weight, "dp", axis=0, tiled=True),
-        lax.all_gather(up_weight, "dp", axis=0, tiled=True),
-    )
+
+    gate_chunks = gather_weight(gate_weight, True)
+    up_chunks = gather_weight(up_weight, False)
+    keys = sorted(gate_chunks)
+    ny, nx, nc = DP_SUB
+    me = lax.axis_index("dp")
+    my_y, my_x, my_c = me // (nx * nc), (me // nc) % nx, me % nc
+    piece_index = jnp.stack(
+        [((my_y + k[0]) % ny) * nx * nc + ((my_x + k[1]) % nx) * nc + (my_c + k[2]) % nc for k in keys]
+    ).astype(jnp.int32)
+    gate_full = jnp.concatenate([gate_chunks[k] for k in keys], axis=0)
+    up_full = jnp.concatenate([up_chunks[k] for k in keys], axis=0)
+
+    nl, nz = TP_SUB
     travelling = normalize(local_batch)
-    hidden = swiglu(lax.all_gather(travelling, "tensor", axis=0, tiled=True), gate_full, up_full)
-    summed = lax.psum_scatter(
-        rounded_term(hidden, down_weight).astype(jnp.bfloat16),
-        "tensor",
-        scatter_dimension=0,
-        tiled=True,
-    ).astype(jnp.float32)
-    return (local_batch.astype(jnp.float32) + summed).astype(jnp.bfloat16)
+    pair = jnp.stack([travelling, lax.ppermute(travelling, "tensor", TP_L_SWAP)])
+    token_chunks = {0: pair}
+    fwd = pair
+    for s in range(nz // 2):
+        fwd = lax.ppermute(fwd, "tensor", TP_Z_FWD)
+        token_chunks[nz - 1 - s] = fwd
+    bwd = pair
+    for s in range(nz // 2 - 1):
+        bwd = lax.ppermute(bwd, "tensor", TP_Z_BWD)
+        token_chunks[s + 1] = bwd
+    gathered = jnp.concatenate([token_chunks[k] for k in range(nz)], axis=0)
+    row_total = gathered.shape[0] * gathered.shape[1]
+    gathered = gathered.reshape(row_total, feature_count)
+    piece_rows = gate_weight.shape[0]
+    by_piece = gathered.reshape(row_total, dp_count, piece_rows)
+    normed = jnp.take(by_piece, piece_index, axis=1).reshape(row_total, feature_count)
+
+    gate_act = jnp.dot(normed, gate_full, preferred_element_type=jnp.float32)
+    up_act = jnp.dot(normed, up_full, preferred_element_type=jnp.float32)
+    hidden = (jax.nn.silu(gate_act) * up_act).astype(jnp.bfloat16)
+    term = jnp.dot(hidden, down_weight, preferred_element_type=jnp.float32).astype(jnp.bfloat16)
+    blocks = term.reshape(nz, nl, shard_rows, feature_count)
+
+    fwd = blocks[nz // 2]
+    for s in range(nz // 2):
+        got = lax.ppermute(fwd, "tensor", TP_Z_FWD)
+        if s < nz // 2 - 1:
+            fwd = (got.astype(jnp.float32) + blocks[nz // 2 - 1 - s].astype(jnp.float32)).astype(jnp.bfloat16)
+        else:
+            fwd_total = got
+    bwd = blocks[nz // 2 + 1]
+    for s in range(nz // 2 - 1):
+        got = lax.ppermute(bwd, "tensor", TP_Z_BWD)
+        if s < nz // 2 - 2:
+            bwd = (got.astype(jnp.float32) + blocks[nz // 2 + 2 + s].astype(jnp.float32)).astype(jnp.bfloat16)
+        else:
+            bwd_total = got
+    column_sum = (
+        fwd_total.astype(jnp.float32) + bwd_total.astype(jnp.float32) + blocks[0].astype(jnp.float32)
+    )
+    from_partner = lax.ppermute(column_sum[1].astype(jnp.bfloat16), "tensor", TP_L_SWAP)
+    total = column_sum[0] + from_partner.astype(jnp.float32)
+    return (local_batch.astype(jnp.float32) + total).astype(jnp.bfloat16)
 
 
 def solution(mesh):

time: 452 us -> 310 us (0.69)
  waiting for transfers between devices: 400 us -> 60.5 us
  starting transfers between devices: 14.5 us -> 161 us
  local copies, waits for them, and re-layouts: 2.29 us -> 64 us
  between operations: 13.8 us -> 1.81 us
    all_gather x3 -> x0, waiting for transfers between devices: 245 us -> none  [the longest x1 140 us: per_device(): lax.all_gather(travelling, 'tensor', axis=0, tiled=True)]
    ppermute x0 -> x42, starting transfers between devices: none -> 150 us  [the longest x7 40.3 us: per_device(): bwd = lax.ppermute(bwd, 'tensor', TP_Z_BWD)]
    reduce_scatter x1 -> x0, waiting for transfers between devices: 143 us -> none  [per_device(): lax.psum_scatter(rounded_term(hidden, down_weight).astype(jnp.bfloat16),...]
    ppermute x0 -> x42, waiting for transfers between devices: none -> 56.3 us  [the longest x8 28.5 us: per_device(): got = lax.ppermute(fwd, 'tensor', TP_Z_FWD)]
    unnamed x2 -> x73, local copies, waits for them, and re-layouts: 0.01 us -> 39.8 us
    gather x0 -> x2, local copies, waits for them, and re-layouts: none -> 11.4 us  [per_device(): jnp.take(by_piece, piece_index, axis=1).reshape(row_total, feature_count)]
    another operation x0 -> x5, local copies, waits for them, and re-layouts: none -> 5.22 us  [the longest x1 3.42 us: per_device(): by_piece = gathered.reshape(row_total, dp_count, piece_rows)]
  transfers between devices with their start and end apart: 6 -> 44, of which waited for: 6 -> 18; matrix products, arithmetic and copies ran while one was open for 2% -> 17% of each run, Pallas kernels for 0% -> 0%
where the time goes in v1:
time: 310 us; the launch traced here: 308 us
  starting transfers between devices  161 us (52%)
  local copies, waits for them, and re-layouts  64 us (21%)
  waiting for transfers between devices  60.5 us (20%)
  matrix products  14.2 us (5%)
  other arithmetic  6.55 us (2%)
    ppermute x7, starting transfers between devices, per_device(): bwd = lax.ppermute(bwd, 'tensor', TP_Z_BWD)  40.3 us
    unnamed x73, local copies, waits for them, and re-layouts  39.8 us
    ppermute x7, starting transfers between devices, per_device(): got = lax.ppermute(bwd, 'tensor', TP_Z_BWD)  37.6 us
    ppermute x8, waiting for transfers between devices, per_device(): got = lax.ppermute(fwd, 'tensor', TP_Z_FWD)  28.5 us
    ppermute x4, starting transfers between devices, y_ring(): fwd = lax.ppermute(fwd, 'dp', DP_Y_FWD)  19.3 us
    ppermute x8, waiting for transfers between devices, per_device(): fwd = lax.ppermute(fwd, 'tensor', TP_Z_FWD)  16.5 us
    ppermute x8, starting transfers between devices, per_device(): fwd = lax.ppermute(fwd, 'tensor', TP_Z_FWD)  15.5 us
    ppermute x8, starting transfers between devices, per_device(): got = lax.ppermute(fwd, 'tensor', TP_Z_FWD)  15.4 us
  transfers between devices with their start and end apart: 44, of which 18 were waited for; matrix products, arithmetic and copies ran while one was open for 17% of the time, Pallas kernels for 0%

profile of v1, /device:TPU:24, one launch (start us, length us, event | category | flops | bytes accessed | tf_op | source)
XLA Modules:
  0.0 308.1 jit_solution(15004875128750717115)
XLA Ops:
  0.0 7.6 %collective-permute-start.17 = (bf16[1,256,512]{2,1,0:T(8,128)(2,1)}, bf16[1,256,512]{2,1,0:T(8,128)(2,1)S(1)}, u32[]{:S(2)}, u32[]{:S(2)}) collective-permute-start(bf16[1,256,512]{2,1,0:T(8,128)(2,1)} %bitcast.224), channel_id=1, source_target_pairs={{0,128},{32,160},{64,192},{96,224},{128,256},{160,288},{192,320},{... | collective-permute-start | bytes 786440 | tf_op jit(solution)/shard_map/ppermute | solution.py:54
  12.1 6.6 %all-to-all-start = ((s32[16,1,2]{2,1,0:T(1,128)}), s32[16,1,2]{2,1,0:T(1,128)S(1)}, u32[]{:S(2)}, u32[]{:S(2)}) async-start(s32[16,1,2]{2,1,0:T(1,128)} %bitcast.2), calls=%async_computation | async-start | bytes 16384 | tf_op jit(solution)/shard_map/all_to_all | solution.py:120
  18.6 4.9 %collective-permute-start.21 = (bf16[1,256,512]{2,1,0:T(8,128)(2,1)}, bf16[1,256,512]{2,1,0:T(8,128)(2,1)S(1)}, u32[]{:S(2)}, u32[]{:S(2)}) collective-permute-start(bf16[1,256,512]{2,1,0:T(8,128)(2,1)} %bitcast.222), channel_id=1, source_target_pairs={{0,64},{32,96},{64,0},{96,32},{128,192},{160,224},{192,128},{224,1... | collective-permute-start | bytes 786440 | tf_op jit(solution)/shard_map/ppermute | solution.py:66
  30.1 4.8 %all-to-all-start.1 = ((bf16[16,2,4096]{2,1,0:T(2,128)(2,1)}), bf16[16,2,4096]{2,1,0:T(2,128)(2,1)S(1)}, u32[]{:S(2)}, u32[]{:S(2)}) async-start(bf16[16,2,4096]{2,1,0:T(2,128)(2,1)} %reshape.873), calls=%async_computation.1 | async-start | bytes 524288 | tf_op jit(solution)/shard_map/all_to_all | solution.py:113
  52.4 9.0 %collective-permute-start.1 = (bf16[2,16,4096]{2,1,0:T(8,128)(2,1)S(1)}, bf16[2,16,4096]{2,1,0:T(8,128)(2,1)S(1)}, u32[]{:S(2)}, u32[]{:S(2)}) collective-permute-start(bf16[2,16,4096]{2,1,0:T(8,128)(2,1)S(1)} %pad_maximum_fusion.2), channel_id=1, source_target_pairs={{0,15},{1,0},{2,1},{3,2},{4,3},{5,4},{6,5},{7,6},{8,7},{9,8},{10,9... | collective-permute-start | bytes 786440 | tf_op jit(solution)/shard_map/ppermute | solution.py:154
  69.9 5.1 %collective-permute-start.2 = (bf16[2,16,4096]{2,1,0:T(8,128)(2,1)S(1)}, bf16[2,16,4096]{2,1,0:T(8,128)(2,1)S(1)}, u32[]{:S(2)}, u32[]{:S(2)}) collective-permute-start(bf16[2,16,4096]{2,1,0:T(8,128)(2,1)S(1)} %collective-permute-done.1), channel_id=1, source_target_pairs={{0,15},{1,0},{2,1},{3,2},{4,3},{5,4},{6,5},{7,6},{8,7},{9,8},{10,9... | collective-permute-start | bytes 786440 | tf_op jit(solution)/shard_map/ppermute | solution.py:154
  82.8 4.8 %collective-permute-start.3 = (bf16[2,16,4096]{2,1,0:T(8,128)(2,1)S(1)}, bf16[2,16,4096]{2,1,0:T(8,128)(2,1)S(1)}, u32[]{:S(2)}, u32[]{:S(2)}) collective-permute-start(bf16[2,16,4096]{2,1,0:T(8,128)(2,1)S(1)} %collective-permute-done.2), channel_id=1, source_target_pairs={{0,15},{1,0},{2,1},{3,2},{4,3},{5,4},{6,5},{7,6},{8,7},{9,8},{10,9... | collective-permute-start | bytes 786440 | tf_op jit(solution)/shard_map/ppermute | solution.py:154
  91.5 5.6 %collective-permute-start.4 = (bf16[2,16,4096]{2,1,0:T(8,128)(2,1)S(1)}, bf16[2,16,4096]{2,1,0:T(8,128)(2,1)S(1)}, u32[]{:S(2)}, u32[]{:S(2)}) collective-permute-start(bf16[2,16,4096]{2,1,0:T(8,128)(2,1)S(1)} %collective-permute-done.3), channel_id=1, source_target_pairs={{0,15},{1,0},{2,1},{3,2},{4,3},{5,4},{6,5},{7,6},{8,7},{9,8},{10,9... | collective-permute-start | bytes 786440 | tf_op jit(solution)/shard_map/ppermute | solution.py:154
  102.7 5.1 %collective-permute-start.5 = (bf16[2,16,4096]{2,1,0:T(8,128)(2,1)S(1)}, bf16[2,16,4096]{2,1,0:T(8,128)(2,1)S(1)}, u32[]{:S(2)}, u32[]{:S(2)}) collective-permute-start(bf16[2,16,4096]{2,1,0:T(8,128)(2,1)S(1)} %collective-permute-done.4), channel_id=1, source_target_pairs={{0,15},{1,0},{2,1},{3,2},{4,3},{5,4},{6,5},{7,6},{8,7},{9,8},{10,9... | collective-permute-start | bytes 786440 | tf_op jit(solution)/shard_map/ppermute | solution.py:154
  117.1 4.9 %collective-permute-start.6 = (bf16[2,16,4096]{2,1,0:T(8,128)(2,1)S(1)}, bf16[2,16,4096]{2,1,0:T(8,128)(2,1)S(1)}, u32[]{:S(2)}, u32[]{:S(2)}) collective-permute-start(bf16[2,16,4096]{2,1,0:T(8,128)(2,1)S(1)} %collective-permute-done.5), channel_id=1, source_target_pairs={{0,15},{1,0},{2,1},{3,2},{4,3},{5,4},{6,5},{7,6},{8,7},{9,8},{10,9... | collective-permute-start | bytes 786440 | tf_op jit(solution)/shard_map/ppermute | solution.py:154
  128.2 5.6 %collective-permute-start.7 = (bf16[2,16,4096]{2,1,0:T(8,128)(2,1)S(1)}, bf16[2,16,4096]{2,1,0:T(8,128)(2,1)S(1)}, u32[]{:S(2)}, u32[]{:S(2)}) collective-permute-start(bf16[2,16,4096]{2,1,0:T(8,128)(2,1)S(1)} %collective-permute-done.6), channel_id=1, source_target_pairs={{0,15},{1,0},{2,1},{3,2},{4,3},{5,4},{6,5},{7,6},{8,7},{9,8},{10,9... | collective-permute-start | bytes 786440 | tf_op jit(solution)/shard_map/ppermute | solution.py:154
  135.8 8.8 %collective-permute-done.14 = bf16[2,16,4096]{2,1,0:T(8,128)(2,1)S(1)} collective-permute-done((bf16[2,16,4096]{2,1,0:T(8,128)(2,1)S(1)}, bf16[2,16,4096]{2,1,0:T(8,128)(2,1)S(1)}, u32[]{:S(2)}, u32[]{:S(2)}) %collective-permute-start.14) | collective-permute-done | bytes 262176 | tf_op jit(solution)/shard_map/ppermute | solution.py:150
  146.7 7.7 %collective-permute-done.15 = bf16[2,16,4096]{2,1,0:T(8,128)(2,1)S(1)} collective-permute-done((bf16[2,16,4096]{2,1,0:T(8,128)(2,1)S(1)}, bf16[2,16,4096]{2,1,0:T(8,128)(2,1)S(1)}, u32[]{:S(2)}, u32[]{:S(2)}) %collective-permute-start.15) | collective-permute-done | bytes 262176 | tf_op jit(solution)/shard_map/ppermute | solution.py:150
  159.5 5.0 %gather_fusion = bf16[16,512,256]{2,1,0:T(8,128)(2,1)} fusion(bf16[512,16,256]{2,0,1:T(8,128)(2,1)} %copy.14, s32[1024]{0:T(1024)S(1)} %pad_clamp_fusion), kind=kCustom, calls=%fused_computation | custom fusion | bytes 8388672 | tf_op jit(solution)/shard_map/jit(_take)/gather | solution.py:161
  164.5 6.4 %copy.15 = bf16[512,16,256]{0,2,1:T(8,128)(2,1)} copy(bf16[512,16,256]{2,0,1:T(8,128)(2,1)} %bitcast.219) | data formatting | bytes 8388608 | tf_op jit(solution)/shard_map/jit(_take)/gather | solution.py:161
  203.4 11.3 %convolution_convert_fusion = bf16[512,4096]{1,0:T(8,128)(2,1)} fusion(bf16[512,4096]{1,0:T(8,128)(2,1)} %param.11, f32[512,512]{1,0:T(8,128)S(1)} %fusion.55, bf16[512,4096]{0,1:T(8,128)(2,1)} %copy-done.2, bf16[4096,512]{1,0:T(8,128)(2,1)} %fusion.32), kind=kOutput, calls=%fused_computation.1 | convolution fusion | flops 4298637312 | bytes 17825792 | tf_op jit(solution)/shard_map/dot_general | solution.py:166
  219.1 5.1 %collective-permute-start.34 = (bf16[2,16,4096]{2,1,0:T(8,128)(2,1)S(1)}, bf16[2,16,4096]{2,1,0:T(8,128)(2,1)S(1)}, u32[]{:S(2)}, u32[]{:S(2)}) collective-permute-start(bf16[2,16,4096]{2,1,0:T(8,128)(2,1)S(1)} %bitcast.243), channel_id=1, source_target_pairs={{0,15},{1,0},{2,1},{3,2},{4,3},{5,4},{6,5},{7,6},{8,7},{9,8},{10,9... | collective-permute-start | bytes 786440 | tf_op jit(solution)/shard_map/ppermute | solution.py:178
  228.7 5.1 %collective-permute-start.35 = (bf16[2,16,4096]{2,1,0:T(8,128)(2,1)S(1)}, bf16[2,16,4096]{2,1,0:T(8,128)(2,1)S(1)}, u32[]{:S(2)}, u32[]{:S(2)}) collective-permute-start(bf16[2,16,4096]{2,1,0:T(8,128)(2,1)S(1)} %fusion.6), channel_id=1, source_target_pairs={{0,15},{1,0},{2,1},{3,2},{4,3},{5,4},{6,5},{7,6},{8,7},{9,8},{10,9... | collective-permute-start | bytes 786440 | tf_op jit(solution)/shard_map/ppermute | solution.py:178
  238.2 5.1 %collective-permute-start.36 = (bf16[2,16,4096]{2,1,0:T(8,128)(2,1)S(1)}, bf16[2,16,4096]{2,1,0:T(8,128)(2,1)S(1)}, u32[]{:S(2)}, u32[]{:S(2)}) collective-permute-start(bf16[2,16,4096]{2,1,0:T(8,128)(2,1)S(1)} %fusion.5), channel_id=1, source_target_pairs={{0,15},{1,0},{2,1},{3,2},{4,3},{5,4},{6,5},{7,6},{8,7},{9,8},{10,9... | collective-permute-start | bytes 786440 | tf_op jit(solution)/shard_map/ppermute | solution.py:178
  247.8 5.4 %collective-permute-start.37 = (bf16[2,16,4096]{2,1,0:T(8,128)(2,1)S(1)}, bf16[2,16,4096]{2,1,0:T(8,128)(2,1)S(1)}, u32[]{:S(2)}, u32[]{:S(2)}) collective-permute-start(bf16[2,16,4096]{2,1,0:T(8,128)(2,1)S(1)} %fusion.4), channel_id=1, source_target_pairs={{0,15},{1,0},{2,1},{3,2},{4,3},{5,4},{6,5},{7,6},{8,7},{9,8},{10,9... | collective-permute-start | bytes 786440 | tf_op jit(solution)/shard_map/ppermute | solution.py:178
  258.6 5.6 %collective-permute-start.38 = (bf16[2,16,4096]{2,1,0:T(8,128)(2,1)S(1)}, bf16[2,16,4096]{2,1,0:T(8,128)(2,1)S(1)}, u32[]{:S(2)}, u32[]{:S(2)}) collective-permute-start(bf16[2,16,4096]{2,1,0:T(8,128)(2,1)S(1)} %fusion.3), channel_id=1, source_target_pairs={{0,15},{1,0},{2,1},{3,2},{4,3},{5,4},{6,5},{7,6},{8,7},{9,8},{10,9... | collective-permute-start | bytes 786440 | tf_op jit(solution)/shard_map/ppermute | solution.py:178
  270.7 5.6 %collective-permute-start.39 = (bf16[2,16,4096]{2,1,0:T(8,128)(2,1)S(1)}, bf16[2,16,4096]{2,1,0:T(8,128)(2,1)S(1)}, u32[]{:S(2)}, u32[]{:S(2)}) collective-permute-start(bf16[2,16,4096]{2,1,0:T(8,128)(2,1)S(1)} %fusion.2), channel_id=1, source_target_pairs={{0,15},{1,0},{2,1},{3,2},{4,3},{5,4},{6,5},{7,6},{8,7},{9,8},{10,9... | collective-permute-start | bytes 786440 | tf_op jit(solution)/shard_map/ppermute | solution.py:178
  282.2 5.6 %collective-permute-start.40 = (bf16[2,16,4096]{2,1,0:T(8,128)(2,1)S(1)}, bf16[2,16,4096]{2,1,0:T(8,128)(2,1)S(1)}, u32[]{:S(2)}, u32[]{:S(2)}) collective-permute-start(bf16[2,16,4096]{2,1,0:T(8,128)(2,1)S(1)} %fusion.1), channel_id=1, source_target_pairs={{0,15},{1,0},{2,1},{3,2},{4,3},{5,4},{6,5},{7,6},{8,7},{9,8},{10,9... | collective-permute-start | bytes 786440 | tf_op jit(solution)/shard_map/ppermute | solution.py:178
  292.9 7.5 %collective-permute-done.33 = bf16[2,16,4096]{2,1,0:T(8,128)(2,1)S(1)} collective-permute-done((bf16[2,16,4096]{2,1,0:T(8,128)(2,1)S(1)}, bf16[2,16,4096]{2,1,0:T(8,128)(2,1)S(1)}, u32[]{:S(2)}, u32[]{:S(2)}) %collective-permute-start.33) | collective-permute-done | bytes 262176 | tf_op jit(solution)/shard_map/ppermute | solution.py:171
  (193 shorter events, 157.8 us)
Async XLA Ops:
  0.0 47.1 %collective-permute-start.17 = (bf16[1,256,512]{2,1,0:T(8,128)(2,1)}, bf16[1,256,512]{2,1,0:T(8,128)(2,1)S(1)}, u32[]{:S(2)}, u32[]{:S(2)}) collective-permute-start(bf16[1,256,512]{2,1,0:T(8,128)(2,1)} %bitcast.224), channel_id=1, source_target_pairs={{0,128},{32,160},{64,192},{96,224},{128,256},{160,288},{192,320},{... | collective-permute-start | bytes 786440 | tf_op jit(solution)/shard_map/ppermute | solution.py:54
  7.6 55.8 %collective-permute-start.16 = (bf16[1,256,512]{2,1,0:T(8,128)(2,1)}, bf16[1,256,512]{2,1,0:T(8,128)(2,1)S(1)}, u32[]{:S(2)}, u32[]{:S(2)}) collective-permute-start(bf16[1,256,512]{2,1,0:T(8,128)(2,1)} %bitcast.225), channel_id=1, source_target_pairs={{0,384},{32,416},{64,448},{96,480},{128,0},{160,32},{192,64},{224,... | collective-permute-start | bytes 786440 | tf_op jit(solution)/shard_map/ppermute | solution.py:57
  12.1 18.0 %all-to-all-start = ((s32[16,1,2]{2,1,0:T(1,128)}), s32[16,1,2]{2,1,0:T(1,128)S(1)}, u32[]{:S(2)}, u32[]{:S(2)}) async-start(s32[16,1,2]{2,1,0:T(1,128)} %bitcast.2), calls=%async_computation | async-start | bytes 16384 | tf_op jit(solution)/shard_map/all_to_all | solution.py:120
  18.6 25.9 %collective-permute-start.21 = (bf16[1,256,512]{2,1,0:T(8,128)(2,1)}, bf16[1,256,512]{2,1,0:T(8,128)(2,1)S(1)}, u32[]{:S(2)}, u32[]{:S(2)}) collective-permute-start(bf16[1,256,512]{2,1,0:T(8,128)(2,1)} %bitcast.222), channel_id=1, source_target_pairs={{0,64},{32,96},{64,0},{96,32},{128,192},{160,224},{192,128},{224,1... | collective-permute-start | bytes 786440 | tf_op jit(solution)/shard_map/ppermute | solution.py:66
  30.1 12.1 %all-to-all-start.1 = ((bf16[16,2,4096]{2,1,0:T(2,128)(2,1)}), bf16[16,2,4096]{2,1,0:T(2,128)(2,1)S(1)}, u32[]{:S(2)}, u32[]{:S(2)}) async-start(bf16[16,2,4096]{2,1,0:T(2,128)(2,1)} %reshape.873), calls=%async_computation.1 | async-start | bytes 524288 | tf_op jit(solution)/shard_map/all_to_all | solution.py:113
  44.6 37.3 %collective-permute-start.22 = (bf16[2,256,512]{2,1,0:T(8,128)(2,1)S(1)}, bf16[2,256,512]{2,1,0:T(8,128)(2,1)S(1)}, u32[]{:S(2)}, u32[]{:S(2)}) collective-permute-start(bf16[2,256,512]{2,1,0:T(8,128)(2,1)S(1)} %pad_maximum_fusion.1), channel_id=1, source_target_pairs={{0,384},{32,416},{64,448},{96,480},{128,0},{160,32},{192,64},{224,... | collective-permute-start | bytes 1572872 | tf_op jit(solution)/shard_map/ppermute | solution.py:57
  47.1 19.4 %collective-permute-start.18 = (bf16[1,256,512]{2,1,0:T(8,128)(2,1)S(1)}, bf16[1,256,512]{2,1,0:T(8,128)(2,1)S(1)}, u32[]{:S(2)}, u32[]{:S(2)}) collective-permute-start(bf16[1,256,512]{2,1,0:T(8,128)(2,1)S(1)} %collective-permute-done.17), channel_id=1, source_target_pairs={{0,128},{32,160},{64,192},{96,224},{128,256},{160,288},{192,320},{... | collective-permute-start | bytes 786440 | tf_op jit(solution)/shard_map/ppermute | solution.py:54
  52.4 17.4 %collective-permute-start.1 = (bf16[2,16,4096]{2,1,0:T(8,128)(2,1)S(1)}, bf16[2,16,4096]{2,1,0:T(8,128)(2,1)S(1)}, u32[]{:S(2)}, u32[]{:S(2)}) collective-permute-start(bf16[2,16,4096]{2,1,0:T(8,128)(2,1)S(1)} %pad_maximum_fusion.2), channel_id=1, source_target_pairs={{0,15},{1,0},{2,1},{3,2},{4,3},{5,4},{6,5},{7,6},{8,7},{9,8},{10,9... | collective-permute-start | bytes 786440 | tf_op jit(solution)/shard_map/ppermute | solution.py:154
  61.5 13.5 %collective-permute-start.8 = (bf16[2,16,4096]{2,1,0:T(8,128)(2,1)S(1)}, bf16[2,16,4096]{2,1,0:T(8,128)(2,1)S(1)}, u32[]{:S(2)}, u32[]{:S(2)}) collective-permute-start(bf16[2,16,4096]{2,1,0:T(8,128)(2,1)S(1)} %pad_maximum_fusion.2), channel_id=1, source_target_pairs={{0,1},{1,2},{2,3},{3,4},{4,5},{5,6},{6,7},{7,8},{8,9},{9,10},{10,1... | collective-permute-start | bytes 786440 | tf_op jit(solution)/shard_map/ppermute | solution.py:150
  63.5 14.4 %collective-permute-start.23 = (bf16[2,256,512]{2,1,0:T(8,128)(2,1)S(1)}, bf16[2,256,512]{2,1,0:T(8,128)(2,1)S(1)}, u32[]{:S(2)}, u32[]{:S(2)}) collective-permute-start(bf16[2,256,512]{2,1,0:T(8,128)(2,1)S(1)} %pad_maximum_fusion.1), channel_id=1, source_target_pairs={{0,128},{32,160},{64,192},{96,224},{128,256},{160,288},{192,320},{... | collective-permute-start | bytes 1572872 | tf_op jit(solution)/shard_map/ppermute | solution.py:54
  66.7 43.1 %collective-permute-start.19 = (bf16[4,256,512]{2,1,0:T(8,128)(2,1)S(1)}, bf16[4,256,512]{2,1,0:T(8,128)(2,1)S(1)}, u32[]{:S(2)}, u32[]{:S(2)}) collective-permute-start(bf16[4,256,512]{2,1,0:T(8,128)(2,1)S(1)} %pad_maximum_fusion), channel_id=1, source_target_pairs={{0,64},{32,96},{64,0},{96,32},{128,192},{160,224},{192,128},{224,1... | collective-permute-start | bytes 3145736 | tf_op jit(solution)/shard_map/ppermute | solution.py:66
  69.9 12.9 %collective-permute-start.2 = (bf16[2,16,4096]{2,1,0:T(8,128)(2,1)S(1)}, bf16[2,16,4096]{2,1,0:T(8,128)(2,1)S(1)}, u32[]{:S(2)}, u32[]{:S(2)}) collective-permute-start(bf16[2,16,4096]{2,1,0:T(8,128)(2,1)S(1)} %collective-permute-done.1), channel_id=1, source_target_pairs={{0,15},{1,0},{2,1},{3,2},{4,3},{5,4},{6,5},{7,6},{8,7},{9,8},{10,9... | collective-permute-start | bytes 786440 | tf_op jit(solution)/shard_map/ppermute | solution.py:154
  75.0 12.6 %collective-permute-start.9 = (bf16[2,16,4096]{2,1,0:T(8,128)(2,1)S(1)}, bf16[2,16,4096]{2,1,0:T(8,128)(2,1)S(1)}, u32[]{:S(2)}, u32[]{:S(2)}) collective-permute-start(bf16[2,16,4096]{2,1,0:T(8,128)(2,1)S(1)} %collective-permute-done.8), channel_id=1, source_target_pairs={{0,1},{1,2},{2,3},{3,4},{4,5},{5,6},{6,7},{7,8},{8,9},{9,10},{10,1... | collective-permute-start | bytes 786440 | tf_op jit(solution)/shard_map/ppermute | solution.py:150
  77.9 21.1 %collective-permute-start.24 = (bf16[2,256,512]{2,1,0:T(8,128)(2,1)S(1)}, bf16[2,256,512]{2,1,0:T(8,128)(2,1)S(1)}, u32[]{:S(2)}, u32[]{:S(2)}) collective-permute-start(bf16[2,256,512]{2,1,0:T(8,128)(2,1)S(1)} %collective-permute-done.23), channel_id=1, source_target_pairs={{0,128},{32,160},{64,192},{96,224},{128,256},{160,288},{192,320},{... | collective-permute-start | bytes 1572872 | tf_op jit(solution)/shard_map/ppermute | solution.py:54
  100.8 72.9 %collective-permute-start.25 = (bf16[8,256,512]{2,1,0:T(8,128)(2,1)}, bf16[8,256,512]{2,1,0:T(8,128)(2,1)}, u32[]{:S(2)}, u32[]{:S(2)}) collective-permute-start(bf16[8,256,512]{2,1,0:T(8,128)(2,1)} %constant_dynamic-update-slice_fusion.22), channel_id=1, source_target_pairs={{0,32},{32,0},{64,96},{96,64},{128,160},{160,128},{192,224},{224,1... | collective-permute-start | bytes 6291464 | tf_op jit(solution)/shard_map/ppermute | solution.py:66
  102.7 14.4 %collective-permute-start.5 = (bf16[2,16,4096]{2,1,0:T(8,128)(2,1)S(1)}, bf16[2,16,4096]{2,1,0:T(8,128)(2,1)S(1)}, u32[]{:S(2)}, u32[]{:S(2)}) collective-permute-start(bf16[2,16,4096]{2,1,0:T(8,128)(2,1)S(1)} %collective-permute-done.4), channel_id=1, source_target_pairs={{0,15},{1,0},{2,1},{3,2},{4,3},{5,4},{6,5},{7,6},{8,7},{9,8},{10,9... | collective-permute-start | bytes 786440 | tf_op jit(solution)/shard_map/ppermute | solution.py:154
  107.9 14.1 %collective-permute-start.12 = (bf16[2,16,4096]{2,1,0:T(8,128)(2,1)S(1)}, bf16[2,16,4096]{2,1,0:T(8,128)(2,1)S(1)}, u32[]{:S(2)}, u32[]{:S(2)}) collective-permute-start(bf16[2,16,4096]{2,1,0:T(8,128)(2,1)S(1)} %collective-permute-done.11), channel_id=1, source_target_pairs={{0,1},{1,2},{2,3},{3,4},{4,5},{5,6},{6,7},{7,8},{8,9},{9,10},{10,1... | collective-permute-start | bytes 786440 | tf_op jit(solution)/shard_map/ppermute | solution.py:150
  115.0 69.9 %collective-permute-start.20 = (bf16[8,256,512]{2,1,0:T(8,128)(2,1)}, bf16[8,256,512]{2,1,0:T(8,128)(2,1)}, u32[]{:S(2)}, u32[]{:S(2)}) collective-permute-start(bf16[8,256,512]{2,1,0:T(8,128)(2,1)} %slice_dynamic-update-slice_fusion), channel_id=1, source_target_pairs={{0,32},{32,0},{64,96},{96,64},{128,160},{160,128},{192,224},{224,1... | collective-permute-start | bytes 6291464 | tf_op jit(solution)/shard_map/ppermute | solution.py:66
  122.0 11.8 %collective-permute-start.13 = (bf16[2,16,4096]{2,1,0:T(8,128)(2,1)S(1)}, bf16[2,16,4096]{2,1,0:T(8,128)(2,1)S(1)}, u32[]{:S(2)}, u32[]{:S(2)}) collective-permute-start(bf16[2,16,4096]{2,1,0:T(8,128)(2,1)S(1)} %collective-permute-done.12), channel_id=1, source_target_pairs={{0,1},{1,2},{2,3},{3,4},{4,5},{5,6},{6,7},{7,8},{8,9},{9,10},{10,1... | collective-permute-start | bytes 786440 | tf_op jit(solution)/shard_map/ppermute | solution.py:150
  128.2 18.5 %collective-permute-start.7 = (bf16[2,16,4096]{2,1,0:T(8,128)(2,1)S(1)}, bf16[2,16,4096]{2,1,0:T(8,128)(2,1)S(1)}, u32[]{:S(2)}, u32[]{:S(2)}) collective-permute-start(bf16[2,16,4096]{2,1,0:T(8,128)(2,1)S(1)} %collective-permute-done.6), channel_id=1, source_target_pairs={{0,15},{1,0},{2,1},{3,2},{4,3},{5,4},{6,5},{7,6},{8,7},{9,8},{10,9... | collective-permute-start | bytes 786440 | tf_op jit(solution)/shard_map/ppermute | solution.py:154
  256.4 11.8 %collective-permute-start.30 = (bf16[2,16,4096]{2,1,0:T(8,128)(2,1)S(1)}, bf16[2,16,4096]{2,1,0:T(8,128)(2,1)S(1)}, u32[]{:S(2)}, u32[]{:S(2)}) collective-permute-start(bf16[2,16,4096]{2,1,0:T(8,128)(2,1)S(1)} %fusion.10), channel_id=1, source_target_pairs={{0,1},{1,2},{2,3},{3,4},{4,5},{5,6},{6,7},{7,8},{8,9},{9,10},{10,1... | collective-permute-start | bytes 786440 | tf_op jit(solution)/shard_map/ppermute | solution.py:171
  258.6 12.0 %collective-permute-start.38 = (bf16[2,16,4096]{2,1,0:T(8,128)(2,1)S(1)}, bf16[2,16,4096]{2,1,0:T(8,128)(2,1)S(1)}, u32[]{:S(2)}, u32[]{:S(2)}) collective-permute-start(bf16[2,16,4096]{2,1,0:T(8,128)(2,1)S(1)} %fusion.3), channel_id=1, source_target_pairs={{0,15},{1,0},{2,1},{3,2},{4,3},{5,4},{6,5},{7,6},{8,7},{9,8},{10,9... | collective-permute-start | bytes 786440 | tf_op jit(solution)/shard_map/ppermute | solution.py:178
  268.3 11.6 %collective-permute-start.31 = (bf16[2,16,4096]{2,1,0:T(8,128)(2,1)S(1)}, bf16[2,16,4096]{2,1,0:T(8,128)(2,1)S(1)}, u32[]{:S(2)}, u32[]{:S(2)}) collective-permute-start(bf16[2,16,4096]{2,1,0:T(8,128)(2,1)S(1)} %fusion.9), channel_id=1, source_target_pairs={{0,1},{1,2},{2,3},{3,4},{4,5},{5,6},{6,7},{7,8},{8,9},{9,10},{10,1... | collective-permute-start | bytes 786440 | tf_op jit(solution)/shard_map/ppermute | solution.py:171
  270.7 11.4 %collective-permute-start.39 = (bf16[2,16,4096]{2,1,0:T(8,128)(2,1)S(1)}, bf16[2,16,4096]{2,1,0:T(8,128)(2,1)S(1)}, u32[]{:S(2)}, u32[]{:S(2)}) collective-permute-start(bf16[2,16,4096]{2,1,0:T(8,128)(2,1)S(1)} %fusion.2), channel_id=1, source_target_pairs={{0,15},{1,0},{2,1},{3,2},{4,3},{5,4},{6,5},{7,6},{8,7},{9,8},{10,9... | collective-permute-start | bytes 786440 | tf_op jit(solution)/shard_map/ppermute | solution.py:178
  (28 other events, 474.0 us)

commit v2 on v1

--- a/solution.py
+++ b/solution.py
@@ -45,43 +45,27 @@
     ).astype(jnp.bfloat16)
 
 
-def y_ring(chunks, key_of):
-    out = dict(chunks)
-    stacked = jnp.stack([chunks[k] for k in sorted(chunks)])
-    keys = sorted(chunks)
-    fwd = stacked
-    for s in range(2):
-        fwd = lax.ppermute(fwd, "dp", DP_Y_FWD)
-        for i, k in enumerate(keys):
-            out[key_of(k, DP_SUB[0] - 1 - s)] = fwd[i]
-    bwd = lax.ppermute(stacked, "dp", DP_Y_BWD)
-    for i, k in enumerate(keys):
-        out[key_of(k, 1)] = bwd[i]
-    return out
-
-
-def swap(chunks, perm, key_of):
-    out = dict(chunks)
-    keys = sorted(chunks)
-    got = lax.ppermute(jnp.stack([chunks[k] for k in keys]), "dp", perm)
-    for i, k in enumerate(keys):
-        out[key_of(k)] = got[i]
-    return out
-
-
-def gather_weight(piece, y_first):
-    set_y = lambda k, v: (v, k[1], k[2])
-    set_x = lambda k: (k[0], 1, k[2])
-    set_c = lambda k: (k[0], k[1], 1)
-    chunks = {(0, 0, 0): piece}
-    if y_first:
-        chunks = y_ring(chunks, set_y)
-        chunks = swap(chunks, DP_X_SWAP, set_x)
-    else:
-        chunks = swap(chunks, DP_X_SWAP, set_x)
-        chunks = y_ring(chunks, set_y)
-    chunks = swap(chunks, DP_C_SWAP, set_c)
-    return chunks
+def gather_pieces(piece):
+    ny = DP_SUB[0]
+    own = piece[None]
+    across = lax.ppermute(own, "dp", DP_X_SWAP)
+    pair = jnp.concatenate([own, across])
+    pair_keys = [(0, 0, 0), (0, 1, 0)]
+    fwd1 = lax.ppermute(pair, "dp", DP_Y_FWD)
+    fwd2 = lax.ppermute(fwd1, "dp", DP_Y_FWD)
+    bwd1 = lax.ppermute(pair, "dp", DP_Y_BWD)
+    shift = lambda keys, dy: [((k[0] + dy) % ny, k[1], k[2]) for k in keys]
+    chip = jnp.concatenate([pair, fwd1, fwd2, bwd1])
+    chip_keys = pair_keys + shift(pair_keys, ny - 1) + shift(pair_keys, ny - 2) + shift(pair_keys, 1)
+    other_core = lax.ppermute(chip, "dp", DP_C_SWAP)
+    return [
+        ([(0, 0, 0)], own),
+        ([(0, 1, 0)], across),
+        (shift(pair_keys, ny - 1), fwd1),
+        (shift(pair_keys, ny - 2), fwd2),
+        (shift(pair_keys, 1), bwd1),
+        ([(k[0], k[1], 1) for k in chip_keys], other_core),
+    ]
 
 
 def per_device(loader_rows, row_counts, row_targets, gate_weight, up_weight, down_weight):
@@ -109,40 +93,38 @@
         pick_matrix.astype(jnp.bfloat16), slot_rows, preferred_element_type=jnp.float32
     ).astype(jnp.bfloat16)
     out_place = jnp.sum(jnp.where(pick_matrix, row_place[None, :] + 1, 0), axis=1) - 1
-    arrived, arrived_place = (
-        lax.all_to_all(
-            outgoing.reshape(dp_count, per_peer, feature_count),
-            "dp",
-            split_axis=0,
-            concat_axis=0,
-            tiled=True,
-        ),
-        lax.all_to_all(
-            out_place.reshape(dp_count, per_peer), "dp", split_axis=0, concat_axis=0, tiled=True
-        ),
-    )
+    place_cols = jnp.broadcast_to(out_place.astype(jnp.bfloat16)[:, None], (slot_count, 128))
+    arrived = lax.all_to_all(
+        jnp.concatenate([outgoing, place_cols], axis=1).reshape(dp_count, per_peer, feature_count + 128),
+        "dp",
+        split_axis=0,
+        concat_axis=0,
+        tiled=True,
+    ).reshape(slot_count, feature_count + 128)
+    arrived_place = arrived[:, feature_count].astype(jnp.int32)
     land_matrix = (
-        arrived_place.reshape(slot_count)[None, :]
-        == jnp.arange(shard_rows, dtype=jnp.int32)[:, None]
+        arrived_place[None, :] == jnp.arange(shard_rows, dtype=jnp.int32)[:, None]
     ).astype(jnp.bfloat16)
     local_batch = jnp.dot(
-        land_matrix, arrived.reshape(slot_count, feature_count), preferred_element_type=jnp.float32
+        land_matrix, arrived[:, :feature_count], preferred_element_type=jnp.float32
     ).astype(jnp.bfloat16)
 
-    gate_chunks = gather_weight(gate_weight, True)
-    up_chunks = gather_weight(up_weight, False)
-    keys = sorted(gate_chunks)
+    ff_cols = gate_weight.shape[1]
+    piece_rows = gate_weight.shape[0]
+    buffers = gather_pieces(jnp.concatenate([gate_weight, up_weight], axis=1))
+    keys = [k for ks, _ in buffers for k in ks]
     ny, nx, nc = DP_SUB
     me = lax.axis_index("dp")
     my_y, my_x, my_c = me // (nx * nc), (me // nc) % nx, me % nc
     piece_index = jnp.stack(
         [((my_y + k[0]) % ny) * nx * nc + ((my_x + k[1]) % nx) * nc + (my_c + k[2]) % nc for k in keys]
     ).astype(jnp.int32)
-    gate_full = jnp.concatenate([gate_chunks[k] for k in keys], axis=0)
-    up_full = jnp.concatenate([up_chunks[k] for k in keys], axis=0)
 
     nl, nz = TP_SUB
     travelling = normalize(local_batch)
+    travelling = jnp.take(
+        travelling.reshape(shard_rows, dp_count, piece_rows), piece_index, axis=1
+    ).reshape(shard_rows, feature_count)
     pair = jnp.stack([travelling, lax.ppermute(travelling, "tensor", TP_L_SWAP)])
     token_chunks = {0: pair}
     fwd = pair
@@ -155,13 +137,21 @@
         token_chunks[s + 1] = bwd
     gathered = jnp.concatenate([token_chunks[k] for k in range(nz)], axis=0)
     row_total = gathered.shape[0] * gathered.shape[1]
-    gathered = gathered.reshape(row_total, feature_count)
-    piece_rows = gate_weight.shape[0]
-    by_piece = gathered.reshape(row_total, dp_count, piece_rows)
-    normed = jnp.take(by_piece, piece_index, axis=1).reshape(row_total, feature_count)
+    normed = gathered.reshape(row_total, feature_count)
 
-    gate_act = jnp.dot(normed, gate_full, preferred_element_type=jnp.float32)
-    up_act = jnp.dot(normed, up_full, preferred_element_type=jnp.float32)
+    act = None
+    col = 0
+    for ks, buf in buffers:
+        width = len(ks) * piece_rows
+        part = jnp.dot(
+            normed[:, col : col + width],
+            buf.reshape(width, 2 * ff_cols),
+            preferred_element_type=jnp.float32,
+        )
+        act = part if act is None else act + part
+        col += width
+    gate_act = act[:, :ff_cols]
+    up_act = act[:, ff_cols:]
     hidden = (jax.nn.silu(gate_act) * up_act).astype(jnp.bfloat16)
     term = jnp.dot(hidden, down_weight, preferred_element_type=jnp.float32).astype(jnp.bfloat16)
     blocks = term.reshape(nz, nl, shard_rows, feature_count)

time: 310 us -> 240 us (0.77)
  local copies, waits for them, and re-layouts: 64 us -> 10.8 us
  starting transfers between devices: 161 us -> 141 us
  waiting for transfers between devices: 60.5 us -> 72.7 us
  matrix products: 14.2 us -> 8.49 us
  other arithmetic: 6.55 us -> 3.31 us
    unnamed x73 -> x24, local copies, waits for them, and re-layouts: 39.8 us -> 6.26 us
    ppermute x10 -> x5, starting transfers between devices: 35.7 us -> 16.3 us  [the longest x1 4.89 us: gather_pieces(): across = lax.ppermute(own, 'dp', DP_X_SWAP)]
    gather x2 -> x4, local copies, waits for them, and re-layouts: 11.4 us -> 0.68 us  [per_device(): jnp.take(travelling.reshape(shard_rows, dp_count, piece_rows), piece_inde...]
    ppermute x1, waiting for transfers between devices: 0.01 us -> 9.57 us  [per_device(): lax.ppermute(travelling, 'tensor', TP_L_SWAP)]
    dot_general x1, matrix products: 11.3 us -> 2.37 us  [per_device(): jnp.dot(hidden, down_weight, preferred_element_type=jnp.float32)]
    another operation x3 -> x0, local copies, waits for them, and re-layouts: 5 us -> none  [the longest x1 3.42 us: per_device(): by_piece = gathered.reshape(row_total, dp_count, piece_rows)]
    all_to_all x2 -> x1, waiting for transfers between devices: 4.23 us -> 0.01 us  [per_device(): lax.all_to_all(jnp.concatenate([outgoing, place_cols], axis=1).reshape(dp...]
    ppermute x10 -> x5, waiting for transfers between devices: 0.92 us -> 4.81 us  [the longest x1 4.8 us: gather_pieces(): other_core = lax.ppermute(chip, 'dp', DP_C_SWAP)]
  transfers between devices with their start and end apart: 44 -> 38, of which waited for: 18 -> 18; matrix products, arithmetic and copies ran while one was open for 17% -> 5% of each run, Pallas kernels for 0% -> 0%
where the time goes in v2:
time: 240 us; the launch traced here: 238 us
  starting transfers between devices  141 us (59%)
  waiting for transfers between devices  72.7 us (30%)
  local copies, waits for them, and re-layouts  10.8 us (4%)
  matrix products  8.49 us (4%)
  other arithmetic  3.31 us (1%)
    ppermute x7, starting transfers between devices, per_device(): bwd = lax.ppermute(bwd, 'tensor', TP_Z_BWD)  43.2 us
    ppermute x7, starting transfers between devices, per_device(): got = lax.ppermute(bwd, 'tensor', TP_Z_BWD)  36.2 us
    ppermute x8, waiting for transfers between devices, per_device(): got = lax.ppermute(fwd, 'tensor', TP_Z_FWD)  28.3 us
    ppermute x8, waiting for transfers between devices, per_device(): fwd = lax.ppermute(fwd, 'tensor', TP_Z_FWD)  17.8 us
    ppermute x8, starting transfers between devices, per_device(): got = lax.ppermute(fwd, 'tensor', TP_Z_FWD)  15.4 us
    ppermute x8, starting transfers between devices, per_device(): fwd = lax.ppermute(fwd, 'tensor', TP_Z_FWD)  15.3 us
    ppermute x1, waiting for transfers between devices, per_device(): lax.ppermute(travelling, 'tensor', TP_L_SWAP)  9.57 us
    all_to_all x1, starting transfers between devices, per_device(): lax.all_to_all(jnp.concatenate([outgoing, place_cols], axis=1).reshape(dp...  8.99 us
  transfers between devices with their start and end apart: 38, of which 18 were waited for; matrix products, arithmetic and copies ran while one was open for 5% of the time, Pallas kernels for 0%

profile of v2, /device:TPU:24, one launch (start us, length us, event | category | flops | bytes accessed | tf_op | source)
XLA Modules:
  0.0 237.5 jit_solution(14514033915709537813)
XLA Ops:
  3.0 9.0 %all-to-all-start = ((bf16[16,2,4224]{2,1,0:T(2,128)(2,1)}), bf16[16,2,4224]{2,1,0:T(2,128)(2,1)S(1)}, u32[]{:S(2)}, u32[]{:S(2)}) async-start(bf16[16,2,4224]{2,1,0:T(2,128)(2,1)} %reshape.916), calls=%async_computation | async-start | bytes 540672 | tf_op jit(solution)/shard_map/all_to_all | solution.py:97
  13.9 4.9 %collective-permute-start.16 = (bf16[1,256,1024]{2,1,0:T(8,128)(2,1)S(1)}, bf16[1,256,1024]{2,1,0:T(8,128)(2,1)S(1)}, u32[]{:S(2)}, u32[]{:S(2)}) collective-permute-start(bf16[1,256,1024]{2,1,0:T(8,128)(2,1)S(1)} %bitcast.119), channel_id=1, source_target_pairs={{0,64},{32,96},{64,0},{96,32},{128,192},{160,224},{192,128},{224,1... | collective-permute-start | bytes 1572872 | tf_op jit(solution)/shard_map/ppermute | solution.py:51
  23.5 9.6 %collective-permute-done = bf16[16,4096]{1,0:T(8,128)(2,1)S(1)} collective-permute-done((bf16[16,4096]{1,0:T(8,128)(2,1)S(1)}, bf16[16,4096]{1,0:T(8,128)(2,1)S(1)}, u32[]{:S(2)}, u32[]{:S(2)}) %collective-permute-start) | collective-permute-done | bytes 131104 | tf_op jit(solution)/shard_map/ppermute | solution.py:128
  33.1 10.6 %collective-permute-start.1 = (bf16[2,16,4096]{2,1,0:T(8,128)(2,1)S(1)}, bf16[2,16,4096]{2,1,0:T(8,128)(2,1)S(1)}, u32[]{:S(2)}, u32[]{:S(2)}) collective-permute-start(bf16[2,16,4096]{2,1,0:T(8,128)(2,1)S(1)} %pad_maximum_fusion.2), channel_id=1, source_target_pairs={{0,15},{1,0},{2,1},{3,2},{4,3},{5,4},{6,5},{7,6},{8,7},{9,8},{10,9... | collective-permute-start | bytes 786440 | tf_op jit(solution)/shard_map/ppermute | solution.py:136
  52.5 5.1 %collective-permute-start.2 = (bf16[2,16,4096]{2,1,0:T(8,128)(2,1)S(1)}, bf16[2,16,4096]{2,1,0:T(8,128)(2,1)S(1)}, u32[]{:S(2)}, u32[]{:S(2)}) collective-permute-start(bf16[2,16,4096]{2,1,0:T(8,128)(2,1)S(1)} %collective-permute-done.1), channel_id=1, source_target_pairs={{0,15},{1,0},{2,1},{3,2},{4,3},{5,4},{6,5},{7,6},{8,7},{9,8},{10,9... | collective-permute-start | bytes 786440 | tf_op jit(solution)/shard_map/ppermute | solution.py:136
  61.6 5.6 %collective-permute-start.3 = (bf16[2,16,4096]{2,1,0:T(8,128)(2,1)S(1)}, bf16[2,16,4096]{2,1,0:T(8,128)(2,1)S(1)}, u32[]{:S(2)}, u32[]{:S(2)}) collective-permute-start(bf16[2,16,4096]{2,1,0:T(8,128)(2,1)S(1)} %collective-permute-done.2), channel_id=1, source_target_pairs={{0,15},{1,0},{2,1},{3,2},{4,3},{5,4},{6,5},{7,6},{8,7},{9,8},{10,9... | collective-permute-start | bytes 786440 | tf_op jit(solution)/shard_map/ppermute | solution.py:136
  71.0 5.6 %collective-permute-start.4 = (bf16[2,16,4096]{2,1,0:T(8,128)(2,1)S(1)}, bf16[2,16,4096]{2,1,0:T(8,128)(2,1)S(1)}, u32[]{:S(2)}, u32[]{:S(2)}) collective-permute-start(bf16[2,16,4096]{2,1,0:T(8,128)(2,1)S(1)} %collective-permute-done.3), channel_id=1, source_target_pairs={{0,15},{1,0},{2,1},{3,2},{4,3},{5,4},{6,5},{7,6},{8,7},{9,8},{10,9... | collective-permute-start | bytes 786440 | tf_op jit(solution)/shard_map/ppermute | solution.py:136
  80.5 5.6 %collective-permute-start.5 = (bf16[2,16,4096]{2,1,0:T(8,128)(2,1)S(1)}, bf16[2,16,4096]{2,1,0:T(8,128)(2,1)S(1)}, u32[]{:S(2)}, u32[]{:S(2)}) collective-permute-start(bf16[2,16,4096]{2,1,0:T(8,128)(2,1)S(1)} %collective-permute-done.4), channel_id=1, source_target_pairs={{0,15},{1,0},{2,1},{3,2},{4,3},{5,4},{6,5},{7,6},{8,7},{9,8},{10,9... | collective-permute-start | bytes 786440 | tf_op jit(solution)/shard_map/ppermute | solution.py:136
  88.1 3.7 %collective-permute-start.18 = (bf16[2,256,1024]{2,1,0:T(8,128)(2,1)S(1)}, bf16[2,256,1024]{2,1,0:T(8,128)(2,1)S(1)}, u32[]{:S(2)}, u32[]{:S(2)}) collective-permute-start(bf16[2,256,1024]{2,1,0:T(8,128)(2,1)S(1)} %collective-permute-done.17), channel_id=1, source_target_pairs={{0,128},{32,160},{64,192},{96,224},{128,256},{160,288},{192,320},{... | collective-permute-start | bytes 3145736 | tf_op jit(solution)/shard_map/ppermute | solution.py:55
  92.8 5.1 %collective-permute-start.6 = (bf16[2,16,4096]{2,1,0:T(8,128)(2,1)S(1)}, bf16[2,16,4096]{2,1,0:T(8,128)(2,1)S(1)}, u32[]{:S(2)}, u32[]{:S(2)}) collective-permute-start(bf16[2,16,4096]{2,1,0:T(8,128)(2,1)S(1)} %collective-permute-done.5), channel_id=1, source_target_pairs={{0,15},{1,0},{2,1},{3,2},{4,3},{5,4},{6,5},{7,6},{8,7},{9,8},{10,9... | collective-permute-start | bytes 786440 | tf_op jit(solution)/shard_map/ppermute | solution.py:136
  102.7 5.6 %collective-permute-start.7 = (bf16[2,16,4096]{2,1,0:T(8,128)(2,1)S(1)}, bf16[2,16,4096]{2,1,0:T(8,128)(2,1)S(1)}, u32[]{:S(2)}, u32[]{:S(2)}) collective-permute-start(bf16[2,16,4096]{2,1,0:T(8,128)(2,1)S(1)} %collective-permute-done.6), channel_id=1, source_target_pairs={{0,15},{1,0},{2,1},{3,2},{4,3},{5,4},{6,5},{7,6},{8,7},{9,8},{10,9... | collective-permute-start | bytes 786440 | tf_op jit(solution)/shard_map/ppermute | solution.py:136
  110.6 10.0 %collective-permute-done.14 = bf16[2,16,4096]{2,1,0:T(8,128)(2,1)S(1)} collective-permute-done((bf16[2,16,4096]{2,1,0:T(8,128)(2,1)S(1)}, bf16[2,16,4096]{2,1,0:T(8,128)(2,1)S(1)}, u32[]{:S(2)}, u32[]{:S(2)}) %collective-permute-start.14) | collective-permute-done | bytes 262176 | tf_op jit(solution)/shard_map/ppermute | solution.py:132
  122.5 7.5 %collective-permute-done.15 = bf16[2,16,4096]{2,1,0:T(8,128)(2,1)S(1)} collective-permute-done((bf16[2,16,4096]{2,1,0:T(8,128)(2,1)S(1)}, bf16[2,16,4096]{2,1,0:T(8,128)(2,1)S(1)}, u32[]{:S(2)}, u32[]{:S(2)}) %collective-permute-start.15) | collective-permute-done | bytes 262176 | tf_op jit(solution)/shard_map/ppermute | solution.py:132
  136.6 4.8 %collective-permute-done.20 = bf16[8,256,1024]{2,1,0:T(8,128)(2,1)S(1)} collective-permute-done((bf16[8,256,1024]{2,1,0:T(8,128)(2,1)}, bf16[8,256,1024]{2,1,0:T(8,128)(2,1)S(1)}, u32[]{:S(2)}, u32[]{:S(2)}) %collective-permute-start.20) | collective-permute-done | bytes 4194336 | tf_op jit(solution)/shard_map/ppermute | solution.py:60
  150.7 5.1 %collective-permute-start.29 = (bf16[2,16,4096]{2,1,0:T(8,128)(2,1)S(1)}, bf16[2,16,4096]{2,1,0:T(8,128)(2,1)S(1)}, u32[]{:S(2)}, u32[]{:S(2)}) collective-permute-start(bf16[2,16,4096]{2,1,0:T(8,128)(2,1)S(1)} %bitcast.150), channel_id=1, source_target_pairs={{0,15},{1,0},{2,1},{3,2},{4,3},{5,4},{6,5},{7,6},{8,7},{9,8},{10,9... | collective-permute-start | bytes 786440 | tf_op jit(solution)/shard_map/ppermute | solution.py:168
  155.9 4.4 %collective-permute-done.21 = bf16[2,16,4096]{2,1,0:T(8,128)(2,1)S(1)} collective-permute-done((bf16[2,16,4096]{2,1,0:T(8,128)(2,1)S(1)}, bf16[2,16,4096]{2,1,0:T(8,128)(2,1)S(1)}, u32[]{:S(2)}, u32[]{:S(2)}) %collective-permute-start.21) | collective-permute-done | bytes 262176 | tf_op jit(solution)/shard_map/ppermute | solution.py:161
  162.3 5.1 %collective-permute-start.30 = (bf16[2,16,4096]{2,1,0:T(8,128)(2,1)S(1)}, bf16[2,16,4096]{2,1,0:T(8,128)(2,1)S(1)}, u32[]{:S(2)}, u32[]{:S(2)}) collective-permute-start(bf16[2,16,4096]{2,1,0:T(8,128)(2,1)S(1)} %fusion.15), channel_id=1, source_target_pairs={{0,15},{1,0},{2,1},{3,2},{4,3},{5,4},{6,5},{7,6},{8,7},{9,8},{10,9... | collective-permute-start | bytes 786440 | tf_op jit(solution)/shard_map/ppermute | solution.py:168
  173.1 5.1 %collective-permute-start.31 = (bf16[2,16,4096]{2,1,0:T(8,128)(2,1)S(1)}, bf16[2,16,4096]{2,1,0:T(8,128)(2,1)S(1)}, u32[]{:S(2)}, u32[]{:S(2)}) collective-permute-start(bf16[2,16,4096]{2,1,0:T(8,128)(2,1)S(1)} %fusion.14), channel_id=1, source_target_pairs={{0,15},{1,0},{2,1},{3,2},{4,3},{5,4},{6,5},{7,6},{8,7},{9,8},{10,9... | collective-permute-start | bytes 786440 | tf_op jit(solution)/shard_map/ppermute | solution.py:168
  182.8 5.1 %collective-permute-start.32 = (bf16[2,16,4096]{2,1,0:T(8,128)(2,1)S(1)}, bf16[2,16,4096]{2,1,0:T(8,128)(2,1)S(1)}, u32[]{:S(2)}, u32[]{:S(2)}) collective-permute-start(bf16[2,16,4096]{2,1,0:T(8,128)(2,1)S(1)} %fusion.13), channel_id=1, source_target_pairs={{0,15},{1,0},{2,1},{3,2},{4,3},{5,4},{6,5},{7,6},{8,7},{9,8},{10,9... | collective-permute-start | bytes 786440 | tf_op jit(solution)/shard_map/ppermute | solution.py:168
  192.4 5.1 %collective-permute-start.33 = (bf16[2,16,4096]{2,1,0:T(8,128)(2,1)S(1)}, bf16[2,16,4096]{2,1,0:T(8,128)(2,1)S(1)}, u32[]{:S(2)}, u32[]{:S(2)}) collective-permute-start(bf16[2,16,4096]{2,1,0:T(8,128)(2,1)S(1)} %fusion.12), channel_id=1, source_target_pairs={{0,15},{1,0},{2,1},{3,2},{4,3},{5,4},{6,5},{7,6},{8,7},{9,8},{10,9... | collective-permute-start | bytes 786440 | tf_op jit(solution)/shard_map/ppermute | solution.py:168
  201.9 5.1 %collective-permute-start.34 = (bf16[2,16,4096]{2,1,0:T(8,128)(2,1)S(1)}, bf16[2,16,4096]{2,1,0:T(8,128)(2,1)S(1)}, u32[]{:S(2)}, u32[]{:S(2)}) collective-permute-start(bf16[2,16,4096]{2,1,0:T(8,128)(2,1)S(1)} %fusion.11), channel_id=1, source_target_pairs={{0,15},{1,0},{2,1},{3,2},{4,3},{5,4},{6,5},{7,6},{8,7},{9,8},{10,9... | collective-permute-start | bytes 786440 | tf_op jit(solution)/shard_map/ppermute | solution.py:168
  211.6 5.4 %collective-permute-start.35 = (bf16[2,16,4096]{2,1,0:T(8,128)(2,1)S(1)}, bf16[2,16,4096]{2,1,0:T(8,128)(2,1)S(1)}, u32[]{:S(2)}, u32[]{:S(2)}) collective-permute-start(bf16[2,16,4096]{2,1,0:T(8,128)(2,1)S(1)} %fusion.10), channel_id=1, source_target_pairs={{0,15},{1,0},{2,1},{3,2},{4,3},{5,4},{6,5},{7,6},{8,7},{9,8},{10,9... | collective-permute-start | bytes 786440 | tf_op jit(solution)/shard_map/ppermute | solution.py:168
  222.3 7.5 %collective-permute-done.28 = bf16[2,16,4096]{2,1,0:T(8,128)(2,1)S(1)} collective-permute-done((bf16[2,16,4096]{2,1,0:T(8,128)(2,1)S(1)}, bf16[2,16,4096]{2,1,0:T(8,128)(2,1)S(1)}, u32[]{:S(2)}, u32[]{:S(2)}) %collective-permute-start.28) | collective-permute-done | bytes 262176 | tf_op jit(solution)/shard_map/ppermute | solution.py:161
  233.3 3.5 %collective-permute-done.36 = bf16[16,4096]{1,0:T(8,128)(2,1)S(1)} collective-permute-done((bf16[16,4096]{1,0:T(8,128)(2,1)S(1)}, bf16[16,4096]{1,0:T(8,128)(2,1)S(1)}, u32[]{:S(2)}, u32[]{:S(2)}) %collective-permute-start.36) | collective-permute-done | bytes 131104 | tf_op jit(solution)/shard_map/ppermute | solution.py:176
  (136 shorter events, 91.6 us)
Async XLA Ops:
  3.0 17.2 %all-to-all-start = ((bf16[16,2,4224]{2,1,0:T(2,128)(2,1)}), bf16[16,2,4224]{2,1,0:T(2,128)(2,1)S(1)}, u32[]{:S(2)}, u32[]{:S(2)}) async-start(bf16[16,2,4224]{2,1,0:T(2,128)(2,1)} %reshape.916), calls=%async_computation | async-start | bytes 540672 | tf_op jit(solution)/shard_map/all_to_all | solution.py:97
  13.9 31.8 %collective-permute-start.16 = (bf16[1,256,1024]{2,1,0:T(8,128)(2,1)S(1)}, bf16[1,256,1024]{2,1,0:T(8,128)(2,1)S(1)}, u32[]{:S(2)}, u32[]{:S(2)}) collective-permute-start(bf16[1,256,1024]{2,1,0:T(8,128)(2,1)S(1)} %bitcast.119), channel_id=1, source_target_pairs={{0,64},{32,96},{64,0},{96,32},{128,192},{160,224},{192,128},{224,1... | collective-permute-start | bytes 1572872 | tf_op jit(solution)/shard_map/ppermute | solution.py:51
  21.6 11.5 %collective-permute-start = (bf16[16,4096]{1,0:T(8,128)(2,1)S(1)}, bf16[16,4096]{1,0:T(8,128)(2,1)S(1)}, u32[]{:S(2)}, u32[]{:S(2)}) collective-permute-start(bf16[16,4096]{1,0:T(8,128)(2,1)S(1)} %broadcast_select_fusion), channel_id=1, source_target_pairs={{0,16},{1,17},{2,18},{3,19},{4,20},{5,21},{6,22},{7,23},{8,24},{9,... | collective-permute-start | bytes 393224 | tf_op jit(solution)/shard_map/ppermute | solution.py:128
  33.1 19.4 %collective-permute-start.1 = (bf16[2,16,4096]{2,1,0:T(8,128)(2,1)S(1)}, bf16[2,16,4096]{2,1,0:T(8,128)(2,1)S(1)}, u32[]{:S(2)}, u32[]{:S(2)}) collective-permute-start(bf16[2,16,4096]{2,1,0:T(8,128)(2,1)S(1)} %pad_maximum_fusion.2), channel_id=1, source_target_pairs={{0,15},{1,0},{2,1},{3,2},{4,3},{5,4},{6,5},{7,6},{8,7},{9,8},{10,9... | collective-permute-start | bytes 786440 | tf_op jit(solution)/shard_map/ppermute | solution.py:136
  43.8 13.9 %collective-permute-start.8 = (bf16[2,16,4096]{2,1,0:T(8,128)(2,1)S(1)}, bf16[2,16,4096]{2,1,0:T(8,128)(2,1)S(1)}, u32[]{:S(2)}, u32[]{:S(2)}) collective-permute-start(bf16[2,16,4096]{2,1,0:T(8,128)(2,1)S(1)} %pad_maximum_fusion.2), channel_id=1, source_target_pairs={{0,1},{1,2},{2,3},{3,4},{4,5},{5,6},{6,7},{7,8},{8,9},{9,10},{10,1... | collective-permute-start | bytes 786440 | tf_op jit(solution)/shard_map/ppermute | solution.py:132
  45.8 42.2 %collective-permute-start.17 = (bf16[2,256,1024]{2,1,0:T(8,128)(2,1)S(1)}, bf16[2,256,1024]{2,1,0:T(8,128)(2,1)S(1)}, u32[]{:S(2)}, u32[]{:S(2)}) collective-permute-start(bf16[2,256,1024]{2,1,0:T(8,128)(2,1)S(1)} %pad_maximum_fusion), channel_id=1, source_target_pairs={{0,128},{32,160},{64,192},{96,224},{128,256},{160,288},{192,320},{... | collective-permute-start | bytes 3145736 | tf_op jit(solution)/shard_map/ppermute | solution.py:54
  48.3 82.8 %collective-permute-start.19 = (bf16[2,256,1024]{2,1,0:T(8,128)(2,1)S(1)}, bf16[2,256,1024]{2,1,0:T(8,128)(2,1)S(1)}, u32[]{:S(2)}, u32[]{:S(2)}) collective-permute-start(bf16[2,256,1024]{2,1,0:T(8,128)(2,1)S(1)} %pad_maximum_fusion), channel_id=1, source_target_pairs={{0,384},{32,416},{64,448},{96,480},{128,0},{160,32},{192,64},{224,... | collective-permute-start | bytes 3145736 | tf_op jit(solution)/shard_map/ppermute | solution.py:56
  80.5 12.3 %collective-permute-start.5 = (bf16[2,16,4096]{2,1,0:T(8,128)(2,1)S(1)}, bf16[2,16,4096]{2,1,0:T(8,128)(2,1)S(1)}, u32[]{:S(2)}, u32[]{:S(2)}) collective-permute-start(bf16[2,16,4096]{2,1,0:T(8,128)(2,1)S(1)} %collective-permute-done.4), channel_id=1, source_target_pairs={{0,15},{1,0},{2,1},{3,2},{4,3},{5,4},{6,5},{7,6},{8,7},{9,8},{10,9... | collective-permute-start | bytes 786440 | tf_op jit(solution)/shard_map/ppermute | solution.py:136
  86.1 11.8 %collective-permute-start.12 = (bf16[2,16,4096]{2,1,0:T(8,128)(2,1)S(1)}, bf16[2,16,4096]{2,1,0:T(8,128)(2,1)S(1)}, u32[]{:S(2)}, u32[]{:S(2)}) collective-permute-start(bf16[2,16,4096]{2,1,0:T(8,128)(2,1)S(1)} %collective-permute-done.11), channel_id=1, source_target_pairs={{0,1},{1,2},{2,3},{3,4},{4,5},{5,6},{6,7},{7,8},{8,9},{9,10},{10,1... | collective-permute-start | bytes 786440 | tf_op jit(solution)/shard_map/ppermute | solution.py:132
  88.1 42.0 %collective-permute-start.18 = (bf16[2,256,1024]{2,1,0:T(8,128)(2,1)S(1)}, bf16[2,256,1024]{2,1,0:T(8,128)(2,1)S(1)}, u32[]{:S(2)}, u32[]{:S(2)}) collective-permute-start(bf16[2,256,1024]{2,1,0:T(8,128)(2,1)S(1)} %collective-permute-done.17), channel_id=1, source_target_pairs={{0,128},{32,160},{64,192},{96,224},{128,256},{160,288},{192,320},{... | collective-permute-start | bytes 3145736 | tf_op jit(solution)/shard_map/ppermute | solution.py:55
  92.8 9.9 %collective-permute-start.6 = (bf16[2,16,4096]{2,1,0:T(8,128)(2,1)S(1)}, bf16[2,16,4096]{2,1,0:T(8,128)(2,1)S(1)}, u32[]{:S(2)}, u32[]{:S(2)}) collective-permute-start(bf16[2,16,4096]{2,1,0:T(8,128)(2,1)S(1)} %collective-permute-done.5), channel_id=1, source_target_pairs={{0,15},{1,0},{2,1},{3,2},{4,3},{5,4},{6,5},{7,6},{8,7},{9,8},{10,9... | collective-permute-start | bytes 786440 | tf_op jit(solution)/shard_map/ppermute | solution.py:136
  97.9 10.7 %collective-permute-start.13 = (bf16[2,16,4096]{2,1,0:T(8,128)(2,1)S(1)}, bf16[2,16,4096]{2,1,0:T(8,128)(2,1)S(1)}, u32[]{:S(2)}, u32[]{:S(2)}) collective-permute-start(bf16[2,16,4096]{2,1,0:T(8,128)(2,1)S(1)} %collective-permute-done.12), channel_id=1, source_target_pairs={{0,1},{1,2},{2,3},{3,4},{4,5},{5,6},{6,7},{7,8},{8,9},{9,10},{10,1... | collective-permute-start | bytes 786440 | tf_op jit(solution)/shard_map/ppermute | solution.py:132
  102.7 19.7 %collective-permute-start.7 = (bf16[2,16,4096]{2,1,0:T(8,128)(2,1)S(1)}, bf16[2,16,4096]{2,1,0:T(8,128)(2,1)S(1)}, u32[]{:S(2)}, u32[]{:S(2)}) collective-permute-start(bf16[2,16,4096]{2,1,0:T(8,128)(2,1)S(1)} %collective-permute-done.6), channel_id=1, source_target_pairs={{0,15},{1,0},{2,1},{3,2},{4,3},{5,4},{6,5},{7,6},{8,7},{9,8},{10,9... | collective-permute-start | bytes 786440 | tf_op jit(solution)/shard_map/ppermute | solution.py:136
  108.6 11.9 %collective-permute-start.14 = (bf16[2,16,4096]{2,1,0:T(8,128)(2,1)S(1)}, bf16[2,16,4096]{2,1,0:T(8,128)(2,1)S(1)}, u32[]{:S(2)}, u32[]{:S(2)}) collective-permute-start(bf16[2,16,4096]{2,1,0:T(8,128)(2,1)S(1)} %collective-permute-done.13), channel_id=1, source_target_pairs={{0,1},{1,2},{2,3},{3,4},{4,5},{5,6},{6,7},{7,8},{8,9},{9,10},{10,1... | collective-permute-start | bytes 786440 | tf_op jit(solution)/shard_map/ppermute | solution.py:132
  148.8 11.5 %collective-permute-start.21 = (bf16[2,16,4096]{2,1,0:T(8,128)(2,1)S(1)}, bf16[2,16,4096]{2,1,0:T(8,128)(2,1)S(1)}, u32[]{:S(2)}, u32[]{:S(2)}) collective-permute-start(bf16[2,16,4096]{2,1,0:T(8,128)(2,1)S(1)} %bitcast.151), channel_id=1, source_target_pairs={{0,1},{1,2},{2,3},{3,4},{4,5},{5,6},{6,7},{7,8},{8,9},{9,10},{10,1... | collective-permute-start | bytes 786440 | tf_op jit(solution)/shard_map/ppermute | solution.py:161
  150.7 11.5 %collective-permute-start.29 = (bf16[2,16,4096]{2,1,0:T(8,128)(2,1)S(1)}, bf16[2,16,4096]{2,1,0:T(8,128)(2,1)S(1)}, u32[]{:S(2)}, u32[]{:S(2)}) collective-permute-start(bf16[2,16,4096]{2,1,0:T(8,128)(2,1)S(1)} %bitcast.150), channel_id=1, source_target_pairs={{0,15},{1,0},{2,1},{3,2},{4,3},{5,4},{6,5},{7,6},{8,7},{9,8},{10,9... | collective-permute-start | bytes 786440 | tf_op jit(solution)/shard_map/ppermute | solution.py:168
  160.3 10.6 %collective-permute-start.22 = (bf16[2,16,4096]{2,1,0:T(8,128)(2,1)S(1)}, bf16[2,16,4096]{2,1,0:T(8,128)(2,1)S(1)}, u32[]{:S(2)}, u32[]{:S(2)}) collective-permute-start(bf16[2,16,4096]{2,1,0:T(8,128)(2,1)S(1)} %fusion.22), channel_id=1, source_target_pairs={{0,1},{1,2},{2,3},{3,4},{4,5},{5,6},{6,7},{7,8},{8,9},{9,10},{10,1... | collective-permute-start | bytes 786440 | tf_op jit(solution)/shard_map/ppermute | solution.py:161
  162.3 10.6 %collective-permute-start.30 = (bf16[2,16,4096]{2,1,0:T(8,128)(2,1)S(1)}, bf16[2,16,4096]{2,1,0:T(8,128)(2,1)S(1)}, u32[]{:S(2)}, u32[]{:S(2)}) collective-permute-start(bf16[2,16,4096]{2,1,0:T(8,128)(2,1)S(1)} %fusion.15), channel_id=1, source_target_pairs={{0,15},{1,0},{2,1},{3,2},{4,3},{5,4},{6,5},{7,6},{8,7},{9,8},{10,9... | collective-permute-start | bytes 786440 | tf_op jit(solution)/shard_map/ppermute | solution.py:168
  171.0 9.7 %collective-permute-start.23 = (bf16[2,16,4096]{2,1,0:T(8,128)(2,1)S(1)}, bf16[2,16,4096]{2,1,0:T(8,128)(2,1)S(1)}, u32[]{:S(2)}, u32[]{:S(2)}) collective-permute-start(bf16[2,16,4096]{2,1,0:T(8,128)(2,1)S(1)} %fusion.21), channel_id=1, source_target_pairs={{0,1},{1,2},{2,3},{3,4},{4,5},{5,6},{6,7},{7,8},{8,9},{9,10},{10,1... | collective-permute-start | bytes 786440 | tf_op jit(solution)/shard_map/ppermute | solution.py:161
  173.1 9.7 %collective-permute-start.31 = (bf16[2,16,4096]{2,1,0:T(8,128)(2,1)S(1)}, bf16[2,16,4096]{2,1,0:T(8,128)(2,1)S(1)}, u32[]{:S(2)}, u32[]{:S(2)}) collective-permute-start(bf16[2,16,4096]{2,1,0:T(8,128)(2,1)S(1)} %fusion.14), channel_id=1, source_target_pairs={{0,15},{1,0},{2,1},{3,2},{4,3},{5,4},{6,5},{7,6},{8,7},{9,8},{10,9... | collective-permute-start | bytes 786440 | tf_op jit(solution)/shard_map/ppermute | solution.py:168
  199.9 9.6 %collective-permute-start.26 = (bf16[2,16,4096]{2,1,0:T(8,128)(2,1)S(1)}, bf16[2,16,4096]{2,1,0:T(8,128)(2,1)S(1)}, u32[]{:S(2)}, u32[]{:S(2)}) collective-permute-start(bf16[2,16,4096]{2,1,0:T(8,128)(2,1)S(1)} %fusion.18), channel_id=1, source_target_pairs={{0,1},{1,2},{2,3},{3,4},{4,5},{5,6},{6,7},{7,8},{8,9},{9,10},{10,1... | collective-permute-start | bytes 786440 | tf_op jit(solution)/shard_map/ppermute | solution.py:161
  201.9 9.6 %collective-permute-start.34 = (bf16[2,16,4096]{2,1,0:T(8,128)(2,1)S(1)}, bf16[2,16,4096]{2,1,0:T(8,128)(2,1)S(1)}, u32[]{:S(2)}, u32[]{:S(2)}) collective-permute-start(bf16[2,16,4096]{2,1,0:T(8,128)(2,1)S(1)} %fusion.11), channel_id=1, source_target_pairs={{0,15},{1,0},{2,1},{3,2},{4,3},{5,4},{6,5},{7,6},{8,7},{9,8},{10,9... | collective-permute-start | bytes 786440 | tf_op jit(solution)/shard_map/ppermute | solution.py:168
  209.6 10.7 %collective-permute-start.27 = (bf16[2,16,4096]{2,1,0:T(8,128)(2,1)S(1)}, bf16[2,16,4096]{2,1,0:T(8,128)(2,1)S(1)}, u32[]{:S(2)}, u32[]{:S(2)}) collective-permute-start(bf16[2,16,4096]{2,1,0:T(8,128)(2,1)S(1)} %fusion.17), channel_id=1, source_target_pairs={{0,1},{1,2},{2,3},{3,4},{4,5},{5,6},{6,7},{7,8},{8,9},{9,10},{10,1... | collective-permute-start | bytes 786440 | tf_op jit(solution)/shard_map/ppermute | solution.py:161
  211.6 10.7 %collective-permute-start.35 = (bf16[2,16,4096]{2,1,0:T(8,128)(2,1)S(1)}, bf16[2,16,4096]{2,1,0:T(8,128)(2,1)S(1)}, u32[]{:S(2)}, u32[]{:S(2)}) collective-permute-start(bf16[2,16,4096]{2,1,0:T(8,128)(2,1)S(1)} %fusion.10), channel_id=1, source_target_pairs={{0,15},{1,0},{2,1},{3,2},{4,3},{5,4},{6,5},{7,6},{8,7},{9,8},{10,9... | collective-permute-start | bytes 786440 | tf_op jit(solution)/shard_map/ppermute | solution.py:168
  (16 other events, 133.4 us)

commit v3 on v2

--- a/solution.py
+++ b/solution.py
@@ -6,6 +6,7 @@
 ROWS_GRP = 512
 DP_SUB = (4, 2, 2)
 TP_SUB = (2, 16)
+SPLIT_COLS = 2688
 
 
 def dp_perm(move):
@@ -125,18 +126,45 @@
     travelling = jnp.take(
         travelling.reshape(shard_rows, dp_count, piece_rows), piece_index, axis=1
     ).reshape(shard_rows, feature_count)
-    pair = jnp.stack([travelling, lax.ppermute(travelling, "tensor", TP_L_SWAP)])
-    token_chunks = {0: pair}
-    fwd = pair
+    cut = SPLIT_COLS
+    rest = feature_count - cut
+    pack = lambda p, q: jnp.concatenate([p, q[0], q[1]], axis=1)
+    unpack = lambda v: (v[:, :cut], jnp.stack([v[:, cut : cut + rest], v[:, cut + rest :]]))
+    partner = lax.ppermute(travelling, "tensor", TP_L_SWAP)
+    col_p = {0: travelling[:, :cut]}
+    far_p = {0: partner[:, :cut]}
+    q_pairs = {0: jnp.stack([travelling[:, cut:], partner[:, cut:]])}
+    fwd = pack(col_p[0], q_pairs[0])
+    bwd = fwd
+    pending = []
     for s in range(nz // 2):
+        if pending:
+            crossed = lax.ppermute(jnp.stack([col_p[k] for k in pending]), "tensor", TP_L_SWAP)
+            for i, k in enumerate(pending):
+                far_p[k] = crossed[i]
+        pending = []
         fwd = lax.ppermute(fwd, "tensor", TP_Z_FWD)
-        token_chunks[nz - 1 - s] = fwd
-    bwd = pair
-    for s in range(nz // 2 - 1):
-        bwd = lax.ppermute(bwd, "tensor", TP_Z_BWD)
-        token_chunks[s + 1] = bwd
-    gathered = jnp.concatenate([token_chunks[k] for k in range(nz)], axis=0)
-    row_total = gathered.shape[0] * gathered.shape[1]
+        col_p[nz - 1 - s], q_pairs[nz - 1 - s] = unpack(fwd)
+        pending.append(nz - 1 - s)
+        if s < nz // 2 - 1:
+            bwd = lax.ppermute(bwd, "tensor", TP_Z_BWD)
+            col_p[s + 1], q_pairs[s + 1] = unpack(bwd)
+            pending.append(s + 1)
+    crossed = lax.ppermute(jnp.stack([col_p[k] for k in pending]), "tensor", TP_L_SWAP)
+    for i, k in enumerate(pending):
+        far_p[k] = crossed[i]
+    gathered = jnp.stack(
+        [
+            jnp.stack(
+                [
+                    jnp.concatenate([col_p[k], q_pairs[k][0]], axis=1),
+                    jnp.concatenate([far_p[k], q_pairs[k][1]], axis=1),
+                ]
+            )
+            for k in range(nz)
+        ]
+    )
+    row_total = nz * nl * shard_rows
     normed = gathered.reshape(row_total, feature_count)
 
     act = None
@@ -156,25 +184,49 @@
     term = jnp.dot(hidden, down_weight, preferred_element_type=jnp.float32).astype(jnp.bfloat16)
     blocks = term.reshape(nz, nl, shard_rows, feature_count)
 
-    fwd = blocks[nz // 2]
+    f32 = lambda v: v.astype(jnp.float32)
+    bf16 = lambda v: v.astype(jnp.bfloat16)
+    head = blocks[..., :cut]
+    tail = blocks[..., cut:]
+    col_sum = {}
+
+    def cross_reduce(ks):
+        got = lax.ppermute(jnp.stack([head[k, 1] for k in ks]), "tensor", TP_L_SWAP)
+        for i, k in enumerate(ks):
+            col_sum[k] = f32(head[k, 0]) + f32(got[i])
+
+    cross_reduce([nz // 2, nz // 2 + 1, 0])
+    fwd = pack(bf16(col_sum[nz // 2]), tail[nz // 2])
+    bwd = pack(bf16(col_sum[nz // 2 + 1]), tail[nz // 2 + 1])
     for s in range(nz // 2):
+        ks = []
+        if s < nz // 2 - 1:
+            ks.append(nz // 2 - 1 - s)
+        if s < nz // 2 - 2:
+            ks.append(nz // 2 + 2 + s)
+        if ks:
+            cross_reduce(ks)
         got = lax.ppermute(fwd, "tensor", TP_Z_FWD)
         if s < nz // 2 - 1:
-            fwd = (got.astype(jnp.float32) + blocks[nz // 2 - 1 - s].astype(jnp.float32)).astype(jnp.bfloat16)
+            k = nz // 2 - 1 - s
+            p, q = unpack(got)
+            fwd = pack(bf16(f32(p) + col_sum[k]), bf16(f32(q) + f32(tail[k])))
         else:
             fwd_total = got
-    bwd = blocks[nz // 2 + 1]
-    for s in range(nz // 2 - 1):
-        got = lax.ppermute(bwd, "tensor", TP_Z_BWD)
-        if s < nz // 2 - 2:
-            bwd = (got.astype(jnp.float32) + blocks[nz // 2 + 2 + s].astype(jnp.float32)).astype(jnp.bfloat16)
-        else:
-            bwd_total = got
-    column_sum = (
-        fwd_total.astype(jnp.float32) + bwd_total.astype(jnp.float32) + blocks[0].astype(jnp.float32)
-    )
-    from_partner = lax.ppermute(column_sum[1].astype(jnp.bfloat16), "tensor", TP_L_SWAP)
-    total = column_sum[0] + from_partner.astype(jnp.float32)
+        if s < nz // 2 - 1:
+            got = lax.ppermute(bwd, "tensor", TP_Z_BWD)
+            if s < nz // 2 - 2:
+                k = nz // 2 + 2 + s
+                p, q = unpack(got)
+                bwd = pack(bf16(f32(p) + col_sum[k]), bf16(f32(q) + f32(tail[k])))
+            else:
+                bwd_total = got
+    f_p, f_q = unpack(fwd_total)
+    b_p, b_q = unpack(bwd_total)
+    total_head = f32(f_p) + f32(b_p) + col_sum[0]
+    tail_sum = f32(f_q) + f32(b_q) + f32(tail[0])
+    from_partner = lax.ppermute(bf16(tail_sum[1]), "tensor", TP_L_SWAP)
+    total = jnp.concatenate([total_head, tail_sum[0] + f32(from_partner)], axis=1)
     return (local_batch.astype(jnp.float32) + total).astype(jnp.bfloat16)
 
 

time: 240 us -> 316 us (1.32)
  waiting for transfers between devices: 72.7 us -> 131 us
  starting transfers between devices: 141 us -> 159 us
    ppermute x2 -> x18, starting transfers between devices: 5.26 us -> 51 us  [the longest x8 23.4 us: per_device(): lax.ppermute(jnp.stack([col_p[k] for k in pending]), 'tensor', TP_L_SWAP)]
    ppermute x7, waiting for transfers between devices: 0.02 us -> 26.4 us  [per_device(): got = lax.ppermute(bwd, 'tensor', TP_Z_BWD)]
    ppermute x8, waiting for transfers between devices: 28.3 us -> 49.2 us  [per_device(): got = lax.ppermute(fwd, 'tensor', TP_Z_FWD)]
    ppermute x7, starting transfers between devices: 36.2 us -> 16.6 us  [per_device(): got = lax.ppermute(bwd, 'tensor', TP_Z_BWD)]
    ppermute x7, starting transfers between devices: 43.2 us -> 26.9 us  [per_device(): bwd = lax.ppermute(bwd, 'tensor', TP_Z_BWD)]
    ppermute x8, starting transfers between devices: 15.3 us -> 23.8 us  [per_device(): fwd = lax.ppermute(fwd, 'tensor', TP_Z_FWD)]
    ppermute x8, waiting for transfers between devices: 17.8 us -> 25.7 us  [per_device(): fwd = lax.ppermute(fwd, 'tensor', TP_Z_FWD)]
    ppermute x2 -> x18, waiting for transfers between devices: 13.1 us -> 18.6 us  [the longest x1 9.6 us: per_device(): partner = lax.ppermute(travelling, 'tensor', TP_L_SWAP)]
  transfers between devices with their start and end apart: 38 -> 54, of which waited for: 18 -> 32; matrix products, arithmetic and copies ran while one was open for 5% -> 3% of each run, Pallas kernels for 0% -> 0%
where the time goes in v3:
time: 316 us; the launch traced here: 313 us
  starting transfers between devices  159 us (50%)
  waiting for transfers between devices  131 us (41%)
  matrix products  8.49 us (3%)
  local copies, waits for them, and re-layouts  7.87 us (2%)
  other arithmetic  4.31 us (1%)
    ppermute x8, waiting for transfers between devices, per_device(): got = lax.ppermute(fwd, 'tensor', TP_Z_FWD)  49.2 us
    ppermute x7, starting transfers between devices, per_device(): bwd = lax.ppermute(bwd, 'tensor', TP_Z_BWD)  26.9 us
    ppermute x7, waiting for transfers between devices, per_device(): got = lax.ppermute(bwd, 'tensor', TP_Z_BWD)  26.4 us
    ppermute x8, waiting for transfers between devices, per_device(): fwd = lax.ppermute(fwd, 'tensor', TP_Z_FWD)  25.7 us
    ppermute x8, starting transfers between devices, per_device(): fwd = lax.ppermute(fwd, 'tensor', TP_Z_FWD)  23.8 us
    ppermute x8, starting transfers between devices, per_device(): lax.ppermute(jnp.stack([col_p[k] for k in pending]), 'tensor', TP_L_SWAP)  23.4 us
    ppermute x8, starting transfers between devices, cross_reduce(): got = lax.ppermute(jnp.stack([head[k, 1] for k in ks]), 'tensor', TP_L_SWAP)  23 us
    ppermute x7, starting transfers between devices, per_device(): got = lax.ppermute(bwd, 'tensor', TP_Z_BWD)  16.6 us
  transfers between devices with their start and end apart: 54, of which 32 were waited for; matrix products, arithmetic and copies ran while one was open for 3% of the time, Pallas kernels for 0%

profile of v3, /device:TPU:24, one launch (start us, length us, event | category | flops | bytes accessed | tf_op | source)
XLA Modules:
  0.0 313.2 jit_solution(4231061486519242097)
XLA Ops:
  3.0 9.0 %all-to-all-start = ((bf16[16,2,4224]{2,1,0:T(2,128)(2,1)}), bf16[16,2,4224]{2,1,0:T(2,128)(2,1)S(1)}, u32[]{:S(2)}, u32[]{:S(2)}) async-start(bf16[16,2,4224]{2,1,0:T(2,128)(2,1)} %reshape.954), calls=%async_computation | async-start | bytes 540672 | tf_op jit(solution)/shard_map/all_to_all | solution.py:98
  13.9 4.9 %collective-permute-start.24 = (bf16[1,256,1024]{2,1,0:T(8,128)(2,1)S(1)}, bf16[1,256,1024]{2,1,0:T(8,128)(2,1)S(1)}, u32[]{:S(2)}, u32[]{:S(2)}) collective-permute-start(bf16[1,256,1024]{2,1,0:T(8,128)(2,1)S(1)} %bitcast.648), channel_id=1, source_target_pairs={{0,64},{32,96},{64,0},{96,32},{128,192},{160,224},{192,128},{224,1... | collective-permute-start | bytes 1572872 | tf_op jit(solution)/shard_map/ppermute | solution.py:52
  23.5 9.6 %collective-permute-done = bf16[16,4096]{1,0:T(8,128)(2,1)S(1)} collective-permute-done((bf16[16,4096]{1,0:T(8,128)(2,1)S(1)}, bf16[16,4096]{1,0:T(8,128)(2,1)S(1)}, u32[]{:S(2)}, u32[]{:S(2)}) %collective-permute-start) | collective-permute-done | bytes 131104 | tf_op jit(solution)/shard_map/ppermute | solution.py:133
  33.1 10.6 %collective-permute-start.1 = (bf16[16,5504]{1,0:T(8,128)(2,1)S(1)}, bf16[16,5504]{1,0:T(8,128)(2,1)S(1)}, u32[]{:S(2)}, u32[]{:S(2)}) collective-permute-start(bf16[16,5504]{1,0:T(8,128)(2,1)S(1)} %pad_maximum_fusion.3), channel_id=1, source_target_pairs={{0,15},{1,0},{2,1},{3,2},{4,3},{5,4},{6,5},{7,6},{8,7},{9,8},{10,9... | collective-permute-start | bytes 528392 | tf_op jit(solution)/shard_map/ppermute | solution.py:150
  56.0 5.1 %collective-permute-start.4 = (bf16[16,5504]{1,0:T(8,128)(2,1)S(1)}, bf16[16,5504]{1,0:T(8,128)(2,1)S(1)}, u32[]{:S(2)}, u32[]{:S(2)}) collective-permute-start(bf16[16,5504]{1,0:T(8,128)(2,1)S(1)} %collective-permute-done.1), channel_id=1, source_target_pairs={{0,15},{1,0},{2,1},{3,2},{4,3},{5,4},{6,5},{7,6},{8,7},{9,8},{10,9... | collective-permute-start | bytes 528392 | tf_op jit(solution)/shard_map/ppermute | solution.py:150
  64.1 5.6 %collective-permute-done.5 = bf16[16,5504]{1,0:T(8,128)(2,1)S(1)} collective-permute-done((bf16[16,5504]{1,0:T(8,128)(2,1)S(1)}, bf16[16,5504]{1,0:T(8,128)(2,1)S(1)}, u32[]{:S(2)}, u32[]{:S(2)}) %collective-permute-start.5) | collective-permute-done | bytes 176160 | tf_op jit(solution)/shard_map/ppermute | solution.py:146
  74.2 3.9 %collective-permute-start.8 = (bf16[16,5504]{1,0:T(8,128)(2,1)S(1)}, bf16[16,5504]{1,0:T(8,128)(2,1)S(1)}, u32[]{:S(2)}, u32[]{:S(2)}) collective-permute-start(bf16[16,5504]{1,0:T(8,128)(2,1)S(1)} %collective-permute-done.5), channel_id=1, source_target_pairs={{0,1},{1,2},{2,3},{3,4},{4,5},{5,6},{6,7},{7,8},{8,9},{9,10},{10,1... | collective-permute-start | bytes 528392 | tf_op jit(solution)/shard_map/ppermute | solution.py:146
  88.0 3.9 %collective-permute-start.11 = (bf16[16,5504]{1,0:T(8,128)(2,1)S(1)}, bf16[16,5504]{1,0:T(8,128)(2,1)S(1)}, u32[]{:S(2)}, u32[]{:S(2)}) collective-permute-start(bf16[16,5504]{1,0:T(8,128)(2,1)S(1)} %collective-permute-done.8), channel_id=1, source_target_pairs={{0,1},{1,2},{2,3},{3,4},{4,5},{5,6},{6,7},{7,8},{8,9},{9,10},{10,1... | collective-permute-start | bytes 528392 | tf_op jit(solution)/shard_map/ppermute | solution.py:146
  106.5 3.9 %collective-permute-done.14 = bf16[16,5504]{1,0:T(8,128)(2,1)S(1)} collective-permute-done((bf16[16,5504]{1,0:T(8,128)(2,1)S(1)}, bf16[16,5504]{1,0:T(8,128)(2,1)S(1)}, u32[]{:S(2)}, u32[]{:S(2)}) %collective-permute-start.14) | collective-permute-done | bytes 176160 | tf_op jit(solution)/shard_map/ppermute | solution.py:146
  121.2 3.9 %collective-permute-done.17 = bf16[16,5504]{1,0:T(8,128)(2,1)S(1)} collective-permute-done((bf16[16,5504]{1,0:T(8,128)(2,1)S(1)}, bf16[16,5504]{1,0:T(8,128)(2,1)S(1)}, u32[]{:S(2)}, u32[]{:S(2)}) %collective-permute-start.17) | collective-permute-done | bytes 176160 | tf_op jit(solution)/shard_map/ppermute | solution.py:146
  129.6 3.9 %collective-permute-start.20 = (bf16[16,5504]{1,0:T(8,128)(2,1)S(1)}, bf16[16,5504]{1,0:T(8,128)(2,1)S(1)}, u32[]{:S(2)}, u32[]{:S(2)}) collective-permute-start(bf16[16,5504]{1,0:T(8,128)(2,1)S(1)} %collective-permute-done.17), channel_id=1, source_target_pairs={{0,1},{1,2},{2,3},{3,4},{4,5},{5,6},{6,7},{7,8},{8,9},{9,10},{10,1... | collective-permute-start | bytes 528392 | tf_op jit(solution)/shard_map/ppermute | solution.py:146
  147.0 3.9 %collective-permute-done.22 = bf16[16,5504]{1,0:T(8,128)(2,1)S(1)} collective-permute-done((bf16[16,5504]{1,0:T(8,128)(2,1)S(1)}, bf16[16,5504]{1,0:T(8,128)(2,1)S(1)}, u32[]{:S(2)}, u32[]{:S(2)}) %collective-permute-start.22) | collective-permute-done | bytes 176160 | tf_op jit(solution)/shard_map/ppermute | solution.py:146
  162.2 4.4 %collective-permute-done.28 = bf16[8,256,1024]{2,1,0:T(8,128)(2,1)S(1)} collective-permute-done((bf16[8,256,1024]{2,1,0:T(8,128)(2,1)S(1)}, bf16[8,256,1024]{2,1,0:T(8,128)(2,1)S(1)}, u32[]{:S(2)}, u32[]{:S(2)}) %collective-permute-start.28) | collective-permute-done | bytes 4194336 | tf_op jit(solution)/shard_map/ppermute | solution.py:61
  190.7 6.6 %collective-permute-done.30 = bf16[16,5504]{1,0:T(8,128)(2,1)S(1)} collective-permute-done((bf16[16,5504]{1,0:T(8,128)(2,1)S(1)}, bf16[16,5504]{1,0:T(8,128)(2,1)S(1)}, u32[]{:S(2)}, u32[]{:S(2)}) %collective-permute-start.30) | collective-permute-done | bytes 176160 | tf_op jit(solution)/shard_map/ppermute | solution.py:209
  206.7 6.6 %collective-permute-done.32 = bf16[16,5504]{1,0:T(8,128)(2,1)S(1)} collective-permute-done((bf16[16,5504]{1,0:T(8,128)(2,1)S(1)}, bf16[16,5504]{1,0:T(8,128)(2,1)S(1)}, u32[]{:S(2)}, u32[]{:S(2)}) %collective-permute-start.32) | collective-permute-done | bytes 176160 | tf_op jit(solution)/shard_map/ppermute | solution.py:209
  222.8 6.6 %collective-permute-done.34 = bf16[16,5504]{1,0:T(8,128)(2,1)S(1)} collective-permute-done((bf16[16,5504]{1,0:T(8,128)(2,1)S(1)}, bf16[16,5504]{1,0:T(8,128)(2,1)S(1)}, u32[]{:S(2)}, u32[]{:S(2)}) %collective-permute-start.34) | collective-permute-done | bytes 176160 | tf_op jit(solution)/shard_map/ppermute | solution.py:209
  238.9 6.6 %collective-permute-done.36 = bf16[16,5504]{1,0:T(8,128)(2,1)S(1)} collective-permute-done((bf16[16,5504]{1,0:T(8,128)(2,1)S(1)}, bf16[16,5504]{1,0:T(8,128)(2,1)S(1)}, u32[]{:S(2)}, u32[]{:S(2)}) %collective-permute-start.36) | collective-permute-done | bytes 176160 | tf_op jit(solution)/shard_map/ppermute | solution.py:209
  247.6 5.4 %collective-permute-done.48 = bf16[16,5504]{1,0:T(8,128)(2,1)S(1)} collective-permute-done((bf16[16,5504]{1,0:T(8,128)(2,1)S(1)}, bf16[16,5504]{1,0:T(8,128)(2,1)S(1)}, u32[]{:S(2)}, u32[]{:S(2)}) %collective-permute-start.48) | collective-permute-done | bytes 176160 | tf_op jit(solution)/shard_map/ppermute | solution.py:217
  255.0 6.6 %collective-permute-done.38 = bf16[16,5504]{1,0:T(8,128)(2,1)S(1)} collective-permute-done((bf16[16,5504]{1,0:T(8,128)(2,1)S(1)}, bf16[16,5504]{1,0:T(8,128)(2,1)S(1)}, u32[]{:S(2)}, u32[]{:S(2)}) %collective-permute-start.38) | collective-permute-done | bytes 176160 | tf_op jit(solution)/shard_map/ppermute | solution.py:209
  263.7 5.7 %collective-permute-done.49 = bf16[16,5504]{1,0:T(8,128)(2,1)S(1)} collective-permute-done((bf16[16,5504]{1,0:T(8,128)(2,1)S(1)}, bf16[16,5504]{1,0:T(8,128)(2,1)S(1)}, u32[]{:S(2)}, u32[]{:S(2)}) %collective-permute-start.49) | collective-permute-done | bytes 176160 | tf_op jit(solution)/shard_map/ppermute | solution.py:217
  271.4 8.1 %collective-permute-done.40 = bf16[16,5504]{1,0:T(8,128)(2,1)S(1)} collective-permute-done((bf16[16,5504]{1,0:T(8,128)(2,1)S(1)}, bf16[16,5504]{1,0:T(8,128)(2,1)S(1)}, u32[]{:S(2)}, u32[]{:S(2)}) %collective-permute-start.40) | collective-permute-done | bytes 176160 | tf_op jit(solution)/shard_map/ppermute | solution.py:209
  281.6 6.0 %collective-permute-done.50 = bf16[16,5504]{1,0:T(8,128)(2,1)S(1)} collective-permute-done((bf16[16,5504]{1,0:T(8,128)(2,1)S(1)}, bf16[16,5504]{1,0:T(8,128)(2,1)S(1)}, u32[]{:S(2)}, u32[]{:S(2)}) %collective-permute-start.50) | collective-permute-done | bytes 176160 | tf_op jit(solution)/shard_map/ppermute | solution.py:217
  289.7 6.6 %collective-permute-done.42 = bf16[16,5504]{1,0:T(8,128)(2,1)S(1)} collective-permute-done((bf16[16,5504]{1,0:T(8,128)(2,1)S(1)}, bf16[16,5504]{1,0:T(8,128)(2,1)S(1)}, u32[]{:S(2)}, u32[]{:S(2)}) %collective-permute-start.42) | collective-permute-done | bytes 176160 | tf_op jit(solution)/shard_map/ppermute | solution.py:209
  298.4 5.1 %collective-permute-start.51 = (bf16[16,5504]{1,0:T(8,128)(2,1)S(1)}, bf16[16,5504]{1,0:T(8,128)(2,1)S(1)}, u32[]{:S(2)}, u32[]{:S(2)}) collective-permute-start(bf16[16,5504]{1,0:T(8,128)(2,1)S(1)} %pad_maximum_fusion.18), channel_id=1, source_target_pairs={{0,15},{1,0},{2,1},{3,2},{4,3},{5,4},{6,5},{7,6},{8,7},{9,8},{10,9... | collective-permute-start | bytes 528392 | tf_op jit(solution)/shard_map/ppermute | solution.py:217
  (302 shorter events, 167.8 us)
Async XLA Ops:
  3.0 17.2 %all-to-all-start = ((bf16[16,2,4224]{2,1,0:T(2,128)(2,1)}), bf16[16,2,4224]{2,1,0:T(2,128)(2,1)S(1)}, u32[]{:S(2)}, u32[]{:S(2)}) async-start(bf16[16,2,4224]{2,1,0:T(2,128)(2,1)} %reshape.954), calls=%async_computation | async-start | bytes 540672 | tf_op jit(solution)/shard_map/all_to_all | solution.py:98
  13.9 31.8 %collective-permute-start.24 = (bf16[1,256,1024]{2,1,0:T(8,128)(2,1)S(1)}, bf16[1,256,1024]{2,1,0:T(8,128)(2,1)S(1)}, u32[]{:S(2)}, u32[]{:S(2)}) collective-permute-start(bf16[1,256,1024]{2,1,0:T(8,128)(2,1)S(1)} %bitcast.648), channel_id=1, source_target_pairs={{0,64},{32,96},{64,0},{96,32},{128,192},{160,224},{192,128},{224,1... | collective-permute-start | bytes 1572872 | tf_op jit(solution)/shard_map/ppermute | solution.py:52
  21.4 11.7 %collective-permute-start = (bf16[16,4096]{1,0:T(8,128)(2,1)S(1)}, bf16[16,4096]{1,0:T(8,128)(2,1)S(1)}, u32[]{:S(2)}, u32[]{:S(2)}) collective-permute-start(bf16[16,4096]{1,0:T(8,128)(2,1)S(1)} %broadcast_select_fusion), channel_id=1, source_target_pairs={{0,16},{1,17},{2,18},{3,19},{4,20},{5,21},{6,22},{7,23},{8,24},{9,... | collective-permute-start | bytes 393224 | tf_op jit(solution)/shard_map/ppermute | solution.py:133
  33.1 19.4 %collective-permute-start.1 = (bf16[16,5504]{1,0:T(8,128)(2,1)S(1)}, bf16[16,5504]{1,0:T(8,128)(2,1)S(1)}, u32[]{:S(2)}, u32[]{:S(2)}) collective-permute-start(bf16[16,5504]{1,0:T(8,128)(2,1)S(1)} %pad_maximum_fusion.3), channel_id=1, source_target_pairs={{0,15},{1,0},{2,1},{3,2},{4,3},{5,4},{6,5},{7,6},{8,7},{9,8},{10,9... | collective-permute-start | bytes 528392 | tf_op jit(solution)/shard_map/ppermute | solution.py:150
  43.8 8.8 %collective-permute-start.2 = (bf16[16,5504]{1,0:T(8,128)(2,1)S(1)}, bf16[16,5504]{1,0:T(8,128)(2,1)S(1)}, u32[]{:S(2)}, u32[]{:S(2)}) collective-permute-start(bf16[16,5504]{1,0:T(8,128)(2,1)S(1)} %pad_maximum_fusion.3), channel_id=1, source_target_pairs={{0,1},{1,2},{2,3},{3,4},{4,5},{5,6},{6,7},{7,8},{8,9},{9,10},{10,1... | collective-permute-start | bytes 528392 | tf_op jit(solution)/shard_map/ppermute | solution.py:146
  45.8 87.7 %collective-permute-start.25 = (bf16[2,256,1024]{2,1,0:T(8,128)(2,1)S(1)}, bf16[2,256,1024]{2,1,0:T(8,128)(2,1)S(1)}, u32[]{:S(2)}, u32[]{:S(2)}) collective-permute-start(bf16[2,256,1024]{2,1,0:T(8,128)(2,1)S(1)} %pad_maximum_fusion), channel_id=1, source_target_pairs={{0,128},{32,160},{64,192},{96,224},{128,256},{160,288},{192,320},{... | collective-permute-start | bytes 3145736 | tf_op jit(solution)/shard_map/ppermute | solution.py:55
  48.3 109.1 %collective-permute-start.27 = (bf16[2,256,1024]{2,1,0:T(8,128)(2,1)S(1)}, bf16[2,256,1024]{2,1,0:T(8,128)(2,1)S(1)}, u32[]{:S(2)}, u32[]{:S(2)}) collective-permute-start(bf16[2,256,1024]{2,1,0:T(8,128)(2,1)S(1)} %pad_maximum_fusion), channel_id=1, source_target_pairs={{0,384},{32,416},{64,448},{96,480},{128,0},{160,32},{192,64},{224,... | collective-permute-start | bytes 3145736 | tf_op jit(solution)/shard_map/ppermute | solution.py:57
  52.6 10.5 %collective-permute-start.3 = (bf16[2,16,2688]{2,1,0:T(8,128)(2,1)S(1)}, bf16[2,16,2688]{2,1,0:T(8,128)(2,1)S(1)}, u32[]{:S(2)}, u32[]{:S(2)}) collective-permute-start(bf16[2,16,2688]{2,1,0:T(8,128)(2,1)S(1)} %pad_maximum_fusion.19), channel_id=1, source_target_pairs={{0,16},{1,17},{2,18},{3,19},{4,20},{5,21},{6,22},{7,23},{8,24},{9,... | collective-permute-start | bytes 516104 | tf_op jit(solution)/shard_map/ppermute | solution.py:142
  82.8 9.3 %collective-permute-start.9 = (bf16[2,16,2688]{2,1,0:T(8,128)(2,1)S(1)}, bf16[2,16,2688]{2,1,0:T(8,128)(2,1)S(1)}, u32[]{:S(2)}, u32[]{:S(2)}) collective-permute-start(bf16[2,16,2688]{2,1,0:T(8,128)(2,1)S(1)} %pad_maximum_fusion.21), channel_id=1, source_target_pairs={{0,16},{1,17},{2,18},{3,19},{4,20},{5,21},{6,22},{7,23},{8,24},{9,... | collective-permute-start | bytes 516104 | tf_op jit(solution)/shard_map/ppermute | solution.py:142
  110.5 9.3 %collective-permute-start.15 = (bf16[2,16,2688]{2,1,0:T(8,128)(2,1)S(1)}, bf16[2,16,2688]{2,1,0:T(8,128)(2,1)S(1)}, u32[]{:S(2)}, u32[]{:S(2)}) collective-permute-start(bf16[2,16,2688]{2,1,0:T(8,128)(2,1)S(1)} %pad_maximum_fusion.23), channel_id=1, source_target_pairs={{0,16},{1,17},{2,18},{3,19},{4,20},{5,21},{6,22},{7,23},{8,24},{9,... | collective-permute-start | bytes 516104 | tf_op jit(solution)/shard_map/ppermute | solution.py:142
  125.1 12.2 %collective-permute-start.18 = (bf16[2,16,2688]{2,1,0:T(8,128)(2,1)S(1)}, bf16[2,16,2688]{2,1,0:T(8,128)(2,1)S(1)}, u32[]{:S(2)}, u32[]{:S(2)}) collective-permute-start(bf16[2,16,2688]{2,1,0:T(8,128)(2,1)S(1)} %pad_maximum_fusion.24), channel_id=1, source_target_pairs={{0,16},{1,17},{2,18},{3,19},{4,20},{5,21},{6,22},{7,23},{8,24},{9,... | collective-permute-start | bytes 516104 | tf_op jit(solution)/shard_map/ppermute | solution.py:142
  127.7 9.8 %collective-permute-start.19 = (bf16[16,5504]{1,0:T(8,128)(2,1)S(1)}, bf16[16,5504]{1,0:T(8,128)(2,1)S(1)}, u32[]{:S(2)}, u32[]{:S(2)}) collective-permute-start(bf16[16,5504]{1,0:T(8,128)(2,1)S(1)} %collective-permute-done.16), channel_id=1, source_target_pairs={{0,15},{1,0},{2,1},{3,2},{4,3},{5,4},{6,5},{7,6},{8,7},{9,8},{10,9... | collective-permute-start | bytes 528392 | tf_op jit(solution)/shard_map/ppermute | solution.py:150
  129.6 10.0 %collective-permute-start.20 = (bf16[16,5504]{1,0:T(8,128)(2,1)S(1)}, bf16[16,5504]{1,0:T(8,128)(2,1)S(1)}, u32[]{:S(2)}, u32[]{:S(2)}) collective-permute-start(bf16[16,5504]{1,0:T(8,128)(2,1)S(1)} %collective-permute-done.17), channel_id=1, source_target_pairs={{0,1},{1,2},{2,3},{3,4},{4,5},{5,6},{6,7},{7,8},{8,9},{9,10},{10,1... | collective-permute-start | bytes 528392 | tf_op jit(solution)/shard_map/ppermute | solution.py:146
  133.6 23.8 %collective-permute-start.26 = (bf16[2,256,1024]{2,1,0:T(8,128)(2,1)S(1)}, bf16[2,256,1024]{2,1,0:T(8,128)(2,1)S(1)}, u32[]{:S(2)}, u32[]{:S(2)}) collective-permute-start(bf16[2,256,1024]{2,1,0:T(8,128)(2,1)S(1)} %collective-permute-done.25), channel_id=1, source_target_pairs={{0,128},{32,160},{64,192},{96,224},{128,256},{160,288},{192,320},{... | collective-permute-start | bytes 3145736 | tf_op jit(solution)/shard_map/ppermute | solution.py:56
  157.5 9.1 %collective-permute-start.28 = (bf16[8,256,1024]{2,1,0:T(8,128)(2,1)S(1)}, bf16[8,256,1024]{2,1,0:T(8,128)(2,1)S(1)}, u32[]{:S(2)}, u32[]{:S(2)}) collective-permute-start(bf16[8,256,1024]{2,1,0:T(8,128)(2,1)S(1)} %constant_dynamic-update-slice_fusion.2), channel_id=1, source_target_pairs={{0,32},{32,0},{64,96},{96,64},{128,160},{160,128},{192,224},{224,1... | collective-permute-start | bytes 12582920 | tf_op jit(solution)/shard_map/ppermute | solution.py:61
  173.7 15.0 %collective-permute-start.29 = (bf16[3,16,2688]{2,1,0:T(8,128)(2,1)S(1)}, bf16[3,16,2688]{2,1,0:T(8,128)(2,1)S(1)}, u32[]{:S(2)}, u32[]{:S(2)}) collective-permute-start(bf16[3,16,2688]{2,1,0:T(8,128)(2,1)S(1)} %pad_maximum_fusion.2), channel_id=1, source_target_pairs={{0,16},{1,17},{2,18},{3,19},{4,20},{5,21},{6,22},{7,23},{8,24},{9,... | collective-permute-start | bytes 774152 | tf_op jit(solution)/shard_map/ppermute | solution.py:194
  176.8 22.5 %collective-permute-start.31 = (bf16[2,16,2688]{2,1,0:T(8,128)(2,1)S(1)}, bf16[2,16,2688]{2,1,0:T(8,128)(2,1)S(1)}, u32[]{:S(2)}, u32[]{:S(2)}) collective-permute-start(bf16[2,16,2688]{2,1,0:T(8,128)(2,1)S(1)} %pad_maximum_fusion.26), channel_id=1, source_target_pairs={{0,16},{1,17},{2,18},{3,19},{4,20},{5,21},{6,22},{7,23},{8,24},{9,... | collective-permute-start | bytes 516104 | tf_op jit(solution)/shard_map/ppermute | solution.py:194
  179.6 35.8 %collective-permute-start.33 = (bf16[2,16,2688]{2,1,0:T(8,128)(2,1)S(1)}, bf16[2,16,2688]{2,1,0:T(8,128)(2,1)S(1)}, u32[]{:S(2)}, u32[]{:S(2)}) collective-permute-start(bf16[2,16,2688]{2,1,0:T(8,128)(2,1)S(1)} %pad_maximum_fusion.27), channel_id=1, source_target_pairs={{0,16},{1,17},{2,18},{3,19},{4,20},{5,21},{6,22},{7,23},{8,24},{9,... | collective-permute-start | bytes 516104 | tf_op jit(solution)/shard_map/ppermute | solution.py:194
  182.7 48.7 %collective-permute-start.35 = (bf16[2,16,2688]{2,1,0:T(8,128)(2,1)S(1)}, bf16[2,16,2688]{2,1,0:T(8,128)(2,1)S(1)}, u32[]{:S(2)}, u32[]{:S(2)}) collective-permute-start(bf16[2,16,2688]{2,1,0:T(8,128)(2,1)S(1)} %pad_maximum_fusion.28), channel_id=1, source_target_pairs={{0,16},{1,17},{2,18},{3,19},{4,20},{5,21},{6,22},{7,23},{8,24},{9,... | collective-permute-start | bytes 516104 | tf_op jit(solution)/shard_map/ppermute | solution.py:194
  185.5 62.1 %collective-permute-start.37 = (bf16[2,16,2688]{2,1,0:T(8,128)(2,1)S(1)}, bf16[2,16,2688]{2,1,0:T(8,128)(2,1)S(1)}, u32[]{:S(2)}, u32[]{:S(2)}) collective-permute-start(bf16[2,16,2688]{2,1,0:T(8,128)(2,1)S(1)} %pad_maximum_fusion.29), channel_id=1, source_target_pairs={{0,16},{1,17},{2,18},{3,19},{4,20},{5,21},{6,22},{7,23},{8,24},{9,... | collective-permute-start | bytes 516104 | tf_op jit(solution)/shard_map/ppermute | solution.py:194
  199.3 64.4 %collective-permute-start.39 = (bf16[2,16,2688]{2,1,0:T(8,128)(2,1)S(1)}, bf16[2,16,2688]{2,1,0:T(8,128)(2,1)S(1)}, u32[]{:S(2)}, u32[]{:S(2)}) collective-permute-start(bf16[2,16,2688]{2,1,0:T(8,128)(2,1)S(1)} %pad_maximum_fusion.30), channel_id=1, source_target_pairs={{0,16},{1,17},{2,18},{3,19},{4,20},{5,21},{6,22},{7,23},{8,24},{9,... | collective-permute-start | bytes 516104 | tf_op jit(solution)/shard_map/ppermute | solution.py:194
  215.4 66.3 %collective-permute-start.41 = (bf16[2,16,2688]{2,1,0:T(8,128)(2,1)S(1)}, bf16[2,16,2688]{2,1,0:T(8,128)(2,1)S(1)}, u32[]{:S(2)}, u32[]{:S(2)}) collective-permute-start(bf16[2,16,2688]{2,1,0:T(8,128)(2,1)S(1)} %pad_maximum_fusion.31), channel_id=1, source_target_pairs={{0,16},{1,17},{2,18},{3,19},{4,20},{5,21},{6,22},{7,23},{8,24},{9,... | collective-permute-start | bytes 516104 | tf_op jit(solution)/shard_map/ppermute | solution.py:194
  231.5 64.9 %collective-permute-start.43 = (bf16[1,16,2688]{2,1,0:T(8,128)(2,1)S(1)}, bf16[1,16,2688]{2,1,0:T(8,128)(2,1)S(1)}, u32[]{:S(2)}, u32[]{:S(2)}) collective-permute-start(bf16[1,16,2688]{2,1,0:T(8,128)(2,1)S(1)} %get-tuple-element.35), channel_id=1, source_target_pairs={{0,16},{1,17},{2,18},{3,19},{4,20},{5,21},{6,22},{7,23},{8,24},{9,... | collective-permute-start | bytes 258056 | tf_op jit(solution)/shard_map/ppermute | solution.py:194
  269.5 10.1 %collective-permute-start.40 = (bf16[16,5504]{1,0:T(8,128)(2,1)S(1)}, bf16[16,5504]{1,0:T(8,128)(2,1)S(1)}, u32[]{:S(2)}, u32[]{:S(2)}) collective-permute-start(bf16[16,5504]{1,0:T(8,128)(2,1)S(1)} %pad_maximum_fusion.9), channel_id=1, source_target_pairs={{0,1},{1,2},{2,3},{3,4},{4,5},{5,6},{6,7},{7,8},{8,9},{9,10},{10,1... | collective-permute-start | bytes 528392 | tf_op jit(solution)/shard_map/ppermute | solution.py:209
  (34 other events, 337.0 us)

commit v4 on v2

--- a/solution.py
+++ b/solution.py
@@ -111,8 +111,17 @@
 
     ff_cols = gate_weight.shape[1]
     piece_rows = gate_weight.shape[0]
-    buffers = gather_pieces(jnp.concatenate([gate_weight, up_weight], axis=1))
-    keys = [k for ks, _ in buffers for k in ks]
+    own = jnp.concatenate([gate_weight, up_weight], axis=1)[None]
+    across = lax.ppermute(own, "dp", DP_X_SWAP)
+    pair_keys = [(0, 0, 0), (0, 1, 0)]
+    shift = lambda ks, dy: [((k[0] + dy) % DP_SUB[0], k[1], k[2]) for k in ks]
+    keys = (
+        [(0, 0, 0), (0, 1, 0)]
+        + shift(pair_keys, DP_SUB[0] - 1)
+        + shift(pair_keys, DP_SUB[0] - 2)
+        + shift(pair_keys, 1)
+    )
+    keys = keys + [(k[0], k[1], 1) for k in keys]
     ny, nx, nc = DP_SUB
     me = lax.axis_index("dp")
     my_y, my_x, my_c = me // (nx * nc), (me // nc) % nx, me % nc
@@ -128,13 +137,32 @@
     pair = jnp.stack([travelling, lax.ppermute(travelling, "tensor", TP_L_SWAP)])
     token_chunks = {0: pair}
     fwd = pair
+    bwd = pair
     for s in range(nz // 2):
+        if s == 1:
+            fwd, bwd, across = lax.optimization_barrier((fwd, bwd, across))
+            w_pair = jnp.concatenate([own, across])
+            w_fwd1 = lax.ppermute(w_pair, "dp", DP_Y_FWD)
+            w_bwd1 = lax.ppermute(w_pair, "dp", DP_Y_BWD)
+        if s == 4:
+            fwd, bwd, w_fwd1, w_bwd1 = lax.optimization_barrier((fwd, bwd, w_fwd1, w_bwd1))
+            w_fwd2 = lax.ppermute(w_fwd1, "dp", DP_Y_FWD)
+        if s == 6:
+            fwd, bwd, w_fwd2 = lax.optimization_barrier((fwd, bwd, w_fwd2))
+            w_chip = jnp.concatenate([w_pair, w_fwd1, w_fwd2, w_bwd1])
+            w_other = lax.ppermute(w_chip, "dp", DP_C_SWAP)
         fwd = lax.ppermute(fwd, "tensor", TP_Z_FWD)
         token_chunks[nz - 1 - s] = fwd
-    bwd = pair
-    for s in range(nz // 2 - 1):
-        bwd = lax.ppermute(bwd, "tensor", TP_Z_BWD)
-        token_chunks[s + 1] = bwd
+        if s < nz // 2 - 1:
+            bwd = lax.ppermute(bwd, "tensor", TP_Z_BWD)
+            token_chunks[s + 1] = bwd
+    buffers = [
+        ([(0, 0, 0), (0, 1, 0)], w_pair),
+        ([None] * 2, w_fwd1),
+        ([None] * 2, w_fwd2),
+        ([None] * 2, w_bwd1),
+        ([None] * 8, w_other),
+    ]
     gathered = jnp.concatenate([token_chunks[k] for k in range(nz)], axis=0)
     row_total = gathered.shape[0] * gathered.shape[1]
     normed = gathered.reshape(row_total, feature_count)

time: 240 us -> 239 us (level)
  waiting for transfers between devices: 72.7 us -> 84 us
  local copies, waits for them, and re-layouts: 10.8 us -> 3.04 us
  starting transfers between devices: 141 us -> 134 us
  other arithmetic: 3.31 us -> 6.2 us
    ppermute x7, starting transfers between devices: 43.2 us -> 25.7 us  [per_device(): bwd = lax.ppermute(bwd, 'tensor', TP_Z_BWD)]
    ppermute x8, starting transfers between devices: 15.3 us -> 24.9 us  [per_device(): fwd = lax.ppermute(fwd, 'tensor', TP_Z_FWD)]
    ppermute x7, waiting for transfers between devices: 8.59 us -> 17 us  [per_device(): bwd = lax.ppermute(bwd, 'tensor', TP_Z_BWD)]
    ppermute x8, waiting for transfers between devices: 17.8 us -> 24.3 us  [per_device(): fwd = lax.ppermute(fwd, 'tensor', TP_Z_FWD)]
    unnamed x24, local copies, waits for them, and re-layouts: 6.26 us -> 0.47 us
    ppermute x5, waiting for transfers between devices: 4.81 us -> 0.01 us  [the longest x1 0.01 us: per_device(): across = lax.ppermute(own, 'dp', DP_X_SWAP)]
    ppermute x8, waiting for transfers between devices: 28.3 us -> 30.9 us  [per_device(): got = lax.ppermute(fwd, 'tensor', TP_Z_FWD)]
    dot_general x6 -> x5, matrix products: 5.62 us -> 5.39 us  [per_device(): jnp.dot(normed[:, col:col + width], buf.reshape(width, 2 * ff_cols), pref...]
  transfers between devices with their start and end apart: 38 -> 38, of which waited for: 18 -> 22; matrix products, arithmetic and copies ran while one was open for 5% -> 4% of each run, Pallas kernels for 0% -> 0%
where the time goes in v4:
time: 239 us; the launch traced here: 237 us
  starting transfers between devices  134 us (56%)
  waiting for transfers between devices  84 us (35%)
  matrix products  8.26 us (3%)
  other arithmetic  6.2 us (3%)
  local copies, waits for them, and re-layouts  3.04 us (1%)
    ppermute x7, starting transfers between devices, per_device(): got = lax.ppermute(bwd, 'tensor', TP_Z_BWD)  37 us
    ppermute x8, waiting for transfers between devices, per_device(): got = lax.ppermute(fwd, 'tensor', TP_Z_FWD)  30.9 us
    ppermute x7, starting transfers between devices, per_device(): bwd = lax.ppermute(bwd, 'tensor', TP_Z_BWD)  25.7 us
    ppermute x8, starting transfers between devices, per_device(): fwd = lax.ppermute(fwd, 'tensor', TP_Z_FWD)  24.9 us
    ppermute x8, waiting for transfers between devices, per_device(): fwd = lax.ppermute(fwd, 'tensor', TP_Z_FWD)  24.3 us
    ppermute x7, waiting for transfers between devices, per_device(): bwd = lax.ppermute(bwd, 'tensor', TP_Z_BWD)  17 us
    ppermute x8, starting transfers between devices, per_device(): got = lax.ppermute(fwd, 'tensor', TP_Z_FWD)  15.4 us
    all_to_all x1, starting transfers between devices, per_device(): lax.all_to_all(jnp.concatenate([outgoing, place_cols], axis=1).reshape(dp...  8.99 us
  transfers between devices with their start and end apart: 38, of which 22 were waited for; matrix products, arithmetic and copies ran while one was open for 4% of the time, Pallas kernels for 0%

profile of v4, /device:TPU:24, one launch (start us, length us, event | category | flops | bytes accessed | tf_op | source)
XLA Modules:
  0.0 237.0 jit_solution(13430877360002757631)
XLA Ops:
  3.0 9.0 %all-to-all-start = ((bf16[16,2,4224]{2,1,0:T(2,128)(2,1)}), bf16[16,2,4224]{2,1,0:T(2,128)(2,1)S(1)}, u32[]{:S(2)}, u32[]{:S(2)}) async-start(bf16[16,2,4224]{2,1,0:T(2,128)(2,1)} %reshape.916), calls=%async_computation | async-start | bytes 540672 | tf_op jit(solution)/shard_map/all_to_all | solution.py:97
  13.1 4.9 %collective-permute-start.3 = (bf16[1,256,1024]{2,1,0:T(8,128)(2,1)S(1)}, bf16[1,256,1024]{2,1,0:T(8,128)(2,1)S(1)}, u32[]{:S(2)}, u32[]{:S(2)}) collective-permute-start(bf16[1,256,1024]{2,1,0:T(8,128)(2,1)S(1)} %maximum_bitcast_fusion), channel_id=1, source_target_pairs={{0,64},{32,96},{64,0},{96,32},{128,192},{160,224},{192,128},{224,1... | collective-permute-start | bytes 1572872 | tf_op jit(solution)/shard_map/ppermute | solution.py:115
  24.0 8.3 %collective-permute-done = bf16[16,4096]{1,0:T(8,128)(2,1)S(1)} collective-permute-done((bf16[16,4096]{1,0:T(8,128)(2,1)S(1)}, bf16[16,4096]{1,0:T(8,128)(2,1)S(1)}, u32[]{:S(2)}, u32[]{:S(2)}) %collective-permute-start) | collective-permute-done | bytes 131104 | tf_op jit(solution)/shard_map/ppermute | solution.py:137
  32.3 10.6 %collective-permute-start.1 = (bf16[2,16,4096]{2,1,0:T(8,128)(2,1)S(1)}, bf16[2,16,4096]{2,1,0:T(8,128)(2,1)S(1)}, u32[]{:S(2)}, u32[]{:S(2)}) collective-permute-start(bf16[2,16,4096]{2,1,0:T(8,128)(2,1)S(1)} %pad_maximum_fusion.2), channel_id=1, source_target_pairs={{0,15},{1,0},{2,1},{3,2},{4,3},{5,4},{6,5},{7,6},{8,7},{9,8},{10,9... | collective-permute-start | bytes 786440 | tf_op jit(solution)/shard_map/ppermute | solution.py:157
  47.9 5.3 %collective-permute-done.2 = bf16[2,16,4096]{2,1,0:T(8,128)(2,1)S(1)} collective-permute-done((bf16[2,16,4096]{2,1,0:T(8,128)(2,1)S(1)}, bf16[2,16,4096]{2,1,0:T(8,128)(2,1)S(1)}, u32[]{:S(2)}, u32[]{:S(2)}) %collective-permute-start.2) | collective-permute-done | bytes 262176 | tf_op jit(solution)/shard_map/ppermute | solution.py:154
  61.1 3.9 %collective-permute-start.7 = (bf16[2,16,4096]{2,1,0:T(8,128)(2,1)S(1)}, bf16[2,16,4096]{2,1,0:T(8,128)(2,1)S(1)}, u32[]{:S(2)}, u32[]{:S(2)}) collective-permute-start(bf16[2,16,4096]{2,1,0:T(8,128)(2,1)S(1)} %collective-permute-done.2), channel_id=1, source_target_pairs={{0,1},{1,2},{2,3},{3,4},{4,5},{5,6},{6,7},{7,8},{8,9},{9,10},{10,1... | collective-permute-start | bytes 786440 | tf_op jit(solution)/shard_map/ppermute | solution.py:154
  75.7 4.3 %collective-permute-start.6 = (bf16[2,16,4096]{2,1,0:T(8,128)(2,1)S(1)}, bf16[2,16,4096]{2,1,0:T(8,128)(2,1)S(1)}, u32[]{:S(2)}, u32[]{:S(2)}) collective-permute-start(bf16[2,16,4096]{2,1,0:T(8,128)(2,1)S(1)} %collective-permute-done.5), channel_id=1, source_target_pairs={{0,15},{1,0},{2,1},{3,2},{4,3},{5,4},{6,5},{7,6},{8,7},{9,8},{10,9... | collective-permute-start | bytes 786440 | tf_op jit(solution)/shard_map/ppermute | solution.py:157
  84.0 5.6 %collective-permute-done.9 = bf16[2,16,4096]{2,1,0:T(8,128)(2,1)S(1)} collective-permute-done((bf16[2,16,4096]{2,1,0:T(8,128)(2,1)S(1)}, bf16[2,16,4096]{2,1,0:T(8,128)(2,1)S(1)}, u32[]{:S(2)}, u32[]{:S(2)}) %collective-permute-start.9) | collective-permute-done | bytes 262176 | tf_op jit(solution)/shard_map/ppermute | solution.py:154
  95.2 3.9 %collective-permute-start.14 = (bf16[2,16,4096]{2,1,0:T(8,128)(2,1)S(1)}, bf16[2,16,4096]{2,1,0:T(8,128)(2,1)S(1)}, u32[]{:S(2)}, u32[]{:S(2)}) collective-permute-start(bf16[2,16,4096]{2,1,0:T(8,128)(2,1)S(1)} %collective-permute-done.9), channel_id=1, source_target_pairs={{0,1},{1,2},{2,3},{3,4},{4,5},{5,6},{6,7},{7,8},{8,9},{9,10},{10,1... | collective-permute-start | bytes 786440 | tf_op jit(solution)/shard_map/ppermute | solution.py:154
  99.2 4.6 %collective-permute-done.12 = bf16[2,16,4096]{2,1,0:T(8,128)(2,1)S(1)} collective-permute-done((bf16[2,16,4096]{2,1,0:T(8,128)(2,1)S(1)}, bf16[2,16,4096]{2,1,0:T(8,128)(2,1)S(1)}, u32[]{:S(2)}, u32[]{:S(2)}) %collective-permute-start.12) | collective-permute-done | bytes 262176 | tf_op jit(solution)/shard_map/ppermute | solution.py:157
  105.7 3.9 %collective-permute-start.15 = (bf16[2,16,4096]{2,1,0:T(8,128)(2,1)S(1)}, bf16[2,16,4096]{2,1,0:T(8,128)(2,1)S(1)}, u32[]{:S(2)}, u32[]{:S(2)}) collective-permute-start(bf16[2,16,4096]{2,1,0:T(8,128)(2,1)S(1)} %collective-permute-done.14), channel_id=1, source_target_pairs={{0,1},{1,2},{2,3},{3,4},{4,5},{5,6},{6,7},{7,8},{8,9},{9,10},{10,1... | collective-permute-start | bytes 786440 | tf_op jit(solution)/shard_map/ppermute | solution.py:154
  117.4 3.9 %collective-permute-start.18 = (bf16[2,16,4096]{2,1,0:T(8,128)(2,1)S(1)}, bf16[2,16,4096]{2,1,0:T(8,128)(2,1)S(1)}, u32[]{:S(2)}, u32[]{:S(2)}) collective-permute-start(bf16[2,16,4096]{2,1,0:T(8,128)(2,1)S(1)} %collective-permute-done.15), channel_id=1, source_target_pairs={{0,1},{1,2},{2,3},{3,4},{4,5},{5,6},{6,7},{7,8},{8,9},{9,10},{10,1... | collective-permute-start | bytes 786440 | tf_op jit(solution)/shard_map/ppermute | solution.py:154
  129.6 6.7 %collective-permute-done.19 = bf16[2,16,4096]{2,1,0:T(8,128)(2,1)S(1)} collective-permute-done((bf16[2,16,4096]{2,1,0:T(8,128)(2,1)S(1)}, bf16[2,16,4096]{2,1,0:T(8,128)(2,1)S(1)}, u32[]{:S(2)}, u32[]{:S(2)}) %collective-permute-start.19) | collective-permute-done | bytes 262176 | tf_op jit(solution)/shard_map/ppermute | solution.py:154
  146.8 5.1 %collective-permute-start.29 = (bf16[2,16,4096]{2,1,0:T(8,128)(2,1)S(1)}, bf16[2,16,4096]{2,1,0:T(8,128)(2,1)S(1)}, u32[]{:S(2)}, u32[]{:S(2)}) collective-permute-start(bf16[2,16,4096]{2,1,0:T(8,128)(2,1)S(1)} %bitcast.148), channel_id=1, source_target_pairs={{0,15},{1,0},{2,1},{3,2},{4,3},{5,4},{6,5},{7,6},{8,7},{9,8},{10,9... | collective-permute-start | bytes 786440 | tf_op jit(solution)/shard_map/ppermute | solution.py:196
  156.5 5.1 %collective-permute-start.30 = (bf16[2,16,4096]{2,1,0:T(8,128)(2,1)S(1)}, bf16[2,16,4096]{2,1,0:T(8,128)(2,1)S(1)}, u32[]{:S(2)}, u32[]{:S(2)}) collective-permute-start(bf16[2,16,4096]{2,1,0:T(8,128)(2,1)S(1)} %fusion.18), channel_id=1, source_target_pairs={{0,15},{1,0},{2,1},{3,2},{4,3},{5,4},{6,5},{7,6},{8,7},{9,8},{10,9... | collective-permute-start | bytes 786440 | tf_op jit(solution)/shard_map/ppermute | solution.py:196
  166.5 5.4 %collective-permute-start.31 = (bf16[2,16,4096]{2,1,0:T(8,128)(2,1)S(1)}, bf16[2,16,4096]{2,1,0:T(8,128)(2,1)S(1)}, u32[]{:S(2)}, u32[]{:S(2)}) collective-permute-start(bf16[2,16,4096]{2,1,0:T(8,128)(2,1)S(1)} %fusion.17), channel_id=1, source_target_pairs={{0,15},{1,0},{2,1},{3,2},{4,3},{5,4},{6,5},{7,6},{8,7},{9,8},{10,9... | collective-permute-start | bytes 786440 | tf_op jit(solution)/shard_map/ppermute | solution.py:196
  172.0 3.7 %collective-permute-done.23 = bf16[2,16,4096]{2,1,0:T(8,128)(2,1)S(1)} collective-permute-done((bf16[2,16,4096]{2,1,0:T(8,128)(2,1)S(1)}, bf16[2,16,4096]{2,1,0:T(8,128)(2,1)S(1)}, u32[]{:S(2)}, u32[]{:S(2)}) %collective-permute-start.23) | collective-permute-done | bytes 262176 | tf_op jit(solution)/shard_map/ppermute | solution.py:189
  177.9 5.6 %collective-permute-start.32 = (bf16[2,16,4096]{2,1,0:T(8,128)(2,1)S(1)}, bf16[2,16,4096]{2,1,0:T(8,128)(2,1)S(1)}, u32[]{:S(2)}, u32[]{:S(2)}) collective-permute-start(bf16[2,16,4096]{2,1,0:T(8,128)(2,1)S(1)} %fusion.16), channel_id=1, source_target_pairs={{0,15},{1,0},{2,1},{3,2},{4,3},{5,4},{6,5},{7,6},{8,7},{9,8},{10,9... | collective-permute-start | bytes 786440 | tf_op jit(solution)/shard_map/ppermute | solution.py:196
  183.5 4.5 %collective-permute-done.24 = bf16[2,16,4096]{2,1,0:T(8,128)(2,1)S(1)} collective-permute-done((bf16[2,16,4096]{2,1,0:T(8,128)(2,1)S(1)}, bf16[2,16,4096]{2,1,0:T(8,128)(2,1)S(1)}, u32[]{:S(2)}, u32[]{:S(2)}) %collective-permute-start.24) | collective-permute-done | bytes 262176 | tf_op jit(solution)/shard_map/ppermute | solution.py:189
  190.1 5.4 %collective-permute-start.33 = (bf16[2,16,4096]{2,1,0:T(8,128)(2,1)S(1)}, bf16[2,16,4096]{2,1,0:T(8,128)(2,1)S(1)}, u32[]{:S(2)}, u32[]{:S(2)}) collective-permute-start(bf16[2,16,4096]{2,1,0:T(8,128)(2,1)S(1)} %fusion.15), channel_id=1, source_target_pairs={{0,15},{1,0},{2,1},{3,2},{4,3},{5,4},{6,5},{7,6},{8,7},{9,8},{10,9... | collective-permute-start | bytes 786440 | tf_op jit(solution)/shard_map/ppermute | solution.py:196
  195.5 4.0 %collective-permute-done.25 = bf16[2,16,4096]{2,1,0:T(8,128)(2,1)S(1)} collective-permute-done((bf16[2,16,4096]{2,1,0:T(8,128)(2,1)S(1)}, bf16[2,16,4096]{2,1,0:T(8,128)(2,1)S(1)}, u32[]{:S(2)}, u32[]{:S(2)}) %collective-permute-start.25) | collective-permute-done | bytes 262176 | tf_op jit(solution)/shard_map/ppermute | solution.py:189
  201.6 5.2 %collective-permute-start.34 = (bf16[2,16,4096]{2,1,0:T(8,128)(2,1)S(1)}, bf16[2,16,4096]{2,1,0:T(8,128)(2,1)S(1)}, u32[]{:S(2)}, u32[]{:S(2)}) collective-permute-start(bf16[2,16,4096]{2,1,0:T(8,128)(2,1)S(1)} %fusion.14), channel_id=1, source_target_pairs={{0,15},{1,0},{2,1},{3,2},{4,3},{5,4},{6,5},{7,6},{8,7},{9,8},{10,9... | collective-permute-start | bytes 786440 | tf_op jit(solution)/shard_map/ppermute | solution.py:196
  212.2 5.1 %collective-permute-start.35 = (bf16[2,16,4096]{2,1,0:T(8,128)(2,1)S(1)}, bf16[2,16,4096]{2,1,0:T(8,128)(2,1)S(1)}, u32[]{:S(2)}, u32[]{:S(2)}) collective-permute-start(bf16[2,16,4096]{2,1,0:T(8,128)(2,1)S(1)} %fusion.13), channel_id=1, source_target_pairs={{0,15},{1,0},{2,1},{3,2},{4,3},{5,4},{6,5},{7,6},{8,7},{9,8},{10,9... | collective-permute-start | bytes 786440 | tf_op jit(solution)/shard_map/ppermute | solution.py:196
  221.8 7.5 %collective-permute-done.28 = bf16[2,16,4096]{2,1,0:T(8,128)(2,1)S(1)} collective-permute-done((bf16[2,16,4096]{2,1,0:T(8,128)(2,1)S(1)}, bf16[2,16,4096]{2,1,0:T(8,128)(2,1)S(1)}, u32[]{:S(2)}, u32[]{:S(2)}) %collective-permute-start.28) | collective-permute-done | bytes 262176 | tf_op jit(solution)/shard_map/ppermute | solution.py:189
  (136 shorter events, 103.6 us)
Async XLA Ops:
  3.0 17.4 %all-to-all-start = ((bf16[16,2,4224]{2,1,0:T(2,128)(2,1)}), bf16[16,2,4224]{2,1,0:T(2,128)(2,1)S(1)}, u32[]{:S(2)}, u32[]{:S(2)}) async-start(bf16[16,2,4224]{2,1,0:T(2,128)(2,1)} %reshape.916), calls=%async_computation | async-start | bytes 540672 | tf_op jit(solution)/shard_map/all_to_all | solution.py:97
  13.1 31.8 %collective-permute-start.3 = (bf16[1,256,1024]{2,1,0:T(8,128)(2,1)S(1)}, bf16[1,256,1024]{2,1,0:T(8,128)(2,1)S(1)}, u32[]{:S(2)}, u32[]{:S(2)}) collective-permute-start(bf16[1,256,1024]{2,1,0:T(8,128)(2,1)S(1)} %maximum_bitcast_fusion), channel_id=1, source_target_pairs={{0,64},{32,96},{64,0},{96,32},{128,192},{160,224},{192,128},{224,1... | collective-permute-start | bytes 1572872 | tf_op jit(solution)/shard_map/ppermute | solution.py:115
  21.7 10.5 %collective-permute-start = (bf16[16,4096]{1,0:T(8,128)(2,1)S(1)}, bf16[16,4096]{1,0:T(8,128)(2,1)S(1)}, u32[]{:S(2)}, u32[]{:S(2)}) collective-permute-start(bf16[16,4096]{1,0:T(8,128)(2,1)S(1)} %broadcast_select_fusion), channel_id=1, source_target_pairs={{0,16},{1,17},{2,18},{3,19},{4,20},{5,21},{6,22},{7,23},{8,24},{9,... | collective-permute-start | bytes 393224 | tf_op jit(solution)/shard_map/ppermute | solution.py:137
  32.3 15.7 %collective-permute-start.1 = (bf16[2,16,4096]{2,1,0:T(8,128)(2,1)S(1)}, bf16[2,16,4096]{2,1,0:T(8,128)(2,1)S(1)}, u32[]{:S(2)}, u32[]{:S(2)}) collective-permute-start(bf16[2,16,4096]{2,1,0:T(8,128)(2,1)S(1)} %pad_maximum_fusion.2), channel_id=1, source_target_pairs={{0,15},{1,0},{2,1},{3,2},{4,3},{5,4},{6,5},{7,6},{8,7},{9,8},{10,9... | collective-permute-start | bytes 786440 | tf_op jit(solution)/shard_map/ppermute | solution.py:157
  42.9 10.4 %collective-permute-start.2 = (bf16[2,16,4096]{2,1,0:T(8,128)(2,1)S(1)}, bf16[2,16,4096]{2,1,0:T(8,128)(2,1)S(1)}, u32[]{:S(2)}, u32[]{:S(2)}) collective-permute-start(bf16[2,16,4096]{2,1,0:T(8,128)(2,1)S(1)} %pad_maximum_fusion.2), channel_id=1, source_target_pairs={{0,1},{1,2},{2,3},{3,4},{4,5},{5,6},{6,7},{7,8},{8,9},{9,10},{10,1... | collective-permute-start | bytes 786440 | tf_op jit(solution)/shard_map/ppermute | solution.py:154
  53.3 36.2 %collective-permute-start.10 = (bf16[2,256,1024]{2,1,0:T(8,128)(2,1)S(1)}, bf16[2,256,1024]{2,1,0:T(8,128)(2,1)S(1)}, u32[]{:S(2)}, u32[]{:S(2)}) collective-permute-start(bf16[2,256,1024]{2,1,0:T(8,128)(2,1)S(1)} %pad_maximum_fusion), channel_id=1, source_target_pairs={{0,128},{32,160},{64,192},{96,224},{128,256},{160,288},{192,320},{... | collective-permute-start | bytes 3145736 | tf_op jit(solution)/shard_map/ppermute | solution.py:145
  55.8 33.7 %collective-permute-start.11 = (bf16[2,256,1024]{2,1,0:T(8,128)(2,1)S(1)}, bf16[2,256,1024]{2,1,0:T(8,128)(2,1)S(1)}, u32[]{:S(2)}, u32[]{:S(2)}) collective-permute-start(bf16[2,256,1024]{2,1,0:T(8,128)(2,1)S(1)} %pad_maximum_fusion), channel_id=1, source_target_pairs={{0,384},{32,416},{64,448},{96,480},{128,0},{160,32},{192,64},{224,... | collective-permute-start | bytes 3145736 | tf_op jit(solution)/shard_map/ppermute | solution.py:146
  89.6 25.9 %collective-permute-start.16 = (bf16[2,256,1024]{2,1,0:T(8,128)(2,1)S(1)}, bf16[2,256,1024]{2,1,0:T(8,128)(2,1)S(1)}, u32[]{:S(2)}, u32[]{:S(2)}) collective-permute-start(bf16[2,256,1024]{2,1,0:T(8,128)(2,1)S(1)} %collective-permute-done.10), channel_id=1, source_target_pairs={{0,128},{32,160},{64,192},{96,224},{128,256},{160,288},{192,320},{... | collective-permute-start | bytes 3145736 | tf_op jit(solution)/shard_map/ppermute | solution.py:149
  93.2 10.6 %collective-permute-start.12 = (bf16[2,16,4096]{2,1,0:T(8,128)(2,1)S(1)}, bf16[2,16,4096]{2,1,0:T(8,128)(2,1)S(1)}, u32[]{:S(2)}, u32[]{:S(2)}) collective-permute-start(bf16[2,16,4096]{2,1,0:T(8,128)(2,1)S(1)} %collective-permute-done.6), channel_id=1, source_target_pairs={{0,15},{1,0},{2,1},{3,2},{4,3},{5,4},{6,5},{7,6},{8,7},{9,8},{10,9... | collective-permute-start | bytes 786440 | tf_op jit(solution)/shard_map/ppermute | solution.py:157
  95.2 10.6 %collective-permute-start.14 = (bf16[2,16,4096]{2,1,0:T(8,128)(2,1)S(1)}, bf16[2,16,4096]{2,1,0:T(8,128)(2,1)S(1)}, u32[]{:S(2)}, u32[]{:S(2)}) collective-permute-start(bf16[2,16,4096]{2,1,0:T(8,128)(2,1)S(1)} %collective-permute-done.9), channel_id=1, source_target_pairs={{0,1},{1,2},{2,3},{3,4},{4,5},{5,6},{6,7},{7,8},{8,9},{9,10},{10,1... | collective-permute-start | bytes 786440 | tf_op jit(solution)/shard_map/ppermute | solution.py:154
  105.7 9.7 %collective-permute-start.15 = (bf16[2,16,4096]{2,1,0:T(8,128)(2,1)S(1)}, bf16[2,16,4096]{2,1,0:T(8,128)(2,1)S(1)}, u32[]{:S(2)}, u32[]{:S(2)}) collective-permute-start(bf16[2,16,4096]{2,1,0:T(8,128)(2,1)S(1)} %collective-permute-done.14), channel_id=1, source_target_pairs={{0,1},{1,2},{2,3},{3,4},{4,5},{5,6},{6,7},{7,8},{8,9},{9,10},{10,1... | collective-permute-start | bytes 786440 | tf_op jit(solution)/shard_map/ppermute | solution.py:154
  115.5 14.1 %collective-permute-start.17 = (bf16[2,16,4096]{2,1,0:T(8,128)(2,1)S(1)}, bf16[2,16,4096]{2,1,0:T(8,128)(2,1)S(1)}, u32[]{:S(2)}, u32[]{:S(2)}) collective-permute-start(bf16[2,16,4096]{2,1,0:T(8,128)(2,1)S(1)} %collective-permute-done.13), channel_id=1, source_target_pairs={{0,15},{1,0},{2,1},{3,2},{4,3},{5,4},{6,5},{7,6},{8,7},{9,8},{10,9... | collective-permute-start | bytes 786440 | tf_op jit(solution)/shard_map/ppermute | solution.py:157
  121.5 18.0 %collective-permute-start.20 = (bf16[8,256,1024]{2,1,0:T(8,128)(2,1)S(1)}, bf16[8,256,1024]{2,1,0:T(8,128)(2,1)S(1)}, u32[]{:S(2)}, u32[]{:S(2)}) collective-permute-start(bf16[8,256,1024]{2,1,0:T(8,128)(2,1)S(1)} %constant_dynamic-update-slice_fusion.17), channel_id=1, source_target_pairs={{0,32},{32,0},{64,96},{96,64},{128,160},{160,128},{192,224},{224,1... | collective-permute-start | bytes 12582920 | tf_op jit(solution)/shard_map/ppermute | solution.py:153
  154.4 10.0 %collective-permute-start.22 = (bf16[2,16,4096]{2,1,0:T(8,128)(2,1)S(1)}, bf16[2,16,4096]{2,1,0:T(8,128)(2,1)S(1)}, u32[]{:S(2)}, u32[]{:S(2)}) collective-permute-start(bf16[2,16,4096]{2,1,0:T(8,128)(2,1)S(1)} %fusion.25), channel_id=1, source_target_pairs={{0,1},{1,2},{2,3},{3,4},{4,5},{5,6},{6,7},{7,8},{8,9},{9,10},{10,1... | collective-permute-start | bytes 786440 | tf_op jit(solution)/shard_map/ppermute | solution.py:189
  156.5 10.0 %collective-permute-start.30 = (bf16[2,16,4096]{2,1,0:T(8,128)(2,1)S(1)}, bf16[2,16,4096]{2,1,0:T(8,128)(2,1)S(1)}, u32[]{:S(2)}, u32[]{:S(2)}) collective-permute-start(bf16[2,16,4096]{2,1,0:T(8,128)(2,1)S(1)} %fusion.18), channel_id=1, source_target_pairs={{0,15},{1,0},{2,1},{3,2},{4,3},{5,4},{6,5},{7,6},{8,7},{9,8},{10,9... | collective-permute-start | bytes 786440 | tf_op jit(solution)/shard_map/ppermute | solution.py:196
  164.5 11.2 %collective-permute-start.23 = (bf16[2,16,4096]{2,1,0:T(8,128)(2,1)S(1)}, bf16[2,16,4096]{2,1,0:T(8,128)(2,1)S(1)}, u32[]{:S(2)}, u32[]{:S(2)}) collective-permute-start(bf16[2,16,4096]{2,1,0:T(8,128)(2,1)S(1)} %fusion.24), channel_id=1, source_target_pairs={{0,1},{1,2},{2,3},{3,4},{4,5},{5,6},{6,7},{7,8},{8,9},{9,10},{10,1... | collective-permute-start | bytes 786440 | tf_op jit(solution)/shard_map/ppermute | solution.py:189
  166.5 11.3 %collective-permute-start.31 = (bf16[2,16,4096]{2,1,0:T(8,128)(2,1)S(1)}, bf16[2,16,4096]{2,1,0:T(8,128)(2,1)S(1)}, u32[]{:S(2)}, u32[]{:S(2)}) collective-permute-start(bf16[2,16,4096]{2,1,0:T(8,128)(2,1)S(1)} %fusion.17), channel_id=1, source_target_pairs={{0,15},{1,0},{2,1},{3,2},{4,3},{5,4},{6,5},{7,6},{8,7},{9,8},{10,9... | collective-permute-start | bytes 786440 | tf_op jit(solution)/shard_map/ppermute | solution.py:196
  175.8 12.3 %collective-permute-start.24 = (bf16[2,16,4096]{2,1,0:T(8,128)(2,1)S(1)}, bf16[2,16,4096]{2,1,0:T(8,128)(2,1)S(1)}, u32[]{:S(2)}, u32[]{:S(2)}) collective-permute-start(bf16[2,16,4096]{2,1,0:T(8,128)(2,1)S(1)} %fusion.23), channel_id=1, source_target_pairs={{0,1},{1,2},{2,3},{3,4},{4,5},{5,6},{6,7},{7,8},{8,9},{9,10},{10,1... | collective-permute-start | bytes 786440 | tf_op jit(solution)/shard_map/ppermute | solution.py:189
  177.9 12.1 %collective-permute-start.32 = (bf16[2,16,4096]{2,1,0:T(8,128)(2,1)S(1)}, bf16[2,16,4096]{2,1,0:T(8,128)(2,1)S(1)}, u32[]{:S(2)}, u32[]{:S(2)}) collective-permute-start(bf16[2,16,4096]{2,1,0:T(8,128)(2,1)S(1)} %fusion.16), channel_id=1, source_target_pairs={{0,15},{1,0},{2,1},{3,2},{4,3},{5,4},{6,5},{7,6},{8,7},{9,8},{10,9... | collective-permute-start | bytes 786440 | tf_op jit(solution)/shard_map/ppermute | solution.py:196
  188.1 11.4 %collective-permute-start.25 = (bf16[2,16,4096]{2,1,0:T(8,128)(2,1)S(1)}, bf16[2,16,4096]{2,1,0:T(8,128)(2,1)S(1)}, u32[]{:S(2)}, u32[]{:S(2)}) collective-permute-start(bf16[2,16,4096]{2,1,0:T(8,128)(2,1)S(1)} %fusion.22), channel_id=1, source_target_pairs={{0,1},{1,2},{2,3},{3,4},{4,5},{5,6},{6,7},{7,8},{8,9},{9,10},{10,1... | collective-permute-start | bytes 786440 | tf_op jit(solution)/shard_map/ppermute | solution.py:189
  190.1 11.4 %collective-permute-start.33 = (bf16[2,16,4096]{2,1,0:T(8,128)(2,1)S(1)}, bf16[2,16,4096]{2,1,0:T(8,128)(2,1)S(1)}, u32[]{:S(2)}, u32[]{:S(2)}) collective-permute-start(bf16[2,16,4096]{2,1,0:T(8,128)(2,1)S(1)} %fusion.15), channel_id=1, source_target_pairs={{0,15},{1,0},{2,1},{3,2},{4,3},{5,4},{6,5},{7,6},{8,7},{9,8},{10,9... | collective-permute-start | bytes 786440 | tf_op jit(solution)/shard_map/ppermute | solution.py:196
  199.6 10.6 %collective-permute-start.26 = (bf16[2,16,4096]{2,1,0:T(8,128)(2,1)S(1)}, bf16[2,16,4096]{2,1,0:T(8,128)(2,1)S(1)}, u32[]{:S(2)}, u32[]{:S(2)}) collective-permute-start(bf16[2,16,4096]{2,1,0:T(8,128)(2,1)S(1)} %fusion.21), channel_id=1, source_target_pairs={{0,1},{1,2},{2,3},{3,4},{4,5},{5,6},{6,7},{7,8},{8,9},{9,10},{10,1... | collective-permute-start | bytes 786440 | tf_op jit(solution)/shard_map/ppermute | solution.py:189
  201.6 10.5 %collective-permute-start.34 = (bf16[2,16,4096]{2,1,0:T(8,128)(2,1)S(1)}, bf16[2,16,4096]{2,1,0:T(8,128)(2,1)S(1)}, u32[]{:S(2)}, u32[]{:S(2)}) collective-permute-start(bf16[2,16,4096]{2,1,0:T(8,128)(2,1)S(1)} %fusion.14), channel_id=1, source_target_pairs={{0,15},{1,0},{2,1},{3,2},{4,3},{5,4},{6,5},{7,6},{8,7},{9,8},{10,9... | collective-permute-start | bytes 786440 | tf_op jit(solution)/shard_map/ppermute | solution.py:196
  210.2 9.6 %collective-permute-start.27 = (bf16[2,16,4096]{2,1,0:T(8,128)(2,1)S(1)}, bf16[2,16,4096]{2,1,0:T(8,128)(2,1)S(1)}, u32[]{:S(2)}, u32[]{:S(2)}) collective-permute-start(bf16[2,16,4096]{2,1,0:T(8,128)(2,1)S(1)} %fusion.20), channel_id=1, source_target_pairs={{0,1},{1,2},{2,3},{3,4},{4,5},{5,6},{6,7},{7,8},{8,9},{9,10},{10,1... | collective-permute-start | bytes 786440 | tf_op jit(solution)/shard_map/ppermute | solution.py:189
  (17 other events, 173.4 us)

commit v5 on v2

--- a/solution.py
+++ b/solution.py
@@ -36,6 +36,23 @@
 TP_L_SWAP = tp_perm(lambda l, z: (l + 1, z))
 TP_Z_FWD = tp_perm(lambda l, z: (l, z + 1))
 TP_Z_BWD = tp_perm(lambda l, z: (l, z - 1))
+
+
+def split_perm(cores):
+    n_tp = TP_SUB[0] * TP_SUB[1]
+    n_dp = DP_SUB[0] * DP_SUB[1] * DP_SUB[2]
+    fwd = dict(TP_Z_FWD)
+    bwd = dict(TP_Z_BWD)
+    return [
+        (d * n_tp + t, d * n_tp + (fwd[t] if d % 2 == 0 else bwd[t]))
+        for d in range(n_dp)
+        for t in range(n_tp)
+        if d % 2 in cores
+    ]
+
+
+SPLIT_BOTH = split_perm((0, 1))
+SPLIT_FWD_ONLY = split_perm((0,))
 
 
 def normalize(row_block):
@@ -125,18 +142,23 @@
     travelling = jnp.take(
         travelling.reshape(shard_rows, dp_count, piece_rows), piece_index, axis=1
     ).reshape(shard_rows, feature_count)
-    pair = jnp.stack([travelling, lax.ppermute(travelling, "tensor", TP_L_SWAP)])
-    token_chunks = {0: pair}
-    fwd = pair
+    on_core0 = (me % nc) == 0
+    pick = lambda a, b: jnp.where(on_core0, a, b)
+    ring_axes = ("dp", "tensor")
+    my_pair = jnp.stack([travelling, lax.ppermute(travelling, "tensor", TP_L_SWAP)])
+    other_pair = lax.ppermute(my_pair, "dp", DP_C_SWAP)
+    carried = pick(jnp.stack([my_pair, other_pair]), jnp.stack([other_pair, my_pair]))
+    arrivals = []
     for s in range(nz // 2):
-        fwd = lax.ppermute(fwd, "tensor", TP_Z_FWD)
-        token_chunks[nz - 1 - s] = fwd
-    bwd = pair
-    for s in range(nz // 2 - 1):
-        bwd = lax.ppermute(bwd, "tensor", TP_Z_BWD)
-        token_chunks[s + 1] = bwd
-    gathered = jnp.concatenate([token_chunks[k] for k in range(nz)], axis=0)
-    row_total = gathered.shape[0] * gathered.shape[1]
+        carried = lax.ppermute(carried, ring_axes, SPLIT_BOTH if s < nz // 2 - 1 else SPLIT_FWD_ONLY)
+        arrivals.append(carried)
+    mine = [pick(r[0], r[1]) for r in arrivals]
+    theirs = jnp.stack([pick(r[1], r[0]) for r in arrivals])
+    swapped = lax.ppermute(theirs, "dp", DP_C_SWAP)
+    slots = [my_pair] + mine[: nz // 2 - 1] + [pick(mine[nz // 2 - 1], swapped[nz // 2 - 1])]
+    slots = slots + [swapped[i] for i in range(nz // 2 - 1)]
+    gathered = jnp.stack(slots)
+    row_total = gathered.shape[0] * gathered.shape[1] * gathered.shape[2]
     normed = gathered.reshape(row_total, feature_count)
 
     act = None
@@ -156,25 +178,30 @@
     term = jnp.dot(hidden, down_weight, preferred_element_type=jnp.float32).astype(jnp.bfloat16)
     blocks = term.reshape(nz, nl, shard_rows, feature_count)
 
-    fwd = blocks[nz // 2]
-    for s in range(nz // 2):
-        got = lax.ppermute(fwd, "tensor", TP_Z_FWD)
-        if s < nz // 2 - 1:
-            fwd = (got.astype(jnp.float32) + blocks[nz // 2 - 1 - s].astype(jnp.float32)).astype(jnp.bfloat16)
+    f32 = lambda v: v.astype(jnp.float32)
+    half = nz // 2
+    other = lax.ppermute(blocks[1 : half + 1], "dp", DP_C_SWAP)
+    by_group = lambda own_part, other_part: pick(
+        jnp.stack([own_part, other_part]), jnp.stack([other_part, own_part])
+    )
+    carried = by_group(pick(blocks[half], blocks[nz - 1]), pick(other[half - 1], other[half - 2]))
+    for s in range(half):
+        got = lax.ppermute(carried, ring_axes, SPLIT_BOTH if s < half - 1 else SPLIT_FWD_ONLY)
+        if s < half - 2:
+            add = by_group(pick(blocks[nz - 1 - s], blocks[nz - 2 - s]), pick(other[half - 2 - s], other[half - 3 - s]))
+            carried = (f32(got) + f32(add)).astype(jnp.bfloat16)
+        elif s == half - 2:
+            core1_total = got
+            add = by_group(blocks[nz - 1 - s], other[half - 2 - s])
+            carried = (f32(got) + f32(add)).astype(jnp.bfloat16)
         else:
-            fwd_total = got
-    bwd = blocks[nz // 2 + 1]
-    for s in range(nz // 2 - 1):
-        got = lax.ppermute(bwd, "tensor", TP_Z_BWD)
-        if s < nz // 2 - 2:
-            bwd = (got.astype(jnp.float32) + blocks[nz // 2 + 2 + s].astype(jnp.float32)).astype(jnp.bfloat16)
-        else:
-            bwd_total = got
-    column_sum = (
-        fwd_total.astype(jnp.float32) + bwd_total.astype(jnp.float32) + blocks[0].astype(jnp.float32)
-    )
+            chain_total = pick(got, core1_total)
+    keep = pick(chain_total[0], chain_total[1])
+    give = pick(chain_total[1], chain_total[0])
+    from_other = lax.ppermute(give, "dp", DP_C_SWAP)
+    column_sum = f32(keep) + f32(from_other) + f32(blocks[0])
     from_partner = lax.ppermute(column_sum[1].astype(jnp.bfloat16), "tensor", TP_L_SWAP)
-    total = column_sum[0] + from_partner.astype(jnp.float32)
+    total = column_sum[0] + f32(from_partner)
     return (local_batch.astype(jnp.float32) + total).astype(jnp.bfloat16)
 
 

time: 240 us -> 289 us (1.20)
  waiting for transfers between devices: 72.7 us -> 190 us
  starting transfers between devices: 141 us -> 71.4 us
    ppermute x30 -> x20, waiting for transfers between devices: 54.7 us -> 163 us  [the longest x8 82.9 us: per_device(): lax.ppermute(carried, ring_axes, SPLIT_BOTH if s < half - 1 else SPLIT_FW...]
    ppermute x30 -> x20, starting transfers between devices: 110 us -> 40.3 us  [the longest x8 17.1 us: per_device(): lax.ppermute(carried, ring_axes, SPLIT_BOTH if s < nz // 2 - 1 else SPLIT...]
    ppermute x1, waiting for transfers between devices: 0.01 us -> 5.1 us  [gather_pieces(): fwd1 = lax.ppermute(pair, 'dp', DP_Y_FWD)]
    unnamed x24 -> x13, local copies, waits for them, and re-layouts: 6.26 us -> 6 us
  transfers between devices with their start and end apart: 38 -> 28, of which waited for: 18 -> 24; matrix products, arithmetic and copies ran while one was open for 5% -> 3% of each run, Pallas kernels for 0% -> 0%
where the time goes in v5:
time: 289 us; the launch traced here: 286 us
  waiting for transfers between devices  190 us (66%)
  starting transfers between devices  71.4 us (25%)
  local copies, waits for them, and re-layouts  9.6 us (3%)
  matrix products  8.53 us (3%)
  other arithmetic  4.86 us (2%)
    ppermute x8, waiting for transfers between devices, per_device(): lax.ppermute(carried, ring_axes, SPLIT_BOTH if s < half - 1 else SPLIT_FW...  82.9 us
    ppermute x8, waiting for transfers between devices, per_device(): lax.ppermute(carried, ring_axes, SPLIT_BOTH if s < nz // 2 - 1 else SPLIT...  73.7 us
    ppermute x8, starting transfers between devices, per_device(): lax.ppermute(carried, ring_axes, SPLIT_BOTH if s < nz // 2 - 1 else SPLIT...  17.1 us
    ppermute x8, starting transfers between devices, per_device(): lax.ppermute(carried, ring_axes, SPLIT_BOTH if s < half - 1 else SPLIT_FW...  15.4 us
    ppermute x1, waiting for transfers between devices, per_device(): lax.ppermute(travelling, 'tensor', TP_L_SWAP)  10.4 us
    all_to_all x1, starting transfers between devices, per_device(): lax.all_to_all(jnp.concatenate([outgoing, place_cols], axis=1).reshape(dp...  8.99 us
    unnamed x13, local copies, waits for them, and re-layouts  6 us
  transfers between devices with their start and end apart: 28, of which 24 were waited for; matrix products, arithmetic and copies ran while one was open for 3% of the time, Pallas kernels for 0%

profile of v5, /device:TPU:24, one launch (start us, length us, event | category | flops | bytes accessed | tf_op | source)
XLA Modules:
  0.0 286.0 jit_solution(2384801089342982820)
XLA Ops:
  3.0 9.0 %all-to-all-start = ((bf16[16,2,4224]{2,1,0:T(2,128)(2,1)}), bf16[16,2,4224]{2,1,0:T(2,128)(2,1)S(1)}, u32[]{:S(2)}, u32[]{:S(2)}) async-start(bf16[16,2,4224]{2,1,0:T(2,128)(2,1)} %reshape.1002), calls=%async_computation | async-start | bytes 540672 | tf_op jit(solution)/shard_map/all_to_all | solution.py:114
  13.9 4.9 %collective-permute-start.11 = (bf16[1,256,1024]{2,1,0:T(8,128)(2,1)S(1)}, bf16[1,256,1024]{2,1,0:T(8,128)(2,1)S(1)}, u32[]{:S(2)}, u32[]{:S(2)}) collective-permute-start(bf16[1,256,1024]{2,1,0:T(8,128)(2,1)S(1)} %bitcast.108), channel_id=1, source_target_pairs={{0,64},{32,96},{64,0},{96,32},{128,192},{160,224},{192,128},{224,1... | collective-permute-start | bytes 1572872 | tf_op jit(solution)/shard_map/ppermute | solution.py:68
  22.7 10.4 %collective-permute-done = bf16[16,4096]{1,0:T(8,128)(2,1)S(1)} collective-permute-done((bf16[16,4096]{1,0:T(8,128)(2,1)S(1)}, bf16[16,4096]{1,0:T(8,128)(2,1)S(1)}, u32[]{:S(2)}, u32[]{:S(2)}) %collective-permute-start) | collective-permute-done | bytes 131104 | tf_op jit(solution)/shard_map/ppermute | solution.py:148
  41.7 3.4 %collective-permute-start.14 = (bf16[2,256,1024]{2,1,0:T(8,128)(2,1)S(1)}, bf16[2,256,1024]{2,1,0:T(8,128)(2,1)S(1)}, u32[]{:S(2)}, u32[]{:S(2)}) collective-permute-start(bf16[2,256,1024]{2,1,0:T(8,128)(2,1)S(1)} %pad_maximum_fusion), channel_id=1, source_target_pairs={{0,384},{32,416},{64,448},{96,480},{128,0},{160,32},{192,64},{224,... | collective-permute-start | bytes 3145736 | tf_op jit(solution)/shard_map/ppermute | solution.py:73
  45.9 10.5 %collective-permute-done.2 = bf16[2,2,16,4096]{3,2,1,0:T(8,128)(2,1)S(1)} collective-permute-done((bf16[2,2,16,4096]{3,2,1,0:T(8,128)(2,1)S(1)}, bf16[2,2,16,4096]{3,2,1,0:T(8,128)(2,1)S(1)}, u32[]{:S(2)}, u32[]{:S(2)}) %collective-permute-start.2) | collective-permute-done | bytes 524320 | tf_op jit(solution)/shard_map/ppermute | solution.py:153
  58.4 5.1 %collective-permute-done.12 = bf16[2,256,1024]{2,1,0:T(8,128)(2,1)S(1)} collective-permute-done((bf16[2,256,1024]{2,1,0:T(8,128)(2,1)S(1)}, bf16[2,256,1024]{2,1,0:T(8,128)(2,1)S(1)}, u32[]{:S(2)}, u32[]{:S(2)}) %collective-permute-start.12) | collective-permute-done | bytes 1048608 | tf_op jit(solution)/shard_map/ppermute | solution.py:71
  63.5 3.6 %collective-permute-start.13 = (bf16[2,256,1024]{2,1,0:T(8,128)(2,1)S(1)}, bf16[2,256,1024]{2,1,0:T(8,128)(2,1)S(1)}, u32[]{:S(2)}, u32[]{:S(2)}) collective-permute-start(bf16[2,256,1024]{2,1,0:T(8,128)(2,1)S(1)} %collective-permute-done.12), channel_id=1, source_target_pairs={{0,128},{32,160},{64,192},{96,224},{128,256},{160,288},{192,320},{... | collective-permute-start | bytes 3145736 | tf_op jit(solution)/shard_map/ppermute | solution.py:72
  71.3 14.6 %collective-permute-done.4 = bf16[2,2,16,4096]{3,2,1,0:T(8,128)(2,1)S(1)} collective-permute-done((bf16[2,2,16,4096]{3,2,1,0:T(8,128)(2,1)S(1)}, bf16[2,2,16,4096]{3,2,1,0:T(8,128)(2,1)S(1)}, u32[]{:S(2)}, u32[]{:S(2)}) %collective-permute-start.4) | collective-permute-done | bytes 524320 | tf_op jit(solution)/shard_map/ppermute | solution.py:153
  91.2 7.0 %collective-permute-done.5 = bf16[2,2,16,4096]{3,2,1,0:T(8,128)(2,1)S(1)} collective-permute-done((bf16[2,2,16,4096]{3,2,1,0:T(8,128)(2,1)S(1)}, bf16[2,2,16,4096]{3,2,1,0:T(8,128)(2,1)S(1)}, u32[]{:S(2)}, u32[]{:S(2)}) %collective-permute-start.5) | collective-permute-done | bytes 524320 | tf_op jit(solution)/shard_map/ppermute | solution.py:153
  100.2 10.3 %collective-permute-done.6 = bf16[2,2,16,4096]{3,2,1,0:T(8,128)(2,1)S(1)} collective-permute-done((bf16[2,2,16,4096]{3,2,1,0:T(8,128)(2,1)S(1)}, bf16[2,2,16,4096]{3,2,1,0:T(8,128)(2,1)S(1)}, u32[]{:S(2)}, u32[]{:S(2)}) %collective-permute-start.6) | collective-permute-done | bytes 524320 | tf_op jit(solution)/shard_map/ppermute | solution.py:153
  112.5 10.3 %collective-permute-done.7 = bf16[2,2,16,4096]{3,2,1,0:T(8,128)(2,1)S(1)} collective-permute-done((bf16[2,2,16,4096]{3,2,1,0:T(8,128)(2,1)S(1)}, bf16[2,2,16,4096]{3,2,1,0:T(8,128)(2,1)S(1)}, u32[]{:S(2)}, u32[]{:S(2)}) %collective-permute-start.7) | collective-permute-done | bytes 524320 | tf_op jit(solution)/shard_map/ppermute | solution.py:153
  124.8 10.3 %collective-permute-done.8 = bf16[2,2,16,4096]{3,2,1,0:T(8,128)(2,1)S(1)} collective-permute-done((bf16[2,2,16,4096]{3,2,1,0:T(8,128)(2,1)S(1)}, bf16[2,2,16,4096]{3,2,1,0:T(8,128)(2,1)S(1)}, u32[]{:S(2)}, u32[]{:S(2)}) %collective-permute-start.8) | collective-permute-done | bytes 524320 | tf_op jit(solution)/shard_map/ppermute | solution.py:153
  137.1 10.3 %collective-permute-done.9 = bf16[2,2,16,4096]{3,2,1,0:T(8,128)(2,1)S(1)} collective-permute-done((bf16[2,2,16,4096]{3,2,1,0:T(8,128)(2,1)S(1)}, bf16[2,2,16,4096]{3,2,1,0:T(8,128)(2,1)S(1)}, u32[]{:S(2)}, u32[]{:S(2)}) %collective-permute-start.9) | collective-permute-done | bytes 524320 | tf_op jit(solution)/shard_map/ppermute | solution.py:153
  154.2 5.2 %collective-permute-done.15 = bf16[8,256,1024]{2,1,0:T(8,128)(2,1)S(1)} collective-permute-done((bf16[8,256,1024]{2,1,0:T(8,128)(2,1)S(1)}, bf16[8,256,1024]{2,1,0:T(8,128)(2,1)S(1)}, u32[]{:S(2)}, u32[]{:S(2)}) %collective-permute-start.15) | collective-permute-done | bytes 4194336 | tf_op jit(solution)/shard_map/ppermute | solution.py:77
  170.9 3.7 %collective-permute-done.16 = bf16[8,2,16,4096]{3,2,1,0:T(8,128)(2,1)S(1)} collective-permute-done((bf16[8,2,16,4096]{3,2,1,0:T(8,128)(2,1)S(1)}, bf16[8,2,16,4096]{3,2,1,0:T(8,128)(2,1)S(1)}, u32[]{:S(2)}, u32[]{:S(2)}) %collective-permute-start.16) | collective-permute-done | bytes 2097184 | tf_op jit(solution)/shard_map/ppermute | solution.py:183
  176.7 10.4 %collective-permute-done.17 = bf16[2,2,16,4096]{3,2,1,0:T(8,128)(2,1)S(1)} collective-permute-done((bf16[2,2,16,4096]{3,2,1,0:T(8,128)(2,1)S(1)}, bf16[2,2,16,4096]{3,2,1,0:T(8,128)(2,1)S(1)}, u32[]{:S(2)}, u32[]{:S(2)}) %collective-permute-start.17) | collective-permute-done | bytes 524320 | tf_op jit(solution)/shard_map/ppermute | solution.py:189
  189.2 10.4 %collective-permute-done.18 = bf16[2,2,16,4096]{3,2,1,0:T(8,128)(2,1)S(1)} collective-permute-done((bf16[2,2,16,4096]{3,2,1,0:T(8,128)(2,1)S(1)}, bf16[2,2,16,4096]{3,2,1,0:T(8,128)(2,1)S(1)}, u32[]{:S(2)}, u32[]{:S(2)}) %collective-permute-start.18) | collective-permute-done | bytes 524320 | tf_op jit(solution)/shard_map/ppermute | solution.py:189
  201.6 10.4 %collective-permute-done.19 = bf16[2,2,16,4096]{3,2,1,0:T(8,128)(2,1)S(1)} collective-permute-done((bf16[2,2,16,4096]{3,2,1,0:T(8,128)(2,1)S(1)}, bf16[2,2,16,4096]{3,2,1,0:T(8,128)(2,1)S(1)}, u32[]{:S(2)}, u32[]{:S(2)}) %collective-permute-start.19) | collective-permute-done | bytes 524320 | tf_op jit(solution)/shard_map/ppermute | solution.py:189
  214.1 10.4 %collective-permute-done.20 = bf16[2,2,16,4096]{3,2,1,0:T(8,128)(2,1)S(1)} collective-permute-done((bf16[2,2,16,4096]{3,2,1,0:T(8,128)(2,1)S(1)}, bf16[2,2,16,4096]{3,2,1,0:T(8,128)(2,1)S(1)}, u32[]{:S(2)}, u32[]{:S(2)}) %collective-permute-start.20) | collective-permute-done | bytes 524320 | tf_op jit(solution)/shard_map/ppermute | solution.py:189
  226.5 10.4 %collective-permute-done.21 = bf16[2,2,16,4096]{3,2,1,0:T(8,128)(2,1)S(1)} collective-permute-done((bf16[2,2,16,4096]{3,2,1,0:T(8,128)(2,1)S(1)}, bf16[2,2,16,4096]{3,2,1,0:T(8,128)(2,1)S(1)}, u32[]{:S(2)}, u32[]{:S(2)}) %collective-permute-start.21) | collective-permute-done | bytes 524320 | tf_op jit(solution)/shard_map/ppermute | solution.py:189
  239.0 10.4 %collective-permute-done.22 = bf16[2,2,16,4096]{3,2,1,0:T(8,128)(2,1)S(1)} collective-permute-done((bf16[2,2,16,4096]{3,2,1,0:T(8,128)(2,1)S(1)}, bf16[2,2,16,4096]{3,2,1,0:T(8,128)(2,1)S(1)}, u32[]{:S(2)}, u32[]{:S(2)}) %collective-permute-start.22) | collective-permute-done | bytes 524320 | tf_op jit(solution)/shard_map/ppermute | solution.py:189
  251.4 10.4 %collective-permute-done.23 = bf16[2,2,16,4096]{3,2,1,0:T(8,128)(2,1)S(1)} collective-permute-done((bf16[2,2,16,4096]{3,2,1,0:T(8,128)(2,1)S(1)}, bf16[2,2,16,4096]{3,2,1,0:T(8,128)(2,1)S(1)}, u32[]{:S(2)}, u32[]{:S(2)}) %collective-permute-start.23) | collective-permute-done | bytes 524320 | tf_op jit(solution)/shard_map/ppermute | solution.py:189
  263.8 10.4 %collective-permute-done.24 = bf16[2,2,16,4096]{3,2,1,0:T(8,128)(2,1)S(1)} collective-permute-done((bf16[2,2,16,4096]{3,2,1,0:T(8,128)(2,1)S(1)}, bf16[2,2,16,4096]{3,2,1,0:T(8,128)(2,1)S(1)}, u32[]{:S(2)}, u32[]{:S(2)}) %collective-permute-start.24) | collective-permute-done | bytes 524320 | tf_op jit(solution)/shard_map/ppermute | solution.py:189
  281.2 4.1 %collective-permute-done.26 = bf16[16,4096]{1,0:T(8,128)(2,1)S(1)} collective-permute-done((bf16[16,4096]{1,0:T(8,128)(2,1)S(1)}, bf16[16,4096]{1,0:T(8,128)(2,1)S(1)}, u32[]{:S(2)}, u32[]{:S(2)}) %collective-permute-start.26) | collective-permute-done | bytes 131104 | tf_op jit(solution)/shard_map/ppermute | solution.py:203
  (116 shorter events, 79.2 us)
Async XLA Ops:
  3.0 16.4 %all-to-all-start = ((bf16[16,2,4224]{2,1,0:T(2,128)(2,1)}), bf16[16,2,4224]{2,1,0:T(2,128)(2,1)S(1)}, u32[]{:S(2)}, u32[]{:S(2)}) async-start(bf16[16,2,4224]{2,1,0:T(2,128)(2,1)} %reshape.1002), calls=%async_computation | async-start | bytes 540672 | tf_op jit(solution)/shard_map/all_to_all | solution.py:114
  13.9 22.0 %collective-permute-start.11 = (bf16[1,256,1024]{2,1,0:T(8,128)(2,1)S(1)}, bf16[1,256,1024]{2,1,0:T(8,128)(2,1)S(1)}, u32[]{:S(2)}, u32[]{:S(2)}) collective-permute-start(bf16[1,256,1024]{2,1,0:T(8,128)(2,1)S(1)} %bitcast.108), channel_id=1, source_target_pairs={{0,64},{32,96},{64,0},{96,32},{128,192},{160,224},{192,128},{224,1... | collective-permute-start | bytes 1572872 | tf_op jit(solution)/shard_map/ppermute | solution.py:68
  20.6 12.5 %collective-permute-start = (bf16[16,4096]{1,0:T(8,128)(2,1)S(1)}, bf16[16,4096]{1,0:T(8,128)(2,1)S(1)}, u32[]{:S(2)}, u32[]{:S(2)}) collective-permute-start(bf16[16,4096]{1,0:T(8,128)(2,1)S(1)} %broadcast_select_fusion.14), channel_id=1, source_target_pairs={{0,16},{1,17},{2,18},{3,19},{4,20},{5,21},{6,22},{7,23},{8,24},{9,... | collective-permute-start | bytes 393224 | tf_op jit(solution)/shard_map/ppermute | solution.py:148
  36.0 27.5 %collective-permute-start.12 = (bf16[2,256,1024]{2,1,0:T(8,128)(2,1)S(1)}, bf16[2,256,1024]{2,1,0:T(8,128)(2,1)S(1)}, u32[]{:S(2)}, u32[]{:S(2)}) collective-permute-start(bf16[2,256,1024]{2,1,0:T(8,128)(2,1)S(1)} %pad_maximum_fusion), channel_id=1, source_target_pairs={{0,128},{32,160},{64,192},{96,224},{128,256},{160,288},{192,320},{... | collective-permute-start | bytes 3145736 | tf_op jit(solution)/shard_map/ppermute | solution.py:71
  38.5 17.8 %collective-permute-start.2 = (bf16[2,2,16,4096]{3,2,1,0:T(8,128)(2,1)S(1)}, bf16[2,2,16,4096]{3,2,1,0:T(8,128)(2,1)S(1)}, u32[]{:S(2)}, u32[]{:S(2)}) collective-permute-start(bf16[2,2,16,4096]{3,2,1,0:T(8,128)(2,1)S(1)} %maximum_select_fusion), channel_id=1, source_target_pairs={{0,1},{1,2},{2,3},{3,4},{4,5},{5,6},{6,7},{7,8},{8,9},{9,10},{10,1... | collective-permute-start | bytes 1572872 | tf_op jit(solution)/shard_map/ppermute | solution.py:153
  41.7 107.6 %collective-permute-start.14 = (bf16[2,256,1024]{2,1,0:T(8,128)(2,1)S(1)}, bf16[2,256,1024]{2,1,0:T(8,128)(2,1)S(1)}, u32[]{:S(2)}, u32[]{:S(2)}) collective-permute-start(bf16[2,256,1024]{2,1,0:T(8,128)(2,1)S(1)} %pad_maximum_fusion), channel_id=1, source_target_pairs={{0,384},{32,416},{64,448},{96,480},{128,0},{160,32},{192,64},{224,... | collective-permute-start | bytes 3145736 | tf_op jit(solution)/shard_map/ppermute | solution.py:73
  56.4 12.3 %collective-permute-start.3 = (bf16[2,2,16,4096]{3,2,1,0:T(8,128)(2,1)S(1)}, bf16[2,2,16,4096]{3,2,1,0:T(8,128)(2,1)S(1)}, u32[]{:S(2)}, u32[]{:S(2)}) collective-permute-start(bf16[2,2,16,4096]{3,2,1,0:T(8,128)(2,1)S(1)} %collective-permute-done.2), channel_id=1, source_target_pairs={{0,1},{1,2},{2,3},{3,4},{4,5},{5,6},{6,7},{7,8},{8,9},{9,10},{10,1... | collective-permute-start | bytes 1572872 | tf_op jit(solution)/shard_map/ppermute | solution.py:153
  63.5 26.7 %collective-permute-start.13 = (bf16[2,256,1024]{2,1,0:T(8,128)(2,1)S(1)}, bf16[2,256,1024]{2,1,0:T(8,128)(2,1)S(1)}, u32[]{:S(2)}, u32[]{:S(2)}) collective-permute-start(bf16[2,256,1024]{2,1,0:T(8,128)(2,1)S(1)} %collective-permute-done.12), channel_id=1, source_target_pairs={{0,128},{32,160},{64,192},{96,224},{128,256},{160,288},{192,320},{... | collective-permute-start | bytes 3145736 | tf_op jit(solution)/shard_map/ppermute | solution.py:72
  68.6 17.3 %collective-permute-start.4 = (bf16[2,2,16,4096]{3,2,1,0:T(8,128)(2,1)S(1)}, bf16[2,2,16,4096]{3,2,1,0:T(8,128)(2,1)S(1)}, u32[]{:S(2)}, u32[]{:S(2)}) collective-permute-start(bf16[2,2,16,4096]{3,2,1,0:T(8,128)(2,1)S(1)} %collective-permute-done.3), channel_id=1, source_target_pairs={{0,1},{1,2},{2,3},{3,4},{4,5},{5,6},{6,7},{7,8},{8,9},{9,10},{10,1... | collective-permute-start | bytes 1572872 | tf_op jit(solution)/shard_map/ppermute | solution.py:153
  85.9 12.3 %collective-permute-start.5 = (bf16[2,2,16,4096]{3,2,1,0:T(8,128)(2,1)S(1)}, bf16[2,2,16,4096]{3,2,1,0:T(8,128)(2,1)S(1)}, u32[]{:S(2)}, u32[]{:S(2)}) collective-permute-start(bf16[2,2,16,4096]{3,2,1,0:T(8,128)(2,1)S(1)} %collective-permute-done.4), channel_id=1, source_target_pairs={{0,1},{1,2},{2,3},{3,4},{4,5},{5,6},{6,7},{7,8},{8,9},{9,10},{10,1... | collective-permute-start | bytes 1572872 | tf_op jit(solution)/shard_map/ppermute | solution.py:153
  98.2 12.3 %collective-permute-start.6 = (bf16[2,2,16,4096]{3,2,1,0:T(8,128)(2,1)S(1)}, bf16[2,2,16,4096]{3,2,1,0:T(8,128)(2,1)S(1)}, u32[]{:S(2)}, u32[]{:S(2)}) collective-permute-start(bf16[2,2,16,4096]{3,2,1,0:T(8,128)(2,1)S(1)} %collective-permute-done.5), channel_id=1, source_target_pairs={{0,1},{1,2},{2,3},{3,4},{4,5},{5,6},{6,7},{7,8},{8,9},{9,10},{10,1... | collective-permute-start | bytes 1572872 | tf_op jit(solution)/shard_map/ppermute | solution.py:153
  110.5 12.3 %collective-permute-start.7 = (bf16[2,2,16,4096]{3,2,1,0:T(8,128)(2,1)S(1)}, bf16[2,2,16,4096]{3,2,1,0:T(8,128)(2,1)S(1)}, u32[]{:S(2)}, u32[]{:S(2)}) collective-permute-start(bf16[2,2,16,4096]{3,2,1,0:T(8,128)(2,1)S(1)} %collective-permute-done.6), channel_id=1, source_target_pairs={{0,1},{1,2},{2,3},{3,4},{4,5},{5,6},{6,7},{7,8},{8,9},{9,10},{10,1... | collective-permute-start | bytes 1572872 | tf_op jit(solution)/shard_map/ppermute | solution.py:153
  122.8 12.3 %collective-permute-start.8 = (bf16[2,2,16,4096]{3,2,1,0:T(8,128)(2,1)S(1)}, bf16[2,2,16,4096]{3,2,1,0:T(8,128)(2,1)S(1)}, u32[]{:S(2)}, u32[]{:S(2)}) collective-permute-start(bf16[2,2,16,4096]{3,2,1,0:T(8,128)(2,1)S(1)} %collective-permute-done.7), channel_id=1, source_target_pairs={{0,1},{1,2},{2,3},{3,4},{4,5},{5,6},{6,7},{7,8},{8,9},{9,10},{10,1... | collective-permute-start | bytes 1572872 | tf_op jit(solution)/shard_map/ppermute | solution.py:153
  135.0 12.3 %collective-permute-start.9 = (bf16[2,2,16,4096]{3,2,1,0:T(8,128)(2,1)S(1)}, bf16[2,2,16,4096]{3,2,1,0:T(8,128)(2,1)S(1)}, u32[]{:S(2)}, u32[]{:S(2)}) collective-permute-start(bf16[2,2,16,4096]{3,2,1,0:T(8,128)(2,1)S(1)} %collective-permute-done.8), channel_id=1, source_target_pairs={{0,1},{1,2},{2,3},{3,4},{4,5},{5,6},{6,7},{7,8},{8,9},{9,10},{10,1... | collective-permute-start | bytes 1572872 | tf_op jit(solution)/shard_map/ppermute | solution.py:153
  149.4 10.0 %collective-permute-start.15 = (bf16[8,256,1024]{2,1,0:T(8,128)(2,1)S(1)}, bf16[8,256,1024]{2,1,0:T(8,128)(2,1)S(1)}, u32[]{:S(2)}, u32[]{:S(2)}) collective-permute-start(bf16[8,256,1024]{2,1,0:T(8,128)(2,1)S(1)} %constant_dynamic-update-slice_fusion.3), channel_id=1, source_target_pairs={{0,32},{32,0},{64,96},{96,64},{128,160},{160,128},{192,224},{224,1... | collective-permute-start | bytes 12582920 | tf_op jit(solution)/shard_map/ppermute | solution.py:77
  174.8 12.3 %collective-permute-start.17 = (bf16[2,2,16,4096]{3,2,1,0:T(8,128)(2,1)S(1)}, bf16[2,2,16,4096]{3,2,1,0:T(8,128)(2,1)S(1)}, u32[]{:S(2)}, u32[]{:S(2)}) collective-permute-start(bf16[2,2,16,4096]{3,2,1,0:T(8,128)(2,1)S(1)} %maximum_select_fusion.1), channel_id=1, source_target_pairs={{0,1},{1,2},{2,3},{3,4},{4,5},{5,6},{6,7},{7,8},{8,9},{9,10},{10,1... | collective-permute-start | bytes 1572872 | tf_op jit(solution)/shard_map/ppermute | solution.py:189
  187.2 12.3 %collective-permute-start.18 = (bf16[2,2,16,4096]{3,2,1,0:T(8,128)(2,1)S(1)}, bf16[2,2,16,4096]{3,2,1,0:T(8,128)(2,1)S(1)}, u32[]{:S(2)}, u32[]{:S(2)}) collective-permute-start(bf16[2,2,16,4096]{3,2,1,0:T(8,128)(2,1)S(1)} %add_convert_fusion.6), channel_id=1, source_target_pairs={{0,1},{1,2},{2,3},{3,4},{4,5},{5,6},{6,7},{7,8},{8,9},{9,10},{10,1... | collective-permute-start | bytes 1572872 | tf_op jit(solution)/shard_map/ppermute | solution.py:189
  199.7 12.3 %collective-permute-start.19 = (bf16[2,2,16,4096]{3,2,1,0:T(8,128)(2,1)S(1)}, bf16[2,2,16,4096]{3,2,1,0:T(8,128)(2,1)S(1)}, u32[]{:S(2)}, u32[]{:S(2)}) collective-permute-start(bf16[2,2,16,4096]{3,2,1,0:T(8,128)(2,1)S(1)} %add_convert_fusion.5), channel_id=1, source_target_pairs={{0,1},{1,2},{2,3},{3,4},{4,5},{5,6},{6,7},{7,8},{8,9},{9,10},{10,1... | collective-permute-start | bytes 1572872 | tf_op jit(solution)/shard_map/ppermute | solution.py:189
  212.1 12.3 %collective-permute-start.20 = (bf16[2,2,16,4096]{3,2,1,0:T(8,128)(2,1)S(1)}, bf16[2,2,16,4096]{3,2,1,0:T(8,128)(2,1)S(1)}, u32[]{:S(2)}, u32[]{:S(2)}) collective-permute-start(bf16[2,2,16,4096]{3,2,1,0:T(8,128)(2,1)S(1)} %add_convert_fusion.4), channel_id=1, source_target_pairs={{0,1},{1,2},{2,3},{3,4},{4,5},{5,6},{6,7},{7,8},{8,9},{9,10},{10,1... | collective-permute-start | bytes 1572872 | tf_op jit(solution)/shard_map/ppermute | solution.py:189
  224.6 12.3 %collective-permute-start.21 = (bf16[2,2,16,4096]{3,2,1,0:T(8,128)(2,1)S(1)}, bf16[2,2,16,4096]{3,2,1,0:T(8,128)(2,1)S(1)}, u32[]{:S(2)}, u32[]{:S(2)}) collective-permute-start(bf16[2,2,16,4096]{3,2,1,0:T(8,128)(2,1)S(1)} %add_convert_fusion.3), channel_id=1, source_target_pairs={{0,1},{1,2},{2,3},{3,4},{4,5},{5,6},{6,7},{7,8},{8,9},{9,10},{10,1... | collective-permute-start | bytes 1572872 | tf_op jit(solution)/shard_map/ppermute | solution.py:189
  237.0 12.3 %collective-permute-start.22 = (bf16[2,2,16,4096]{3,2,1,0:T(8,128)(2,1)S(1)}, bf16[2,2,16,4096]{3,2,1,0:T(8,128)(2,1)S(1)}, u32[]{:S(2)}, u32[]{:S(2)}) collective-permute-start(bf16[2,2,16,4096]{3,2,1,0:T(8,128)(2,1)S(1)} %add_convert_fusion.2), channel_id=1, source_target_pairs={{0,1},{1,2},{2,3},{3,4},{4,5},{5,6},{6,7},{7,8},{8,9},{9,10},{10,1... | collective-permute-start | bytes 1572872 | tf_op jit(solution)/shard_map/ppermute | solution.py:189
  249.5 12.3 %collective-permute-start.23 = (bf16[2,2,16,4096]{3,2,1,0:T(8,128)(2,1)S(1)}, bf16[2,2,16,4096]{3,2,1,0:T(8,128)(2,1)S(1)}, u32[]{:S(2)}, u32[]{:S(2)}) collective-permute-start(bf16[2,2,16,4096]{3,2,1,0:T(8,128)(2,1)S(1)} %add_convert_fusion.1), channel_id=1, source_target_pairs={{0,1},{1,2},{2,3},{3,4},{4,5},{5,6},{6,7},{7,8},{8,9},{9,10},{10,1... | collective-permute-start | bytes 1572872 | tf_op jit(solution)/shard_map/ppermute | solution.py:189
  261.9 12.3 %collective-permute-start.24 = (bf16[2,2,16,4096]{3,2,1,0:T(8,128)(2,1)S(1)}, bf16[2,2,16,4096]{3,2,1,0:T(8,128)(2,1)S(1)}, u32[]{:S(2)}, u32[]{:S(2)}) collective-permute-start(bf16[2,2,16,4096]{3,2,1,0:T(8,128)(2,1)S(1)} %add_convert_fusion), channel_id=1, source_target_pairs={{0,1},{1,2},{2,3},{3,4},{4,5},{5,6},{6,7},{7,8},{8,9},{9,10},{10,1... | collective-permute-start | bytes 1572872 | tf_op jit(solution)/shard_map/ppermute | solution.py:189
  277.9 7.4 %collective-permute-start.26 = (bf16[16,4096]{1,0:T(8,128)(2,1)S(1)}, bf16[16,4096]{1,0:T(8,128)(2,1)S(1)}, u32[]{:S(2)}, u32[]{:S(2)}) collective-permute-start(bf16[16,4096]{1,0:T(8,128)(2,1)S(1)} %fusion.22), channel_id=1, source_target_pairs={{0,16},{1,17},{2,18},{3,19},{4,20},{5,21},{6,22},{7,23},{8,24},{9,... | collective-permute-start | bytes 393224 | tf_op jit(solution)/shard_map/ppermute | solution.py:203
  (8 other events, 132.1 us)

commit v6 on v2

--- a/solution.py
+++ b/solution.py
@@ -36,6 +36,16 @@
 TP_L_SWAP = tp_perm(lambda l, z: (l + 1, z))
 TP_Z_FWD = tp_perm(lambda l, z: (l, z + 1))
 TP_Z_BWD = tp_perm(lambda l, z: (l, z - 1))
+
+
+RING_PIECES = 4
+
+
+def ring_permute(x, perm):
+    width = x.shape[-1] // RING_PIECES
+    return jnp.concatenate(
+        [lax.ppermute(x[..., i * width : (i + 1) * width], "tensor", perm) for i in range(RING_PIECES)], axis=-1
+    )
 
 
 def normalize(row_block):
@@ -129,11 +139,11 @@
     token_chunks = {0: pair}
     fwd = pair
     for s in range(nz // 2):
-        fwd = lax.ppermute(fwd, "tensor", TP_Z_FWD)
+        fwd = ring_permute(fwd, TP_Z_FWD)
         token_chunks[nz - 1 - s] = fwd
     bwd = pair
     for s in range(nz // 2 - 1):
-        bwd = lax.ppermute(bwd, "tensor", TP_Z_BWD)
+        bwd = ring_permute(bwd, TP_Z_BWD)
         token_chunks[s + 1] = bwd
     gathered = jnp.concatenate([token_chunks[k] for k in range(nz)], axis=0)
     row_total = gathered.shape[0] * gathered.shape[1]
@@ -158,14 +168,14 @@
 
     fwd = blocks[nz // 2]
     for s in range(nz // 2):
-        got = lax.ppermute(fwd, "tensor", TP_Z_FWD)
+        got = ring_permute(fwd, TP_Z_FWD)
         if s < nz // 2 - 1:
             fwd = (got.astype(jnp.float32) + blocks[nz // 2 - 1 - s].astype(jnp.float32)).astype(jnp.bfloat16)
         else:
             fwd_total = got
     bwd = blocks[nz // 2 + 1]
     for s in range(nz // 2 - 1):
-        got = lax.ppermute(bwd, "tensor", TP_Z_BWD)
+        got = ring_permute(bwd, TP_Z_BWD)
         if s < nz // 2 - 2:
             bwd = (got.astype(jnp.float32) + blocks[nz // 2 + 2 + s].astype(jnp.float32)).astype(jnp.bfloat16)
         else:

time: 240 us -> 457 us (1.90)
  starting transfers between devices: 141 us -> 403 us
  waiting for transfers between devices: 72.7 us -> 29.1 us
  local copies, waits for them, and re-layouts: 10.8 us -> 4.33 us
    ppermute x30 -> x120, starting transfers between devices: 110 us -> 374 us  [ring_permute(): lax.ppermute(x[..., i * width:(i + 1) * width], 'tensor', perm)]
    ppermute x30 -> x120, waiting for transfers between devices: 54.7 us -> 6.33 us  [ring_permute(): lax.ppermute(x[..., i * width:(i + 1) * width], 'tensor', perm)]
    all_to_all x1, waiting for transfers between devices: 0.01 us -> 7 us  [per_device(): lax.all_to_all(jnp.concatenate([outgoing, place_cols], axis=1).reshape(dp...]
    unnamed x24 -> x14, local copies, waits for them, and re-layouts: 6.26 us -> 1.48 us
  transfers between devices with their start and end apart: 38 -> 128, of which waited for: 18 -> 8; matrix products, arithmetic and copies ran while one was open for 5% -> 1% of each run, Pallas kernels for 0% -> 0%
where the time goes in v6:
time: 457 us; the launch traced here: 452 us
  starting transfers between devices  403 us (88%)
  waiting for transfers between devices  29.1 us (6%)
  matrix products  8.47 us (2%)
    ppermute x120, starting transfers between devices, ring_permute(): lax.ppermute(x[..., i * width:(i + 1) * width], 'tensor', perm)  374 us
  transfers between devices with their start and end apart: 128, of which 8 were waited for; matrix products, arithmetic and copies ran while one was open for 1% of the time, Pallas kernels for 0%

profile of v6, /device:TPU:24, one launch (start us, length us, event | category | flops | bytes accessed | tf_op | source)
XLA Modules:
  0.0 451.6 jit_solution(7164759600704614379)
XLA Ops:
  3.0 9.0 %all-to-all-start = ((bf16[16,2,4224]{2,1,0:T(2,128)(2,1)}), bf16[16,2,4224]{2,1,0:T(2,128)(2,1)S(1)}, u32[]{:S(2)}, u32[]{:S(2)}) async-start(bf16[16,2,4224]{2,1,0:T(2,128)(2,1)} %reshape.916), calls=%async_computation | async-start | bytes 540672 | tf_op jit(solution)/shard_map/all_to_all | solution.py:107
  12.3 7.0 %all-to-all-done = bf16[16,2,4224]{2,1,0:T(2,128)(2,1)S(1)} async-done(((bf16[16,2,4224]{2,1,0:T(2,128)(2,1)}), bf16[16,2,4224]{2,1,0:T(2,128)(2,1)S(1)}, u32[]{:S(2)}, u32[]{:S(2)}) %all-to-all-start) | async-done | bytes 270368 | tf_op jit(solution)/shard_map/all_to_all | solution.py:107
  22.7 5.1 %collective-permute-done = bf16[16,4096]{1,0:T(8,128)(2,1)S(1)} collective-permute-done((bf16[16,4096]{1,0:T(8,128)(2,1)S(1)}, bf16[16,4096]{1,0:T(8,128)(2,1)S(1)}, u32[]{:S(2)}, u32[]{:S(2)}) %collective-permute-start) | collective-permute-done | bytes 131104 | tf_op jit(solution)/shard_map/ppermute | solution.py:138
  27.8 9.6 %collective-permute-start.4 = (bf16[2,16,1024]{2,1,0:T(8,128)(2,1)S(1)}, bf16[2,16,1024]{2,1,0:T(8,128)(2,1)S(1)}, u32[]{:S(2)}, u32[]{:S(2)}) collective-permute-start(bf16[2,16,1024]{2,1,0:T(8,128)(2,1)S(1)} %get-tuple-element.85), channel_id=1, source_target_pairs={{0,15},{1,0},{2,1},{3,2},{4,3},{5,4},{6,5},{7,6},{8,7},{9,8},{10,9... | collective-permute-start | bytes 196616 | tf_op jit(solution)/shard_map/ppermute | solution.py:47
  39.4 5.1 %collective-permute-start.3 = (bf16[2,16,1024]{2,1,0:T(8,128)(2,1)S(1)}, bf16[2,16,1024]{2,1,0:T(8,128)(2,1)S(1)}, u32[]{:S(2)}, u32[]{:S(2)}) collective-permute-start(bf16[2,16,1024]{2,1,0:T(8,128)(2,1)S(1)} %get-tuple-element.86), channel_id=1, source_target_pairs={{0,15},{1,0},{2,1},{3,2},{4,3},{5,4},{6,5},{7,6},{8,7},{9,8},{10,9... | collective-permute-start | bytes 196616 | tf_op jit(solution)/shard_map/ppermute | solution.py:47
  46.4 5.1 %collective-permute-start.2 = (bf16[2,16,1024]{2,1,0:T(8,128)(2,1)S(1)}, bf16[2,16,1024]{2,1,0:T(8,128)(2,1)S(1)}, u32[]{:S(2)}, u32[]{:S(2)}) collective-permute-start(bf16[2,16,1024]{2,1,0:T(8,128)(2,1)S(1)} %get-tuple-element.84), channel_id=1, source_target_pairs={{0,15},{1,0},{2,1},{3,2},{4,3},{5,4},{6,5},{7,6},{8,7},{9,8},{10,9... | collective-permute-start | bytes 196616 | tf_op jit(solution)/shard_map/ppermute | solution.py:47
  59.4 5.1 %collective-permute-start.8 = (bf16[2,16,1024]{2,1,0:T(8,128)(2,1)S(1)}, bf16[2,16,1024]{2,1,0:T(8,128)(2,1)S(1)}, u32[]{:S(2)}, u32[]{:S(2)}) collective-permute-start(bf16[2,16,1024]{2,1,0:T(8,128)(2,1)S(1)} %collective-permute-done.4), channel_id=1, source_target_pairs={{0,15},{1,0},{2,1},{3,2},{4,3},{5,4},{6,5},{7,6},{8,7},{9,8},{10,9... | collective-permute-start | bytes 196616 | tf_op jit(solution)/shard_map/ppermute | solution.py:47
  87.0 5.1 %collective-permute-start.12 = (bf16[2,16,1024]{2,1,0:T(8,128)(2,1)S(1)}, bf16[2,16,1024]{2,1,0:T(8,128)(2,1)S(1)}, u32[]{:S(2)}, u32[]{:S(2)}) collective-permute-start(bf16[2,16,1024]{2,1,0:T(8,128)(2,1)S(1)} %collective-permute-done.8), channel_id=1, source_target_pairs={{0,15},{1,0},{2,1},{3,2},{4,3},{5,4},{6,5},{7,6},{8,7},{9,8},{10,9... | collective-permute-start | bytes 196616 | tf_op jit(solution)/shard_map/ppermute | solution.py:47
  111.8 5.1 %collective-permute-start.16 = (bf16[2,16,1024]{2,1,0:T(8,128)(2,1)S(1)}, bf16[2,16,1024]{2,1,0:T(8,128)(2,1)S(1)}, u32[]{:S(2)}, u32[]{:S(2)}) collective-permute-start(bf16[2,16,1024]{2,1,0:T(8,128)(2,1)S(1)} %collective-permute-done.12), channel_id=1, source_target_pairs={{0,15},{1,0},{2,1},{3,2},{4,3},{5,4},{6,5},{7,6},{8,7},{9,8},{10,9... | collective-permute-start | bytes 196616 | tf_op jit(solution)/shard_map/ppermute | solution.py:47
  126.7 3.9 collective-permute-start.48
  136.6 5.1 %collective-permute-start.20 = (bf16[2,16,1024]{2,1,0:T(8,128)(2,1)S(1)}, bf16[2,16,1024]{2,1,0:T(8,128)(2,1)S(1)}, u32[]{:S(2)}, u32[]{:S(2)}) collective-permute-start(bf16[2,16,1024]{2,1,0:T(8,128)(2,1)S(1)} %collective-permute-done.16), channel_id=1, source_target_pairs={{0,15},{1,0},{2,1},{3,2},{4,3},{5,4},{6,5},{7,6},{8,7},{9,8},{10,9... | collective-permute-start | bytes 196616 | tf_op jit(solution)/shard_map/ppermute | solution.py:47
  161.4 5.1 %collective-permute-start.24 = (bf16[2,16,1024]{2,1,0:T(8,128)(2,1)S(1)}, bf16[2,16,1024]{2,1,0:T(8,128)(2,1)S(1)}, u32[]{:S(2)}, u32[]{:S(2)}) collective-permute-start(bf16[2,16,1024]{2,1,0:T(8,128)(2,1)S(1)} %collective-permute-done.20), channel_id=1, source_target_pairs={{0,15},{1,0},{2,1},{3,2},{4,3},{5,4},{6,5},{7,6},{8,7},{9,8},{10,9... | collective-permute-start | bytes 196616 | tf_op jit(solution)/shard_map/ppermute | solution.py:47
  176.4 4.4 collective-permute-start.62
  190.7 5.1 %collective-permute-start.28 = (bf16[2,16,1024]{2,1,0:T(8,128)(2,1)S(1)}, bf16[2,16,1024]{2,1,0:T(8,128)(2,1)S(1)}, u32[]{:S(2)}, u32[]{:S(2)}) collective-permute-start(bf16[2,16,1024]{2,1,0:T(8,128)(2,1)S(1)} %collective-permute-done.24), channel_id=1, source_target_pairs={{0,15},{1,0},{2,1},{3,2},{4,3},{5,4},{6,5},{7,6},{8,7},{9,8},{10,9... | collective-permute-start | bytes 196616 | tf_op jit(solution)/shard_map/ppermute | solution.py:47
  242.0 4.4 collective-permute-done.65
  262.1 5.1 %collective-permute-start.66 = (bf16[2,16,1024]{2,1,0:T(8,128)(2,1)S(1)}, bf16[2,16,1024]{2,1,0:T(8,128)(2,1)S(1)}, u32[]{:S(2)}, u32[]{:S(2)}) collective-permute-start(bf16[2,16,1024]{2,1,0:T(8,128)(2,1)S(1)} %get-tuple-element.79), channel_id=1, source_target_pairs={{0,1},{1,2},{2,3},{3,4},{4,5},{5,6},{6,7},{7,8},{8,9},{9,10},{10,1... | collective-permute-start | bytes 196616 | tf_op jit(solution)/shard_map/ppermute | solution.py:47
  287.0 5.1 %collective-permute-start.70 = (bf16[2,16,1024]{2,1,0:T(8,128)(2,1)S(1)}, bf16[2,16,1024]{2,1,0:T(8,128)(2,1)S(1)}, u32[]{:S(2)}, u32[]{:S(2)}) collective-permute-start(bf16[2,16,1024]{2,1,0:T(8,128)(2,1)S(1)} %get-tuple-element.75), channel_id=1, source_target_pairs={{0,1},{1,2},{2,3},{3,4},{4,5},{5,6},{6,7},{7,8},{8,9},{9,10},{10,1... | collective-permute-start | bytes 196616 | tf_op jit(solution)/shard_map/ppermute | solution.py:47
  311.9 5.1 %collective-permute-start.74 = (bf16[2,16,1024]{2,1,0:T(8,128)(2,1)S(1)}, bf16[2,16,1024]{2,1,0:T(8,128)(2,1)S(1)}, u32[]{:S(2)}, u32[]{:S(2)}) collective-permute-start(bf16[2,16,1024]{2,1,0:T(8,128)(2,1)S(1)} %get-tuple-element.71), channel_id=1, source_target_pairs={{0,1},{1,2},{2,3},{3,4},{4,5},{5,6},{6,7},{7,8},{8,9},{9,10},{10,1... | collective-permute-start | bytes 196616 | tf_op jit(solution)/shard_map/ppermute | solution.py:47
  336.9 5.1 %collective-permute-start.78 = (bf16[2,16,1024]{2,1,0:T(8,128)(2,1)S(1)}, bf16[2,16,1024]{2,1,0:T(8,128)(2,1)S(1)}, u32[]{:S(2)}, u32[]{:S(2)}) collective-permute-start(bf16[2,16,1024]{2,1,0:T(8,128)(2,1)S(1)} %get-tuple-element.67), channel_id=1, source_target_pairs={{0,1},{1,2},{2,3},{3,4},{4,5},{5,6},{6,7},{7,8},{8,9},{9,10},{10,1... | collective-permute-start | bytes 196616 | tf_op jit(solution)/shard_map/ppermute | solution.py:47
  361.8 5.1 %collective-permute-start.82 = (bf16[2,16,1024]{2,1,0:T(8,128)(2,1)S(1)}, bf16[2,16,1024]{2,1,0:T(8,128)(2,1)S(1)}, u32[]{:S(2)}, u32[]{:S(2)}) collective-permute-start(bf16[2,16,1024]{2,1,0:T(8,128)(2,1)S(1)} %get-tuple-element.63), channel_id=1, source_target_pairs={{0,1},{1,2},{2,3},{3,4},{4,5},{5,6},{6,7},{7,8},{8,9},{9,10},{10,1... | collective-permute-start | bytes 196616 | tf_op jit(solution)/shard_map/ppermute | solution.py:47
  386.7 5.1 %collective-permute-start.86 = (bf16[2,16,1024]{2,1,0:T(8,128)(2,1)S(1)}, bf16[2,16,1024]{2,1,0:T(8,128)(2,1)S(1)}, u32[]{:S(2)}, u32[]{:S(2)}) collective-permute-start(bf16[2,16,1024]{2,1,0:T(8,128)(2,1)S(1)} %get-tuple-element.59), channel_id=1, source_target_pairs={{0,1},{1,2},{2,3},{3,4},{4,5},{5,6},{6,7},{7,8},{8,9},{9,10},{10,1... | collective-permute-start | bytes 196616 | tf_op jit(solution)/shard_map/ppermute | solution.py:47
  411.6 5.1 %collective-permute-start.90 = (bf16[2,16,1024]{2,1,0:T(8,128)(2,1)S(1)}, bf16[2,16,1024]{2,1,0:T(8,128)(2,1)S(1)}, u32[]{:S(2)}, u32[]{:S(2)}) collective-permute-start(bf16[2,16,1024]{2,1,0:T(8,128)(2,1)S(1)} %get-tuple-element.55), channel_id=1, source_target_pairs={{0,1},{1,2},{2,3},{3,4},{4,5},{5,6},{6,7},{7,8},{8,9},{9,10},{10,1... | collective-permute-start | bytes 196616 | tf_op jit(solution)/shard_map/ppermute | solution.py:47
  436.6 5.1 %collective-permute-start.94 = (bf16[2,16,1024]{2,1,0:T(8,128)(2,1)S(1)}, bf16[2,16,1024]{2,1,0:T(8,128)(2,1)S(1)}, u32[]{:S(2)}, u32[]{:S(2)}) collective-permute-start(bf16[2,16,1024]{2,1,0:T(8,128)(2,1)S(1)} %get-tuple-element.51), channel_id=1, source_target_pairs={{0,1},{1,2},{2,3},{3,4},{4,5},{5,6},{6,7},{7,8},{8,9},{9,10},{10,1... | collective-permute-start | bytes 196616 | tf_op jit(solution)/shard_map/ppermute | solution.py:47
  446.6 4.3 collective-permute-done.126
  (335 shorter events, 318.4 us)
Async XLA Ops:
  27.8 23.8 %collective-permute-start.4 = (bf16[2,16,1024]{2,1,0:T(8,128)(2,1)S(1)}, bf16[2,16,1024]{2,1,0:T(8,128)(2,1)S(1)}, u32[]{:S(2)}, u32[]{:S(2)}) collective-permute-start(bf16[2,16,1024]{2,1,0:T(8,128)(2,1)S(1)} %get-tuple-element.85), channel_id=1, source_target_pairs={{0,15},{1,0},{2,1},{3,2},{4,3},{5,4},{6,5},{7,6},{8,7},{9,8},{10,9... | collective-permute-start | bytes 196616 | tf_op jit(solution)/shard_map/ppermute | solution.py:47
  37.4 27.2 %collective-permute-start.53 = (bf16[2,16,1024]{2,1,0:T(8,128)(2,1)S(1)}, bf16[2,16,1024]{2,1,0:T(8,128)(2,1)S(1)}, u32[]{:S(2)}, u32[]{:S(2)}) collective-permute-start(bf16[2,16,1024]{2,1,0:T(8,128)(2,1)S(1)} %get-tuple-element.85), channel_id=1, source_target_pairs={{0,1},{1,2},{2,3},{3,4},{4,5},{5,6},{6,7},{7,8},{8,9},{9,10},{10,1... | collective-permute-start | bytes 196616 | tf_op jit(solution)/shard_map/ppermute | solution.py:47
  44.5 22.0 %collective-permute-start.45 = (bf16[2,16,1024]{2,1,0:T(8,128)(2,1)S(1)}, bf16[2,16,1024]{2,1,0:T(8,128)(2,1)S(1)}, u32[]{:S(2)}, u32[]{:S(2)}) collective-permute-start(bf16[2,16,1024]{2,1,0:T(8,128)(2,1)S(1)} %get-tuple-element.86), channel_id=1, source_target_pairs={{0,1},{1,2},{2,3},{3,4},{4,5},{5,6},{6,7},{7,8},{8,9},{9,10},{10,1... | collective-permute-start | bytes 196616 | tf_op jit(solution)/shard_map/ppermute | solution.py:47
  74.4 17.8 %collective-permute-start.46 = (bf16[2,16,1024]{2,1,0:T(8,128)(2,1)S(1)}, bf16[2,16,1024]{2,1,0:T(8,128)(2,1)S(1)}, u32[]{:S(2)}, u32[]{:S(2)}) collective-permute-start(bf16[2,16,1024]{2,1,0:T(8,128)(2,1)S(1)} %collective-permute-done.45), channel_id=1, source_target_pairs={{0,1},{1,2},{2,3},{3,4},{4,5},{5,6},{6,7},{7,8},{8,9},{9,10},{10,1... | collective-permute-start | bytes 196616 | tf_op jit(solution)/shard_map/ppermute | solution.py:47
  100.0 17.0 %collective-permute-start.55 = (bf16[2,16,1024]{2,1,0:T(8,128)(2,1)S(1)}, bf16[2,16,1024]{2,1,0:T(8,128)(2,1)S(1)}, u32[]{:S(2)}, u32[]{:S(2)}) collective-permute-start(bf16[2,16,1024]{2,1,0:T(8,128)(2,1)S(1)} %collective-permute-done.54), channel_id=1, source_target_pairs={{0,1},{1,2},{2,3},{3,4},{4,5},{5,6},{6,7},{7,8},{8,9},{9,10},{10,1... | collective-permute-start | bytes 196616 | tf_op jit(solution)/shard_map/ppermute | solution.py:47
  102.0 16.9 %collective-permute-start.47 = (bf16[2,16,1024]{2,1,0:T(8,128)(2,1)S(1)}, bf16[2,16,1024]{2,1,0:T(8,128)(2,1)S(1)}, u32[]{:S(2)}, u32[]{:S(2)}) collective-permute-start(bf16[2,16,1024]{2,1,0:T(8,128)(2,1)S(1)} %collective-permute-done.46), channel_id=1, source_target_pairs={{0,1},{1,2},{2,3},{3,4},{4,5},{5,6},{6,7},{7,8},{8,9},{9,10},{10,1... | collective-permute-start | bytes 196616 | tf_op jit(solution)/shard_map/ppermute | solution.py:47
  124.7 17.0 %collective-permute-start.56 = (bf16[2,16,1024]{2,1,0:T(8,128)(2,1)S(1)}, bf16[2,16,1024]{2,1,0:T(8,128)(2,1)S(1)}, u32[]{:S(2)}, u32[]{:S(2)}) collective-permute-start(bf16[2,16,1024]{2,1,0:T(8,128)(2,1)S(1)} %collective-permute-done.55), channel_id=1, source_target_pairs={{0,1},{1,2},{2,3},{3,4},{4,5},{5,6},{6,7},{7,8},{8,9},{9,10},{10,1... | collective-permute-start | bytes 196616 | tf_op jit(solution)/shard_map/ppermute | solution.py:47
  126.7 16.9 %collective-permute-start.48 = (bf16[2,16,1024]{2,1,0:T(8,128)(2,1)S(1)}, bf16[2,16,1024]{2,1,0:T(8,128)(2,1)S(1)}, u32[]{:S(2)}, u32[]{:S(2)}) collective-permute-start(bf16[2,16,1024]{2,1,0:T(8,128)(2,1)S(1)} %collective-permute-done.47), channel_id=1, source_target_pairs={{0,1},{1,2},{2,3},{3,4},{4,5},{5,6},{6,7},{7,8},{8,9},{9,10},{10,1... | collective-permute-start | bytes 196616 | tf_op jit(solution)/shard_map/ppermute | solution.py:47
  149.6 17.0 %collective-permute-start.57 = (bf16[2,16,1024]{2,1,0:T(8,128)(2,1)S(1)}, bf16[2,16,1024]{2,1,0:T(8,128)(2,1)S(1)}, u32[]{:S(2)}, u32[]{:S(2)}) collective-permute-start(bf16[2,16,1024]{2,1,0:T(8,128)(2,1)S(1)} %collective-permute-done.56), channel_id=1, source_target_pairs={{0,1},{1,2},{2,3},{3,4},{4,5},{5,6},{6,7},{7,8},{8,9},{9,10},{10,1... | collective-permute-start | bytes 196616 | tf_op jit(solution)/shard_map/ppermute | solution.py:47
  151.6 16.9 %collective-permute-start.49 = (bf16[2,16,1024]{2,1,0:T(8,128)(2,1)S(1)}, bf16[2,16,1024]{2,1,0:T(8,128)(2,1)S(1)}, u32[]{:S(2)}, u32[]{:S(2)}) collective-permute-start(bf16[2,16,1024]{2,1,0:T(8,128)(2,1)S(1)} %collective-permute-done.48), channel_id=1, source_target_pairs={{0,1},{1,2},{2,3},{3,4},{4,5},{5,6},{6,7},{7,8},{8,9},{9,10},{10,1... | collective-permute-start | bytes 196616 | tf_op jit(solution)/shard_map/ppermute | solution.py:47
  170.5 18.2 %collective-permute-start.21 = (bf16[2,16,1024]{2,1,0:T(8,128)(2,1)S(1)}, bf16[2,16,1024]{2,1,0:T(8,128)(2,1)S(1)}, u32[]{:S(2)}, u32[]{:S(2)}) collective-permute-start(bf16[2,16,1024]{2,1,0:T(8,128)(2,1)S(1)} %collective-permute-done.17), channel_id=1, source_target_pairs={{0,15},{1,0},{2,1},{3,2},{4,3},{5,4},{6,5},{7,6},{8,7},{9,8},{10,9... | collective-permute-start | bytes 196616 | tf_op jit(solution)/shard_map/ppermute | solution.py:47
  176.4 41.0 %collective-permute-start.62 = (bf16[2,256,1024]{2,1,0:T(8,128)(2,1)S(1)}, bf16[2,256,1024]{2,1,0:T(8,128)(2,1)S(1)}, u32[]{:S(2)}, u32[]{:S(2)}) collective-permute-start(bf16[2,256,1024]{2,1,0:T(8,128)(2,1)S(1)} %pad_maximum_fusion), channel_id=1, source_target_pairs={{0,128},{32,160},{64,192},{96,224},{128,256},{160,288},{192,320},{... | collective-permute-start | bytes 3145736 | tf_op jit(solution)/shard_map/ppermute | solution.py:64
  217.4 17.9 %collective-permute-start.63 = (bf16[2,256,1024]{2,1,0:T(8,128)(2,1)S(1)}, bf16[2,256,1024]{2,1,0:T(8,128)(2,1)S(1)}, u32[]{:S(2)}, u32[]{:S(2)}) collective-permute-start(bf16[2,256,1024]{2,1,0:T(8,128)(2,1)S(1)} %collective-permute-done.62), channel_id=1, source_target_pairs={{0,128},{32,160},{64,192},{96,224},{128,256},{160,288},{192,320},{... | collective-permute-start | bytes 3145736 | tf_op jit(solution)/shard_map/ppermute | solution.py:65
  219.4 17.9 %collective-permute-start.64 = (bf16[2,256,1024]{2,1,0:T(8,128)(2,1)S(1)}, bf16[2,256,1024]{2,1,0:T(8,128)(2,1)S(1)}, u32[]{:S(2)}, u32[]{:S(2)}) collective-permute-start(bf16[2,256,1024]{2,1,0:T(8,128)(2,1)S(1)} %pad_maximum_fusion), channel_id=1, source_target_pairs={{0,384},{32,416},{64,448},{96,480},{128,0},{160,32},{192,64},{224,... | collective-permute-start | bytes 3145736 | tf_op jit(solution)/shard_map/ppermute | solution.py:66
  274.7 17.4 %collective-permute-start.98 = (bf16[2,16,1024]{2,1,0:T(8,128)(2,1)S(1)}, bf16[2,16,1024]{2,1,0:T(8,128)(2,1)S(1)}, u32[]{:S(2)}, u32[]{:S(2)}) collective-permute-start(bf16[2,16,1024]{2,1,0:T(8,128)(2,1)S(1)} %get-tuple-element.47), channel_id=1, source_target_pairs={{0,15},{1,0},{2,1},{3,2},{4,3},{5,4},{6,5},{7,6},{8,7},{9,8},{10,9... | collective-permute-start | bytes 196616 | tf_op jit(solution)/shard_map/ppermute | solution.py:47
  287.0 16.6 %collective-permute-start.70 = (bf16[2,16,1024]{2,1,0:T(8,128)(2,1)S(1)}, bf16[2,16,1024]{2,1,0:T(8,128)(2,1)S(1)}, u32[]{:S(2)}, u32[]{:S(2)}) collective-permute-start(bf16[2,16,1024]{2,1,0:T(8,128)(2,1)S(1)} %get-tuple-element.75), channel_id=1, source_target_pairs={{0,1},{1,2},{2,3},{3,4},{4,5},{5,6},{6,7},{7,8},{8,9},{9,10},{10,1... | collective-permute-start | bytes 196616 | tf_op jit(solution)/shard_map/ppermute | solution.py:47
  299.7 17.4 %collective-permute-start.102 = (bf16[2,16,1024]{2,1,0:T(8,128)(2,1)S(1)}, bf16[2,16,1024]{2,1,0:T(8,128)(2,1)S(1)}, u32[]{:S(2)}, u32[]{:S(2)}) collective-permute-start(bf16[2,16,1024]{2,1,0:T(8,128)(2,1)S(1)} %get-tuple-element.43), channel_id=1, source_target_pairs={{0,15},{1,0},{2,1},{3,2},{4,3},{5,4},{6,5},{7,6},{8,7},{9,8},{10,9... | collective-permute-start | bytes 196616 | tf_op jit(solution)/shard_map/ppermute | solution.py:47
  324.6 17.4 %collective-permute-start.106 = (bf16[2,16,1024]{2,1,0:T(8,128)(2,1)S(1)}, bf16[2,16,1024]{2,1,0:T(8,128)(2,1)S(1)}, u32[]{:S(2)}, u32[]{:S(2)}) collective-permute-start(bf16[2,16,1024]{2,1,0:T(8,128)(2,1)S(1)} %get-tuple-element.39), channel_id=1, source_target_pairs={{0,15},{1,0},{2,1},{3,2},{4,3},{5,4},{6,5},{7,6},{8,7},{9,8},{10,9... | collective-permute-start | bytes 196616 | tf_op jit(solution)/shard_map/ppermute | solution.py:47
  336.9 16.6 %collective-permute-start.78 = (bf16[2,16,1024]{2,1,0:T(8,128)(2,1)S(1)}, bf16[2,16,1024]{2,1,0:T(8,128)(2,1)S(1)}, u32[]{:S(2)}, u32[]{:S(2)}) collective-permute-start(bf16[2,16,1024]{2,1,0:T(8,128)(2,1)S(1)} %get-tuple-element.67), channel_id=1, source_target_pairs={{0,1},{1,2},{2,3},{3,4},{4,5},{5,6},{6,7},{7,8},{8,9},{9,10},{10,1... | collective-permute-start | bytes 196616 | tf_op jit(solution)/shard_map/ppermute | solution.py:47
  349.5 17.4 %collective-permute-start.110 = (bf16[2,16,1024]{2,1,0:T(8,128)(2,1)S(1)}, bf16[2,16,1024]{2,1,0:T(8,128)(2,1)S(1)}, u32[]{:S(2)}, u32[]{:S(2)}) collective-permute-start(bf16[2,16,1024]{2,1,0:T(8,128)(2,1)S(1)} %get-tuple-element.35), channel_id=1, source_target_pairs={{0,15},{1,0},{2,1},{3,2},{4,3},{5,4},{6,5},{7,6},{8,7},{9,8},{10,9... | collective-permute-start | bytes 196616 | tf_op jit(solution)/shard_map/ppermute | solution.py:47
  374.4 17.4 %collective-permute-start.114 = (bf16[2,16,1024]{2,1,0:T(8,128)(2,1)S(1)}, bf16[2,16,1024]{2,1,0:T(8,128)(2,1)S(1)}, u32[]{:S(2)}, u32[]{:S(2)}) collective-permute-start(bf16[2,16,1024]{2,1,0:T(8,128)(2,1)S(1)} %get-tuple-element.31), channel_id=1, source_target_pairs={{0,15},{1,0},{2,1},{3,2},{4,3},{5,4},{6,5},{7,6},{8,7},{9,8},{10,9... | collective-permute-start | bytes 196616 | tf_op jit(solution)/shard_map/ppermute | solution.py:47
  399.4 17.4 %collective-permute-start.118 = (bf16[2,16,1024]{2,1,0:T(8,128)(2,1)S(1)}, bf16[2,16,1024]{2,1,0:T(8,128)(2,1)S(1)}, u32[]{:S(2)}, u32[]{:S(2)}) collective-permute-start(bf16[2,16,1024]{2,1,0:T(8,128)(2,1)S(1)} %get-tuple-element.27), channel_id=1, source_target_pairs={{0,15},{1,0},{2,1},{3,2},{4,3},{5,4},{6,5},{7,6},{8,7},{9,8},{10,9... | collective-permute-start | bytes 196616 | tf_op jit(solution)/shard_map/ppermute | solution.py:47
  411.6 16.6 %collective-permute-start.90 = (bf16[2,16,1024]{2,1,0:T(8,128)(2,1)S(1)}, bf16[2,16,1024]{2,1,0:T(8,128)(2,1)S(1)}, u32[]{:S(2)}, u32[]{:S(2)}) collective-permute-start(bf16[2,16,1024]{2,1,0:T(8,128)(2,1)S(1)} %get-tuple-element.55), channel_id=1, source_target_pairs={{0,1},{1,2},{2,3},{3,4},{4,5},{5,6},{6,7},{7,8},{8,9},{9,10},{10,1... | collective-permute-start | bytes 196616 | tf_op jit(solution)/shard_map/ppermute | solution.py:47
  424.3 17.4 %collective-permute-start.122 = (bf16[2,16,1024]{2,1,0:T(8,128)(2,1)S(1)}, bf16[2,16,1024]{2,1,0:T(8,128)(2,1)S(1)}, u32[]{:S(2)}, u32[]{:S(2)}) collective-permute-start(bf16[2,16,1024]{2,1,0:T(8,128)(2,1)S(1)} %get-tuple-element.23), channel_id=1, source_target_pairs={{0,15},{1,0},{2,1},{3,2},{4,3},{5,4},{6,5},{7,6},{8,7},{9,8},{10,9... | collective-permute-start | bytes 196616 | tf_op jit(solution)/shard_map/ppermute | solution.py:47
  (108 other events, 1592.9 us)

commit v7 on v2

--- a/solution.py
+++ b/solution.py
@@ -48,23 +48,21 @@
 def gather_pieces(piece):
     ny = DP_SUB[0]
     own = piece[None]
-    across = lax.ppermute(own, "dp", DP_X_SWAP)
-    pair = jnp.concatenate([own, across])
-    pair_keys = [(0, 0, 0), (0, 1, 0)]
-    fwd1 = lax.ppermute(pair, "dp", DP_Y_FWD)
+    fwd1 = lax.ppermute(own, "dp", DP_Y_FWD)
     fwd2 = lax.ppermute(fwd1, "dp", DP_Y_FWD)
-    bwd1 = lax.ppermute(pair, "dp", DP_Y_BWD)
-    shift = lambda keys, dy: [((k[0] + dy) % ny, k[1], k[2]) for k in keys]
-    chip = jnp.concatenate([pair, fwd1, fwd2, bwd1])
-    chip_keys = pair_keys + shift(pair_keys, ny - 1) + shift(pair_keys, ny - 2) + shift(pair_keys, 1)
+    bwd1 = lax.ppermute(own, "dp", DP_Y_BWD)
+    col_keys = [(0, 0, 0), (ny - 1, 0, 0), (ny - 2, 0, 0), (1, 0, 0)]
+    across = lax.ppermute(jnp.concatenate([own, fwd1, fwd2, bwd1]), "dp", DP_X_SWAP)
+    across_keys = [(k[0], 1, 0) for k in col_keys]
+    chip = jnp.concatenate([own, fwd1, fwd2, bwd1, across])
     other_core = lax.ppermute(chip, "dp", DP_C_SWAP)
     return [
-        ([(0, 0, 0)], own),
-        ([(0, 1, 0)], across),
-        (shift(pair_keys, ny - 1), fwd1),
-        (shift(pair_keys, ny - 2), fwd2),
-        (shift(pair_keys, 1), bwd1),
-        ([(k[0], k[1], 1) for k in chip_keys], other_core),
+        (col_keys[0:1], own),
+        (col_keys[1:2], fwd1),
+        (col_keys[2:3], fwd2),
+        (col_keys[3:4], bwd1),
+        (across_keys, across),
+        ([(k[0], k[1], 1) for k in col_keys + across_keys], other_core),
     ]
 
 

time: 240 us -> 236 us (0.983)
  local copies, waits for them, and re-layouts: 10.8 us -> 8.13 us
    all_to_all x1, waiting for transfers between devices: 0.01 us -> 6.16 us  [per_device(): lax.all_to_all(jnp.concatenate([outgoing, place_cols], axis=1).reshape(dp...]
    ppermute x1, waiting for transfers between devices: 9.57 us -> 5.11 us  [per_device(): lax.ppermute(travelling, 'tensor', TP_L_SWAP)]
    unnamed x24 -> x26, local copies, waits for them, and re-layouts: 6.26 us -> 4.52 us
  transfers between devices with their start and end apart: 38 -> 38, of which waited for: 18 -> 19; matrix products, arithmetic and copies ran while one was open for 5% -> 4% of each run, Pallas kernels for 0% -> 0%
where the time goes in v7:
time: 236 us; the launch traced here: 232 us
  starting transfers between devices  139 us (59%)
  waiting for transfers between devices  71.3 us (30%)
  matrix products  8.53 us (4%)
  local copies, waits for them, and re-layouts  8.13 us (3%)
  other arithmetic  3.44 us (1%)
    ppermute x7, starting transfers between devices, per_device(): bwd = lax.ppermute(bwd, 'tensor', TP_Z_BWD)  41.3 us
    ppermute x7, starting transfers between devices, per_device(): got = lax.ppermute(bwd, 'tensor', TP_Z_BWD)  36.2 us
    ppermute x8, waiting for transfers between devices, per_device(): got = lax.ppermute(fwd, 'tensor', TP_Z_FWD)  28.3 us
    ppermute x8, waiting for transfers between devices, per_device(): fwd = lax.ppermute(fwd, 'tensor', TP_Z_FWD)  16.6 us
    ppermute x8, starting transfers between devices, per_device(): got = lax.ppermute(fwd, 'tensor', TP_Z_FWD)  15.4 us
    ppermute x8, starting transfers between devices, per_device(): fwd = lax.ppermute(fwd, 'tensor', TP_Z_FWD)  15.3 us
    ppermute x7, waiting for transfers between devices, per_device(): bwd = lax.ppermute(bwd, 'tensor', TP_Z_BWD)  7.74 us
    ppermute x1, starting transfers between devices, gather_pieces(): fwd1 = lax.ppermute(own, 'dp', DP_Y_FWD)  7.5 us
  transfers between devices with their start and end apart: 38, of which 19 were waited for; matrix products, arithmetic and copies ran while one was open for 4% of the time, Pallas kernels for 0%

profile of v7, /device:TPU:24, one launch (start us, length us, event | category | flops | bytes accessed | tf_op | source)
XLA Modules:
  0.0 232.2 jit_solution(8734897374603230176)
XLA Ops:
  2.0 7.5 %collective-permute-start.16 = (bf16[1,256,1024]{2,1,0:T(8,128)(2,1)S(1)}, bf16[1,256,1024]{2,1,0:T(8,128)(2,1)S(1)}, u32[]{:S(2)}, u32[]{:S(2)}) collective-permute-start(bf16[1,256,1024]{2,1,0:T(8,128)(2,1)S(1)} %bitcast.121), channel_id=1, source_target_pairs={{0,128},{32,160},{64,192},{96,224},{128,256},{160,288},{192,320},{... | collective-permute-start | bytes 1572872 | tf_op jit(solution)/shard_map/ppermute | solution.py:51
  14.4 6.6 %all-to-all-start = ((bf16[16,2,4224]{2,1,0:T(2,128)(2,1)}), bf16[16,2,4224]{2,1,0:T(2,128)(2,1)S(1)}, u32[]{:S(2)}, u32[]{:S(2)}) async-start(bf16[16,2,4224]{2,1,0:T(2,128)(2,1)} %reshape.916), calls=%async_computation | async-start | bytes 540672 | tf_op jit(solution)/shard_map/all_to_all | solution.py:95
  22.2 6.2 %all-to-all-done = bf16[16,2,4224]{2,1,0:T(2,128)(2,1)S(1)} async-done(((bf16[16,2,4224]{2,1,0:T(2,128)(2,1)}), bf16[16,2,4224]{2,1,0:T(2,128)(2,1)S(1)}, u32[]{:S(2)}, u32[]{:S(2)}) %all-to-all-start) | async-done | bytes 270368 | tf_op jit(solution)/shard_map/all_to_all | solution.py:95
  31.7 5.1 %collective-permute-done = bf16[16,4096]{1,0:T(8,128)(2,1)S(1)} collective-permute-done((bf16[16,4096]{1,0:T(8,128)(2,1)S(1)}, bf16[16,4096]{1,0:T(8,128)(2,1)S(1)}, u32[]{:S(2)}, u32[]{:S(2)}) %collective-permute-start) | collective-permute-done | bytes 131104 | tf_op jit(solution)/shard_map/ppermute | solution.py:126
  36.8 8.4 %collective-permute-start.1 = (bf16[2,16,4096]{2,1,0:T(8,128)(2,1)S(1)}, bf16[2,16,4096]{2,1,0:T(8,128)(2,1)S(1)}, u32[]{:S(2)}, u32[]{:S(2)}) collective-permute-start(bf16[2,16,4096]{2,1,0:T(8,128)(2,1)S(1)} %pad_maximum_fusion.2), channel_id=1, source_target_pairs={{0,15},{1,0},{2,1},{3,2},{4,3},{5,4},{6,5},{7,6},{8,7},{9,8},{10,9... | collective-permute-start | bytes 786440 | tf_op jit(solution)/shard_map/ppermute | solution.py:134
  47.2 4.0 %collective-permute-start.17 = (bf16[1,256,1024]{2,1,0:T(8,128)(2,1)S(1)}, bf16[1,256,1024]{2,1,0:T(8,128)(2,1)S(1)}, u32[]{:S(2)}, u32[]{:S(2)}) collective-permute-start(bf16[1,256,1024]{2,1,0:T(8,128)(2,1)S(1)} %collective-permute-done.16), channel_id=1, source_target_pairs={{0,128},{32,160},{64,192},{96,224},{128,256},{160,288},{192,320},{... | collective-permute-start | bytes 1572872 | tf_op jit(solution)/shard_map/ppermute | solution.py:52
  52.1 5.4 %collective-permute-start.2 = (bf16[2,16,4096]{2,1,0:T(8,128)(2,1)S(1)}, bf16[2,16,4096]{2,1,0:T(8,128)(2,1)S(1)}, u32[]{:S(2)}, u32[]{:S(2)}) collective-permute-start(bf16[2,16,4096]{2,1,0:T(8,128)(2,1)S(1)} %collective-permute-done.1), channel_id=1, source_target_pairs={{0,15},{1,0},{2,1},{3,2},{4,3},{5,4},{6,5},{7,6},{8,7},{9,8},{10,9... | collective-permute-start | bytes 786440 | tf_op jit(solution)/shard_map/ppermute | solution.py:134
  61.4 5.6 %collective-permute-start.3 = (bf16[2,16,4096]{2,1,0:T(8,128)(2,1)S(1)}, bf16[2,16,4096]{2,1,0:T(8,128)(2,1)S(1)}, u32[]{:S(2)}, u32[]{:S(2)}) collective-permute-start(bf16[2,16,4096]{2,1,0:T(8,128)(2,1)S(1)} %collective-permute-done.2), channel_id=1, source_target_pairs={{0,15},{1,0},{2,1},{3,2},{4,3},{5,4},{6,5},{7,6},{8,7},{9,8},{10,9... | collective-permute-start | bytes 786440 | tf_op jit(solution)/shard_map/ppermute | solution.py:134
  72.8 5.1 %collective-permute-start.4 = (bf16[2,16,4096]{2,1,0:T(8,128)(2,1)S(1)}, bf16[2,16,4096]{2,1,0:T(8,128)(2,1)S(1)}, u32[]{:S(2)}, u32[]{:S(2)}) collective-permute-start(bf16[2,16,4096]{2,1,0:T(8,128)(2,1)S(1)} %collective-permute-done.3), channel_id=1, source_target_pairs={{0,15},{1,0},{2,1},{3,2},{4,3},{5,4},{6,5},{7,6},{8,7},{9,8},{10,9... | collective-permute-start | bytes 786440 | tf_op jit(solution)/shard_map/ppermute | solution.py:134
  81.8 5.6 %collective-permute-start.5 = (bf16[2,16,4096]{2,1,0:T(8,128)(2,1)S(1)}, bf16[2,16,4096]{2,1,0:T(8,128)(2,1)S(1)}, u32[]{:S(2)}, u32[]{:S(2)}) collective-permute-start(bf16[2,16,4096]{2,1,0:T(8,128)(2,1)S(1)} %collective-permute-done.4), channel_id=1, source_target_pairs={{0,15},{1,0},{2,1},{3,2},{4,3},{5,4},{6,5},{7,6},{8,7},{9,8},{10,9... | collective-permute-start | bytes 786440 | tf_op jit(solution)/shard_map/ppermute | solution.py:134
  91.2 5.6 %collective-permute-start.6 = (bf16[2,16,4096]{2,1,0:T(8,128)(2,1)S(1)}, bf16[2,16,4096]{2,1,0:T(8,128)(2,1)S(1)}, u32[]{:S(2)}, u32[]{:S(2)}) collective-permute-start(bf16[2,16,4096]{2,1,0:T(8,128)(2,1)S(1)} %collective-permute-done.5), channel_id=1, source_target_pairs={{0,15},{1,0},{2,1},{3,2},{4,3},{5,4},{6,5},{7,6},{8,7},{9,8},{10,9... | collective-permute-start | bytes 786440 | tf_op jit(solution)/shard_map/ppermute | solution.py:134
  100.8 5.6 %collective-permute-start.7 = (bf16[2,16,4096]{2,1,0:T(8,128)(2,1)S(1)}, bf16[2,16,4096]{2,1,0:T(8,128)(2,1)S(1)}, u32[]{:S(2)}, u32[]{:S(2)}) collective-permute-start(bf16[2,16,4096]{2,1,0:T(8,128)(2,1)S(1)} %collective-permute-done.6), channel_id=1, source_target_pairs={{0,15},{1,0},{2,1},{3,2},{4,3},{5,4},{6,5},{7,6},{8,7},{9,8},{10,9... | collective-permute-start | bytes 786440 | tf_op jit(solution)/shard_map/ppermute | solution.py:134
  108.7 8.7 %collective-permute-done.14 = bf16[2,16,4096]{2,1,0:T(8,128)(2,1)S(1)} collective-permute-done((bf16[2,16,4096]{2,1,0:T(8,128)(2,1)S(1)}, bf16[2,16,4096]{2,1,0:T(8,128)(2,1)S(1)}, u32[]{:S(2)}, u32[]{:S(2)}) %collective-permute-start.14) | collective-permute-done | bytes 262176 | tf_op jit(solution)/shard_map/ppermute | solution.py:130
  119.3 7.5 %collective-permute-done.15 = bf16[2,16,4096]{2,1,0:T(8,128)(2,1)S(1)} collective-permute-done((bf16[2,16,4096]{2,1,0:T(8,128)(2,1)S(1)}, bf16[2,16,4096]{2,1,0:T(8,128)(2,1)S(1)}, u32[]{:S(2)}, u32[]{:S(2)}) %collective-permute-start.15) | collective-permute-done | bytes 262176 | tf_op jit(solution)/shard_map/ppermute | solution.py:130
  132.0 4.2 %collective-permute-done.20 = bf16[8,256,1024]{2,1,0:T(8,128)(2,1)S(1)} collective-permute-done((bf16[8,256,1024]{2,1,0:T(8,128)(2,1)S(1)}, bf16[8,256,1024]{2,1,0:T(8,128)(2,1)S(1)}, u32[]{:S(2)}, u32[]{:S(2)}) %collective-permute-start.20) | collective-permute-done | bytes 4194336 | tf_op jit(solution)/shard_map/ppermute | solution.py:58
  145.4 5.1 %collective-permute-start.29 = (bf16[2,16,4096]{2,1,0:T(8,128)(2,1)S(1)}, bf16[2,16,4096]{2,1,0:T(8,128)(2,1)S(1)}, u32[]{:S(2)}, u32[]{:S(2)}) collective-permute-start(bf16[2,16,4096]{2,1,0:T(8,128)(2,1)S(1)} %bitcast.151), channel_id=1, source_target_pairs={{0,15},{1,0},{2,1},{3,2},{4,3},{5,4},{6,5},{7,6},{8,7},{9,8},{10,9... | collective-permute-start | bytes 786440 | tf_op jit(solution)/shard_map/ppermute | solution.py:166
  150.6 4.4 %collective-permute-done.21 = bf16[2,16,4096]{2,1,0:T(8,128)(2,1)S(1)} collective-permute-done((bf16[2,16,4096]{2,1,0:T(8,128)(2,1)S(1)}, bf16[2,16,4096]{2,1,0:T(8,128)(2,1)S(1)}, u32[]{:S(2)}, u32[]{:S(2)}) %collective-permute-start.21) | collective-permute-done | bytes 262176 | tf_op jit(solution)/shard_map/ppermute | solution.py:159
  157.0 5.1 %collective-permute-start.30 = (bf16[2,16,4096]{2,1,0:T(8,128)(2,1)S(1)}, bf16[2,16,4096]{2,1,0:T(8,128)(2,1)S(1)}, u32[]{:S(2)}, u32[]{:S(2)}) collective-permute-start(bf16[2,16,4096]{2,1,0:T(8,128)(2,1)S(1)} %fusion.12), channel_id=1, source_target_pairs={{0,15},{1,0},{2,1},{3,2},{4,3},{5,4},{6,5},{7,6},{8,7},{9,8},{10,9... | collective-permute-start | bytes 786440 | tf_op jit(solution)/shard_map/ppermute | solution.py:166
  167.7 5.1 %collective-permute-start.31 = (bf16[2,16,4096]{2,1,0:T(8,128)(2,1)S(1)}, bf16[2,16,4096]{2,1,0:T(8,128)(2,1)S(1)}, u32[]{:S(2)}, u32[]{:S(2)}) collective-permute-start(bf16[2,16,4096]{2,1,0:T(8,128)(2,1)S(1)} %fusion.11), channel_id=1, source_target_pairs={{0,15},{1,0},{2,1},{3,2},{4,3},{5,4},{6,5},{7,6},{8,7},{9,8},{10,9... | collective-permute-start | bytes 786440 | tf_op jit(solution)/shard_map/ppermute | solution.py:166
  177.5 5.1 %collective-permute-start.32 = (bf16[2,16,4096]{2,1,0:T(8,128)(2,1)S(1)}, bf16[2,16,4096]{2,1,0:T(8,128)(2,1)S(1)}, u32[]{:S(2)}, u32[]{:S(2)}) collective-permute-start(bf16[2,16,4096]{2,1,0:T(8,128)(2,1)S(1)} %fusion.10), channel_id=1, source_target_pairs={{0,15},{1,0},{2,1},{3,2},{4,3},{5,4},{6,5},{7,6},{8,7},{9,8},{10,9... | collective-permute-start | bytes 786440 | tf_op jit(solution)/shard_map/ppermute | solution.py:166
  187.1 5.1 %collective-permute-start.33 = (bf16[2,16,4096]{2,1,0:T(8,128)(2,1)S(1)}, bf16[2,16,4096]{2,1,0:T(8,128)(2,1)S(1)}, u32[]{:S(2)}, u32[]{:S(2)}) collective-permute-start(bf16[2,16,4096]{2,1,0:T(8,128)(2,1)S(1)} %fusion.9), channel_id=1, source_target_pairs={{0,15},{1,0},{2,1},{3,2},{4,3},{5,4},{6,5},{7,6},{8,7},{9,8},{10,9... | collective-permute-start | bytes 786440 | tf_op jit(solution)/shard_map/ppermute | solution.py:166
  196.6 5.1 %collective-permute-start.34 = (bf16[2,16,4096]{2,1,0:T(8,128)(2,1)S(1)}, bf16[2,16,4096]{2,1,0:T(8,128)(2,1)S(1)}, u32[]{:S(2)}, u32[]{:S(2)}) collective-permute-start(bf16[2,16,4096]{2,1,0:T(8,128)(2,1)S(1)} %fusion.8), channel_id=1, source_target_pairs={{0,15},{1,0},{2,1},{3,2},{4,3},{5,4},{6,5},{7,6},{8,7},{9,8},{10,9... | collective-permute-start | bytes 786440 | tf_op jit(solution)/shard_map/ppermute | solution.py:166
  206.3 5.4 %collective-permute-start.35 = (bf16[2,16,4096]{2,1,0:T(8,128)(2,1)S(1)}, bf16[2,16,4096]{2,1,0:T(8,128)(2,1)S(1)}, u32[]{:S(2)}, u32[]{:S(2)}) collective-permute-start(bf16[2,16,4096]{2,1,0:T(8,128)(2,1)S(1)} %fusion.7), channel_id=1, source_target_pairs={{0,15},{1,0},{2,1},{3,2},{4,3},{5,4},{6,5},{7,6},{8,7},{9,8},{10,9... | collective-permute-start | bytes 786440 | tf_op jit(solution)/shard_map/ppermute | solution.py:166
  217.0 7.5 %collective-permute-done.28 = bf16[2,16,4096]{2,1,0:T(8,128)(2,1)S(1)} collective-permute-done((bf16[2,16,4096]{2,1,0:T(8,128)(2,1)S(1)}, bf16[2,16,4096]{2,1,0:T(8,128)(2,1)S(1)}, u32[]{:S(2)}, u32[]{:S(2)}) %collective-permute-start.28) | collective-permute-done | bytes 262176 | tf_op jit(solution)/shard_map/ppermute | solution.py:159
  (138 shorter events, 91.5 us)
Async XLA Ops:
  2.0 45.2 %collective-permute-start.16 = (bf16[1,256,1024]{2,1,0:T(8,128)(2,1)S(1)}, bf16[1,256,1024]{2,1,0:T(8,128)(2,1)S(1)}, u32[]{:S(2)}, u32[]{:S(2)}) collective-permute-start(bf16[1,256,1024]{2,1,0:T(8,128)(2,1)S(1)} %bitcast.121), channel_id=1, source_target_pairs={{0,128},{32,160},{64,192},{96,224},{128,256},{160,288},{192,320},{... | collective-permute-start | bytes 1572872 | tf_op jit(solution)/shard_map/ppermute | solution.py:51
  9.5 59.4 %collective-permute-start.18 = (bf16[1,256,1024]{2,1,0:T(8,128)(2,1)S(1)}, bf16[1,256,1024]{2,1,0:T(8,128)(2,1)S(1)}, u32[]{:S(2)}, u32[]{:S(2)}) collective-permute-start(bf16[1,256,1024]{2,1,0:T(8,128)(2,1)S(1)} %bitcast.122), channel_id=1, source_target_pairs={{0,384},{32,416},{64,448},{96,480},{128,0},{160,32},{192,64},{224,... | collective-permute-start | bytes 1572872 | tf_op jit(solution)/shard_map/ppermute | solution.py:53
  14.4 14.0 %all-to-all-start = ((bf16[16,2,4224]{2,1,0:T(2,128)(2,1)}), bf16[16,2,4224]{2,1,0:T(2,128)(2,1)S(1)}, u32[]{:S(2)}, u32[]{:S(2)}) async-start(bf16[16,2,4224]{2,1,0:T(2,128)(2,1)} %reshape.916), calls=%async_computation | async-start | bytes 540672 | tf_op jit(solution)/shard_map/all_to_all | solution.py:95
  36.8 15.3 %collective-permute-start.1 = (bf16[2,16,4096]{2,1,0:T(8,128)(2,1)S(1)}, bf16[2,16,4096]{2,1,0:T(8,128)(2,1)S(1)}, u32[]{:S(2)}, u32[]{:S(2)}) collective-permute-start(bf16[2,16,4096]{2,1,0:T(8,128)(2,1)S(1)} %pad_maximum_fusion.2), channel_id=1, source_target_pairs={{0,15},{1,0},{2,1},{3,2},{4,3},{5,4},{6,5},{7,6},{8,7},{9,8},{10,9... | collective-permute-start | bytes 786440 | tf_op jit(solution)/shard_map/ppermute | solution.py:134
  45.2 12.3 %collective-permute-start.8 = (bf16[2,16,4096]{2,1,0:T(8,128)(2,1)S(1)}, bf16[2,16,4096]{2,1,0:T(8,128)(2,1)S(1)}, u32[]{:S(2)}, u32[]{:S(2)}) collective-permute-start(bf16[2,16,4096]{2,1,0:T(8,128)(2,1)S(1)} %pad_maximum_fusion.2), channel_id=1, source_target_pairs={{0,1},{1,2},{2,3},{3,4},{4,5},{5,6},{6,7},{7,8},{8,9},{9,10},{10,1... | collective-permute-start | bytes 786440 | tf_op jit(solution)/shard_map/ppermute | solution.py:130
  47.2 21.8 %collective-permute-start.17 = (bf16[1,256,1024]{2,1,0:T(8,128)(2,1)S(1)}, bf16[1,256,1024]{2,1,0:T(8,128)(2,1)S(1)}, u32[]{:S(2)}, u32[]{:S(2)}) collective-permute-start(bf16[1,256,1024]{2,1,0:T(8,128)(2,1)S(1)} %collective-permute-done.16), channel_id=1, source_target_pairs={{0,128},{32,160},{64,192},{96,224},{128,256},{160,288},{192,320},{... | collective-permute-start | bytes 1572872 | tf_op jit(solution)/shard_map/ppermute | solution.py:52
  57.5 9.5 %collective-permute-start.9 = (bf16[2,16,4096]{2,1,0:T(8,128)(2,1)S(1)}, bf16[2,16,4096]{2,1,0:T(8,128)(2,1)S(1)}, u32[]{:S(2)}, u32[]{:S(2)}) collective-permute-start(bf16[2,16,4096]{2,1,0:T(8,128)(2,1)S(1)} %collective-permute-done.8), channel_id=1, source_target_pairs={{0,1},{1,2},{2,3},{3,4},{4,5},{5,6},{6,7},{7,8},{8,9},{9,10},{10,1... | collective-permute-start | bytes 786440 | tf_op jit(solution)/shard_map/ppermute | solution.py:130
  61.4 11.4 %collective-permute-start.3 = (bf16[2,16,4096]{2,1,0:T(8,128)(2,1)S(1)}, bf16[2,16,4096]{2,1,0:T(8,128)(2,1)S(1)}, u32[]{:S(2)}, u32[]{:S(2)}) collective-permute-start(bf16[2,16,4096]{2,1,0:T(8,128)(2,1)S(1)} %collective-permute-done.2), channel_id=1, source_target_pairs={{0,15},{1,0},{2,1},{3,2},{4,3},{5,4},{6,5},{7,6},{8,7},{9,8},{10,9... | collective-permute-start | bytes 786440 | tf_op jit(solution)/shard_map/ppermute | solution.py:134
  67.0 10.9 %collective-permute-start.10 = (bf16[2,16,4096]{2,1,0:T(8,128)(2,1)S(1)}, bf16[2,16,4096]{2,1,0:T(8,128)(2,1)S(1)}, u32[]{:S(2)}, u32[]{:S(2)}) collective-permute-start(bf16[2,16,4096]{2,1,0:T(8,128)(2,1)S(1)} %collective-permute-done.9), channel_id=1, source_target_pairs={{0,1},{1,2},{2,3},{3,4},{4,5},{5,6},{6,7},{7,8},{8,9},{9,10},{10,1... | collective-permute-start | bytes 786440 | tf_op jit(solution)/shard_map/ppermute | solution.py:130
  69.2 57.6 %collective-permute-start.19 = (bf16[4,256,1024]{2,1,0:T(8,128)(2,1)S(1)}, bf16[4,256,1024]{2,1,0:T(8,128)(2,1)S(1)}, u32[]{:S(2)}, u32[]{:S(2)}) collective-permute-start(bf16[4,256,1024]{2,1,0:T(8,128)(2,1)S(1)} %pad_maximum_fusion), channel_id=1, source_target_pairs={{0,64},{32,96},{64,0},{96,32},{128,192},{160,224},{192,128},{224,1... | collective-permute-start | bytes 6291464 | tf_op jit(solution)/shard_map/ppermute | solution.py:55
  91.2 9.6 %collective-permute-start.6 = (bf16[2,16,4096]{2,1,0:T(8,128)(2,1)S(1)}, bf16[2,16,4096]{2,1,0:T(8,128)(2,1)S(1)}, u32[]{:S(2)}, u32[]{:S(2)}) collective-permute-start(bf16[2,16,4096]{2,1,0:T(8,128)(2,1)S(1)} %collective-permute-done.5), channel_id=1, source_target_pairs={{0,15},{1,0},{2,1},{3,2},{4,3},{5,4},{6,5},{7,6},{8,7},{9,8},{10,9... | collective-permute-start | bytes 786440 | tf_op jit(solution)/shard_map/ppermute | solution.py:134
  96.9 9.9 %collective-permute-start.13 = (bf16[2,16,4096]{2,1,0:T(8,128)(2,1)S(1)}, bf16[2,16,4096]{2,1,0:T(8,128)(2,1)S(1)}, u32[]{:S(2)}, u32[]{:S(2)}) collective-permute-start(bf16[2,16,4096]{2,1,0:T(8,128)(2,1)S(1)} %collective-permute-done.12), channel_id=1, source_target_pairs={{0,1},{1,2},{2,3},{3,4},{4,5},{5,6},{6,7},{7,8},{8,9},{9,10},{10,1... | collective-permute-start | bytes 786440 | tf_op jit(solution)/shard_map/ppermute | solution.py:130
  100.8 18.5 %collective-permute-start.7 = (bf16[2,16,4096]{2,1,0:T(8,128)(2,1)S(1)}, bf16[2,16,4096]{2,1,0:T(8,128)(2,1)S(1)}, u32[]{:S(2)}, u32[]{:S(2)}) collective-permute-start(bf16[2,16,4096]{2,1,0:T(8,128)(2,1)S(1)} %collective-permute-done.6), channel_id=1, source_target_pairs={{0,15},{1,0},{2,1},{3,2},{4,3},{5,4},{6,5},{7,6},{8,7},{9,8},{10,9... | collective-permute-start | bytes 786440 | tf_op jit(solution)/shard_map/ppermute | solution.py:134
  106.7 10.7 %collective-permute-start.14 = (bf16[2,16,4096]{2,1,0:T(8,128)(2,1)S(1)}, bf16[2,16,4096]{2,1,0:T(8,128)(2,1)S(1)}, u32[]{:S(2)}, u32[]{:S(2)}) collective-permute-start(bf16[2,16,4096]{2,1,0:T(8,128)(2,1)S(1)} %collective-permute-done.13), channel_id=1, source_target_pairs={{0,1},{1,2},{2,3},{3,4},{4,5},{5,6},{6,7},{7,8},{8,9},{9,10},{10,1... | collective-permute-start | bytes 786440 | tf_op jit(solution)/shard_map/ppermute | solution.py:130
  143.5 11.4 %collective-permute-start.21 = (bf16[2,16,4096]{2,1,0:T(8,128)(2,1)S(1)}, bf16[2,16,4096]{2,1,0:T(8,128)(2,1)S(1)}, u32[]{:S(2)}, u32[]{:S(2)}) collective-permute-start(bf16[2,16,4096]{2,1,0:T(8,128)(2,1)S(1)} %bitcast.152), channel_id=1, source_target_pairs={{0,1},{1,2},{2,3},{3,4},{4,5},{5,6},{6,7},{7,8},{8,9},{9,10},{10,1... | collective-permute-start | bytes 786440 | tf_op jit(solution)/shard_map/ppermute | solution.py:159
  145.4 11.5 %collective-permute-start.29 = (bf16[2,16,4096]{2,1,0:T(8,128)(2,1)S(1)}, bf16[2,16,4096]{2,1,0:T(8,128)(2,1)S(1)}, u32[]{:S(2)}, u32[]{:S(2)}) collective-permute-start(bf16[2,16,4096]{2,1,0:T(8,128)(2,1)S(1)} %bitcast.151), channel_id=1, source_target_pairs={{0,15},{1,0},{2,1},{3,2},{4,3},{5,4},{6,5},{7,6},{8,7},{9,8},{10,9... | collective-permute-start | bytes 786440 | tf_op jit(solution)/shard_map/ppermute | solution.py:166
  155.0 10.6 %collective-permute-start.22 = (bf16[2,16,4096]{2,1,0:T(8,128)(2,1)S(1)}, bf16[2,16,4096]{2,1,0:T(8,128)(2,1)S(1)}, u32[]{:S(2)}, u32[]{:S(2)}) collective-permute-start(bf16[2,16,4096]{2,1,0:T(8,128)(2,1)S(1)} %fusion.19), channel_id=1, source_target_pairs={{0,1},{1,2},{2,3},{3,4},{4,5},{5,6},{6,7},{7,8},{8,9},{9,10},{10,1... | collective-permute-start | bytes 786440 | tf_op jit(solution)/shard_map/ppermute | solution.py:159
  157.0 10.6 %collective-permute-start.30 = (bf16[2,16,4096]{2,1,0:T(8,128)(2,1)S(1)}, bf16[2,16,4096]{2,1,0:T(8,128)(2,1)S(1)}, u32[]{:S(2)}, u32[]{:S(2)}) collective-permute-start(bf16[2,16,4096]{2,1,0:T(8,128)(2,1)S(1)} %fusion.12), channel_id=1, source_target_pairs={{0,15},{1,0},{2,1},{3,2},{4,3},{5,4},{6,5},{7,6},{8,7},{9,8},{10,9... | collective-permute-start | bytes 786440 | tf_op jit(solution)/shard_map/ppermute | solution.py:166
  165.7 9.7 %collective-permute-start.23 = (bf16[2,16,4096]{2,1,0:T(8,128)(2,1)S(1)}, bf16[2,16,4096]{2,1,0:T(8,128)(2,1)S(1)}, u32[]{:S(2)}, u32[]{:S(2)}) collective-permute-start(bf16[2,16,4096]{2,1,0:T(8,128)(2,1)S(1)} %fusion.18), channel_id=1, source_target_pairs={{0,1},{1,2},{2,3},{3,4},{4,5},{5,6},{6,7},{7,8},{8,9},{9,10},{10,1... | collective-permute-start | bytes 786440 | tf_op jit(solution)/shard_map/ppermute | solution.py:159
  167.7 9.7 %collective-permute-start.31 = (bf16[2,16,4096]{2,1,0:T(8,128)(2,1)S(1)}, bf16[2,16,4096]{2,1,0:T(8,128)(2,1)S(1)}, u32[]{:S(2)}, u32[]{:S(2)}) collective-permute-start(bf16[2,16,4096]{2,1,0:T(8,128)(2,1)S(1)} %fusion.11), channel_id=1, source_target_pairs={{0,15},{1,0},{2,1},{3,2},{4,3},{5,4},{6,5},{7,6},{8,7},{9,8},{10,9... | collective-permute-start | bytes 786440 | tf_op jit(solution)/shard_map/ppermute | solution.py:166
  194.6 9.6 %collective-permute-start.26 = (bf16[2,16,4096]{2,1,0:T(8,128)(2,1)S(1)}, bf16[2,16,4096]{2,1,0:T(8,128)(2,1)S(1)}, u32[]{:S(2)}, u32[]{:S(2)}) collective-permute-start(bf16[2,16,4096]{2,1,0:T(8,128)(2,1)S(1)} %fusion.15), channel_id=1, source_target_pairs={{0,1},{1,2},{2,3},{3,4},{4,5},{5,6},{6,7},{7,8},{8,9},{9,10},{10,1... | collective-permute-start | bytes 786440 | tf_op jit(solution)/shard_map/ppermute | solution.py:159
  196.6 9.6 %collective-permute-start.34 = (bf16[2,16,4096]{2,1,0:T(8,128)(2,1)S(1)}, bf16[2,16,4096]{2,1,0:T(8,128)(2,1)S(1)}, u32[]{:S(2)}, u32[]{:S(2)}) collective-permute-start(bf16[2,16,4096]{2,1,0:T(8,128)(2,1)S(1)} %fusion.8), channel_id=1, source_target_pairs={{0,15},{1,0},{2,1},{3,2},{4,3},{5,4},{6,5},{7,6},{8,7},{9,8},{10,9... | collective-permute-start | bytes 786440 | tf_op jit(solution)/shard_map/ppermute | solution.py:166
  204.3 10.7 %collective-permute-start.27 = (bf16[2,16,4096]{2,1,0:T(8,128)(2,1)S(1)}, bf16[2,16,4096]{2,1,0:T(8,128)(2,1)S(1)}, u32[]{:S(2)}, u32[]{:S(2)}) collective-permute-start(bf16[2,16,4096]{2,1,0:T(8,128)(2,1)S(1)} %fusion.14), channel_id=1, source_target_pairs={{0,1},{1,2},{2,3},{3,4},{4,5},{5,6},{6,7},{7,8},{8,9},{9,10},{10,1... | collective-permute-start | bytes 786440 | tf_op jit(solution)/shard_map/ppermute | solution.py:159
  206.3 10.7 %collective-permute-start.35 = (bf16[2,16,4096]{2,1,0:T(8,128)(2,1)S(1)}, bf16[2,16,4096]{2,1,0:T(8,128)(2,1)S(1)}, u32[]{:S(2)}, u32[]{:S(2)}) collective-permute-start(bf16[2,16,4096]{2,1,0:T(8,128)(2,1)S(1)} %fusion.7), channel_id=1, source_target_pairs={{0,15},{1,0},{2,1},{3,2},{4,3},{5,4},{6,5},{7,6},{8,7},{9,8},{10,9... | collective-permute-start | bytes 786440 | tf_op jit(solution)/shard_map/ppermute | solution.py:166
  (17 other events, 162.5 us)

commit v8 on v7

--- a/solution.py
+++ b/solution.py
@@ -137,21 +137,26 @@
     row_total = gathered.shape[0] * gathered.shape[1]
     normed = gathered.reshape(row_total, feature_count)
 
-    act = None
-    col = 0
-    for ks, buf in buffers:
-        width = len(ks) * piece_rows
-        part = jnp.dot(
-            normed[:, col : col + width],
-            buf.reshape(width, 2 * ff_cols),
-            preferred_element_type=jnp.float32,
-        )
-        act = part if act is None else act + part
-        col += width
-    gate_act = act[:, :ff_cols]
-    up_act = act[:, ff_cols:]
-    hidden = (jax.nn.silu(gate_act) * up_act).astype(jnp.bfloat16)
-    term = jnp.dot(hidden, down_weight, preferred_element_type=jnp.float32).astype(jnp.bfloat16)
+    def ffn(rows):
+        act = None
+        col = 0
+        for ks, buf in buffers:
+            width = len(ks) * piece_rows
+            part = jnp.dot(
+                rows[:, col : col + width],
+                buf.reshape(width, 2 * ff_cols),
+                preferred_element_type=jnp.float32,
+            )
+            act = part if act is None else act + part
+            col += width
+        hidden = (jax.nn.silu(act[:, :ff_cols]) * act[:, ff_cols:]).astype(jnp.bfloat16)
+        return jnp.dot(hidden, down_weight, preferred_element_type=jnp.float32).astype(jnp.bfloat16)
+
+    chunk = nl * shard_rows
+    lead = slice((nz // 2) * chunk, (nz // 2 + 2) * chunk)
+    term = jnp.concatenate(
+        [ffn(normed[: lead.start]), ffn(normed[lead]), ffn(normed[lead.stop :])], axis=0
+    )
     blocks = term.reshape(nz, nl, shard_rows, feature_count)
 
     fwd = blocks[nz // 2]

time: 236 us -> 236 us (level)
  matrix products: 8.53 us -> 11.9 us
    ppermute x1, waiting for transfers between devices: 4.15 us -> 0.01 us  [gather_pieces(): other_core = lax.ppermute(chip, 'dp', DP_C_SWAP)]
    dot_general x7 -> x21, matrix products: 8.04 us -> 11.4 us  [the longest x18 8.22 us: ffn(): jnp.dot(rows[:, col:col + width], buf.reshape(width, 2 * ff_cols), prefer...]
  transfers between devices with their start and end apart: 38 -> 38, of which waited for: 19 -> 17; matrix products, arithmetic and copies ran while one was open for 4% -> 5% of each run, Pallas kernels for 0% -> 0%
where the time goes in v8:
time: 236 us; the launch traced here: 232 us
  starting transfers between devices  138 us (58%)
  waiting for transfers between devices  69.1 us (29%)
  matrix products  11.9 us (5%)
  local copies, waits for them, and re-layouts  8.16 us (3%)
  other arithmetic  3.44 us (1%)
    ppermute x7, starting transfers between devices, per_device(): bwd = lax.ppermute(bwd, 'tensor', TP_Z_BWD)  40.6 us
    ppermute x7, starting transfers between devices, per_device(): got = lax.ppermute(bwd, 'tensor', TP_Z_BWD)  36.2 us
    ppermute x8, waiting for transfers between devices, per_device(): got = lax.ppermute(fwd, 'tensor', TP_Z_FWD)  28.7 us
    ppermute x8, waiting for transfers between devices, per_device(): fwd = lax.ppermute(fwd, 'tensor', TP_Z_FWD)  16.7 us
    ppermute x8, starting transfers between devices, per_device(): fwd = lax.ppermute(fwd, 'tensor', TP_Z_FWD)  15.5 us
    ppermute x8, starting transfers between devices, per_device(): got = lax.ppermute(fwd, 'tensor', TP_Z_FWD)  15.4 us
    dot_general x18, matrix products, ffn(): jnp.dot(rows[:, col:col + width], buf.reshape(width, 2 * ff_cols), prefer...  8.22 us
    ppermute x1, starting transfers between devices, gather_pieces(): fwd1 = lax.ppermute(own, 'dp', DP_Y_FWD)  7.5 us
  transfers between devices with their start and end apart: 38, of which 17 were waited for; matrix products, arithmetic and copies ran while one was open for 5% of the time, Pallas kernels for 0%

profile of v8, /device:TPU:24, one launch (start us, length us, event | category | flops | bytes accessed | tf_op | source)
XLA Modules:
  0.0 231.9 jit_solution(1259837152071790900)
XLA Ops:
  2.0 7.5 %collective-permute-start.9 = (bf16[1,256,1024]{2,1,0:T(8,128)(2,1)S(1)}, bf16[1,256,1024]{2,1,0:T(8,128)(2,1)S(1)}, u32[]{:S(2)}, u32[]{:S(2)}) collective-permute-start(bf16[1,256,1024]{2,1,0:T(8,128)(2,1)S(1)} %bitcast.149), channel_id=1, source_target_pairs={{0,128},{32,160},{64,192},{96,224},{128,256},{160,288},{192,320},{... | collective-permute-start | bytes 1572872 | tf_op jit(solution)/shard_map/ppermute | solution.py:51
  14.4 6.6 %all-to-all-start = ((bf16[16,2,4224]{2,1,0:T(2,128)(2,1)}), bf16[16,2,4224]{2,1,0:T(2,128)(2,1)S(1)}, u32[]{:S(2)}, u32[]{:S(2)}) async-start(bf16[16,2,4224]{2,1,0:T(2,128)(2,1)} %reshape.927), calls=%async_computation | async-start | bytes 540672 | tf_op jit(solution)/shard_map/all_to_all | solution.py:95
  22.2 6.2 %all-to-all-done = bf16[16,2,4224]{2,1,0:T(2,128)(2,1)S(1)} async-done(((bf16[16,2,4224]{2,1,0:T(2,128)(2,1)}), bf16[16,2,4224]{2,1,0:T(2,128)(2,1)S(1)}, u32[]{:S(2)}, u32[]{:S(2)}) %all-to-all-start) | async-done | bytes 270368 | tf_op jit(solution)/shard_map/all_to_all | solution.py:95
  31.7 5.1 %collective-permute-done = bf16[16,4096]{1,0:T(8,128)(2,1)S(1)} collective-permute-done((bf16[16,4096]{1,0:T(8,128)(2,1)S(1)}, bf16[16,4096]{1,0:T(8,128)(2,1)S(1)}, u32[]{:S(2)}, u32[]{:S(2)}) %collective-permute-start) | collective-permute-done | bytes 131104 | tf_op jit(solution)/shard_map/ppermute | solution.py:126
  36.8 8.4 %collective-permute-start.15 = (bf16[2,16,4096]{2,1,0:T(8,128)(2,1)S(1)}, bf16[2,16,4096]{2,1,0:T(8,128)(2,1)S(1)}, u32[]{:S(2)}, u32[]{:S(2)}) collective-permute-start(bf16[2,16,4096]{2,1,0:T(8,128)(2,1)S(1)} %pad_maximum_fusion.3), channel_id=1, source_target_pairs={{0,15},{1,0},{2,1},{3,2},{4,3},{5,4},{6,5},{7,6},{8,7},{9,8},{10,9... | collective-permute-start | bytes 786440 | tf_op jit(solution)/shard_map/ppermute | solution.py:134
  47.2 4.0 %collective-permute-start.10 = (bf16[1,256,1024]{2,1,0:T(8,128)(2,1)S(1)}, bf16[1,256,1024]{2,1,0:T(8,128)(2,1)S(1)}, u32[]{:S(2)}, u32[]{:S(2)}) collective-permute-start(bf16[1,256,1024]{2,1,0:T(8,128)(2,1)S(1)} %collective-permute-done.9), channel_id=1, source_target_pairs={{0,128},{32,160},{64,192},{96,224},{128,256},{160,288},{192,320},{... | collective-permute-start | bytes 1572872 | tf_op jit(solution)/shard_map/ppermute | solution.py:52
  52.1 5.1 %collective-permute-start.16 = (bf16[2,16,4096]{2,1,0:T(8,128)(2,1)S(1)}, bf16[2,16,4096]{2,1,0:T(8,128)(2,1)S(1)}, u32[]{:S(2)}, u32[]{:S(2)}) collective-permute-start(bf16[2,16,4096]{2,1,0:T(8,128)(2,1)S(1)} %collective-permute-done.15), channel_id=1, source_target_pairs={{0,15},{1,0},{2,1},{3,2},{4,3},{5,4},{6,5},{7,6},{8,7},{9,8},{10,9... | collective-permute-start | bytes 786440 | tf_op jit(solution)/shard_map/ppermute | solution.py:134
  61.1 5.6 %collective-permute-start.17 = (bf16[2,16,4096]{2,1,0:T(8,128)(2,1)S(1)}, bf16[2,16,4096]{2,1,0:T(8,128)(2,1)S(1)}, u32[]{:S(2)}, u32[]{:S(2)}) collective-permute-start(bf16[2,16,4096]{2,1,0:T(8,128)(2,1)S(1)} %collective-permute-done.16), channel_id=1, source_target_pairs={{0,15},{1,0},{2,1},{3,2},{4,3},{5,4},{6,5},{7,6},{8,7},{9,8},{10,9... | collective-permute-start | bytes 786440 | tf_op jit(solution)/shard_map/ppermute | solution.py:134
  72.7 5.1 %collective-permute-start.18 = (bf16[2,16,4096]{2,1,0:T(8,128)(2,1)S(1)}, bf16[2,16,4096]{2,1,0:T(8,128)(2,1)S(1)}, u32[]{:S(2)}, u32[]{:S(2)}) collective-permute-start(bf16[2,16,4096]{2,1,0:T(8,128)(2,1)S(1)} %collective-permute-done.17), channel_id=1, source_target_pairs={{0,15},{1,0},{2,1},{3,2},{4,3},{5,4},{6,5},{7,6},{8,7},{9,8},{10,9... | collective-permute-start | bytes 786440 | tf_op jit(solution)/shard_map/ppermute | solution.py:134
  81.8 5.6 %collective-permute-start.19 = (bf16[2,16,4096]{2,1,0:T(8,128)(2,1)S(1)}, bf16[2,16,4096]{2,1,0:T(8,128)(2,1)S(1)}, u32[]{:S(2)}, u32[]{:S(2)}) collective-permute-start(bf16[2,16,4096]{2,1,0:T(8,128)(2,1)S(1)} %collective-permute-done.18), channel_id=1, source_target_pairs={{0,15},{1,0},{2,1},{3,2},{4,3},{5,4},{6,5},{7,6},{8,7},{9,8},{10,9... | collective-permute-start | bytes 786440 | tf_op jit(solution)/shard_map/ppermute | solution.py:134
  91.2 5.6 %collective-permute-start.20 = (bf16[2,16,4096]{2,1,0:T(8,128)(2,1)S(1)}, bf16[2,16,4096]{2,1,0:T(8,128)(2,1)S(1)}, u32[]{:S(2)}, u32[]{:S(2)}) collective-permute-start(bf16[2,16,4096]{2,1,0:T(8,128)(2,1)S(1)} %collective-permute-done.19), channel_id=1, source_target_pairs={{0,15},{1,0},{2,1},{3,2},{4,3},{5,4},{6,5},{7,6},{8,7},{9,8},{10,9... | collective-permute-start | bytes 786440 | tf_op jit(solution)/shard_map/ppermute | solution.py:134
  98.8 7.9 %collective-permute-done.6 = bf16[2,16,4096]{2,1,0:T(8,128)(2,1)S(1)} collective-permute-done((bf16[2,16,4096]{2,1,0:T(8,128)(2,1)S(1)}, bf16[2,16,4096]{2,1,0:T(8,128)(2,1)S(1)}, u32[]{:S(2)}, u32[]{:S(2)}) %collective-permute-start.6) | collective-permute-done | bytes 262176 | tf_op jit(solution)/shard_map/ppermute | solution.py:130
  108.7 5.1 %collective-permute-start.21 = (bf16[2,16,4096]{2,1,0:T(8,128)(2,1)S(1)}, bf16[2,16,4096]{2,1,0:T(8,128)(2,1)S(1)}, u32[]{:S(2)}, u32[]{:S(2)}) collective-permute-start(bf16[2,16,4096]{2,1,0:T(8,128)(2,1)S(1)} %collective-permute-done.20), channel_id=1, source_target_pairs={{0,15},{1,0},{2,1},{3,2},{4,3},{5,4},{6,5},{7,6},{8,7},{9,8},{10,9... | collective-permute-start | bytes 786440 | tf_op jit(solution)/shard_map/ppermute | solution.py:134
  122.3 8.7 %collective-permute-done.8 = bf16[2,16,4096]{2,1,0:T(8,128)(2,1)S(1)} collective-permute-done((bf16[2,16,4096]{2,1,0:T(8,128)(2,1)S(1)}, bf16[2,16,4096]{2,1,0:T(8,128)(2,1)S(1)}, u32[]{:S(2)}, u32[]{:S(2)}) %collective-permute-start.8) | collective-permute-done | bytes 262176 | tf_op jit(solution)/shard_map/ppermute | solution.py:130
  144.8 5.1 %collective-permute-start.29 = (bf16[2,16,4096]{2,1,0:T(8,128)(2,1)S(1)}, bf16[2,16,4096]{2,1,0:T(8,128)(2,1)S(1)}, u32[]{:S(2)}, u32[]{:S(2)}) collective-permute-start(bf16[2,16,4096]{2,1,0:T(8,128)(2,1)S(1)} %bitcast.190), channel_id=1, source_target_pairs={{0,15},{1,0},{2,1},{3,2},{4,3},{5,4},{6,5},{7,6},{8,7},{9,8},{10,9... | collective-permute-start | bytes 786440 | tf_op jit(solution)/shard_map/ppermute | solution.py:171
  155.9 5.1 %collective-permute-start.30 = (bf16[2,16,4096]{2,1,0:T(8,128)(2,1)S(1)}, bf16[2,16,4096]{2,1,0:T(8,128)(2,1)S(1)}, u32[]{:S(2)}, u32[]{:S(2)}) collective-permute-start(bf16[2,16,4096]{2,1,0:T(8,128)(2,1)S(1)} %fusion.23), channel_id=1, source_target_pairs={{0,15},{1,0},{2,1},{3,2},{4,3},{5,4},{6,5},{7,6},{8,7},{9,8},{10,9... | collective-permute-start | bytes 786440 | tf_op jit(solution)/shard_map/ppermute | solution.py:171
  166.1 5.1 %collective-permute-start.31 = (bf16[2,16,4096]{2,1,0:T(8,128)(2,1)S(1)}, bf16[2,16,4096]{2,1,0:T(8,128)(2,1)S(1)}, u32[]{:S(2)}, u32[]{:S(2)}) collective-permute-start(bf16[2,16,4096]{2,1,0:T(8,128)(2,1)S(1)} %fusion.22), channel_id=1, source_target_pairs={{0,15},{1,0},{2,1},{3,2},{4,3},{5,4},{6,5},{7,6},{8,7},{9,8},{10,9... | collective-permute-start | bytes 786440 | tf_op jit(solution)/shard_map/ppermute | solution.py:171
  175.6 5.1 %collective-permute-start.32 = (bf16[2,16,4096]{2,1,0:T(8,128)(2,1)S(1)}, bf16[2,16,4096]{2,1,0:T(8,128)(2,1)S(1)}, u32[]{:S(2)}, u32[]{:S(2)}) collective-permute-start(bf16[2,16,4096]{2,1,0:T(8,128)(2,1)S(1)} %fusion.21), channel_id=1, source_target_pairs={{0,15},{1,0},{2,1},{3,2},{4,3},{5,4},{6,5},{7,6},{8,7},{9,8},{10,9... | collective-permute-start | bytes 786440 | tf_op jit(solution)/shard_map/ppermute | solution.py:171
  185.2 5.1 %collective-permute-start.33 = (bf16[2,16,4096]{2,1,0:T(8,128)(2,1)S(1)}, bf16[2,16,4096]{2,1,0:T(8,128)(2,1)S(1)}, u32[]{:S(2)}, u32[]{:S(2)}) collective-permute-start(bf16[2,16,4096]{2,1,0:T(8,128)(2,1)S(1)} %fusion.20), channel_id=1, source_target_pairs={{0,15},{1,0},{2,1},{3,2},{4,3},{5,4},{6,5},{7,6},{8,7},{9,8},{10,9... | collective-permute-start | bytes 786440 | tf_op jit(solution)/shard_map/ppermute | solution.py:171
  194.7 5.1 %collective-permute-start.34 = (bf16[2,16,4096]{2,1,0:T(8,128)(2,1)S(1)}, bf16[2,16,4096]{2,1,0:T(8,128)(2,1)S(1)}, u32[]{:S(2)}, u32[]{:S(2)}) collective-permute-start(bf16[2,16,4096]{2,1,0:T(8,128)(2,1)S(1)} %fusion.19), channel_id=1, source_target_pairs={{0,15},{1,0},{2,1},{3,2},{4,3},{5,4},{6,5},{7,6},{8,7},{9,8},{10,9... | collective-permute-start | bytes 786440 | tf_op jit(solution)/shard_map/ppermute | solution.py:171
  205.2 5.4 %collective-permute-start.35 = (bf16[2,16,4096]{2,1,0:T(8,128)(2,1)S(1)}, bf16[2,16,4096]{2,1,0:T(8,128)(2,1)S(1)}, u32[]{:S(2)}, u32[]{:S(2)}) collective-permute-start(bf16[2,16,4096]{2,1,0:T(8,128)(2,1)S(1)} %fusion.18), channel_id=1, source_target_pairs={{0,15},{1,0},{2,1},{3,2},{4,3},{5,4},{6,5},{7,6},{8,7},{9,8},{10,9... | collective-permute-start | bytes 786440 | tf_op jit(solution)/shard_map/ppermute | solution.py:171
  210.5 4.1 %collective-permute-done.27 = bf16[2,16,4096]{2,1,0:T(8,128)(2,1)S(1)} collective-permute-done((bf16[2,16,4096]{2,1,0:T(8,128)(2,1)S(1)}, bf16[2,16,4096]{2,1,0:T(8,128)(2,1)S(1)}, u32[]{:S(2)}, u32[]{:S(2)}) %collective-permute-start.27) | collective-permute-done | bytes 262176 | tf_op jit(solution)/shard_map/ppermute | solution.py:164
  216.7 7.5 %collective-permute-done.28 = bf16[2,16,4096]{2,1,0:T(8,128)(2,1)S(1)} collective-permute-done((bf16[2,16,4096]{2,1,0:T(8,128)(2,1)S(1)}, bf16[2,16,4096]{2,1,0:T(8,128)(2,1)S(1)}, u32[]{:S(2)}, u32[]{:S(2)}) %collective-permute-start.28) | collective-permute-done | bytes 262176 | tf_op jit(solution)/shard_map/ppermute | solution.py:164
  226.8 4.4 %collective-permute-done.36 = bf16[16,4096]{1,0:T(8,128)(2,1)S(1)} collective-permute-done((bf16[16,4096]{1,0:T(8,128)(2,1)S(1)}, bf16[16,4096]{1,0:T(8,128)(2,1)S(1)}, u32[]{:S(2)}, u32[]{:S(2)}) %collective-permute-start.36) | collective-permute-done | bytes 131104 | tf_op jit(solution)/shard_map/ppermute | solution.py:179
  (153 shorter events, 91.4 us)
Async XLA Ops:
  2.0 45.2 %collective-permute-start.9 = (bf16[1,256,1024]{2,1,0:T(8,128)(2,1)S(1)}, bf16[1,256,1024]{2,1,0:T(8,128)(2,1)S(1)}, u32[]{:S(2)}, u32[]{:S(2)}) collective-permute-start(bf16[1,256,1024]{2,1,0:T(8,128)(2,1)S(1)} %bitcast.149), channel_id=1, source_target_pairs={{0,128},{32,160},{64,192},{96,224},{128,256},{160,288},{192,320},{... | collective-permute-start | bytes 1572872 | tf_op jit(solution)/shard_map/ppermute | solution.py:51
  9.5 59.1 %collective-permute-start.11 = (bf16[1,256,1024]{2,1,0:T(8,128)(2,1)S(1)}, bf16[1,256,1024]{2,1,0:T(8,128)(2,1)S(1)}, u32[]{:S(2)}, u32[]{:S(2)}) collective-permute-start(bf16[1,256,1024]{2,1,0:T(8,128)(2,1)S(1)} %bitcast.150), channel_id=1, source_target_pairs={{0,384},{32,416},{64,448},{96,480},{128,0},{160,32},{192,64},{224,... | collective-permute-start | bytes 1572872 | tf_op jit(solution)/shard_map/ppermute | solution.py:53
  14.4 14.0 %all-to-all-start = ((bf16[16,2,4224]{2,1,0:T(2,128)(2,1)}), bf16[16,2,4224]{2,1,0:T(2,128)(2,1)S(1)}, u32[]{:S(2)}, u32[]{:S(2)}) async-start(bf16[16,2,4224]{2,1,0:T(2,128)(2,1)} %reshape.927), calls=%async_computation | async-start | bytes 540672 | tf_op jit(solution)/shard_map/all_to_all | solution.py:95
  36.8 15.3 %collective-permute-start.15 = (bf16[2,16,4096]{2,1,0:T(8,128)(2,1)S(1)}, bf16[2,16,4096]{2,1,0:T(8,128)(2,1)S(1)}, u32[]{:S(2)}, u32[]{:S(2)}) collective-permute-start(bf16[2,16,4096]{2,1,0:T(8,128)(2,1)S(1)} %pad_maximum_fusion.3), channel_id=1, source_target_pairs={{0,15},{1,0},{2,1},{3,2},{4,3},{5,4},{6,5},{7,6},{8,7},{9,8},{10,9... | collective-permute-start | bytes 786440 | tf_op jit(solution)/shard_map/ppermute | solution.py:134
  45.2 12.0 %collective-permute-start.1 = (bf16[2,16,4096]{2,1,0:T(8,128)(2,1)S(1)}, bf16[2,16,4096]{2,1,0:T(8,128)(2,1)S(1)}, u32[]{:S(2)}, u32[]{:S(2)}) collective-permute-start(bf16[2,16,4096]{2,1,0:T(8,128)(2,1)S(1)} %pad_maximum_fusion.3), channel_id=1, source_target_pairs={{0,1},{1,2},{2,3},{3,4},{4,5},{5,6},{6,7},{7,8},{8,9},{9,10},{10,1... | collective-permute-start | bytes 786440 | tf_op jit(solution)/shard_map/ppermute | solution.py:130
  47.2 21.5 %collective-permute-start.10 = (bf16[1,256,1024]{2,1,0:T(8,128)(2,1)S(1)}, bf16[1,256,1024]{2,1,0:T(8,128)(2,1)S(1)}, u32[]{:S(2)}, u32[]{:S(2)}) collective-permute-start(bf16[1,256,1024]{2,1,0:T(8,128)(2,1)S(1)} %collective-permute-done.9), channel_id=1, source_target_pairs={{0,128},{32,160},{64,192},{96,224},{128,256},{160,288},{192,320},{... | collective-permute-start | bytes 1572872 | tf_op jit(solution)/shard_map/ppermute | solution.py:52
  57.2 9.5 %collective-permute-start.2 = (bf16[2,16,4096]{2,1,0:T(8,128)(2,1)S(1)}, bf16[2,16,4096]{2,1,0:T(8,128)(2,1)S(1)}, u32[]{:S(2)}, u32[]{:S(2)}) collective-permute-start(bf16[2,16,4096]{2,1,0:T(8,128)(2,1)S(1)} %collective-permute-done.1), channel_id=1, source_target_pairs={{0,1},{1,2},{2,3},{3,4},{4,5},{5,6},{6,7},{7,8},{8,9},{9,10},{10,1... | collective-permute-start | bytes 786440 | tf_op jit(solution)/shard_map/ppermute | solution.py:130
  61.1 11.6 %collective-permute-start.17 = (bf16[2,16,4096]{2,1,0:T(8,128)(2,1)S(1)}, bf16[2,16,4096]{2,1,0:T(8,128)(2,1)S(1)}, u32[]{:S(2)}, u32[]{:S(2)}) collective-permute-start(bf16[2,16,4096]{2,1,0:T(8,128)(2,1)S(1)} %collective-permute-done.16), channel_id=1, source_target_pairs={{0,15},{1,0},{2,1},{3,2},{4,3},{5,4},{6,5},{7,6},{8,7},{9,8},{10,9... | collective-permute-start | bytes 786440 | tf_op jit(solution)/shard_map/ppermute | solution.py:134
  66.7 11.2 %collective-permute-start.3 = (bf16[2,16,4096]{2,1,0:T(8,128)(2,1)S(1)}, bf16[2,16,4096]{2,1,0:T(8,128)(2,1)S(1)}, u32[]{:S(2)}, u32[]{:S(2)}) collective-permute-start(bf16[2,16,4096]{2,1,0:T(8,128)(2,1)S(1)} %collective-permute-done.2), channel_id=1, source_target_pairs={{0,1},{1,2},{2,3},{3,4},{4,5},{5,6},{6,7},{7,8},{8,9},{9,10},{10,1... | collective-permute-start | bytes 786440 | tf_op jit(solution)/shard_map/ppermute | solution.py:130
  69.0 47.3 %collective-permute-start.12 = (bf16[4,256,1024]{2,1,0:T(8,128)(2,1)S(1)}, bf16[4,256,1024]{2,1,0:T(8,128)(2,1)S(1)}, u32[]{:S(2)}, u32[]{:S(2)}) collective-permute-start(bf16[4,256,1024]{2,1,0:T(8,128)(2,1)S(1)} %pad_maximum_fusion), channel_id=1, source_target_pairs={{0,64},{32,96},{64,0},{96,32},{128,192},{160,224},{192,128},{224,1... | collective-permute-start | bytes 6291464 | tf_op jit(solution)/shard_map/ppermute | solution.py:55
  91.2 17.4 %collective-permute-start.20 = (bf16[2,16,4096]{2,1,0:T(8,128)(2,1)S(1)}, bf16[2,16,4096]{2,1,0:T(8,128)(2,1)S(1)}, u32[]{:S(2)}, u32[]{:S(2)}) collective-permute-start(bf16[2,16,4096]{2,1,0:T(8,128)(2,1)S(1)} %collective-permute-done.19), channel_id=1, source_target_pairs={{0,15},{1,0},{2,1},{3,2},{4,3},{5,4},{6,5},{7,6},{8,7},{9,8},{10,9... | collective-permute-start | bytes 786440 | tf_op jit(solution)/shard_map/ppermute | solution.py:134
  96.8 9.9 %collective-permute-start.6 = (bf16[2,16,4096]{2,1,0:T(8,128)(2,1)S(1)}, bf16[2,16,4096]{2,1,0:T(8,128)(2,1)S(1)}, u32[]{:S(2)}, u32[]{:S(2)}) collective-permute-start(bf16[2,16,4096]{2,1,0:T(8,128)(2,1)S(1)} %collective-permute-done.5), channel_id=1, source_target_pairs={{0,1},{1,2},{2,3},{3,4},{4,5},{5,6},{6,7},{7,8},{8,9},{9,10},{10,1... | collective-permute-start | bytes 786440 | tf_op jit(solution)/shard_map/ppermute | solution.py:130
  106.7 12.5 %collective-permute-start.7 = (bf16[2,16,4096]{2,1,0:T(8,128)(2,1)S(1)}, bf16[2,16,4096]{2,1,0:T(8,128)(2,1)S(1)}, u32[]{:S(2)}, u32[]{:S(2)}) collective-permute-start(bf16[2,16,4096]{2,1,0:T(8,128)(2,1)S(1)} %collective-permute-done.6), channel_id=1, source_target_pairs={{0,1},{1,2},{2,3},{3,4},{4,5},{5,6},{6,7},{7,8},{8,9},{9,10},{10,1... | collective-permute-start | bytes 786440 | tf_op jit(solution)/shard_map/ppermute | solution.py:130
  108.7 12.7 %collective-permute-start.21 = (bf16[2,16,4096]{2,1,0:T(8,128)(2,1)S(1)}, bf16[2,16,4096]{2,1,0:T(8,128)(2,1)S(1)}, u32[]{:S(2)}, u32[]{:S(2)}) collective-permute-start(bf16[2,16,4096]{2,1,0:T(8,128)(2,1)S(1)} %collective-permute-done.20), channel_id=1, source_target_pairs={{0,15},{1,0},{2,1},{3,2},{4,3},{5,4},{6,5},{7,6},{8,7},{9,8},{10,9... | collective-permute-start | bytes 786440 | tf_op jit(solution)/shard_map/ppermute | solution.py:134
  116.4 17.1 %collective-permute-start.13 = (bf16[8,256,1024]{2,1,0:T(8,128)(2,1)S(1)}, bf16[8,256,1024]{2,1,0:T(8,128)(2,1)S(1)}, u32[]{:S(2)}, u32[]{:S(2)}) collective-permute-start(bf16[8,256,1024]{2,1,0:T(8,128)(2,1)S(1)} %constant_dynamic-update-slice_fusion.2), channel_id=1, source_target_pairs={{0,32},{32,0},{64,96},{96,64},{128,160},{160,128},{192,224},{224,1... | collective-permute-start | bytes 12582920 | tf_op jit(solution)/shard_map/ppermute | solution.py:58
  119.2 11.8 %collective-permute-start.8 = (bf16[2,16,4096]{2,1,0:T(8,128)(2,1)S(1)}, bf16[2,16,4096]{2,1,0:T(8,128)(2,1)S(1)}, u32[]{:S(2)}, u32[]{:S(2)}) collective-permute-start(bf16[2,16,4096]{2,1,0:T(8,128)(2,1)S(1)} %collective-permute-done.7), channel_id=1, source_target_pairs={{0,1},{1,2},{2,3},{3,4},{4,5},{5,6},{6,7},{7,8},{8,9},{9,10},{10,1... | collective-permute-start | bytes 786440 | tf_op jit(solution)/shard_map/ppermute | solution.py:130
  142.8 11.0 %collective-permute-start.14 = (bf16[2,16,4096]{2,1,0:T(8,128)(2,1)S(1)}, bf16[2,16,4096]{2,1,0:T(8,128)(2,1)S(1)}, u32[]{:S(2)}, u32[]{:S(2)}) collective-permute-start(bf16[2,16,4096]{2,1,0:T(8,128)(2,1)S(1)} %bitcast.191), channel_id=1, source_target_pairs={{0,1},{1,2},{2,3},{3,4},{4,5},{5,6},{6,7},{7,8},{8,9},{9,10},{10,1... | collective-permute-start | bytes 786440 | tf_op jit(solution)/shard_map/ppermute | solution.py:164
  144.8 11.0 %collective-permute-start.29 = (bf16[2,16,4096]{2,1,0:T(8,128)(2,1)S(1)}, bf16[2,16,4096]{2,1,0:T(8,128)(2,1)S(1)}, u32[]{:S(2)}, u32[]{:S(2)}) collective-permute-start(bf16[2,16,4096]{2,1,0:T(8,128)(2,1)S(1)} %bitcast.190), channel_id=1, source_target_pairs={{0,15},{1,0},{2,1},{3,2},{4,3},{5,4},{6,5},{7,6},{8,7},{9,8},{10,9... | collective-permute-start | bytes 786440 | tf_op jit(solution)/shard_map/ppermute | solution.py:171
  153.9 10.1 %collective-permute-start.22 = (bf16[2,16,4096]{2,1,0:T(8,128)(2,1)S(1)}, bf16[2,16,4096]{2,1,0:T(8,128)(2,1)S(1)}, u32[]{:S(2)}, u32[]{:S(2)}) collective-permute-start(bf16[2,16,4096]{2,1,0:T(8,128)(2,1)S(1)} %fusion.30), channel_id=1, source_target_pairs={{0,1},{1,2},{2,3},{3,4},{4,5},{5,6},{6,7},{7,8},{8,9},{9,10},{10,1... | collective-permute-start | bytes 786440 | tf_op jit(solution)/shard_map/ppermute | solution.py:164
  155.9 10.1 %collective-permute-start.30 = (bf16[2,16,4096]{2,1,0:T(8,128)(2,1)S(1)}, bf16[2,16,4096]{2,1,0:T(8,128)(2,1)S(1)}, u32[]{:S(2)}, u32[]{:S(2)}) collective-permute-start(bf16[2,16,4096]{2,1,0:T(8,128)(2,1)S(1)} %fusion.23), channel_id=1, source_target_pairs={{0,15},{1,0},{2,1},{3,2},{4,3},{5,4},{6,5},{7,6},{8,7},{9,8},{10,9... | collective-permute-start | bytes 786440 | tf_op jit(solution)/shard_map/ppermute | solution.py:171
  192.7 10.3 %collective-permute-start.26 = (bf16[2,16,4096]{2,1,0:T(8,128)(2,1)S(1)}, bf16[2,16,4096]{2,1,0:T(8,128)(2,1)S(1)}, u32[]{:S(2)}, u32[]{:S(2)}) collective-permute-start(bf16[2,16,4096]{2,1,0:T(8,128)(2,1)S(1)} %fusion.26), channel_id=1, source_target_pairs={{0,1},{1,2},{2,3},{3,4},{4,5},{5,6},{6,7},{7,8},{8,9},{9,10},{10,1... | collective-permute-start | bytes 786440 | tf_op jit(solution)/shard_map/ppermute | solution.py:164
  194.7 10.3 %collective-permute-start.34 = (bf16[2,16,4096]{2,1,0:T(8,128)(2,1)S(1)}, bf16[2,16,4096]{2,1,0:T(8,128)(2,1)S(1)}, u32[]{:S(2)}, u32[]{:S(2)}) collective-permute-start(bf16[2,16,4096]{2,1,0:T(8,128)(2,1)S(1)} %fusion.19), channel_id=1, source_target_pairs={{0,15},{1,0},{2,1},{3,2},{4,3},{5,4},{6,5},{7,6},{8,7},{9,8},{10,9... | collective-permute-start | bytes 786440 | tf_op jit(solution)/shard_map/ppermute | solution.py:171
  203.1 11.5 %collective-permute-start.27 = (bf16[2,16,4096]{2,1,0:T(8,128)(2,1)S(1)}, bf16[2,16,4096]{2,1,0:T(8,128)(2,1)S(1)}, u32[]{:S(2)}, u32[]{:S(2)}) collective-permute-start(bf16[2,16,4096]{2,1,0:T(8,128)(2,1)S(1)} %fusion.25), channel_id=1, source_target_pairs={{0,1},{1,2},{2,3},{3,4},{4,5},{5,6},{6,7},{7,8},{8,9},{9,10},{10,1... | collective-permute-start | bytes 786440 | tf_op jit(solution)/shard_map/ppermute | solution.py:164
  205.2 11.5 %collective-permute-start.35 = (bf16[2,16,4096]{2,1,0:T(8,128)(2,1)S(1)}, bf16[2,16,4096]{2,1,0:T(8,128)(2,1)S(1)}, u32[]{:S(2)}, u32[]{:S(2)}) collective-permute-start(bf16[2,16,4096]{2,1,0:T(8,128)(2,1)S(1)} %fusion.18), channel_id=1, source_target_pairs={{0,15},{1,0},{2,1},{3,2},{4,3},{5,4},{6,5},{7,6},{8,7},{9,8},{10,9... | collective-permute-start | bytes 786440 | tf_op jit(solution)/shard_map/ppermute | solution.py:171
  (17 other events, 146.1 us)

commit v9 on v8

--- a/solution.py
+++ b/solution.py
@@ -153,11 +153,12 @@
         return jnp.dot(hidden, down_weight, preferred_element_type=jnp.float32).astype(jnp.bfloat16)
 
     chunk = nl * shard_rows
-    lead = slice((nz // 2) * chunk, (nz // 2 + 2) * chunk)
-    term = jnp.concatenate(
-        [ffn(normed[: lead.start]), ffn(normed[lead]), ffn(normed[lead.stop :])], axis=0
-    )
-    blocks = term.reshape(nz, nl, shard_rows, feature_count)
+    blocks = {}
+    for group in ([8, 9], [5, 6, 7, 10, 11, 12], [0, 1, 2, 3, 4, 13, 14, 15]):
+        rows = jnp.concatenate([normed[k * chunk : (k + 1) * chunk] for k in group], axis=0)
+        out = ffn(rows).reshape(len(group), nl, shard_rows, feature_count)
+        for i, k in enumerate(group):
+            blocks[k] = out[i]
 
     fwd = blocks[nz // 2]
     for s in range(nz // 2):

time: 236 us -> 232 us (0.983)
  waiting for transfers between devices: 69.1 us -> 63.1 us
    ppermute x8, waiting for transfers between devices: 16.7 us -> 13.4 us  [per_device(): fwd = lax.ppermute(fwd, 'tensor', TP_Z_FWD)]
  transfers between devices with their start and end apart: 38 -> 38, of which waited for: 17 -> 18; matrix products, arithmetic and copies ran while one was open for 5% -> 5% of each run, Pallas kernels for 0% -> 0%
where the time goes in v9:
time: 232 us; the launch traced here: 228 us
  starting transfers between devices  139 us (60%)
  waiting for transfers between devices  63.1 us (27%)
  matrix products  11.9 us (5%)
  local copies, waits for them, and re-layouts  8.21 us (4%)
  other arithmetic  3.33 us (1%)
    ppermute x7, starting transfers between devices, per_device(): bwd = lax.ppermute(bwd, 'tensor', TP_Z_BWD)  41 us
    ppermute x7, starting transfers between devices, per_device(): got = lax.ppermute(bwd, 'tensor', TP_Z_BWD)  36.2 us
    ppermute x8, waiting for transfers between devices, per_device(): got = lax.ppermute(fwd, 'tensor', TP_Z_FWD)  28.6 us
    ppermute x8, starting transfers between devices, per_device(): got = lax.ppermute(fwd, 'tensor', TP_Z_FWD)  15.4 us
    ppermute x8, starting transfers between devices, per_device(): fwd = lax.ppermute(fwd, 'tensor', TP_Z_FWD)  15.3 us
    ppermute x8, waiting for transfers between devices, per_device(): fwd = lax.ppermute(fwd, 'tensor', TP_Z_FWD)  13.4 us
    dot_general x18, matrix products, ffn(): jnp.dot(rows[:, col:col + width], buf.reshape(width, 2 * ff_cols), prefer...  8.24 us
    ppermute x1, starting transfers between devices, gather_pieces(): fwd1 = lax.ppermute(own, 'dp', DP_Y_FWD)  7.5 us
  transfers between devices with their start and end apart: 38, of which 18 were waited for; matrix products, arithmetic and copies ran while one was open for 5% of the time, Pallas kernels for 0%

profile of v9, /device:TPU:24, one launch (start us, length us, event | category | flops | bytes accessed | tf_op | source)
XLA Modules:
  0.0 227.6 jit_solution(2504616425942622230)
XLA Ops:
  2.0 7.5 %collective-permute-start.9 = (bf16[1,256,1024]{2,1,0:T(8,128)(2,1)S(1)}, bf16[1,256,1024]{2,1,0:T(8,128)(2,1)S(1)}, u32[]{:S(2)}, u32[]{:S(2)}) collective-permute-start(bf16[1,256,1024]{2,1,0:T(8,128)(2,1)S(1)} %bitcast.161), channel_id=1, source_target_pairs={{0,128},{32,160},{64,192},{96,224},{128,256},{160,288},{192,320},{... | collective-permute-start | bytes 1572872 | tf_op jit(solution)/shard_map/ppermute | solution.py:51
  14.4 6.6 %all-to-all-start = ((bf16[16,2,4224]{2,1,0:T(2,128)(2,1)}), bf16[16,2,4224]{2,1,0:T(2,128)(2,1)S(1)}, u32[]{:S(2)}, u32[]{:S(2)}) async-start(bf16[16,2,4224]{2,1,0:T(2,128)(2,1)} %reshape.942), calls=%async_computation | async-start | bytes 540672 | tf_op jit(solution)/shard_map/all_to_all | solution.py:95
  22.2 6.2 %all-to-all-done = bf16[16,2,4224]{2,1,0:T(2,128)(2,1)S(1)} async-done(((bf16[16,2,4224]{2,1,0:T(2,128)(2,1)}), bf16[16,2,4224]{2,1,0:T(2,128)(2,1)S(1)}, u32[]{:S(2)}, u32[]{:S(2)}) %all-to-all-start) | async-done | bytes 270368 | tf_op jit(solution)/shard_map/all_to_all | solution.py:95
  31.7 5.0 %collective-permute-done = bf16[16,4096]{1,0:T(8,128)(2,1)S(1)} collective-permute-done((bf16[16,4096]{1,0:T(8,128)(2,1)S(1)}, bf16[16,4096]{1,0:T(8,128)(2,1)S(1)}, u32[]{:S(2)}, u32[]{:S(2)}) %collective-permute-start) | collective-permute-done | bytes 131104 | tf_op jit(solution)/shard_map/ppermute | solution.py:126
  36.7 8.4 %collective-permute-start.15 = (bf16[2,16,4096]{2,1,0:T(8,128)(2,1)S(1)}, bf16[2,16,4096]{2,1,0:T(8,128)(2,1)S(1)}, u32[]{:S(2)}, u32[]{:S(2)}) collective-permute-start(bf16[2,16,4096]{2,1,0:T(8,128)(2,1)S(1)} %pad_maximum_fusion.4), channel_id=1, source_target_pairs={{0,15},{1,0},{2,1},{3,2},{4,3},{5,4},{6,5},{7,6},{8,7},{9,8},{10,9... | collective-permute-start | bytes 786440 | tf_op jit(solution)/shard_map/ppermute | solution.py:134
  47.1 4.0 %collective-permute-start.10 = (bf16[1,256,1024]{2,1,0:T(8,128)(2,1)S(1)}, bf16[1,256,1024]{2,1,0:T(8,128)(2,1)S(1)}, u32[]{:S(2)}, u32[]{:S(2)}) collective-permute-start(bf16[1,256,1024]{2,1,0:T(8,128)(2,1)S(1)} %collective-permute-done.9), channel_id=1, source_target_pairs={{0,128},{32,160},{64,192},{96,224},{128,256},{160,288},{192,320},{... | collective-permute-start | bytes 1572872 | tf_op jit(solution)/shard_map/ppermute | solution.py:52
  52.0 5.1 %collective-permute-start.16 = (bf16[2,16,4096]{2,1,0:T(8,128)(2,1)S(1)}, bf16[2,16,4096]{2,1,0:T(8,128)(2,1)S(1)}, u32[]{:S(2)}, u32[]{:S(2)}) collective-permute-start(bf16[2,16,4096]{2,1,0:T(8,128)(2,1)S(1)} %collective-permute-done.15), channel_id=1, source_target_pairs={{0,15},{1,0},{2,1},{3,2},{4,3},{5,4},{6,5},{7,6},{8,7},{9,8},{10,9... | collective-permute-start | bytes 786440 | tf_op jit(solution)/shard_map/ppermute | solution.py:134
  61.0 5.6 %collective-permute-start.17 = (bf16[2,16,4096]{2,1,0:T(8,128)(2,1)S(1)}, bf16[2,16,4096]{2,1,0:T(8,128)(2,1)S(1)}, u32[]{:S(2)}, u32[]{:S(2)}) collective-permute-start(bf16[2,16,4096]{2,1,0:T(8,128)(2,1)S(1)} %collective-permute-done.16), channel_id=1, source_target_pairs={{0,15},{1,0},{2,1},{3,2},{4,3},{5,4},{6,5},{7,6},{8,7},{9,8},{10,9... | collective-permute-start | bytes 786440 | tf_op jit(solution)/shard_map/ppermute | solution.py:134
  72.6 5.1 %collective-permute-start.18 = (bf16[2,16,4096]{2,1,0:T(8,128)(2,1)S(1)}, bf16[2,16,4096]{2,1,0:T(8,128)(2,1)S(1)}, u32[]{:S(2)}, u32[]{:S(2)}) collective-permute-start(bf16[2,16,4096]{2,1,0:T(8,128)(2,1)S(1)} %collective-permute-done.17), channel_id=1, source_target_pairs={{0,15},{1,0},{2,1},{3,2},{4,3},{5,4},{6,5},{7,6},{8,7},{9,8},{10,9... | collective-permute-start | bytes 786440 | tf_op jit(solution)/shard_map/ppermute | solution.py:134
  81.7 5.6 %collective-permute-start.19 = (bf16[2,16,4096]{2,1,0:T(8,128)(2,1)S(1)}, bf16[2,16,4096]{2,1,0:T(8,128)(2,1)S(1)}, u32[]{:S(2)}, u32[]{:S(2)}) collective-permute-start(bf16[2,16,4096]{2,1,0:T(8,128)(2,1)S(1)} %collective-permute-done.18), channel_id=1, source_target_pairs={{0,15},{1,0},{2,1},{3,2},{4,3},{5,4},{6,5},{7,6},{8,7},{9,8},{10,9... | collective-permute-start | bytes 786440 | tf_op jit(solution)/shard_map/ppermute | solution.py:134
  91.2 5.6 %collective-permute-start.20 = (bf16[2,16,4096]{2,1,0:T(8,128)(2,1)S(1)}, bf16[2,16,4096]{2,1,0:T(8,128)(2,1)S(1)}, u32[]{:S(2)}, u32[]{:S(2)}) collective-permute-start(bf16[2,16,4096]{2,1,0:T(8,128)(2,1)S(1)} %collective-permute-done.19), channel_id=1, source_target_pairs={{0,15},{1,0},{2,1},{3,2},{4,3},{5,4},{6,5},{7,6},{8,7},{9,8},{10,9... | collective-permute-start | bytes 786440 | tf_op jit(solution)/shard_map/ppermute | solution.py:134
  100.8 5.6 %collective-permute-start.21 = (bf16[2,16,4096]{2,1,0:T(8,128)(2,1)S(1)}, bf16[2,16,4096]{2,1,0:T(8,128)(2,1)S(1)}, u32[]{:S(2)}, u32[]{:S(2)}) collective-permute-start(bf16[2,16,4096]{2,1,0:T(8,128)(2,1)S(1)} %collective-permute-done.20), channel_id=1, source_target_pairs={{0,15},{1,0},{2,1},{3,2},{4,3},{5,4},{6,5},{7,6},{8,7},{9,8},{10,9... | collective-permute-start | bytes 786440 | tf_op jit(solution)/shard_map/ppermute | solution.py:134
  108.6 8.7 %collective-permute-done.7 = bf16[2,16,4096]{2,1,0:T(8,128)(2,1)S(1)} collective-permute-done((bf16[2,16,4096]{2,1,0:T(8,128)(2,1)S(1)}, bf16[2,16,4096]{2,1,0:T(8,128)(2,1)S(1)}, u32[]{:S(2)}, u32[]{:S(2)}) %collective-permute-start.7) | collective-permute-done | bytes 262176 | tf_op jit(solution)/shard_map/ppermute | solution.py:130
  122.5 4.3 %collective-permute-done.8 = bf16[2,16,4096]{2,1,0:T(8,128)(2,1)S(1)} collective-permute-done((bf16[2,16,4096]{2,1,0:T(8,128)(2,1)S(1)}, bf16[2,16,4096]{2,1,0:T(8,128)(2,1)S(1)}, u32[]{:S(2)}, u32[]{:S(2)}) %collective-permute-start.8) | collective-permute-done | bytes 262176 | tf_op jit(solution)/shard_map/ppermute | solution.py:130
  140.6 5.1 %collective-permute-start.29 = (bf16[2,16,4096]{2,1,0:T(8,128)(2,1)S(1)}, bf16[2,16,4096]{2,1,0:T(8,128)(2,1)S(1)}, u32[]{:S(2)}, u32[]{:S(2)}) collective-permute-start(bf16[2,16,4096]{2,1,0:T(8,128)(2,1)S(1)} %bitcast.209), channel_id=1, source_target_pairs={{0,15},{1,0},{2,1},{3,2},{4,3},{5,4},{6,5},{7,6},{8,7},{9,8},{10,9... | collective-permute-start | bytes 786440 | tf_op jit(solution)/shard_map/ppermute | solution.py:172
  145.7 3.8 %collective-permute-done.14 = bf16[2,16,4096]{2,1,0:T(8,128)(2,1)S(1)} collective-permute-done((bf16[2,16,4096]{2,1,0:T(8,128)(2,1)S(1)}, bf16[2,16,4096]{2,1,0:T(8,128)(2,1)S(1)}, u32[]{:S(2)}, u32[]{:S(2)}) %collective-permute-start.14) | collective-permute-done | bytes 262176 | tf_op jit(solution)/shard_map/ppermute | solution.py:165
  151.6 5.1 %collective-permute-start.30 = (bf16[2,16,4096]{2,1,0:T(8,128)(2,1)S(1)}, bf16[2,16,4096]{2,1,0:T(8,128)(2,1)S(1)}, u32[]{:S(2)}, u32[]{:S(2)}) collective-permute-start(bf16[2,16,4096]{2,1,0:T(8,128)(2,1)S(1)} %fusion.24), channel_id=1, source_target_pairs={{0,15},{1,0},{2,1},{3,2},{4,3},{5,4},{6,5},{7,6},{8,7},{9,8},{10,9... | collective-permute-start | bytes 786440 | tf_op jit(solution)/shard_map/ppermute | solution.py:172
  161.7 5.1 %collective-permute-start.31 = (bf16[2,16,4096]{2,1,0:T(8,128)(2,1)S(1)}, bf16[2,16,4096]{2,1,0:T(8,128)(2,1)S(1)}, u32[]{:S(2)}, u32[]{:S(2)}) collective-permute-start(bf16[2,16,4096]{2,1,0:T(8,128)(2,1)S(1)} %fusion.23), channel_id=1, source_target_pairs={{0,15},{1,0},{2,1},{3,2},{4,3},{5,4},{6,5},{7,6},{8,7},{9,8},{10,9... | collective-permute-start | bytes 786440 | tf_op jit(solution)/shard_map/ppermute | solution.py:172
  171.3 5.1 %collective-permute-start.32 = (bf16[2,16,4096]{2,1,0:T(8,128)(2,1)S(1)}, bf16[2,16,4096]{2,1,0:T(8,128)(2,1)S(1)}, u32[]{:S(2)}, u32[]{:S(2)}) collective-permute-start(bf16[2,16,4096]{2,1,0:T(8,128)(2,1)S(1)} %fusion.22), channel_id=1, source_target_pairs={{0,15},{1,0},{2,1},{3,2},{4,3},{5,4},{6,5},{7,6},{8,7},{9,8},{10,9... | collective-permute-start | bytes 786440 | tf_op jit(solution)/shard_map/ppermute | solution.py:172
  180.8 5.1 %collective-permute-start.33 = (bf16[2,16,4096]{2,1,0:T(8,128)(2,1)S(1)}, bf16[2,16,4096]{2,1,0:T(8,128)(2,1)S(1)}, u32[]{:S(2)}, u32[]{:S(2)}) collective-permute-start(bf16[2,16,4096]{2,1,0:T(8,128)(2,1)S(1)} %fusion.21), channel_id=1, source_target_pairs={{0,15},{1,0},{2,1},{3,2},{4,3},{5,4},{6,5},{7,6},{8,7},{9,8},{10,9... | collective-permute-start | bytes 786440 | tf_op jit(solution)/shard_map/ppermute | solution.py:172
  190.4 5.2 %collective-permute-start.34 = (bf16[2,16,4096]{2,1,0:T(8,128)(2,1)S(1)}, bf16[2,16,4096]{2,1,0:T(8,128)(2,1)S(1)}, u32[]{:S(2)}, u32[]{:S(2)}) collective-permute-start(bf16[2,16,4096]{2,1,0:T(8,128)(2,1)S(1)} %fusion.20), channel_id=1, source_target_pairs={{0,15},{1,0},{2,1},{3,2},{4,3},{5,4},{6,5},{7,6},{8,7},{9,8},{10,9... | collective-permute-start | bytes 786440 | tf_op jit(solution)/shard_map/ppermute | solution.py:172
  200.8 5.4 %collective-permute-start.35 = (bf16[2,16,4096]{2,1,0:T(8,128)(2,1)S(1)}, bf16[2,16,4096]{2,1,0:T(8,128)(2,1)S(1)}, u32[]{:S(2)}, u32[]{:S(2)}) collective-permute-start(bf16[2,16,4096]{2,1,0:T(8,128)(2,1)S(1)} %fusion.19), channel_id=1, source_target_pairs={{0,15},{1,0},{2,1},{3,2},{4,3},{5,4},{6,5},{7,6},{8,7},{9,8},{10,9... | collective-permute-start | bytes 786440 | tf_op jit(solution)/shard_map/ppermute | solution.py:172
  206.2 4.2 %collective-permute-done.27 = bf16[2,16,4096]{2,1,0:T(8,128)(2,1)S(1)} collective-permute-done((bf16[2,16,4096]{2,1,0:T(8,128)(2,1)S(1)}, bf16[2,16,4096]{2,1,0:T(8,128)(2,1)S(1)}, u32[]{:S(2)}, u32[]{:S(2)}) %collective-permute-start.27) | collective-permute-done | bytes 262176 | tf_op jit(solution)/shard_map/ppermute | solution.py:165
  212.4 7.5 %collective-permute-done.28 = bf16[2,16,4096]{2,1,0:T(8,128)(2,1)S(1)} collective-permute-done((bf16[2,16,4096]{2,1,0:T(8,128)(2,1)S(1)}, bf16[2,16,4096]{2,1,0:T(8,128)(2,1)S(1)}, u32[]{:S(2)}, u32[]{:S(2)}) %collective-permute-start.28) | collective-permute-done | bytes 262176 | tf_op jit(solution)/shard_map/ppermute | solution.py:165
  (152 shorter events, 90.9 us)
Async XLA Ops:
  2.0 45.1 %collective-permute-start.9 = (bf16[1,256,1024]{2,1,0:T(8,128)(2,1)S(1)}, bf16[1,256,1024]{2,1,0:T(8,128)(2,1)S(1)}, u32[]{:S(2)}, u32[]{:S(2)}) collective-permute-start(bf16[1,256,1024]{2,1,0:T(8,128)(2,1)S(1)} %bitcast.161), channel_id=1, source_target_pairs={{0,128},{32,160},{64,192},{96,224},{128,256},{160,288},{192,320},{... | collective-permute-start | bytes 1572872 | tf_op jit(solution)/shard_map/ppermute | solution.py:51
  9.5 59.0 %collective-permute-start.11 = (bf16[1,256,1024]{2,1,0:T(8,128)(2,1)S(1)}, bf16[1,256,1024]{2,1,0:T(8,128)(2,1)S(1)}, u32[]{:S(2)}, u32[]{:S(2)}) collective-permute-start(bf16[1,256,1024]{2,1,0:T(8,128)(2,1)S(1)} %bitcast.162), channel_id=1, source_target_pairs={{0,384},{32,416},{64,448},{96,480},{128,0},{160,32},{192,64},{224,... | collective-permute-start | bytes 1572872 | tf_op jit(solution)/shard_map/ppermute | solution.py:53
  14.4 14.0 %all-to-all-start = ((bf16[16,2,4224]{2,1,0:T(2,128)(2,1)}), bf16[16,2,4224]{2,1,0:T(2,128)(2,1)S(1)}, u32[]{:S(2)}, u32[]{:S(2)}) async-start(bf16[16,2,4224]{2,1,0:T(2,128)(2,1)} %reshape.942), calls=%async_computation | async-start | bytes 540672 | tf_op jit(solution)/shard_map/all_to_all | solution.py:95
  36.7 15.3 %collective-permute-start.15 = (bf16[2,16,4096]{2,1,0:T(8,128)(2,1)S(1)}, bf16[2,16,4096]{2,1,0:T(8,128)(2,1)S(1)}, u32[]{:S(2)}, u32[]{:S(2)}) collective-permute-start(bf16[2,16,4096]{2,1,0:T(8,128)(2,1)S(1)} %pad_maximum_fusion.4), channel_id=1, source_target_pairs={{0,15},{1,0},{2,1},{3,2},{4,3},{5,4},{6,5},{7,6},{8,7},{9,8},{10,9... | collective-permute-start | bytes 786440 | tf_op jit(solution)/shard_map/ppermute | solution.py:134
  45.1 12.0 %collective-permute-start.1 = (bf16[2,16,4096]{2,1,0:T(8,128)(2,1)S(1)}, bf16[2,16,4096]{2,1,0:T(8,128)(2,1)S(1)}, u32[]{:S(2)}, u32[]{:S(2)}) collective-permute-start(bf16[2,16,4096]{2,1,0:T(8,128)(2,1)S(1)} %pad_maximum_fusion.4), channel_id=1, source_target_pairs={{0,1},{1,2},{2,3},{3,4},{4,5},{5,6},{6,7},{7,8},{8,9},{9,10},{10,1... | collective-permute-start | bytes 786440 | tf_op jit(solution)/shard_map/ppermute | solution.py:130
  47.1 21.5 %collective-permute-start.10 = (bf16[1,256,1024]{2,1,0:T(8,128)(2,1)S(1)}, bf16[1,256,1024]{2,1,0:T(8,128)(2,1)S(1)}, u32[]{:S(2)}, u32[]{:S(2)}) collective-permute-start(bf16[1,256,1024]{2,1,0:T(8,128)(2,1)S(1)} %collective-permute-done.9), channel_id=1, source_target_pairs={{0,128},{32,160},{64,192},{96,224},{128,256},{160,288},{192,320},{... | collective-permute-start | bytes 1572872 | tf_op jit(solution)/shard_map/ppermute | solution.py:52
  61.0 11.6 %collective-permute-start.17 = (bf16[2,16,4096]{2,1,0:T(8,128)(2,1)S(1)}, bf16[2,16,4096]{2,1,0:T(8,128)(2,1)S(1)}, u32[]{:S(2)}, u32[]{:S(2)}) collective-permute-start(bf16[2,16,4096]{2,1,0:T(8,128)(2,1)S(1)} %collective-permute-done.16), channel_id=1, source_target_pairs={{0,15},{1,0},{2,1},{3,2},{4,3},{5,4},{6,5},{7,6},{8,7},{9,8},{10,9... | collective-permute-start | bytes 786440 | tf_op jit(solution)/shard_map/ppermute | solution.py:134
  66.6 11.2 %collective-permute-start.3 = (bf16[2,16,4096]{2,1,0:T(8,128)(2,1)S(1)}, bf16[2,16,4096]{2,1,0:T(8,128)(2,1)S(1)}, u32[]{:S(2)}, u32[]{:S(2)}) collective-permute-start(bf16[2,16,4096]{2,1,0:T(8,128)(2,1)S(1)} %collective-permute-done.2), channel_id=1, source_target_pairs={{0,1},{1,2},{2,3},{3,4},{4,5},{5,6},{6,7},{7,8},{8,9},{9,10},{10,1... | collective-permute-start | bytes 786440 | tf_op jit(solution)/shard_map/ppermute | solution.py:130
  68.9 50.4 %collective-permute-start.12 = (bf16[4,256,1024]{2,1,0:T(8,128)(2,1)S(1)}, bf16[4,256,1024]{2,1,0:T(8,128)(2,1)S(1)}, u32[]{:S(2)}, u32[]{:S(2)}) collective-permute-start(bf16[4,256,1024]{2,1,0:T(8,128)(2,1)S(1)} %pad_maximum_fusion), channel_id=1, source_target_pairs={{0,64},{32,96},{64,0},{96,32},{128,192},{160,224},{192,128},{224,1... | collective-permute-start | bytes 6291464 | tf_op jit(solution)/shard_map/ppermute | solution.py:55
  77.8 9.5 %collective-permute-start.4 = (bf16[2,16,4096]{2,1,0:T(8,128)(2,1)S(1)}, bf16[2,16,4096]{2,1,0:T(8,128)(2,1)S(1)}, u32[]{:S(2)}, u32[]{:S(2)}) collective-permute-start(bf16[2,16,4096]{2,1,0:T(8,128)(2,1)S(1)} %collective-permute-done.3), channel_id=1, source_target_pairs={{0,1},{1,2},{2,3},{3,4},{4,5},{5,6},{6,7},{7,8},{8,9},{9,10},{10,1... | collective-permute-start | bytes 786440 | tf_op jit(solution)/shard_map/ppermute | solution.py:130
  81.7 9.5 %collective-permute-start.19 = (bf16[2,16,4096]{2,1,0:T(8,128)(2,1)S(1)}, bf16[2,16,4096]{2,1,0:T(8,128)(2,1)S(1)}, u32[]{:S(2)}, u32[]{:S(2)}) collective-permute-start(bf16[2,16,4096]{2,1,0:T(8,128)(2,1)S(1)} %collective-permute-done.18), channel_id=1, source_target_pairs={{0,15},{1,0},{2,1},{3,2},{4,3},{5,4},{6,5},{7,6},{8,7},{9,8},{10,9... | collective-permute-start | bytes 786440 | tf_op jit(solution)/shard_map/ppermute | solution.py:134
  91.2 9.6 %collective-permute-start.20 = (bf16[2,16,4096]{2,1,0:T(8,128)(2,1)S(1)}, bf16[2,16,4096]{2,1,0:T(8,128)(2,1)S(1)}, u32[]{:S(2)}, u32[]{:S(2)}) collective-permute-start(bf16[2,16,4096]{2,1,0:T(8,128)(2,1)S(1)} %collective-permute-done.19), channel_id=1, source_target_pairs={{0,15},{1,0},{2,1},{3,2},{4,3},{5,4},{6,5},{7,6},{8,7},{9,8},{10,9... | collective-permute-start | bytes 786440 | tf_op jit(solution)/shard_map/ppermute | solution.py:134
  96.8 9.9 %collective-permute-start.6 = (bf16[2,16,4096]{2,1,0:T(8,128)(2,1)S(1)}, bf16[2,16,4096]{2,1,0:T(8,128)(2,1)S(1)}, u32[]{:S(2)}, u32[]{:S(2)}) collective-permute-start(bf16[2,16,4096]{2,1,0:T(8,128)(2,1)S(1)} %collective-permute-done.5), channel_id=1, source_target_pairs={{0,1},{1,2},{2,3},{3,4},{4,5},{5,6},{6,7},{7,8},{8,9},{9,10},{10,1... | collective-permute-start | bytes 786440 | tf_op jit(solution)/shard_map/ppermute | solution.py:130
  100.8 20.8 %collective-permute-start.21 = (bf16[2,16,4096]{2,1,0:T(8,128)(2,1)S(1)}, bf16[2,16,4096]{2,1,0:T(8,128)(2,1)S(1)}, u32[]{:S(2)}, u32[]{:S(2)}) collective-permute-start(bf16[2,16,4096]{2,1,0:T(8,128)(2,1)S(1)} %collective-permute-done.20), channel_id=1, source_target_pairs={{0,15},{1,0},{2,1},{3,2},{4,3},{5,4},{6,5},{7,6},{8,7},{9,8},{10,9... | collective-permute-start | bytes 786440 | tf_op jit(solution)/shard_map/ppermute | solution.py:134
  106.7 10.7 %collective-permute-start.7 = (bf16[2,16,4096]{2,1,0:T(8,128)(2,1)S(1)}, bf16[2,16,4096]{2,1,0:T(8,128)(2,1)S(1)}, u32[]{:S(2)}, u32[]{:S(2)}) collective-permute-start(bf16[2,16,4096]{2,1,0:T(8,128)(2,1)S(1)} %collective-permute-done.6), channel_id=1, source_target_pairs={{0,1},{1,2},{2,3},{3,4},{4,5},{5,6},{6,7},{7,8},{8,9},{9,10},{10,1... | collective-permute-start | bytes 786440 | tf_op jit(solution)/shard_map/ppermute | solution.py:130
  119.5 9.8 %collective-permute-start.13 = (bf16[8,256,1024]{2,1,0:T(8,128)(2,1)S(1)}, bf16[8,256,1024]{2,1,0:T(8,128)(2,1)S(1)}, u32[]{:S(2)}, u32[]{:S(2)}) collective-permute-start(bf16[8,256,1024]{2,1,0:T(8,128)(2,1)S(1)} %constant_dynamic-update-slice_fusion.2), channel_id=1, source_target_pairs={{0,32},{32,0},{64,96},{96,64},{128,160},{160,128},{192,224},{224,1... | collective-permute-start | bytes 12582920 | tf_op jit(solution)/shard_map/ppermute | solution.py:58
  138.5 11.0 %collective-permute-start.14 = (bf16[2,16,4096]{2,1,0:T(8,128)(2,1)S(1)}, bf16[2,16,4096]{2,1,0:T(8,128)(2,1)S(1)}, u32[]{:S(2)}, u32[]{:S(2)}) collective-permute-start(bf16[2,16,4096]{2,1,0:T(8,128)(2,1)S(1)} %bitcast.210), channel_id=1, source_target_pairs={{0,1},{1,2},{2,3},{3,4},{4,5},{5,6},{6,7},{7,8},{8,9},{9,10},{10,1... | collective-permute-start | bytes 786440 | tf_op jit(solution)/shard_map/ppermute | solution.py:165
  140.6 10.9 %collective-permute-start.29 = (bf16[2,16,4096]{2,1,0:T(8,128)(2,1)S(1)}, bf16[2,16,4096]{2,1,0:T(8,128)(2,1)S(1)}, u32[]{:S(2)}, u32[]{:S(2)}) collective-permute-start(bf16[2,16,4096]{2,1,0:T(8,128)(2,1)S(1)} %bitcast.209), channel_id=1, source_target_pairs={{0,15},{1,0},{2,1},{3,2},{4,3},{5,4},{6,5},{7,6},{8,7},{9,8},{10,9... | collective-permute-start | bytes 786440 | tf_op jit(solution)/shard_map/ppermute | solution.py:172
  149.6 10.1 %collective-permute-start.22 = (bf16[2,16,4096]{2,1,0:T(8,128)(2,1)S(1)}, bf16[2,16,4096]{2,1,0:T(8,128)(2,1)S(1)}, u32[]{:S(2)}, u32[]{:S(2)}) collective-permute-start(bf16[2,16,4096]{2,1,0:T(8,128)(2,1)S(1)} %fusion.31), channel_id=1, source_target_pairs={{0,1},{1,2},{2,3},{3,4},{4,5},{5,6},{6,7},{7,8},{8,9},{9,10},{10,1... | collective-permute-start | bytes 786440 | tf_op jit(solution)/shard_map/ppermute | solution.py:165
  151.6 10.1 %collective-permute-start.30 = (bf16[2,16,4096]{2,1,0:T(8,128)(2,1)S(1)}, bf16[2,16,4096]{2,1,0:T(8,128)(2,1)S(1)}, u32[]{:S(2)}, u32[]{:S(2)}) collective-permute-start(bf16[2,16,4096]{2,1,0:T(8,128)(2,1)S(1)} %fusion.24), channel_id=1, source_target_pairs={{0,15},{1,0},{2,1},{3,2},{4,3},{5,4},{6,5},{7,6},{8,7},{9,8},{10,9... | collective-permute-start | bytes 786440 | tf_op jit(solution)/shard_map/ppermute | solution.py:172
  188.4 10.4 %collective-permute-start.26 = (bf16[2,16,4096]{2,1,0:T(8,128)(2,1)S(1)}, bf16[2,16,4096]{2,1,0:T(8,128)(2,1)S(1)}, u32[]{:S(2)}, u32[]{:S(2)}) collective-permute-start(bf16[2,16,4096]{2,1,0:T(8,128)(2,1)S(1)} %fusion.27), channel_id=1, source_target_pairs={{0,1},{1,2},{2,3},{3,4},{4,5},{5,6},{6,7},{7,8},{8,9},{9,10},{10,1... | collective-permute-start | bytes 786440 | tf_op jit(solution)/shard_map/ppermute | solution.py:165
  190.4 10.4 %collective-permute-start.34 = (bf16[2,16,4096]{2,1,0:T(8,128)(2,1)S(1)}, bf16[2,16,4096]{2,1,0:T(8,128)(2,1)S(1)}, u32[]{:S(2)}, u32[]{:S(2)}) collective-permute-start(bf16[2,16,4096]{2,1,0:T(8,128)(2,1)S(1)} %fusion.20), channel_id=1, source_target_pairs={{0,15},{1,0},{2,1},{3,2},{4,3},{5,4},{6,5},{7,6},{8,7},{9,8},{10,9... | collective-permute-start | bytes 786440 | tf_op jit(solution)/shard_map/ppermute | solution.py:172
  198.8 11.6 %collective-permute-start.27 = (bf16[2,16,4096]{2,1,0:T(8,128)(2,1)S(1)}, bf16[2,16,4096]{2,1,0:T(8,128)(2,1)S(1)}, u32[]{:S(2)}, u32[]{:S(2)}) collective-permute-start(bf16[2,16,4096]{2,1,0:T(8,128)(2,1)S(1)} %fusion.26), channel_id=1, source_target_pairs={{0,1},{1,2},{2,3},{3,4},{4,5},{5,6},{6,7},{7,8},{8,9},{9,10},{10,1... | collective-permute-start | bytes 786440 | tf_op jit(solution)/shard_map/ppermute | solution.py:165
  200.8 11.6 %collective-permute-start.35 = (bf16[2,16,4096]{2,1,0:T(8,128)(2,1)S(1)}, bf16[2,16,4096]{2,1,0:T(8,128)(2,1)S(1)}, u32[]{:S(2)}, u32[]{:S(2)}) collective-permute-start(bf16[2,16,4096]{2,1,0:T(8,128)(2,1)S(1)} %fusion.19), channel_id=1, source_target_pairs={{0,15},{1,0},{2,1},{3,2},{4,3},{5,4},{6,5},{7,6},{8,7},{9,8},{10,9... | collective-permute-start | bytes 786440 | tf_op jit(solution)/shard_map/ppermute | solution.py:172
  (17 other events, 146.1 us)

commit v10 on v9

--- a/solution.py
+++ b/solution.py
@@ -149,20 +149,31 @@
             )
             act = part if act is None else act + part
             col += width
-        hidden = (jax.nn.silu(act[:, :ff_cols]) * act[:, ff_cols:]).astype(jnp.bfloat16)
+        return (jax.nn.silu(act[:, :ff_cols]) * act[:, ff_cols:]).astype(jnp.bfloat16)
+
+    def project(hidden):
         return jnp.dot(hidden, down_weight, preferred_element_type=jnp.float32).astype(jnp.bfloat16)
 
     chunk = nl * shard_rows
     blocks = {}
-    for group in ([8, 9], [5, 6, 7, 10, 11, 12], [0, 1, 2, 3, 4, 13, 14, 15]):
-        rows = jnp.concatenate([normed[k * chunk : (k + 1) * chunk] for k in group], axis=0)
-        out = ffn(rows).reshape(len(group), nl, shard_rows, feature_count)
-        for i, k in enumerate(group):
+    groups = ([8, 9], [5, 6, 7, 10, 11, 12], [0, 1, 2, 3, 4, 13, 14, 15])
+    hiddens = [
+        ffn(jnp.concatenate([normed[k * chunk : (k + 1) * chunk] for k in group], axis=0)) for group in groups
+    ]
+
+    def place(g, hidden):
+        out = project(hidden).reshape(len(groups[g]), nl, shard_rows, feature_count)
+        for i, k in enumerate(groups[g]):
             blocks[k] = out[i]
+
+    place(0, hiddens[0])
 
     fwd = blocks[nz // 2]
     for s in range(nz // 2):
         got = lax.ppermute(fwd, "tensor", TP_Z_FWD)
+        if s < len(groups) - 1:
+            late, got = lax.optimization_barrier((hiddens[s + 1], got))
+            place(s + 1, late)
         if s < nz // 2 - 1:
             fwd = (got.astype(jnp.float32) + blocks[nz // 2 - 1 - s].astype(jnp.float32)).astype(jnp.bfloat16)
         else:

time: 232 us -> 232 us (level)
  transfers between devices with their start and end apart: 38 -> 38, of which waited for: 18 -> 18; matrix products, arithmetic and copies ran while one was open for 5% -> 6% of each run, Pallas kernels for 0% -> 0%
where the time goes in v10:
time: 232 us; the launch traced here: 227 us
  starting transfers between devices  139 us (60%)
  waiting for transfers between devices  62.6 us (27%)
  matrix products  11.9 us (5%)
  local copies, waits for them, and re-layouts  7.98 us (3%)
  other arithmetic  3.63 us (2%)
    ppermute x7, starting transfers between devices, per_device(): bwd = lax.ppermute(bwd, 'tensor', TP_Z_BWD)  41 us
    ppermute x7, starting transfers between devices, per_device(): got = lax.ppermute(bwd, 'tensor', TP_Z_BWD)  36.4 us
    ppermute x8, waiting for transfers between devices, per_device(): got = lax.ppermute(fwd, 'tensor', TP_Z_FWD)  27.9 us
    ppermute x8, starting transfers between devices, per_device(): got = lax.ppermute(fwd, 'tensor', TP_Z_FWD)  15.4 us
    ppermute x8, starting transfers between devices, per_device(): fwd = lax.ppermute(fwd, 'tensor', TP_Z_FWD)  15.3 us
    ppermute x8, waiting for transfers between devices, per_device(): fwd = lax.ppermute(fwd, 'tensor', TP_Z_FWD)  13.6 us
    dot_general x18, matrix products, ffn(): jnp.dot(rows[:, col:col + width], buf.reshape(width, 2 * ff_cols), prefer...  8.28 us
    ppermute x1, starting transfers between devices, gather_pieces(): fwd1 = lax.ppermute(own, 'dp', DP_Y_FWD)  7.5 us
  transfers between devices with their start and end apart: 38, of which 18 were waited for; matrix products, arithmetic and copies ran while one was open for 6% of the time, Pallas kernels for 0%

profile of v10, /device:TPU:24, one launch (start us, length us, event | category | flops | bytes accessed | tf_op | source)
XLA Modules:
  0.0 227.3 jit_solution(2764042694251657562)
XLA Ops:
  2.0 7.5 %collective-permute-start.8 = (bf16[1,256,1024]{2,1,0:T(8,128)(2,1)S(1)}, bf16[1,256,1024]{2,1,0:T(8,128)(2,1)S(1)}, u32[]{:S(2)}, u32[]{:S(2)}) collective-permute-start(bf16[1,256,1024]{2,1,0:T(8,128)(2,1)S(1)} %bitcast.163), channel_id=1, source_target_pairs={{0,128},{32,160},{64,192},{96,224},{128,256},{160,288},{192,320},{... | collective-permute-start | bytes 1572872 | tf_op jit(solution)/shard_map/ppermute | solution.py:51
  14.4 6.6 %all-to-all-start = ((bf16[16,2,4224]{2,1,0:T(2,128)(2,1)}), bf16[16,2,4224]{2,1,0:T(2,128)(2,1)S(1)}, u32[]{:S(2)}, u32[]{:S(2)}) async-start(bf16[16,2,4224]{2,1,0:T(2,128)(2,1)} %reshape.942), calls=%async_computation | async-start | bytes 540672 | tf_op jit(solution)/shard_map/all_to_all | solution.py:95
  22.2 6.2 %all-to-all-done = bf16[16,2,4224]{2,1,0:T(2,128)(2,1)S(1)} async-done(((bf16[16,2,4224]{2,1,0:T(2,128)(2,1)}), bf16[16,2,4224]{2,1,0:T(2,128)(2,1)S(1)}, u32[]{:S(2)}, u32[]{:S(2)}) %all-to-all-start) | async-done | bytes 270368 | tf_op jit(solution)/shard_map/all_to_all | solution.py:95
  31.7 5.0 %collective-permute-done = bf16[16,4096]{1,0:T(8,128)(2,1)S(1)} collective-permute-done((bf16[16,4096]{1,0:T(8,128)(2,1)S(1)}, bf16[16,4096]{1,0:T(8,128)(2,1)S(1)}, u32[]{:S(2)}, u32[]{:S(2)}) %collective-permute-start) | collective-permute-done | bytes 131104 | tf_op jit(solution)/shard_map/ppermute | solution.py:126
  36.7 8.4 %collective-permute-start.1 = (bf16[2,16,4096]{2,1,0:T(8,128)(2,1)S(1)}, bf16[2,16,4096]{2,1,0:T(8,128)(2,1)S(1)}, u32[]{:S(2)}, u32[]{:S(2)}) collective-permute-start(bf16[2,16,4096]{2,1,0:T(8,128)(2,1)S(1)} %pad_maximum_fusion.4), channel_id=1, source_target_pairs={{0,15},{1,0},{2,1},{3,2},{4,3},{5,4},{6,5},{7,6},{8,7},{9,8},{10,9... | collective-permute-start | bytes 786440 | tf_op jit(solution)/shard_map/ppermute | solution.py:134
  47.1 4.0 %collective-permute-start.9 = (bf16[1,256,1024]{2,1,0:T(8,128)(2,1)S(1)}, bf16[1,256,1024]{2,1,0:T(8,128)(2,1)S(1)}, u32[]{:S(2)}, u32[]{:S(2)}) collective-permute-start(bf16[1,256,1024]{2,1,0:T(8,128)(2,1)S(1)} %collective-permute-done.8), channel_id=1, source_target_pairs={{0,128},{32,160},{64,192},{96,224},{128,256},{160,288},{192,320},{... | collective-permute-start | bytes 1572872 | tf_op jit(solution)/shard_map/ppermute | solution.py:52
  52.0 5.1 %collective-permute-start.2 = (bf16[2,16,4096]{2,1,0:T(8,128)(2,1)S(1)}, bf16[2,16,4096]{2,1,0:T(8,128)(2,1)S(1)}, u32[]{:S(2)}, u32[]{:S(2)}) collective-permute-start(bf16[2,16,4096]{2,1,0:T(8,128)(2,1)S(1)} %collective-permute-done.1), channel_id=1, source_target_pairs={{0,15},{1,0},{2,1},{3,2},{4,3},{5,4},{6,5},{7,6},{8,7},{9,8},{10,9... | collective-permute-start | bytes 786440 | tf_op jit(solution)/shard_map/ppermute | solution.py:134
  61.0 5.6 %collective-permute-start.3 = (bf16[2,16,4096]{2,1,0:T(8,128)(2,1)S(1)}, bf16[2,16,4096]{2,1,0:T(8,128)(2,1)S(1)}, u32[]{:S(2)}, u32[]{:S(2)}) collective-permute-start(bf16[2,16,4096]{2,1,0:T(8,128)(2,1)S(1)} %collective-permute-done.2), channel_id=1, source_target_pairs={{0,15},{1,0},{2,1},{3,2},{4,3},{5,4},{6,5},{7,6},{8,7},{9,8},{10,9... | collective-permute-start | bytes 786440 | tf_op jit(solution)/shard_map/ppermute | solution.py:134
  68.9 3.7 %collective-permute-start.11 = (bf16[4,256,1024]{2,1,0:T(8,128)(2,1)S(1)}, bf16[4,256,1024]{2,1,0:T(8,128)(2,1)S(1)}, u32[]{:S(2)}, u32[]{:S(2)}) collective-permute-start(bf16[4,256,1024]{2,1,0:T(8,128)(2,1)S(1)} %pad_maximum_fusion), channel_id=1, source_target_pairs={{0,64},{32,96},{64,0},{96,32},{128,192},{160,224},{192,128},{224,1... | collective-permute-start | bytes 6291464 | tf_op jit(solution)/shard_map/ppermute | solution.py:55
  72.6 5.1 %collective-permute-start.4 = (bf16[2,16,4096]{2,1,0:T(8,128)(2,1)S(1)}, bf16[2,16,4096]{2,1,0:T(8,128)(2,1)S(1)}, u32[]{:S(2)}, u32[]{:S(2)}) collective-permute-start(bf16[2,16,4096]{2,1,0:T(8,128)(2,1)S(1)} %collective-permute-done.3), channel_id=1, source_target_pairs={{0,15},{1,0},{2,1},{3,2},{4,3},{5,4},{6,5},{7,6},{8,7},{9,8},{10,9... | collective-permute-start | bytes 786440 | tf_op jit(solution)/shard_map/ppermute | solution.py:134
  81.7 5.6 %collective-permute-start.13 = (bf16[2,16,4096]{2,1,0:T(8,128)(2,1)S(1)}, bf16[2,16,4096]{2,1,0:T(8,128)(2,1)S(1)}, u32[]{:S(2)}, u32[]{:S(2)}) collective-permute-start(bf16[2,16,4096]{2,1,0:T(8,128)(2,1)S(1)} %collective-permute-done.4), channel_id=1, source_target_pairs={{0,15},{1,0},{2,1},{3,2},{4,3},{5,4},{6,5},{7,6},{8,7},{9,8},{10,9... | collective-permute-start | bytes 786440 | tf_op jit(solution)/shard_map/ppermute | solution.py:134
  91.2 5.6 %collective-permute-start.14 = (bf16[2,16,4096]{2,1,0:T(8,128)(2,1)S(1)}, bf16[2,16,4096]{2,1,0:T(8,128)(2,1)S(1)}, u32[]{:S(2)}, u32[]{:S(2)}) collective-permute-start(bf16[2,16,4096]{2,1,0:T(8,128)(2,1)S(1)} %collective-permute-done.13), channel_id=1, source_target_pairs={{0,15},{1,0},{2,1},{3,2},{4,3},{5,4},{6,5},{7,6},{8,7},{9,8},{10,9... | collective-permute-start | bytes 786440 | tf_op jit(solution)/shard_map/ppermute | solution.py:134
  100.8 5.6 %collective-permute-start.15 = (bf16[2,16,4096]{2,1,0:T(8,128)(2,1)S(1)}, bf16[2,16,4096]{2,1,0:T(8,128)(2,1)S(1)}, u32[]{:S(2)}, u32[]{:S(2)}) collective-permute-start(bf16[2,16,4096]{2,1,0:T(8,128)(2,1)S(1)} %collective-permute-done.14), channel_id=1, source_target_pairs={{0,15},{1,0},{2,1},{3,2},{4,3},{5,4},{6,5},{7,6},{8,7},{9,8},{10,9... | collective-permute-start | bytes 786440 | tf_op jit(solution)/shard_map/ppermute | solution.py:134
  108.6 8.7 %collective-permute-done.19 = bf16[2,16,4096]{2,1,0:T(8,128)(2,1)S(1)} collective-permute-done((bf16[2,16,4096]{2,1,0:T(8,128)(2,1)S(1)}, bf16[2,16,4096]{2,1,0:T(8,128)(2,1)S(1)}, u32[]{:S(2)}, u32[]{:S(2)}) %collective-permute-start.19) | collective-permute-done | bytes 262176 | tf_op jit(solution)/shard_map/ppermute | solution.py:130
  122.3 4.5 %collective-permute-done.20 = bf16[2,16,4096]{2,1,0:T(8,128)(2,1)S(1)} collective-permute-done((bf16[2,16,4096]{2,1,0:T(8,128)(2,1)S(1)}, bf16[2,16,4096]{2,1,0:T(8,128)(2,1)S(1)}, u32[]{:S(2)}, u32[]{:S(2)}) %collective-permute-start.20) | collective-permute-done | bytes 262176 | tf_op jit(solution)/shard_map/ppermute | solution.py:130
  137.4 5.3 %collective-permute-start.29 = (bf16[2,16,4096]{2,1,0:T(8,128)(2,1)S(1)}, bf16[2,16,4096]{2,1,0:T(8,128)(2,1)S(1)}, u32[]{:S(2)}, u32[]{:S(2)}) collective-permute-start(bf16[2,16,4096]{2,1,0:T(8,128)(2,1)S(1)} %bitcast.211), channel_id=1, source_target_pairs={{0,15},{1,0},{2,1},{3,2},{4,3},{5,4},{6,5},{7,6},{8,7},{9,8},{10,9... | collective-permute-start | bytes 786440 | tf_op jit(solution)/shard_map/ppermute | solution.py:183
  149.8 5.1 %collective-permute-start.30 = (bf16[2,16,4096]{2,1,0:T(8,128)(2,1)S(1)}, bf16[2,16,4096]{2,1,0:T(8,128)(2,1)S(1)}, u32[]{:S(2)}, u32[]{:S(2)}) collective-permute-start(bf16[2,16,4096]{2,1,0:T(8,128)(2,1)S(1)} %fusion.24), channel_id=1, source_target_pairs={{0,15},{1,0},{2,1},{3,2},{4,3},{5,4},{6,5},{7,6},{8,7},{9,8},{10,9... | collective-permute-start | bytes 786440 | tf_op jit(solution)/shard_map/ppermute | solution.py:183
  161.4 5.1 %collective-permute-start.31 = (bf16[2,16,4096]{2,1,0:T(8,128)(2,1)S(1)}, bf16[2,16,4096]{2,1,0:T(8,128)(2,1)S(1)}, u32[]{:S(2)}, u32[]{:S(2)}) collective-permute-start(bf16[2,16,4096]{2,1,0:T(8,128)(2,1)S(1)} %fusion.23), channel_id=1, source_target_pairs={{0,15},{1,0},{2,1},{3,2},{4,3},{5,4},{6,5},{7,6},{8,7},{9,8},{10,9... | collective-permute-start | bytes 786440 | tf_op jit(solution)/shard_map/ppermute | solution.py:183
  170.9 5.1 %collective-permute-start.32 = (bf16[2,16,4096]{2,1,0:T(8,128)(2,1)S(1)}, bf16[2,16,4096]{2,1,0:T(8,128)(2,1)S(1)}, u32[]{:S(2)}, u32[]{:S(2)}) collective-permute-start(bf16[2,16,4096]{2,1,0:T(8,128)(2,1)S(1)} %fusion.22), channel_id=1, source_target_pairs={{0,15},{1,0},{2,1},{3,2},{4,3},{5,4},{6,5},{7,6},{8,7},{9,8},{10,9... | collective-permute-start | bytes 786440 | tf_op jit(solution)/shard_map/ppermute | solution.py:183
  180.4 5.1 %collective-permute-start.33 = (bf16[2,16,4096]{2,1,0:T(8,128)(2,1)S(1)}, bf16[2,16,4096]{2,1,0:T(8,128)(2,1)S(1)}, u32[]{:S(2)}, u32[]{:S(2)}) collective-permute-start(bf16[2,16,4096]{2,1,0:T(8,128)(2,1)S(1)} %fusion.21), channel_id=1, source_target_pairs={{0,15},{1,0},{2,1},{3,2},{4,3},{5,4},{6,5},{7,6},{8,7},{9,8},{10,9... | collective-permute-start | bytes 786440 | tf_op jit(solution)/shard_map/ppermute | solution.py:183
  190.0 5.2 %collective-permute-start.34 = (bf16[2,16,4096]{2,1,0:T(8,128)(2,1)S(1)}, bf16[2,16,4096]{2,1,0:T(8,128)(2,1)S(1)}, u32[]{:S(2)}, u32[]{:S(2)}) collective-permute-start(bf16[2,16,4096]{2,1,0:T(8,128)(2,1)S(1)} %fusion.20), channel_id=1, source_target_pairs={{0,15},{1,0},{2,1},{3,2},{4,3},{5,4},{6,5},{7,6},{8,7},{9,8},{10,9... | collective-permute-start | bytes 786440 | tf_op jit(solution)/shard_map/ppermute | solution.py:183
  200.5 5.4 %collective-permute-start.35 = (bf16[2,16,4096]{2,1,0:T(8,128)(2,1)S(1)}, bf16[2,16,4096]{2,1,0:T(8,128)(2,1)S(1)}, u32[]{:S(2)}, u32[]{:S(2)}) collective-permute-start(bf16[2,16,4096]{2,1,0:T(8,128)(2,1)S(1)} %fusion.19), channel_id=1, source_target_pairs={{0,15},{1,0},{2,1},{3,2},{4,3},{5,4},{6,5},{7,6},{8,7},{9,8},{10,9... | collective-permute-start | bytes 786440 | tf_op jit(solution)/shard_map/ppermute | solution.py:183
  205.9 4.2 %collective-permute-done.27 = bf16[2,16,4096]{2,1,0:T(8,128)(2,1)S(1)} collective-permute-done((bf16[2,16,4096]{2,1,0:T(8,128)(2,1)S(1)}, bf16[2,16,4096]{2,1,0:T(8,128)(2,1)S(1)}, u32[]{:S(2)}, u32[]{:S(2)}) %collective-permute-start.27) | collective-permute-done | bytes 262176 | tf_op jit(solution)/shard_map/ppermute | solution.py:173
  212.0 7.5 %collective-permute-done.28 = bf16[2,16,4096]{2,1,0:T(8,128)(2,1)S(1)} collective-permute-done((bf16[2,16,4096]{2,1,0:T(8,128)(2,1)S(1)}, bf16[2,16,4096]{2,1,0:T(8,128)(2,1)S(1)}, u32[]{:S(2)}, u32[]{:S(2)}) %collective-permute-start.28) | collective-permute-done | bytes 262176 | tf_op jit(solution)/shard_map/ppermute | solution.py:173
  (154 shorter events, 90.2 us)
Async XLA Ops:
  2.0 45.1 %collective-permute-start.8 = (bf16[1,256,1024]{2,1,0:T(8,128)(2,1)S(1)}, bf16[1,256,1024]{2,1,0:T(8,128)(2,1)S(1)}, u32[]{:S(2)}, u32[]{:S(2)}) collective-permute-start(bf16[1,256,1024]{2,1,0:T(8,128)(2,1)S(1)} %bitcast.163), channel_id=1, source_target_pairs={{0,128},{32,160},{64,192},{96,224},{128,256},{160,288},{192,320},{... | collective-permute-start | bytes 1572872 | tf_op jit(solution)/shard_map/ppermute | solution.py:51
  9.5 59.0 %collective-permute-start.10 = (bf16[1,256,1024]{2,1,0:T(8,128)(2,1)S(1)}, bf16[1,256,1024]{2,1,0:T(8,128)(2,1)S(1)}, u32[]{:S(2)}, u32[]{:S(2)}) collective-permute-start(bf16[1,256,1024]{2,1,0:T(8,128)(2,1)S(1)} %bitcast.164), channel_id=1, source_target_pairs={{0,384},{32,416},{64,448},{96,480},{128,0},{160,32},{192,64},{224,... | collective-permute-start | bytes 1572872 | tf_op jit(solution)/shard_map/ppermute | solution.py:53
  14.4 14.0 %all-to-all-start = ((bf16[16,2,4224]{2,1,0:T(2,128)(2,1)}), bf16[16,2,4224]{2,1,0:T(2,128)(2,1)S(1)}, u32[]{:S(2)}, u32[]{:S(2)}) async-start(bf16[16,2,4224]{2,1,0:T(2,128)(2,1)} %reshape.942), calls=%async_computation | async-start | bytes 540672 | tf_op jit(solution)/shard_map/all_to_all | solution.py:95
  36.7 15.3 %collective-permute-start.1 = (bf16[2,16,4096]{2,1,0:T(8,128)(2,1)S(1)}, bf16[2,16,4096]{2,1,0:T(8,128)(2,1)S(1)}, u32[]{:S(2)}, u32[]{:S(2)}) collective-permute-start(bf16[2,16,4096]{2,1,0:T(8,128)(2,1)S(1)} %pad_maximum_fusion.4), channel_id=1, source_target_pairs={{0,15},{1,0},{2,1},{3,2},{4,3},{5,4},{6,5},{7,6},{8,7},{9,8},{10,9... | collective-permute-start | bytes 786440 | tf_op jit(solution)/shard_map/ppermute | solution.py:134
  45.1 12.0 %collective-permute-start.5 = (bf16[2,16,4096]{2,1,0:T(8,128)(2,1)S(1)}, bf16[2,16,4096]{2,1,0:T(8,128)(2,1)S(1)}, u32[]{:S(2)}, u32[]{:S(2)}) collective-permute-start(bf16[2,16,4096]{2,1,0:T(8,128)(2,1)S(1)} %pad_maximum_fusion.4), channel_id=1, source_target_pairs={{0,1},{1,2},{2,3},{3,4},{4,5},{5,6},{6,7},{7,8},{8,9},{9,10},{10,1... | collective-permute-start | bytes 786440 | tf_op jit(solution)/shard_map/ppermute | solution.py:130
  47.1 21.5 %collective-permute-start.9 = (bf16[1,256,1024]{2,1,0:T(8,128)(2,1)S(1)}, bf16[1,256,1024]{2,1,0:T(8,128)(2,1)S(1)}, u32[]{:S(2)}, u32[]{:S(2)}) collective-permute-start(bf16[1,256,1024]{2,1,0:T(8,128)(2,1)S(1)} %collective-permute-done.8), channel_id=1, source_target_pairs={{0,128},{32,160},{64,192},{96,224},{128,256},{160,288},{192,320},{... | collective-permute-start | bytes 1572872 | tf_op jit(solution)/shard_map/ppermute | solution.py:52
  61.0 11.6 %collective-permute-start.3 = (bf16[2,16,4096]{2,1,0:T(8,128)(2,1)S(1)}, bf16[2,16,4096]{2,1,0:T(8,128)(2,1)S(1)}, u32[]{:S(2)}, u32[]{:S(2)}) collective-permute-start(bf16[2,16,4096]{2,1,0:T(8,128)(2,1)S(1)} %collective-permute-done.2), channel_id=1, source_target_pairs={{0,15},{1,0},{2,1},{3,2},{4,3},{5,4},{6,5},{7,6},{8,7},{9,8},{10,9... | collective-permute-start | bytes 786440 | tf_op jit(solution)/shard_map/ppermute | solution.py:134
  66.6 11.2 %collective-permute-start.7 = (bf16[2,16,4096]{2,1,0:T(8,128)(2,1)S(1)}, bf16[2,16,4096]{2,1,0:T(8,128)(2,1)S(1)}, u32[]{:S(2)}, u32[]{:S(2)}) collective-permute-start(bf16[2,16,4096]{2,1,0:T(8,128)(2,1)S(1)} %collective-permute-done.6), channel_id=1, source_target_pairs={{0,1},{1,2},{2,3},{3,4},{4,5},{5,6},{6,7},{7,8},{8,9},{9,10},{10,1... | collective-permute-start | bytes 786440 | tf_op jit(solution)/shard_map/ppermute | solution.py:130
  68.9 50.4 %collective-permute-start.11 = (bf16[4,256,1024]{2,1,0:T(8,128)(2,1)S(1)}, bf16[4,256,1024]{2,1,0:T(8,128)(2,1)S(1)}, u32[]{:S(2)}, u32[]{:S(2)}) collective-permute-start(bf16[4,256,1024]{2,1,0:T(8,128)(2,1)S(1)} %pad_maximum_fusion), channel_id=1, source_target_pairs={{0,64},{32,96},{64,0},{96,32},{128,192},{160,224},{192,128},{224,1... | collective-permute-start | bytes 6291464 | tf_op jit(solution)/shard_map/ppermute | solution.py:55
  77.8 9.5 %collective-permute-start.16 = (bf16[2,16,4096]{2,1,0:T(8,128)(2,1)S(1)}, bf16[2,16,4096]{2,1,0:T(8,128)(2,1)S(1)}, u32[]{:S(2)}, u32[]{:S(2)}) collective-permute-start(bf16[2,16,4096]{2,1,0:T(8,128)(2,1)S(1)} %collective-permute-done.7), channel_id=1, source_target_pairs={{0,1},{1,2},{2,3},{3,4},{4,5},{5,6},{6,7},{7,8},{8,9},{9,10},{10,1... | collective-permute-start | bytes 786440 | tf_op jit(solution)/shard_map/ppermute | solution.py:130
  81.7 9.5 %collective-permute-start.13 = (bf16[2,16,4096]{2,1,0:T(8,128)(2,1)S(1)}, bf16[2,16,4096]{2,1,0:T(8,128)(2,1)S(1)}, u32[]{:S(2)}, u32[]{:S(2)}) collective-permute-start(bf16[2,16,4096]{2,1,0:T(8,128)(2,1)S(1)} %collective-permute-done.4), channel_id=1, source_target_pairs={{0,15},{1,0},{2,1},{3,2},{4,3},{5,4},{6,5},{7,6},{8,7},{9,8},{10,9... | collective-permute-start | bytes 786440 | tf_op jit(solution)/shard_map/ppermute | solution.py:134
  91.2 9.6 %collective-permute-start.14 = (bf16[2,16,4096]{2,1,0:T(8,128)(2,1)S(1)}, bf16[2,16,4096]{2,1,0:T(8,128)(2,1)S(1)}, u32[]{:S(2)}, u32[]{:S(2)}) collective-permute-start(bf16[2,16,4096]{2,1,0:T(8,128)(2,1)S(1)} %collective-permute-done.13), channel_id=1, source_target_pairs={{0,15},{1,0},{2,1},{3,2},{4,3},{5,4},{6,5},{7,6},{8,7},{9,8},{10,9... | collective-permute-start | bytes 786440 | tf_op jit(solution)/shard_map/ppermute | solution.py:134
  96.8 9.9 %collective-permute-start.18 = (bf16[2,16,4096]{2,1,0:T(8,128)(2,1)S(1)}, bf16[2,16,4096]{2,1,0:T(8,128)(2,1)S(1)}, u32[]{:S(2)}, u32[]{:S(2)}) collective-permute-start(bf16[2,16,4096]{2,1,0:T(8,128)(2,1)S(1)} %collective-permute-done.17), channel_id=1, source_target_pairs={{0,1},{1,2},{2,3},{3,4},{4,5},{5,6},{6,7},{7,8},{8,9},{9,10},{10,1... | collective-permute-start | bytes 786440 | tf_op jit(solution)/shard_map/ppermute | solution.py:130
  100.8 20.6 %collective-permute-start.15 = (bf16[2,16,4096]{2,1,0:T(8,128)(2,1)S(1)}, bf16[2,16,4096]{2,1,0:T(8,128)(2,1)S(1)}, u32[]{:S(2)}, u32[]{:S(2)}) collective-permute-start(bf16[2,16,4096]{2,1,0:T(8,128)(2,1)S(1)} %collective-permute-done.14), channel_id=1, source_target_pairs={{0,15},{1,0},{2,1},{3,2},{4,3},{5,4},{6,5},{7,6},{8,7},{9,8},{10,9... | collective-permute-start | bytes 786440 | tf_op jit(solution)/shard_map/ppermute | solution.py:134
  106.7 10.7 %collective-permute-start.19 = (bf16[2,16,4096]{2,1,0:T(8,128)(2,1)S(1)}, bf16[2,16,4096]{2,1,0:T(8,128)(2,1)S(1)}, u32[]{:S(2)}, u32[]{:S(2)}) collective-permute-start(bf16[2,16,4096]{2,1,0:T(8,128)(2,1)S(1)} %collective-permute-done.18), channel_id=1, source_target_pairs={{0,1},{1,2},{2,3},{3,4},{4,5},{5,6},{6,7},{7,8},{8,9},{9,10},{10,1... | collective-permute-start | bytes 786440 | tf_op jit(solution)/shard_map/ppermute | solution.py:130
  119.5 9.8 %collective-permute-start.12 = (bf16[8,256,1024]{2,1,0:T(8,128)(2,1)S(1)}, bf16[8,256,1024]{2,1,0:T(8,128)(2,1)S(1)}, u32[]{:S(2)}, u32[]{:S(2)}) collective-permute-start(bf16[8,256,1024]{2,1,0:T(8,128)(2,1)S(1)} %constant_dynamic-update-slice_fusion.10), channel_id=1, source_target_pairs={{0,32},{32,0},{64,96},{96,64},{128,160},{160,128},{192,224},{224,1... | collective-permute-start | bytes 12582920 | tf_op jit(solution)/shard_map/ppermute | solution.py:58
  135.5 11.0 %collective-permute-start.21 = (bf16[2,16,4096]{2,1,0:T(8,128)(2,1)S(1)}, bf16[2,16,4096]{2,1,0:T(8,128)(2,1)S(1)}, u32[]{:S(2)}, u32[]{:S(2)}) collective-permute-start(bf16[2,16,4096]{2,1,0:T(8,128)(2,1)S(1)} %bitcast.212), channel_id=1, source_target_pairs={{0,1},{1,2},{2,3},{3,4},{4,5},{5,6},{6,7},{7,8},{8,9},{9,10},{10,1... | collective-permute-start | bytes 786440 | tf_op jit(solution)/shard_map/ppermute | solution.py:173
  137.4 12.3 %collective-permute-start.29 = (bf16[2,16,4096]{2,1,0:T(8,128)(2,1)S(1)}, bf16[2,16,4096]{2,1,0:T(8,128)(2,1)S(1)}, u32[]{:S(2)}, u32[]{:S(2)}) collective-permute-start(bf16[2,16,4096]{2,1,0:T(8,128)(2,1)S(1)} %bitcast.211), channel_id=1, source_target_pairs={{0,15},{1,0},{2,1},{3,2},{4,3},{5,4},{6,5},{7,6},{8,7},{9,8},{10,9... | collective-permute-start | bytes 786440 | tf_op jit(solution)/shard_map/ppermute | solution.py:183
  147.7 10.1 %collective-permute-start.22 = (bf16[2,16,4096]{2,1,0:T(8,128)(2,1)S(1)}, bf16[2,16,4096]{2,1,0:T(8,128)(2,1)S(1)}, u32[]{:S(2)}, u32[]{:S(2)}) collective-permute-start(bf16[2,16,4096]{2,1,0:T(8,128)(2,1)S(1)} %fusion.31), channel_id=1, source_target_pairs={{0,1},{1,2},{2,3},{3,4},{4,5},{5,6},{6,7},{7,8},{8,9},{9,10},{10,1... | collective-permute-start | bytes 786440 | tf_op jit(solution)/shard_map/ppermute | solution.py:173
  149.8 11.5 %collective-permute-start.30 = (bf16[2,16,4096]{2,1,0:T(8,128)(2,1)S(1)}, bf16[2,16,4096]{2,1,0:T(8,128)(2,1)S(1)}, u32[]{:S(2)}, u32[]{:S(2)}) collective-permute-start(bf16[2,16,4096]{2,1,0:T(8,128)(2,1)S(1)} %fusion.24), channel_id=1, source_target_pairs={{0,15},{1,0},{2,1},{3,2},{4,3},{5,4},{6,5},{7,6},{8,7},{9,8},{10,9... | collective-permute-start | bytes 786440 | tf_op jit(solution)/shard_map/ppermute | solution.py:183
  188.0 10.4 %collective-permute-start.26 = (bf16[2,16,4096]{2,1,0:T(8,128)(2,1)S(1)}, bf16[2,16,4096]{2,1,0:T(8,128)(2,1)S(1)}, u32[]{:S(2)}, u32[]{:S(2)}) collective-permute-start(bf16[2,16,4096]{2,1,0:T(8,128)(2,1)S(1)} %fusion.27), channel_id=1, source_target_pairs={{0,1},{1,2},{2,3},{3,4},{4,5},{5,6},{6,7},{7,8},{8,9},{9,10},{10,1... | collective-permute-start | bytes 786440 | tf_op jit(solution)/shard_map/ppermute | solution.py:173
  190.0 10.4 %collective-permute-start.34 = (bf16[2,16,4096]{2,1,0:T(8,128)(2,1)S(1)}, bf16[2,16,4096]{2,1,0:T(8,128)(2,1)S(1)}, u32[]{:S(2)}, u32[]{:S(2)}) collective-permute-start(bf16[2,16,4096]{2,1,0:T(8,128)(2,1)S(1)} %fusion.20), channel_id=1, source_target_pairs={{0,15},{1,0},{2,1},{3,2},{4,3},{5,4},{6,5},{7,6},{8,7},{9,8},{10,9... | collective-permute-start | bytes 786440 | tf_op jit(solution)/shard_map/ppermute | solution.py:183
  198.4 11.6 %collective-permute-start.27 = (bf16[2,16,4096]{2,1,0:T(8,128)(2,1)S(1)}, bf16[2,16,4096]{2,1,0:T(8,128)(2,1)S(1)}, u32[]{:S(2)}, u32[]{:S(2)}) collective-permute-start(bf16[2,16,4096]{2,1,0:T(8,128)(2,1)S(1)} %fusion.26), channel_id=1, source_target_pairs={{0,1},{1,2},{2,3},{3,4},{4,5},{5,6},{6,7},{7,8},{8,9},{9,10},{10,1... | collective-permute-start | bytes 786440 | tf_op jit(solution)/shard_map/ppermute | solution.py:173
  200.5 11.6 %collective-permute-start.35 = (bf16[2,16,4096]{2,1,0:T(8,128)(2,1)S(1)}, bf16[2,16,4096]{2,1,0:T(8,128)(2,1)S(1)}, u32[]{:S(2)}, u32[]{:S(2)}) collective-permute-start(bf16[2,16,4096]{2,1,0:T(8,128)(2,1)S(1)} %fusion.19), channel_id=1, source_target_pairs={{0,15},{1,0},{2,1},{3,2},{4,3},{5,4},{6,5},{7,6},{8,7},{9,8},{10,9... | collective-permute-start | bytes 786440 | tf_op jit(solution)/shard_map/ppermute | solution.py:183
  (17 other events, 146.1 us)

commit v11 on v10

--- a/solution.py
+++ b/solution.py
@@ -126,13 +126,21 @@
     pair = jnp.stack([travelling, lax.ppermute(travelling, "tensor", TP_L_SWAP)])
     token_chunks = {0: pair}
     fwd = pair
-    for s in range(nz // 2):
+    for s in range(nz // 2 - 1):
         fwd = lax.ppermute(fwd, "tensor", TP_Z_FWD)
         token_chunks[nz - 1 - s] = fwd
     bwd = pair
     for s in range(nz // 2 - 1):
         bwd = lax.ppermute(bwd, "tensor", TP_Z_BWD)
         token_chunks[s + 1] = bwd
+    half = feature_count // 2
+    token_chunks[nz // 2] = jnp.concatenate(
+        [
+            lax.ppermute(fwd[..., :half], "tensor", TP_Z_FWD),
+            lax.ppermute(bwd[..., half:], "tensor", TP_Z_BWD),
+        ],
+        axis=-1,
+    )
     gathered = jnp.concatenate([token_chunks[k] for k in range(nz)], axis=0)
     row_total = gathered.shape[0] * gathered.shape[1]
     normed = gathered.reshape(row_total, feature_count)

time: 232 us -> 230 us (level)
  waiting for transfers between devices: 62.6 us -> 57.1 us
  starting transfers between devices: 139 us -> 144 us
    ppermute x8 -> x7, waiting for transfers between devices: 13.6 us -> 0.99 us  [per_device(): fwd = lax.ppermute(fwd, 'tensor', TP_Z_FWD)]
    ppermute x0 -> x2, starting transfers between devices: none -> 7.52 us  [the longest x1 5.6 us: per_device(): lax.ppermute(bwd[..., half:], 'tensor', TP_Z_BWD)]
    ppermute x0 -> x2, waiting for transfers between devices: none -> 3.08 us  [the longest x1 3.08 us: per_device(): lax.ppermute(fwd[..., :half], 'tensor', TP_Z_FWD)]
    ppermute x7, waiting for transfers between devices: 6.75 us -> 9.25 us  [per_device(): bwd = lax.ppermute(bwd, 'tensor', TP_Z_BWD)]
    ppermute x8 -> x7, starting transfers between devices: 15.3 us -> 13.4 us  [per_device(): fwd = lax.ppermute(fwd, 'tensor', TP_Z_FWD)]
  transfers between devices with their start and end apart: 38 -> 39, of which waited for: 18 -> 20; matrix products, arithmetic and copies ran while one was open for 6% -> 6% of each run, Pallas kernels for 0% -> 0%
where the time goes in v11:
time: 230 us; the launch traced here: 227 us
  starting transfers between devices  144 us (63%)
  waiting for transfers between devices  57.1 us (25%)
  matrix products  11.9 us (5%)
  local copies, waits for them, and re-layouts  7.9 us (3%)
  other arithmetic  3.64 us (2%)
    ppermute x7, starting transfers between devices, per_device(): bwd = lax.ppermute(bwd, 'tensor', TP_Z_BWD)  41 us
    ppermute x7, starting transfers between devices, per_device(): got = lax.ppermute(bwd, 'tensor', TP_Z_BWD)  36 us
    ppermute x8, waiting for transfers between devices, per_device(): got = lax.ppermute(fwd, 'tensor', TP_Z_FWD)  28.2 us
    ppermute x8, starting transfers between devices, per_device(): got = lax.ppermute(fwd, 'tensor', TP_Z_FWD)  15.5 us
    ppermute x7, starting transfers between devices, per_device(): fwd = lax.ppermute(fwd, 'tensor', TP_Z_FWD)  13.4 us
    ppermute x7, waiting for transfers between devices, per_device(): bwd = lax.ppermute(bwd, 'tensor', TP_Z_BWD)  9.25 us
    dot_general x18, matrix products, ffn(): jnp.dot(rows[:, col:col + width], buf.reshape(width, 2 * ff_cols), prefer...  8.32 us
    ppermute x1, starting transfers between devices, gather_pieces(): fwd1 = lax.ppermute(own, 'dp', DP_Y_FWD)  7.5 us
  transfers between devices with their start and end apart: 39, of which 20 were waited for; matrix products, arithmetic and copies ran while one was open for 6% of the time, Pallas kernels for 0%

profile of v11, /device:TPU:24, one launch (start us, length us, event | category | flops | bytes accessed | tf_op | source)
XLA Modules:
  0.0 226.5 jit_solution(15937878296328157833)
XLA Ops:
  2.0 7.5 %collective-permute-start.8 = (bf16[1,256,1024]{2,1,0:T(8,128)(2,1)S(1)}, bf16[1,256,1024]{2,1,0:T(8,128)(2,1)S(1)}, u32[]{:S(2)}, u32[]{:S(2)}) collective-permute-start(bf16[1,256,1024]{2,1,0:T(8,128)(2,1)S(1)} %bitcast.163), channel_id=1, source_target_pairs={{0,128},{32,160},{64,192},{96,224},{128,256},{160,288},{192,320},{... | collective-permute-start | bytes 1572872 | tf_op jit(solution)/shard_map/ppermute | solution.py:51
  14.4 6.6 %all-to-all-start = ((bf16[16,2,4224]{2,1,0:T(2,128)(2,1)}), bf16[16,2,4224]{2,1,0:T(2,128)(2,1)S(1)}, u32[]{:S(2)}, u32[]{:S(2)}) async-start(bf16[16,2,4224]{2,1,0:T(2,128)(2,1)} %reshape.942), calls=%async_computation | async-start | bytes 540672 | tf_op jit(solution)/shard_map/all_to_all | solution.py:95
  22.2 6.2 %all-to-all-done = bf16[16,2,4224]{2,1,0:T(2,128)(2,1)S(1)} async-done(((bf16[16,2,4224]{2,1,0:T(2,128)(2,1)}), bf16[16,2,4224]{2,1,0:T(2,128)(2,1)S(1)}, u32[]{:S(2)}, u32[]{:S(2)}) %all-to-all-start) | async-done | bytes 270368 | tf_op jit(solution)/shard_map/all_to_all | solution.py:95
  31.7 5.0 %collective-permute-done = bf16[16,4096]{1,0:T(8,128)(2,1)S(1)} collective-permute-done((bf16[16,4096]{1,0:T(8,128)(2,1)S(1)}, bf16[16,4096]{1,0:T(8,128)(2,1)S(1)}, u32[]{:S(2)}, u32[]{:S(2)}) %collective-permute-start) | collective-permute-done | bytes 131104 | tf_op jit(solution)/shard_map/ppermute | solution.py:126
  36.7 8.4 %collective-permute-start.1 = (bf16[2,16,4096]{2,1,0:T(8,128)(2,1)S(1)}, bf16[2,16,4096]{2,1,0:T(8,128)(2,1)S(1)}, u32[]{:S(2)}, u32[]{:S(2)}) collective-permute-start(bf16[2,16,4096]{2,1,0:T(8,128)(2,1)S(1)} %pad_maximum_fusion.4), channel_id=1, source_target_pairs={{0,15},{1,0},{2,1},{3,2},{4,3},{5,4},{6,5},{7,6},{8,7},{9,8},{10,9... | collective-permute-start | bytes 786440 | tf_op jit(solution)/shard_map/ppermute | solution.py:134
  47.1 4.0 %collective-permute-start.9 = (bf16[1,256,1024]{2,1,0:T(8,128)(2,1)S(1)}, bf16[1,256,1024]{2,1,0:T(8,128)(2,1)S(1)}, u32[]{:S(2)}, u32[]{:S(2)}) collective-permute-start(bf16[1,256,1024]{2,1,0:T(8,128)(2,1)S(1)} %collective-permute-done.8), channel_id=1, source_target_pairs={{0,128},{32,160},{64,192},{96,224},{128,256},{160,288},{192,320},{... | collective-permute-start | bytes 1572872 | tf_op jit(solution)/shard_map/ppermute | solution.py:52
  52.0 5.1 %collective-permute-start.2 = (bf16[2,16,4096]{2,1,0:T(8,128)(2,1)S(1)}, bf16[2,16,4096]{2,1,0:T(8,128)(2,1)S(1)}, u32[]{:S(2)}, u32[]{:S(2)}) collective-permute-start(bf16[2,16,4096]{2,1,0:T(8,128)(2,1)S(1)} %collective-permute-done.1), channel_id=1, source_target_pairs={{0,15},{1,0},{2,1},{3,2},{4,3},{5,4},{6,5},{7,6},{8,7},{9,8},{10,9... | collective-permute-start | bytes 786440 | tf_op jit(solution)/shard_map/ppermute | solution.py:134
  61.0 5.6 %collective-permute-start.3 = (bf16[2,16,4096]{2,1,0:T(8,128)(2,1)S(1)}, bf16[2,16,4096]{2,1,0:T(8,128)(2,1)S(1)}, u32[]{:S(2)}, u32[]{:S(2)}) collective-permute-start(bf16[2,16,4096]{2,1,0:T(8,128)(2,1)S(1)} %collective-permute-done.2), channel_id=1, source_target_pairs={{0,15},{1,0},{2,1},{3,2},{4,3},{5,4},{6,5},{7,6},{8,7},{9,8},{10,9... | collective-permute-start | bytes 786440 | tf_op jit(solution)/shard_map/ppermute | solution.py:134
  68.8 3.7 %collective-permute-start.11 = (bf16[4,256,1024]{2,1,0:T(8,128)(2,1)S(1)}, bf16[4,256,1024]{2,1,0:T(8,128)(2,1)S(1)}, u32[]{:S(2)}, u32[]{:S(2)}) collective-permute-start(bf16[4,256,1024]{2,1,0:T(8,128)(2,1)S(1)} %pad_maximum_fusion), channel_id=1, source_target_pairs={{0,64},{32,96},{64,0},{96,32},{128,192},{160,224},{192,128},{224,1... | collective-permute-start | bytes 6291464 | tf_op jit(solution)/shard_map/ppermute | solution.py:55
  72.6 5.1 %collective-permute-start.4 = (bf16[2,16,4096]{2,1,0:T(8,128)(2,1)S(1)}, bf16[2,16,4096]{2,1,0:T(8,128)(2,1)S(1)}, u32[]{:S(2)}, u32[]{:S(2)}) collective-permute-start(bf16[2,16,4096]{2,1,0:T(8,128)(2,1)S(1)} %collective-permute-done.3), channel_id=1, source_target_pairs={{0,15},{1,0},{2,1},{3,2},{4,3},{5,4},{6,5},{7,6},{8,7},{9,8},{10,9... | collective-permute-start | bytes 786440 | tf_op jit(solution)/shard_map/ppermute | solution.py:134
  81.7 5.6 %collective-permute-start.13 = (bf16[2,16,4096]{2,1,0:T(8,128)(2,1)S(1)}, bf16[2,16,4096]{2,1,0:T(8,128)(2,1)S(1)}, u32[]{:S(2)}, u32[]{:S(2)}) collective-permute-start(bf16[2,16,4096]{2,1,0:T(8,128)(2,1)S(1)} %collective-permute-done.4), channel_id=1, source_target_pairs={{0,15},{1,0},{2,1},{3,2},{4,3},{5,4},{6,5},{7,6},{8,7},{9,8},{10,9... | collective-permute-start | bytes 786440 | tf_op jit(solution)/shard_map/ppermute | solution.py:134
  91.2 5.6 %collective-permute-start.14 = (bf16[2,16,4096]{2,1,0:T(8,128)(2,1)S(1)}, bf16[2,16,4096]{2,1,0:T(8,128)(2,1)S(1)}, u32[]{:S(2)}, u32[]{:S(2)}) collective-permute-start(bf16[2,16,4096]{2,1,0:T(8,128)(2,1)S(1)} %collective-permute-done.13), channel_id=1, source_target_pairs={{0,15},{1,0},{2,1},{3,2},{4,3},{5,4},{6,5},{7,6},{8,7},{9,8},{10,9... | collective-permute-start | bytes 786440 | tf_op jit(solution)/shard_map/ppermute | solution.py:134
  100.8 5.6 %collective-permute-start.15 = (bf16[2,16,4096]{2,1,0:T(8,128)(2,1)S(1)}, bf16[2,16,4096]{2,1,0:T(8,128)(2,1)S(1)}, u32[]{:S(2)}, u32[]{:S(2)}) collective-permute-start(bf16[2,16,4096]{2,1,0:T(8,128)(2,1)S(1)} %collective-permute-done.14), channel_id=1, source_target_pairs={{0,15},{1,0},{2,1},{3,2},{4,3},{5,4},{6,5},{7,6},{8,7},{9,8},{10,9... | collective-permute-start | bytes 786440 | tf_op jit(solution)/shard_map/ppermute | solution.py:134
  111.2 5.6 %collective-permute-start.21 = (bf16[2,16,2048]{2,1,0:T(8,128)(2,1)S(1)}, bf16[2,16,2048]{2,1,0:T(8,128)(2,1)S(1)}, u32[]{:S(2)}, u32[]{:S(2)}) collective-permute-start(bf16[2,16,2048]{2,1,0:T(8,128)(2,1)S(1)} %slice.303), channel_id=1, source_target_pairs={{0,15},{1,0},{2,1},{3,2},{4,3},{5,4},{6,5},{7,6},{8,7},{9,8},{10,9... | collective-permute-start | bytes 393224 | tf_op jit(solution)/shard_map/ppermute | solution.py:140
  136.9 5.1 %collective-permute-start.30 = (bf16[2,16,4096]{2,1,0:T(8,128)(2,1)S(1)}, bf16[2,16,4096]{2,1,0:T(8,128)(2,1)S(1)}, u32[]{:S(2)}, u32[]{:S(2)}) collective-permute-start(bf16[2,16,4096]{2,1,0:T(8,128)(2,1)S(1)} %bitcast.211), channel_id=1, source_target_pairs={{0,15},{1,0},{2,1},{3,2},{4,3},{5,4},{6,5},{7,6},{8,7},{9,8},{10,9... | collective-permute-start | bytes 786440 | tf_op jit(solution)/shard_map/ppermute | solution.py:191
  142.6 3.9 %collective-permute-done.22 = bf16[2,16,4096]{2,1,0:T(8,128)(2,1)S(1)} collective-permute-done((bf16[2,16,4096]{2,1,0:T(8,128)(2,1)S(1)}, bf16[2,16,4096]{2,1,0:T(8,128)(2,1)S(1)}, u32[]{:S(2)}, u32[]{:S(2)}) %collective-permute-start.22) | collective-permute-done | bytes 262176 | tf_op jit(solution)/shard_map/ppermute | solution.py:181
  149.7 5.1 %collective-permute-start.31 = (bf16[2,16,4096]{2,1,0:T(8,128)(2,1)S(1)}, bf16[2,16,4096]{2,1,0:T(8,128)(2,1)S(1)}, u32[]{:S(2)}, u32[]{:S(2)}) collective-permute-start(bf16[2,16,4096]{2,1,0:T(8,128)(2,1)S(1)} %fusion.24), channel_id=1, source_target_pairs={{0,15},{1,0},{2,1},{3,2},{4,3},{5,4},{6,5},{7,6},{8,7},{9,8},{10,9... | collective-permute-start | bytes 786440 | tf_op jit(solution)/shard_map/ppermute | solution.py:191
  154.8 3.8 %collective-permute-done.23 = bf16[2,16,4096]{2,1,0:T(8,128)(2,1)S(1)} collective-permute-done((bf16[2,16,4096]{2,1,0:T(8,128)(2,1)S(1)}, bf16[2,16,4096]{2,1,0:T(8,128)(2,1)S(1)}, u32[]{:S(2)}, u32[]{:S(2)}) %collective-permute-start.23) | collective-permute-done | bytes 262176 | tf_op jit(solution)/shard_map/ppermute | solution.py:181
  162.2 5.1 %collective-permute-start.32 = (bf16[2,16,4096]{2,1,0:T(8,128)(2,1)S(1)}, bf16[2,16,4096]{2,1,0:T(8,128)(2,1)S(1)}, u32[]{:S(2)}, u32[]{:S(2)}) collective-permute-start(bf16[2,16,4096]{2,1,0:T(8,128)(2,1)S(1)} %fusion.23), channel_id=1, source_target_pairs={{0,15},{1,0},{2,1},{3,2},{4,3},{5,4},{6,5},{7,6},{8,7},{9,8},{10,9... | collective-permute-start | bytes 786440 | tf_op jit(solution)/shard_map/ppermute | solution.py:191
  172.3 5.1 %collective-permute-start.33 = (bf16[2,16,4096]{2,1,0:T(8,128)(2,1)S(1)}, bf16[2,16,4096]{2,1,0:T(8,128)(2,1)S(1)}, u32[]{:S(2)}, u32[]{:S(2)}) collective-permute-start(bf16[2,16,4096]{2,1,0:T(8,128)(2,1)S(1)} %fusion.22), channel_id=1, source_target_pairs={{0,15},{1,0},{2,1},{3,2},{4,3},{5,4},{6,5},{7,6},{8,7},{9,8},{10,9... | collective-permute-start | bytes 786440 | tf_op jit(solution)/shard_map/ppermute | solution.py:191
  181.8 5.1 %collective-permute-start.34 = (bf16[2,16,4096]{2,1,0:T(8,128)(2,1)S(1)}, bf16[2,16,4096]{2,1,0:T(8,128)(2,1)S(1)}, u32[]{:S(2)}, u32[]{:S(2)}) collective-permute-start(bf16[2,16,4096]{2,1,0:T(8,128)(2,1)S(1)} %fusion.21), channel_id=1, source_target_pairs={{0,15},{1,0},{2,1},{3,2},{4,3},{5,4},{6,5},{7,6},{8,7},{9,8},{10,9... | collective-permute-start | bytes 786440 | tf_op jit(solution)/shard_map/ppermute | solution.py:191
  191.3 5.1 %collective-permute-start.35 = (bf16[2,16,4096]{2,1,0:T(8,128)(2,1)S(1)}, bf16[2,16,4096]{2,1,0:T(8,128)(2,1)S(1)}, u32[]{:S(2)}, u32[]{:S(2)}) collective-permute-start(bf16[2,16,4096]{2,1,0:T(8,128)(2,1)S(1)} %fusion.20), channel_id=1, source_target_pairs={{0,15},{1,0},{2,1},{3,2},{4,3},{5,4},{6,5},{7,6},{8,7},{9,8},{10,9... | collective-permute-start | bytes 786440 | tf_op jit(solution)/shard_map/ppermute | solution.py:191
  200.9 5.2 %collective-permute-start.36 = (bf16[2,16,4096]{2,1,0:T(8,128)(2,1)S(1)}, bf16[2,16,4096]{2,1,0:T(8,128)(2,1)S(1)}, u32[]{:S(2)}, u32[]{:S(2)}) collective-permute-start(bf16[2,16,4096]{2,1,0:T(8,128)(2,1)S(1)} %fusion.19), channel_id=1, source_target_pairs={{0,15},{1,0},{2,1},{3,2},{4,3},{5,4},{6,5},{7,6},{8,7},{9,8},{10,9... | collective-permute-start | bytes 786440 | tf_op jit(solution)/shard_map/ppermute | solution.py:191
  211.3 7.5 %collective-permute-done.29 = bf16[2,16,4096]{2,1,0:T(8,128)(2,1)S(1)} collective-permute-done((bf16[2,16,4096]{2,1,0:T(8,128)(2,1)S(1)}, bf16[2,16,4096]{2,1,0:T(8,128)(2,1)S(1)}, u32[]{:S(2)}, u32[]{:S(2)}) %collective-permute-start.29) | collective-permute-done | bytes 262176 | tf_op jit(solution)/shard_map/ppermute | solution.py:181
  (159 shorter events, 94.0 us)
Async XLA Ops:
  2.0 45.1 %collective-permute-start.8 = (bf16[1,256,1024]{2,1,0:T(8,128)(2,1)S(1)}, bf16[1,256,1024]{2,1,0:T(8,128)(2,1)S(1)}, u32[]{:S(2)}, u32[]{:S(2)}) collective-permute-start(bf16[1,256,1024]{2,1,0:T(8,128)(2,1)S(1)} %bitcast.163), channel_id=1, source_target_pairs={{0,128},{32,160},{64,192},{96,224},{128,256},{160,288},{192,320},{... | collective-permute-start | bytes 1572872 | tf_op jit(solution)/shard_map/ppermute | solution.py:51
  9.5 59.0 %collective-permute-start.10 = (bf16[1,256,1024]{2,1,0:T(8,128)(2,1)S(1)}, bf16[1,256,1024]{2,1,0:T(8,128)(2,1)S(1)}, u32[]{:S(2)}, u32[]{:S(2)}) collective-permute-start(bf16[1,256,1024]{2,1,0:T(8,128)(2,1)S(1)} %bitcast.164), channel_id=1, source_target_pairs={{0,384},{32,416},{64,448},{96,480},{128,0},{160,32},{192,64},{224,... | collective-permute-start | bytes 1572872 | tf_op jit(solution)/shard_map/ppermute | solution.py:53
  14.4 14.0 %all-to-all-start = ((bf16[16,2,4224]{2,1,0:T(2,128)(2,1)}), bf16[16,2,4224]{2,1,0:T(2,128)(2,1)S(1)}, u32[]{:S(2)}, u32[]{:S(2)}) async-start(bf16[16,2,4224]{2,1,0:T(2,128)(2,1)} %reshape.942), calls=%async_computation | async-start | bytes 540672 | tf_op jit(solution)/shard_map/all_to_all | solution.py:95
  36.7 15.3 %collective-permute-start.1 = (bf16[2,16,4096]{2,1,0:T(8,128)(2,1)S(1)}, bf16[2,16,4096]{2,1,0:T(8,128)(2,1)S(1)}, u32[]{:S(2)}, u32[]{:S(2)}) collective-permute-start(bf16[2,16,4096]{2,1,0:T(8,128)(2,1)S(1)} %pad_maximum_fusion.4), channel_id=1, source_target_pairs={{0,15},{1,0},{2,1},{3,2},{4,3},{5,4},{6,5},{7,6},{8,7},{9,8},{10,9... | collective-permute-start | bytes 786440 | tf_op jit(solution)/shard_map/ppermute | solution.py:134
  45.1 12.0 %collective-permute-start.5 = (bf16[2,16,4096]{2,1,0:T(8,128)(2,1)S(1)}, bf16[2,16,4096]{2,1,0:T(8,128)(2,1)S(1)}, u32[]{:S(2)}, u32[]{:S(2)}) collective-permute-start(bf16[2,16,4096]{2,1,0:T(8,128)(2,1)S(1)} %pad_maximum_fusion.4), channel_id=1, source_target_pairs={{0,1},{1,2},{2,3},{3,4},{4,5},{5,6},{6,7},{7,8},{8,9},{9,10},{10,1... | collective-permute-start | bytes 786440 | tf_op jit(solution)/shard_map/ppermute | solution.py:130
  47.1 21.5 %collective-permute-start.9 = (bf16[1,256,1024]{2,1,0:T(8,128)(2,1)S(1)}, bf16[1,256,1024]{2,1,0:T(8,128)(2,1)S(1)}, u32[]{:S(2)}, u32[]{:S(2)}) collective-permute-start(bf16[1,256,1024]{2,1,0:T(8,128)(2,1)S(1)} %collective-permute-done.8), channel_id=1, source_target_pairs={{0,128},{32,160},{64,192},{96,224},{128,256},{160,288},{192,320},{... | collective-permute-start | bytes 1572872 | tf_op jit(solution)/shard_map/ppermute | solution.py:52
  61.0 11.6 %collective-permute-start.3 = (bf16[2,16,4096]{2,1,0:T(8,128)(2,1)S(1)}, bf16[2,16,4096]{2,1,0:T(8,128)(2,1)S(1)}, u32[]{:S(2)}, u32[]{:S(2)}) collective-permute-start(bf16[2,16,4096]{2,1,0:T(8,128)(2,1)S(1)} %collective-permute-done.2), channel_id=1, source_target_pairs={{0,15},{1,0},{2,1},{3,2},{4,3},{5,4},{6,5},{7,6},{8,7},{9,8},{10,9... | collective-permute-start | bytes 786440 | tf_op jit(solution)/shard_map/ppermute | solution.py:134
  66.6 11.2 %collective-permute-start.7 = (bf16[2,16,4096]{2,1,0:T(8,128)(2,1)S(1)}, bf16[2,16,4096]{2,1,0:T(8,128)(2,1)S(1)}, u32[]{:S(2)}, u32[]{:S(2)}) collective-permute-start(bf16[2,16,4096]{2,1,0:T(8,128)(2,1)S(1)} %collective-permute-done.6), channel_id=1, source_target_pairs={{0,1},{1,2},{2,3},{3,4},{4,5},{5,6},{6,7},{7,8},{8,9},{9,10},{10,1... | collective-permute-start | bytes 786440 | tf_op jit(solution)/shard_map/ppermute | solution.py:130
  68.8 50.5 %collective-permute-start.11 = (bf16[4,256,1024]{2,1,0:T(8,128)(2,1)S(1)}, bf16[4,256,1024]{2,1,0:T(8,128)(2,1)S(1)}, u32[]{:S(2)}, u32[]{:S(2)}) collective-permute-start(bf16[4,256,1024]{2,1,0:T(8,128)(2,1)S(1)} %pad_maximum_fusion), channel_id=1, source_target_pairs={{0,64},{32,96},{64,0},{96,32},{128,192},{160,224},{192,128},{224,1... | collective-permute-start | bytes 6291464 | tf_op jit(solution)/shard_map/ppermute | solution.py:55
  77.8 9.6 %collective-permute-start.16 = (bf16[2,16,4096]{2,1,0:T(8,128)(2,1)S(1)}, bf16[2,16,4096]{2,1,0:T(8,128)(2,1)S(1)}, u32[]{:S(2)}, u32[]{:S(2)}) collective-permute-start(bf16[2,16,4096]{2,1,0:T(8,128)(2,1)S(1)} %collective-permute-done.7), channel_id=1, source_target_pairs={{0,1},{1,2},{2,3},{3,4},{4,5},{5,6},{6,7},{7,8},{8,9},{9,10},{10,1... | collective-permute-start | bytes 786440 | tf_op jit(solution)/shard_map/ppermute | solution.py:130
  81.7 9.5 %collective-permute-start.13 = (bf16[2,16,4096]{2,1,0:T(8,128)(2,1)S(1)}, bf16[2,16,4096]{2,1,0:T(8,128)(2,1)S(1)}, u32[]{:S(2)}, u32[]{:S(2)}) collective-permute-start(bf16[2,16,4096]{2,1,0:T(8,128)(2,1)S(1)} %collective-permute-done.4), channel_id=1, source_target_pairs={{0,15},{1,0},{2,1},{3,2},{4,3},{5,4},{6,5},{7,6},{8,7},{9,8},{10,9... | collective-permute-start | bytes 786440 | tf_op jit(solution)/shard_map/ppermute | solution.py:134
  91.2 9.6 %collective-permute-start.14 = (bf16[2,16,4096]{2,1,0:T(8,128)(2,1)S(1)}, bf16[2,16,4096]{2,1,0:T(8,128)(2,1)S(1)}, u32[]{:S(2)}, u32[]{:S(2)}) collective-permute-start(bf16[2,16,4096]{2,1,0:T(8,128)(2,1)S(1)} %collective-permute-done.13), channel_id=1, source_target_pairs={{0,15},{1,0},{2,1},{3,2},{4,3},{5,4},{6,5},{7,6},{8,7},{9,8},{10,9... | collective-permute-start | bytes 786440 | tf_op jit(solution)/shard_map/ppermute | solution.py:134
  96.8 9.9 %collective-permute-start.18 = (bf16[2,16,4096]{2,1,0:T(8,128)(2,1)S(1)}, bf16[2,16,4096]{2,1,0:T(8,128)(2,1)S(1)}, u32[]{:S(2)}, u32[]{:S(2)}) collective-permute-start(bf16[2,16,4096]{2,1,0:T(8,128)(2,1)S(1)} %collective-permute-done.17), channel_id=1, source_target_pairs={{0,1},{1,2},{2,3},{3,4},{4,5},{5,6},{6,7},{7,8},{8,9},{9,10},{10,1... | collective-permute-start | bytes 786440 | tf_op jit(solution)/shard_map/ppermute | solution.py:130
  100.8 10.4 %collective-permute-start.15 = (bf16[2,16,4096]{2,1,0:T(8,128)(2,1)S(1)}, bf16[2,16,4096]{2,1,0:T(8,128)(2,1)S(1)}, u32[]{:S(2)}, u32[]{:S(2)}) collective-permute-start(bf16[2,16,4096]{2,1,0:T(8,128)(2,1)S(1)} %collective-permute-done.14), channel_id=1, source_target_pairs={{0,15},{1,0},{2,1},{3,2},{4,3},{5,4},{6,5},{7,6},{8,7},{9,8},{10,9... | collective-permute-start | bytes 786440 | tf_op jit(solution)/shard_map/ppermute | solution.py:134
  106.7 10.6 %collective-permute-start.19 = (bf16[2,16,4096]{2,1,0:T(8,128)(2,1)S(1)}, bf16[2,16,4096]{2,1,0:T(8,128)(2,1)S(1)}, u32[]{:S(2)}, u32[]{:S(2)}) collective-permute-start(bf16[2,16,4096]{2,1,0:T(8,128)(2,1)S(1)} %collective-permute-done.18), channel_id=1, source_target_pairs={{0,1},{1,2},{2,3},{3,4},{4,5},{5,6},{6,7},{7,8},{8,9},{9,10},{10,1... | collective-permute-start | bytes 786440 | tf_op jit(solution)/shard_map/ppermute | solution.py:130
  111.2 11.2 %collective-permute-start.21 = (bf16[2,16,2048]{2,1,0:T(8,128)(2,1)S(1)}, bf16[2,16,2048]{2,1,0:T(8,128)(2,1)S(1)}, u32[]{:S(2)}, u32[]{:S(2)}) collective-permute-start(bf16[2,16,2048]{2,1,0:T(8,128)(2,1)S(1)} %slice.303), channel_id=1, source_target_pairs={{0,15},{1,0},{2,1},{3,2},{4,3},{5,4},{6,5},{7,6},{8,7},{9,8},{10,9... | collective-permute-start | bytes 393224 | tf_op jit(solution)/shard_map/ppermute | solution.py:140
  134.8 11.7 %collective-permute-start.22 = (bf16[2,16,4096]{2,1,0:T(8,128)(2,1)S(1)}, bf16[2,16,4096]{2,1,0:T(8,128)(2,1)S(1)}, u32[]{:S(2)}, u32[]{:S(2)}) collective-permute-start(bf16[2,16,4096]{2,1,0:T(8,128)(2,1)S(1)} %bitcast.212), channel_id=1, source_target_pairs={{0,1},{1,2},{2,3},{3,4},{4,5},{5,6},{6,7},{7,8},{8,9},{9,10},{10,1... | collective-permute-start | bytes 786440 | tf_op jit(solution)/shard_map/ppermute | solution.py:181
  136.9 12.7 %collective-permute-start.30 = (bf16[2,16,4096]{2,1,0:T(8,128)(2,1)S(1)}, bf16[2,16,4096]{2,1,0:T(8,128)(2,1)S(1)}, u32[]{:S(2)}, u32[]{:S(2)}) collective-permute-start(bf16[2,16,4096]{2,1,0:T(8,128)(2,1)S(1)} %bitcast.211), channel_id=1, source_target_pairs={{0,15},{1,0},{2,1},{3,2},{4,3},{5,4},{6,5},{7,6},{8,7},{9,8},{10,9... | collective-permute-start | bytes 786440 | tf_op jit(solution)/shard_map/ppermute | solution.py:191
  147.7 10.9 %collective-permute-start.23 = (bf16[2,16,4096]{2,1,0:T(8,128)(2,1)S(1)}, bf16[2,16,4096]{2,1,0:T(8,128)(2,1)S(1)}, u32[]{:S(2)}, u32[]{:S(2)}) collective-permute-start(bf16[2,16,4096]{2,1,0:T(8,128)(2,1)S(1)} %fusion.31), channel_id=1, source_target_pairs={{0,1},{1,2},{2,3},{3,4},{4,5},{5,6},{6,7},{7,8},{8,9},{9,10},{10,1... | collective-permute-start | bytes 786440 | tf_op jit(solution)/shard_map/ppermute | solution.py:181
  149.7 12.4 %collective-permute-start.31 = (bf16[2,16,4096]{2,1,0:T(8,128)(2,1)S(1)}, bf16[2,16,4096]{2,1,0:T(8,128)(2,1)S(1)}, u32[]{:S(2)}, u32[]{:S(2)}) collective-permute-start(bf16[2,16,4096]{2,1,0:T(8,128)(2,1)S(1)} %fusion.24), channel_id=1, source_target_pairs={{0,15},{1,0},{2,1},{3,2},{4,3},{5,4},{6,5},{7,6},{8,7},{9,8},{10,9... | collective-permute-start | bytes 786440 | tf_op jit(solution)/shard_map/ppermute | solution.py:191
  160.1 10.0 %collective-permute-start.24 = (bf16[2,16,4096]{2,1,0:T(8,128)(2,1)S(1)}, bf16[2,16,4096]{2,1,0:T(8,128)(2,1)S(1)}, u32[]{:S(2)}, u32[]{:S(2)}) collective-permute-start(bf16[2,16,4096]{2,1,0:T(8,128)(2,1)S(1)} %fusion.30), channel_id=1, source_target_pairs={{0,1},{1,2},{2,3},{3,4},{4,5},{5,6},{6,7},{7,8},{8,9},{9,10},{10,1... | collective-permute-start | bytes 786440 | tf_op jit(solution)/shard_map/ppermute | solution.py:181
  162.2 10.0 %collective-permute-start.32 = (bf16[2,16,4096]{2,1,0:T(8,128)(2,1)S(1)}, bf16[2,16,4096]{2,1,0:T(8,128)(2,1)S(1)}, u32[]{:S(2)}, u32[]{:S(2)}) collective-permute-start(bf16[2,16,4096]{2,1,0:T(8,128)(2,1)S(1)} %fusion.23), channel_id=1, source_target_pairs={{0,15},{1,0},{2,1},{3,2},{4,3},{5,4},{6,5},{7,6},{8,7},{9,8},{10,9... | collective-permute-start | bytes 786440 | tf_op jit(solution)/shard_map/ppermute | solution.py:191
  198.9 10.4 %collective-permute-start.28 = (bf16[2,16,4096]{2,1,0:T(8,128)(2,1)S(1)}, bf16[2,16,4096]{2,1,0:T(8,128)(2,1)S(1)}, u32[]{:S(2)}, u32[]{:S(2)}) collective-permute-start(bf16[2,16,4096]{2,1,0:T(8,128)(2,1)S(1)} %fusion.26), channel_id=1, source_target_pairs={{0,1},{1,2},{2,3},{3,4},{4,5},{5,6},{6,7},{7,8},{8,9},{9,10},{10,1... | collective-permute-start | bytes 786440 | tf_op jit(solution)/shard_map/ppermute | solution.py:181
  200.9 10.4 %collective-permute-start.36 = (bf16[2,16,4096]{2,1,0:T(8,128)(2,1)S(1)}, bf16[2,16,4096]{2,1,0:T(8,128)(2,1)S(1)}, u32[]{:S(2)}, u32[]{:S(2)}) collective-permute-start(bf16[2,16,4096]{2,1,0:T(8,128)(2,1)S(1)} %fusion.19), channel_id=1, source_target_pairs={{0,15},{1,0},{2,1},{3,2},{4,3},{5,4},{6,5},{7,6},{8,7},{9,8},{10,9... | collective-permute-start | bytes 786440 | tf_op jit(solution)/shard_map/ppermute | solution.py:191
  (18 other events, 153.7 us)

commit v12 on v11

--- a/solution.py
+++ b/solution.py
@@ -176,21 +176,31 @@
 
     place(0, hiddens[0])
 
-    fwd = blocks[nz // 2]
-    for s in range(nz // 2):
+    f32 = lambda v: v.astype(jnp.float32)
+    bf16 = lambda v: v.astype(jnp.bfloat16)
+    half = feature_count // 2
+    far = nz // 2
+    fwd = blocks[far][..., :half]
+    for s in range(far):
         got = lax.ppermute(fwd, "tensor", TP_Z_FWD)
         if s < len(groups) - 1:
             late, got = lax.optimization_barrier((hiddens[s + 1], got))
             place(s + 1, late)
-        if s < nz // 2 - 1:
-            fwd = (got.astype(jnp.float32) + blocks[nz // 2 - 1 - s].astype(jnp.float32)).astype(jnp.bfloat16)
+        k = far - 1 - s
+        if s == 0:
+            fwd = jnp.concatenate([bf16(f32(got) + f32(blocks[k][..., :half])), blocks[k][..., half:]], axis=-1)
+        elif s < far - 1:
+            fwd = bf16(f32(got) + f32(blocks[k]))
         else:
             fwd_total = got
-    bwd = blocks[nz // 2 + 1]
-    for s in range(nz // 2 - 1):
+    bwd = blocks[far][..., half:]
+    for s in range(far):
         got = lax.ppermute(bwd, "tensor", TP_Z_BWD)
-        if s < nz // 2 - 2:
-            bwd = (got.astype(jnp.float32) + blocks[nz // 2 + 2 + s].astype(jnp.float32)).astype(jnp.bfloat16)
+        k = far + 1 + s
+        if s == 0:
+            bwd = jnp.concatenate([blocks[k][..., :half], bf16(f32(got) + f32(blocks[k][..., half:]))], axis=-1)
+        elif s < far - 1:
+            bwd = bf16(f32(got) + f32(blocks[k]))
         else:
             bwd_total = got
     column_sum = (

time: 230 us -> 233 us (1.013)
  starting transfers between devices: 144 us -> 152 us
  waiting for transfers between devices: 57.1 us -> 52.8 us
    ppermute x8, waiting for transfers between devices: 28.2 us -> 12.3 us  [per_device(): got = lax.ppermute(fwd, 'tensor', TP_Z_FWD)]
    ppermute x7 -> x8, waiting for transfers between devices: 0.02 us -> 11.9 us  [per_device(): got = lax.ppermute(bwd, 'tensor', TP_Z_BWD)]
    ppermute x7 -> x8, starting transfers between devices: 36 us -> 43.7 us  [per_device(): got = lax.ppermute(bwd, 'tensor', TP_Z_BWD)]
  transfers between devices with their start and end apart: 39 -> 40, of which waited for: 20 -> 23; matrix products, arithmetic and copies ran while one was open for 6% -> 6% of each run, Pallas kernels for 0% -> 0%
where the time goes in v12:
time: 233 us; the launch traced here: 230 us
  starting transfers between devices  152 us (65%)
  waiting for transfers between devices  52.8 us (23%)
  matrix products  11.9 us (5%)
  local copies, waits for them, and re-layouts  7.89 us (3%)
  other arithmetic  3.69 us (2%)
    ppermute x8, starting transfers between devices, per_device(): got = lax.ppermute(bwd, 'tensor', TP_Z_BWD)  43.7 us
    ppermute x7, starting transfers between devices, per_device(): bwd = lax.ppermute(bwd, 'tensor', TP_Z_BWD)  41 us
    ppermute x8, starting transfers between devices, per_device(): got = lax.ppermute(fwd, 'tensor', TP_Z_FWD)  15.4 us
    ppermute x7, starting transfers between devices, per_device(): fwd = lax.ppermute(fwd, 'tensor', TP_Z_FWD)  13.4 us
    ppermute x8, waiting for transfers between devices, per_device(): got = lax.ppermute(fwd, 'tensor', TP_Z_FWD)  12.3 us
    ppermute x8, waiting for transfers between devices, per_device(): got = lax.ppermute(bwd, 'tensor', TP_Z_BWD)  11.9 us
    ppermute x7, waiting for transfers between devices, per_device(): bwd = lax.ppermute(bwd, 'tensor', TP_Z_BWD)  9.26 us
    dot_general x18, matrix products, ffn(): jnp.dot(rows[:, col:col + width], buf.reshape(width, 2 * ff_cols), prefer...  8.33 us
  transfers between devices with their start and end apart: 40, of which 23 were waited for; matrix products, arithmetic and copies ran while one was open for 6% of the time, Pallas kernels for 0%

profile of v12, /device:TPU:24, one launch (start us, length us, event | category | flops | bytes accessed | tf_op | source)
XLA Modules:
  0.0 229.9 jit_solution(4887522490223801154)
XLA Ops:
  2.0 7.5 %collective-permute-start.8 = (bf16[1,256,1024]{2,1,0:T(8,128)(2,1)S(1)}, bf16[1,256,1024]{2,1,0:T(8,128)(2,1)S(1)}, u32[]{:S(2)}, u32[]{:S(2)}) collective-permute-start(bf16[1,256,1024]{2,1,0:T(8,128)(2,1)S(1)} %bitcast.162), channel_id=1, source_target_pairs={{0,128},{32,160},{64,192},{96,224},{128,256},{160,288},{192,320},{... | collective-permute-start | bytes 1572872 | tf_op jit(solution)/shard_map/ppermute | solution.py:51
  14.4 6.6 %all-to-all-start = ((bf16[16,2,4224]{2,1,0:T(2,128)(2,1)}), bf16[16,2,4224]{2,1,0:T(2,128)(2,1)S(1)}, u32[]{:S(2)}, u32[]{:S(2)}) async-start(bf16[16,2,4224]{2,1,0:T(2,128)(2,1)} %reshape.940), calls=%async_computation | async-start | bytes 540672 | tf_op jit(solution)/shard_map/all_to_all | solution.py:95
  22.2 6.2 %all-to-all-done = bf16[16,2,4224]{2,1,0:T(2,128)(2,1)S(1)} async-done(((bf16[16,2,4224]{2,1,0:T(2,128)(2,1)}), bf16[16,2,4224]{2,1,0:T(2,128)(2,1)S(1)}, u32[]{:S(2)}, u32[]{:S(2)}) %all-to-all-start) | async-done | bytes 270368 | tf_op jit(solution)/shard_map/all_to_all | solution.py:95
  31.7 5.0 %collective-permute-done = bf16[16,4096]{1,0:T(8,128)(2,1)S(1)} collective-permute-done((bf16[16,4096]{1,0:T(8,128)(2,1)S(1)}, bf16[16,4096]{1,0:T(8,128)(2,1)S(1)}, u32[]{:S(2)}, u32[]{:S(2)}) %collective-permute-start) | collective-permute-done | bytes 131104 | tf_op jit(solution)/shard_map/ppermute | solution.py:126
  36.7 8.4 %collective-permute-start.1 = (bf16[2,16,4096]{2,1,0:T(8,128)(2,1)S(1)}, bf16[2,16,4096]{2,1,0:T(8,128)(2,1)S(1)}, u32[]{:S(2)}, u32[]{:S(2)}) collective-permute-start(bf16[2,16,4096]{2,1,0:T(8,128)(2,1)S(1)} %pad_maximum_fusion.4), channel_id=1, source_target_pairs={{0,15},{1,0},{2,1},{3,2},{4,3},{5,4},{6,5},{7,6},{8,7},{9,8},{10,9... | collective-permute-start | bytes 786440 | tf_op jit(solution)/shard_map/ppermute | solution.py:134
  47.1 4.0 %collective-permute-start.9 = (bf16[1,256,1024]{2,1,0:T(8,128)(2,1)S(1)}, bf16[1,256,1024]{2,1,0:T(8,128)(2,1)S(1)}, u32[]{:S(2)}, u32[]{:S(2)}) collective-permute-start(bf16[1,256,1024]{2,1,0:T(8,128)(2,1)S(1)} %collective-permute-done.8), channel_id=1, source_target_pairs={{0,128},{32,160},{64,192},{96,224},{128,256},{160,288},{192,320},{... | collective-permute-start | bytes 1572872 | tf_op jit(solution)/shard_map/ppermute | solution.py:52
  52.0 5.1 %collective-permute-start.2 = (bf16[2,16,4096]{2,1,0:T(8,128)(2,1)S(1)}, bf16[2,16,4096]{2,1,0:T(8,128)(2,1)S(1)}, u32[]{:S(2)}, u32[]{:S(2)}) collective-permute-start(bf16[2,16,4096]{2,1,0:T(8,128)(2,1)S(1)} %collective-permute-done.1), channel_id=1, source_target_pairs={{0,15},{1,0},{2,1},{3,2},{4,3},{5,4},{6,5},{7,6},{8,7},{9,8},{10,9... | collective-permute-start | bytes 786440 | tf_op jit(solution)/shard_map/ppermute | solution.py:134
  61.0 5.6 %collective-permute-start.3 = (bf16[2,16,4096]{2,1,0:T(8,128)(2,1)S(1)}, bf16[2,16,4096]{2,1,0:T(8,128)(2,1)S(1)}, u32[]{:S(2)}, u32[]{:S(2)}) collective-permute-start(bf16[2,16,4096]{2,1,0:T(8,128)(2,1)S(1)} %collective-permute-done.2), channel_id=1, source_target_pairs={{0,15},{1,0},{2,1},{3,2},{4,3},{5,4},{6,5},{7,6},{8,7},{9,8},{10,9... | collective-permute-start | bytes 786440 | tf_op jit(solution)/shard_map/ppermute | solution.py:134
  68.9 3.7 %collective-permute-start.11 = (bf16[4,256,1024]{2,1,0:T(8,128)(2,1)S(1)}, bf16[4,256,1024]{2,1,0:T(8,128)(2,1)S(1)}, u32[]{:S(2)}, u32[]{:S(2)}) collective-permute-start(bf16[4,256,1024]{2,1,0:T(8,128)(2,1)S(1)} %pad_maximum_fusion), channel_id=1, source_target_pairs={{0,64},{32,96},{64,0},{96,32},{128,192},{160,224},{192,128},{224,1... | collective-permute-start | bytes 6291464 | tf_op jit(solution)/shard_map/ppermute | solution.py:55
  72.7 5.1 %collective-permute-start.4 = (bf16[2,16,4096]{2,1,0:T(8,128)(2,1)S(1)}, bf16[2,16,4096]{2,1,0:T(8,128)(2,1)S(1)}, u32[]{:S(2)}, u32[]{:S(2)}) collective-permute-start(bf16[2,16,4096]{2,1,0:T(8,128)(2,1)S(1)} %collective-permute-done.3), channel_id=1, source_target_pairs={{0,15},{1,0},{2,1},{3,2},{4,3},{5,4},{6,5},{7,6},{8,7},{9,8},{10,9... | collective-permute-start | bytes 786440 | tf_op jit(solution)/shard_map/ppermute | solution.py:134
  81.7 5.6 %collective-permute-start.13 = (bf16[2,16,4096]{2,1,0:T(8,128)(2,1)S(1)}, bf16[2,16,4096]{2,1,0:T(8,128)(2,1)S(1)}, u32[]{:S(2)}, u32[]{:S(2)}) collective-permute-start(bf16[2,16,4096]{2,1,0:T(8,128)(2,1)S(1)} %collective-permute-done.4), channel_id=1, source_target_pairs={{0,15},{1,0},{2,1},{3,2},{4,3},{5,4},{6,5},{7,6},{8,7},{9,8},{10,9... | collective-permute-start | bytes 786440 | tf_op jit(solution)/shard_map/ppermute | solution.py:134
  91.2 5.6 %collective-permute-start.14 = (bf16[2,16,4096]{2,1,0:T(8,128)(2,1)S(1)}, bf16[2,16,4096]{2,1,0:T(8,128)(2,1)S(1)}, u32[]{:S(2)}, u32[]{:S(2)}) collective-permute-start(bf16[2,16,4096]{2,1,0:T(8,128)(2,1)S(1)} %collective-permute-done.13), channel_id=1, source_target_pairs={{0,15},{1,0},{2,1},{3,2},{4,3},{5,4},{6,5},{7,6},{8,7},{9,8},{10,9... | collective-permute-start | bytes 786440 | tf_op jit(solution)/shard_map/ppermute | solution.py:134
  100.8 5.6 %collective-permute-start.15 = (bf16[2,16,4096]{2,1,0:T(8,128)(2,1)S(1)}, bf16[2,16,4096]{2,1,0:T(8,128)(2,1)S(1)}, u32[]{:S(2)}, u32[]{:S(2)}) collective-permute-start(bf16[2,16,4096]{2,1,0:T(8,128)(2,1)S(1)} %collective-permute-done.14), channel_id=1, source_target_pairs={{0,15},{1,0},{2,1},{3,2},{4,3},{5,4},{6,5},{7,6},{8,7},{9,8},{10,9... | collective-permute-start | bytes 786440 | tf_op jit(solution)/shard_map/ppermute | solution.py:134
  111.2 5.6 %collective-permute-start.21 = (bf16[2,16,2048]{2,1,0:T(8,128)(2,1)S(1)}, bf16[2,16,2048]{2,1,0:T(8,128)(2,1)S(1)}, u32[]{:S(2)}, u32[]{:S(2)}) collective-permute-start(bf16[2,16,2048]{2,1,0:T(8,128)(2,1)S(1)} %slice.327), channel_id=1, source_target_pairs={{0,15},{1,0},{2,1},{3,2},{4,3},{5,4},{6,5},{7,6},{8,7},{9,8},{10,9... | collective-permute-start | bytes 393224 | tf_op jit(solution)/shard_map/ppermute | solution.py:140
  136.7 5.1 %collective-permute-start.30 = (bf16[2,16,2048]{2,1,0:T(8,128)(2,1)S(1)}, bf16[2,16,2048]{2,1,0:T(8,128)(2,1)S(1)}, u32[]{:S(2)}, u32[]{:S(2)}) collective-permute-start(bf16[2,16,2048]{2,1,0:T(8,128)(2,1)S(1)} %get-tuple-element.29), channel_id=1, source_target_pairs={{0,15},{1,0},{2,1},{3,2},{4,3},{5,4},{6,5},{7,6},{8,7},{9,8},{10,9... | collective-permute-start | bytes 393224 | tf_op jit(solution)/shard_map/ppermute | solution.py:198
  146.9 5.1 %collective-permute-start.31 = (bf16[2,16,4096]{2,1,0:T(8,128)(2,1)S(1)}, bf16[2,16,4096]{2,1,0:T(8,128)(2,1)S(1)}, u32[]{:S(2)}, u32[]{:S(2)}) collective-permute-start(bf16[2,16,4096]{2,1,0:T(8,128)(2,1)S(1)} %pad_maximum_fusion.7), channel_id=1, source_target_pairs={{0,15},{1,0},{2,1},{3,2},{4,3},{5,4},{6,5},{7,6},{8,7},{9,8},{10,9... | collective-permute-start | bytes 786440 | tf_op jit(solution)/shard_map/ppermute | solution.py:198
  152.1 3.8 %collective-permute-done.23 = bf16[2,16,4096]{2,1,0:T(8,128)(2,1)S(1)} collective-permute-done((bf16[2,16,4096]{2,1,0:T(8,128)(2,1)S(1)}, bf16[2,16,4096]{2,1,0:T(8,128)(2,1)S(1)}, u32[]{:S(2)}, u32[]{:S(2)}) %collective-permute-start.23) | collective-permute-done | bytes 262176 | tf_op jit(solution)/shard_map/ppermute | solution.py:185
  157.4 5.4 %collective-permute-start.32 = (bf16[2,16,4096]{2,1,0:T(8,128)(2,1)S(1)}, bf16[2,16,4096]{2,1,0:T(8,128)(2,1)S(1)}, u32[]{:S(2)}, u32[]{:S(2)}) collective-permute-start(bf16[2,16,4096]{2,1,0:T(8,128)(2,1)S(1)} %fusion.24), channel_id=1, source_target_pairs={{0,15},{1,0},{2,1},{3,2},{4,3},{5,4},{6,5},{7,6},{8,7},{9,8},{10,9... | collective-permute-start | bytes 786440 | tf_op jit(solution)/shard_map/ppermute | solution.py:198
  167.0 5.6 %collective-permute-start.33 = (bf16[2,16,4096]{2,1,0:T(8,128)(2,1)S(1)}, bf16[2,16,4096]{2,1,0:T(8,128)(2,1)S(1)}, u32[]{:S(2)}, u32[]{:S(2)}) collective-permute-start(bf16[2,16,4096]{2,1,0:T(8,128)(2,1)S(1)} %fusion.23), channel_id=1, source_target_pairs={{0,15},{1,0},{2,1},{3,2},{4,3},{5,4},{6,5},{7,6},{8,7},{9,8},{10,9... | collective-permute-start | bytes 786440 | tf_op jit(solution)/shard_map/ppermute | solution.py:198
  176.6 5.6 %collective-permute-start.34 = (bf16[2,16,4096]{2,1,0:T(8,128)(2,1)S(1)}, bf16[2,16,4096]{2,1,0:T(8,128)(2,1)S(1)}, u32[]{:S(2)}, u32[]{:S(2)}) collective-permute-start(bf16[2,16,4096]{2,1,0:T(8,128)(2,1)S(1)} %fusion.22), channel_id=1, source_target_pairs={{0,15},{1,0},{2,1},{3,2},{4,3},{5,4},{6,5},{7,6},{8,7},{9,8},{10,9... | collective-permute-start | bytes 786440 | tf_op jit(solution)/shard_map/ppermute | solution.py:198
  186.1 5.6 %collective-permute-start.35 = (bf16[2,16,4096]{2,1,0:T(8,128)(2,1)S(1)}, bf16[2,16,4096]{2,1,0:T(8,128)(2,1)S(1)}, u32[]{:S(2)}, u32[]{:S(2)}) collective-permute-start(bf16[2,16,4096]{2,1,0:T(8,128)(2,1)S(1)} %fusion.21), channel_id=1, source_target_pairs={{0,15},{1,0},{2,1},{3,2},{4,3},{5,4},{6,5},{7,6},{8,7},{9,8},{10,9... | collective-permute-start | bytes 786440 | tf_op jit(solution)/shard_map/ppermute | solution.py:198
  195.8 5.6 %collective-permute-start.36 = (bf16[2,16,4096]{2,1,0:T(8,128)(2,1)S(1)}, bf16[2,16,4096]{2,1,0:T(8,128)(2,1)S(1)}, u32[]{:S(2)}, u32[]{:S(2)}) collective-permute-start(bf16[2,16,4096]{2,1,0:T(8,128)(2,1)S(1)} %fusion.20), channel_id=1, source_target_pairs={{0,15},{1,0},{2,1},{3,2},{4,3},{5,4},{6,5},{7,6},{8,7},{9,8},{10,9... | collective-permute-start | bytes 786440 | tf_op jit(solution)/shard_map/ppermute | solution.py:198
  206.5 5.6 %collective-permute-start.37 = (bf16[2,16,4096]{2,1,0:T(8,128)(2,1)S(1)}, bf16[2,16,4096]{2,1,0:T(8,128)(2,1)S(1)}, u32[]{:S(2)}, u32[]{:S(2)}) collective-permute-start(bf16[2,16,4096]{2,1,0:T(8,128)(2,1)S(1)} %fusion.19), channel_id=1, source_target_pairs={{0,15},{1,0},{2,1},{3,2},{4,3},{5,4},{6,5},{7,6},{8,7},{9,8},{10,9... | collective-permute-start | bytes 786440 | tf_op jit(solution)/shard_map/ppermute | solution.py:198
  216.0 6.3 %collective-permute-done.29 = bf16[2,16,4096]{2,1,0:T(8,128)(2,1)S(1)} collective-permute-done((bf16[2,16,4096]{2,1,0:T(8,128)(2,1)S(1)}, bf16[2,16,4096]{2,1,0:T(8,128)(2,1)S(1)}, u32[]{:S(2)}, u32[]{:S(2)}) %collective-permute-start.29) | collective-permute-done | bytes 262176 | tf_op jit(solution)/shard_map/ppermute | solution.py:185
  (167 shorter events, 94.9 us)
Async XLA Ops:
  2.0 45.1 %collective-permute-start.8 = (bf16[1,256,1024]{2,1,0:T(8,128)(2,1)S(1)}, bf16[1,256,1024]{2,1,0:T(8,128)(2,1)S(1)}, u32[]{:S(2)}, u32[]{:S(2)}) collective-permute-start(bf16[1,256,1024]{2,1,0:T(8,128)(2,1)S(1)} %bitcast.162), channel_id=1, source_target_pairs={{0,128},{32,160},{64,192},{96,224},{128,256},{160,288},{192,320},{... | collective-permute-start | bytes 1572872 | tf_op jit(solution)/shard_map/ppermute | solution.py:51
  9.5 59.1 %collective-permute-start.10 = (bf16[1,256,1024]{2,1,0:T(8,128)(2,1)S(1)}, bf16[1,256,1024]{2,1,0:T(8,128)(2,1)S(1)}, u32[]{:S(2)}, u32[]{:S(2)}) collective-permute-start(bf16[1,256,1024]{2,1,0:T(8,128)(2,1)S(1)} %bitcast.163), channel_id=1, source_target_pairs={{0,384},{32,416},{64,448},{96,480},{128,0},{160,32},{192,64},{224,... | collective-permute-start | bytes 1572872 | tf_op jit(solution)/shard_map/ppermute | solution.py:53
  14.4 14.0 %all-to-all-start = ((bf16[16,2,4224]{2,1,0:T(2,128)(2,1)}), bf16[16,2,4224]{2,1,0:T(2,128)(2,1)S(1)}, u32[]{:S(2)}, u32[]{:S(2)}) async-start(bf16[16,2,4224]{2,1,0:T(2,128)(2,1)} %reshape.940), calls=%async_computation | async-start | bytes 540672 | tf_op jit(solution)/shard_map/all_to_all | solution.py:95
  36.7 15.3 %collective-permute-start.1 = (bf16[2,16,4096]{2,1,0:T(8,128)(2,1)S(1)}, bf16[2,16,4096]{2,1,0:T(8,128)(2,1)S(1)}, u32[]{:S(2)}, u32[]{:S(2)}) collective-permute-start(bf16[2,16,4096]{2,1,0:T(8,128)(2,1)S(1)} %pad_maximum_fusion.4), channel_id=1, source_target_pairs={{0,15},{1,0},{2,1},{3,2},{4,3},{5,4},{6,5},{7,6},{8,7},{9,8},{10,9... | collective-permute-start | bytes 786440 | tf_op jit(solution)/shard_map/ppermute | solution.py:134
  45.1 12.0 %collective-permute-start.5 = (bf16[2,16,4096]{2,1,0:T(8,128)(2,1)S(1)}, bf16[2,16,4096]{2,1,0:T(8,128)(2,1)S(1)}, u32[]{:S(2)}, u32[]{:S(2)}) collective-permute-start(bf16[2,16,4096]{2,1,0:T(8,128)(2,1)S(1)} %pad_maximum_fusion.4), channel_id=1, source_target_pairs={{0,1},{1,2},{2,3},{3,4},{4,5},{5,6},{6,7},{7,8},{8,9},{9,10},{10,1... | collective-permute-start | bytes 786440 | tf_op jit(solution)/shard_map/ppermute | solution.py:130
  47.1 21.5 %collective-permute-start.9 = (bf16[1,256,1024]{2,1,0:T(8,128)(2,1)S(1)}, bf16[1,256,1024]{2,1,0:T(8,128)(2,1)S(1)}, u32[]{:S(2)}, u32[]{:S(2)}) collective-permute-start(bf16[1,256,1024]{2,1,0:T(8,128)(2,1)S(1)} %collective-permute-done.8), channel_id=1, source_target_pairs={{0,128},{32,160},{64,192},{96,224},{128,256},{160,288},{192,320},{... | collective-permute-start | bytes 1572872 | tf_op jit(solution)/shard_map/ppermute | solution.py:52
  61.0 11.7 %collective-permute-start.3 = (bf16[2,16,4096]{2,1,0:T(8,128)(2,1)S(1)}, bf16[2,16,4096]{2,1,0:T(8,128)(2,1)S(1)}, u32[]{:S(2)}, u32[]{:S(2)}) collective-permute-start(bf16[2,16,4096]{2,1,0:T(8,128)(2,1)S(1)} %collective-permute-done.2), channel_id=1, source_target_pairs={{0,15},{1,0},{2,1},{3,2},{4,3},{5,4},{6,5},{7,6},{8,7},{9,8},{10,9... | collective-permute-start | bytes 786440 | tf_op jit(solution)/shard_map/ppermute | solution.py:134
  66.6 11.2 %collective-permute-start.7 = (bf16[2,16,4096]{2,1,0:T(8,128)(2,1)S(1)}, bf16[2,16,4096]{2,1,0:T(8,128)(2,1)S(1)}, u32[]{:S(2)}, u32[]{:S(2)}) collective-permute-start(bf16[2,16,4096]{2,1,0:T(8,128)(2,1)S(1)} %collective-permute-done.6), channel_id=1, source_target_pairs={{0,1},{1,2},{2,3},{3,4},{4,5},{5,6},{6,7},{7,8},{8,9},{9,10},{10,1... | collective-permute-start | bytes 786440 | tf_op jit(solution)/shard_map/ppermute | solution.py:130
  68.9 50.5 %collective-permute-start.11 = (bf16[4,256,1024]{2,1,0:T(8,128)(2,1)S(1)}, bf16[4,256,1024]{2,1,0:T(8,128)(2,1)S(1)}, u32[]{:S(2)}, u32[]{:S(2)}) collective-permute-start(bf16[4,256,1024]{2,1,0:T(8,128)(2,1)S(1)} %pad_maximum_fusion), channel_id=1, source_target_pairs={{0,64},{32,96},{64,0},{96,32},{128,192},{160,224},{192,128},{224,1... | collective-permute-start | bytes 6291464 | tf_op jit(solution)/shard_map/ppermute | solution.py:55
  77.8 9.6 %collective-permute-start.16 = (bf16[2,16,4096]{2,1,0:T(8,128)(2,1)S(1)}, bf16[2,16,4096]{2,1,0:T(8,128)(2,1)S(1)}, u32[]{:S(2)}, u32[]{:S(2)}) collective-permute-start(bf16[2,16,4096]{2,1,0:T(8,128)(2,1)S(1)} %collective-permute-done.7), channel_id=1, source_target_pairs={{0,1},{1,2},{2,3},{3,4},{4,5},{5,6},{6,7},{7,8},{8,9},{9,10},{10,1... | collective-permute-start | bytes 786440 | tf_op jit(solution)/shard_map/ppermute | solution.py:130
  91.2 9.6 %collective-permute-start.14 = (bf16[2,16,4096]{2,1,0:T(8,128)(2,1)S(1)}, bf16[2,16,4096]{2,1,0:T(8,128)(2,1)S(1)}, u32[]{:S(2)}, u32[]{:S(2)}) collective-permute-start(bf16[2,16,4096]{2,1,0:T(8,128)(2,1)S(1)} %collective-permute-done.13), channel_id=1, source_target_pairs={{0,15},{1,0},{2,1},{3,2},{4,3},{5,4},{6,5},{7,6},{8,7},{9,8},{10,9... | collective-permute-start | bytes 786440 | tf_op jit(solution)/shard_map/ppermute | solution.py:134
  96.9 9.9 %collective-permute-start.18 = (bf16[2,16,4096]{2,1,0:T(8,128)(2,1)S(1)}, bf16[2,16,4096]{2,1,0:T(8,128)(2,1)S(1)}, u32[]{:S(2)}, u32[]{:S(2)}) collective-permute-start(bf16[2,16,4096]{2,1,0:T(8,128)(2,1)S(1)} %collective-permute-done.17), channel_id=1, source_target_pairs={{0,1},{1,2},{2,3},{3,4},{4,5},{5,6},{6,7},{7,8},{8,9},{9,10},{10,1... | collective-permute-start | bytes 786440 | tf_op jit(solution)/shard_map/ppermute | solution.py:130
  100.8 10.4 %collective-permute-start.15 = (bf16[2,16,4096]{2,1,0:T(8,128)(2,1)S(1)}, bf16[2,16,4096]{2,1,0:T(8,128)(2,1)S(1)}, u32[]{:S(2)}, u32[]{:S(2)}) collective-permute-start(bf16[2,16,4096]{2,1,0:T(8,128)(2,1)S(1)} %collective-permute-done.14), channel_id=1, source_target_pairs={{0,15},{1,0},{2,1},{3,2},{4,3},{5,4},{6,5},{7,6},{8,7},{9,8},{10,9... | collective-permute-start | bytes 786440 | tf_op jit(solution)/shard_map/ppermute | solution.py:134
  106.7 10.6 %collective-permute-start.19 = (bf16[2,16,4096]{2,1,0:T(8,128)(2,1)S(1)}, bf16[2,16,4096]{2,1,0:T(8,128)(2,1)S(1)}, u32[]{:S(2)}, u32[]{:S(2)}) collective-permute-start(bf16[2,16,4096]{2,1,0:T(8,128)(2,1)S(1)} %collective-permute-done.18), channel_id=1, source_target_pairs={{0,1},{1,2},{2,3},{3,4},{4,5},{5,6},{6,7},{7,8},{8,9},{9,10},{10,1... | collective-permute-start | bytes 786440 | tf_op jit(solution)/shard_map/ppermute | solution.py:130
  111.2 11.4 %collective-permute-start.21 = (bf16[2,16,2048]{2,1,0:T(8,128)(2,1)S(1)}, bf16[2,16,2048]{2,1,0:T(8,128)(2,1)S(1)}, u32[]{:S(2)}, u32[]{:S(2)}) collective-permute-start(bf16[2,16,2048]{2,1,0:T(8,128)(2,1)S(1)} %slice.327), channel_id=1, source_target_pairs={{0,15},{1,0},{2,1},{3,2},{4,3},{5,4},{6,5},{7,6},{8,7},{9,8},{10,9... | collective-permute-start | bytes 393224 | tf_op jit(solution)/shard_map/ppermute | solution.py:140
  136.7 10.1 %collective-permute-start.30 = (bf16[2,16,2048]{2,1,0:T(8,128)(2,1)S(1)}, bf16[2,16,2048]{2,1,0:T(8,128)(2,1)S(1)}, u32[]{:S(2)}, u32[]{:S(2)}) collective-permute-start(bf16[2,16,2048]{2,1,0:T(8,128)(2,1)S(1)} %get-tuple-element.29), channel_id=1, source_target_pairs={{0,15},{1,0},{2,1},{3,2},{4,3},{5,4},{6,5},{7,6},{8,7},{9,8},{10,9... | collective-permute-start | bytes 393224 | tf_op jit(solution)/shard_map/ppermute | solution.py:198
  144.9 10.9 %collective-permute-start.23 = (bf16[2,16,4096]{2,1,0:T(8,128)(2,1)S(1)}, bf16[2,16,4096]{2,1,0:T(8,128)(2,1)S(1)}, u32[]{:S(2)}, u32[]{:S(2)}) collective-permute-start(bf16[2,16,4096]{2,1,0:T(8,128)(2,1)S(1)} %pad_maximum_fusion.6), channel_id=1, source_target_pairs={{0,1},{1,2},{2,3},{3,4},{4,5},{5,6},{6,7},{7,8},{8,9},{9,10},{10,1... | collective-permute-start | bytes 786440 | tf_op jit(solution)/shard_map/ppermute | solution.py:185
  146.9 10.4 %collective-permute-start.31 = (bf16[2,16,4096]{2,1,0:T(8,128)(2,1)S(1)}, bf16[2,16,4096]{2,1,0:T(8,128)(2,1)S(1)}, u32[]{:S(2)}, u32[]{:S(2)}) collective-permute-start(bf16[2,16,4096]{2,1,0:T(8,128)(2,1)S(1)} %pad_maximum_fusion.7), channel_id=1, source_target_pairs={{0,15},{1,0},{2,1},{3,2},{4,3},{5,4},{6,5},{7,6},{8,7},{9,8},{10,9... | collective-permute-start | bytes 786440 | tf_op jit(solution)/shard_map/ppermute | solution.py:198
  157.4 9.5 %collective-permute-start.32 = (bf16[2,16,4096]{2,1,0:T(8,128)(2,1)S(1)}, bf16[2,16,4096]{2,1,0:T(8,128)(2,1)S(1)}, u32[]{:S(2)}, u32[]{:S(2)}) collective-permute-start(bf16[2,16,4096]{2,1,0:T(8,128)(2,1)S(1)} %fusion.24), channel_id=1, source_target_pairs={{0,15},{1,0},{2,1},{3,2},{4,3},{5,4},{6,5},{7,6},{8,7},{9,8},{10,9... | collective-permute-start | bytes 786440 | tf_op jit(solution)/shard_map/ppermute | solution.py:198
  162.9 9.7 %collective-permute-start.24 = (bf16[2,16,4096]{2,1,0:T(8,128)(2,1)S(1)}, bf16[2,16,4096]{2,1,0:T(8,128)(2,1)S(1)}, u32[]{:S(2)}, u32[]{:S(2)}) collective-permute-start(bf16[2,16,4096]{2,1,0:T(8,128)(2,1)S(1)} %fusion.30), channel_id=1, source_target_pairs={{0,1},{1,2},{2,3},{3,4},{4,5},{5,6},{6,7},{7,8},{8,9},{9,10},{10,1... | collective-permute-start | bytes 786440 | tf_op jit(solution)/shard_map/ppermute | solution.py:185
  186.1 9.6 %collective-permute-start.35 = (bf16[2,16,4096]{2,1,0:T(8,128)(2,1)S(1)}, bf16[2,16,4096]{2,1,0:T(8,128)(2,1)S(1)}, u32[]{:S(2)}, u32[]{:S(2)}) collective-permute-start(bf16[2,16,4096]{2,1,0:T(8,128)(2,1)S(1)} %fusion.21), channel_id=1, source_target_pairs={{0,15},{1,0},{2,1},{3,2},{4,3},{5,4},{6,5},{7,6},{8,7},{9,8},{10,9... | collective-permute-start | bytes 786440 | tf_op jit(solution)/shard_map/ppermute | solution.py:198
  191.8 9.9 %collective-permute-start.27 = (bf16[2,16,4096]{2,1,0:T(8,128)(2,1)S(1)}, bf16[2,16,4096]{2,1,0:T(8,128)(2,1)S(1)}, u32[]{:S(2)}, u32[]{:S(2)}) collective-permute-start(bf16[2,16,4096]{2,1,0:T(8,128)(2,1)S(1)} %fusion.27), channel_id=1, source_target_pairs={{0,1},{1,2},{2,3},{3,4},{4,5},{5,6},{6,7},{7,8},{8,9},{9,10},{10,1... | collective-permute-start | bytes 786440 | tf_op jit(solution)/shard_map/ppermute | solution.py:185
  195.8 10.7 %collective-permute-start.36 = (bf16[2,16,4096]{2,1,0:T(8,128)(2,1)S(1)}, bf16[2,16,4096]{2,1,0:T(8,128)(2,1)S(1)}, u32[]{:S(2)}, u32[]{:S(2)}) collective-permute-start(bf16[2,16,4096]{2,1,0:T(8,128)(2,1)S(1)} %fusion.20), channel_id=1, source_target_pairs={{0,15},{1,0},{2,1},{3,2},{4,3},{5,4},{6,5},{7,6},{8,7},{9,8},{10,9... | collective-permute-start | bytes 786440 | tf_op jit(solution)/shard_map/ppermute | solution.py:198
  201.7 11.0 %collective-permute-start.28 = (bf16[2,16,4096]{2,1,0:T(8,128)(2,1)S(1)}, bf16[2,16,4096]{2,1,0:T(8,128)(2,1)S(1)}, u32[]{:S(2)}, u32[]{:S(2)}) collective-permute-start(bf16[2,16,4096]{2,1,0:T(8,128)(2,1)S(1)} %fusion.26), channel_id=1, source_target_pairs={{0,1},{1,2},{2,3},{3,4},{4,5},{5,6},{6,7},{7,8},{8,9},{9,10},{10,1... | collective-permute-start | bytes 786440 | tf_op jit(solution)/shard_map/ppermute | solution.py:185
  (19 other events, 162.7 us)

commit v13 on v11

--- a/solution.py
+++ b/solution.py
@@ -36,6 +36,7 @@
 TP_L_SWAP = tp_perm(lambda l, z: (l + 1, z))
 TP_Z_FWD = tp_perm(lambda l, z: (l, z + 1))
 TP_Z_BWD = tp_perm(lambda l, z: (l, z - 1))
+TP_DIAG_FWD = tp_perm(lambda l, z: (l + 1, z + 1))
 
 
 def normalize(row_block):
@@ -178,14 +179,15 @@
 
     fwd = blocks[nz // 2]
     for s in range(nz // 2):
+        if s == nz // 2 - 1:
+            fwd_own = lax.ppermute(fwd[0], "tensor", TP_Z_FWD)
+            fwd_diag = lax.ppermute(fwd[1], "tensor", TP_DIAG_FWD)
+            break
         got = lax.ppermute(fwd, "tensor", TP_Z_FWD)
         if s < len(groups) - 1:
             late, got = lax.optimization_barrier((hiddens[s + 1], got))
             place(s + 1, late)
-        if s < nz // 2 - 1:
-            fwd = (got.astype(jnp.float32) + blocks[nz // 2 - 1 - s].astype(jnp.float32)).astype(jnp.bfloat16)
-        else:
-            fwd_total = got
+        fwd = (got.astype(jnp.float32) + blocks[nz // 2 - 1 - s].astype(jnp.float32)).astype(jnp.bfloat16)
     bwd = blocks[nz // 2 + 1]
     for s in range(nz // 2 - 1):
         got = lax.ppermute(bwd, "tensor", TP_Z_BWD)
@@ -193,11 +195,10 @@
             bwd = (got.astype(jnp.float32) + blocks[nz // 2 + 2 + s].astype(jnp.float32)).astype(jnp.bfloat16)
         else:
             bwd_total = got
-    column_sum = (
-        fwd_total.astype(jnp.float32) + bwd_total.astype(jnp.float32) + blocks[0].astype(jnp.float32)
-    )
-    from_partner = lax.ppermute(column_sum[1].astype(jnp.bfloat16), "tensor", TP_L_SWAP)
-    total = column_sum[0] + from_partner.astype(jnp.float32)
+    f32 = lambda v: v.astype(jnp.float32)
+    to_partner = (f32(bwd_total[1]) + f32(blocks[0][1])).astype(jnp.bfloat16)
+    from_partner = lax.ppermute(to_partner, "tensor", TP_L_SWAP)
+    total = f32(fwd_own) + f32(fwd_diag) + f32(bwd_total[0]) + f32(blocks[0][0]) + f32(from_partner)
     return (local_batch.astype(jnp.float32) + total).astype(jnp.bfloat16)
 
 

time: 230 us -> 230 us (level)
  starting transfers between devices: 144 us -> 148 us
  waiting for transfers between devices: 57.1 us -> 53.4 us
    ppermute x8 -> x7, waiting for transfers between devices: 28.2 us -> 11.4 us  [per_device(): got = lax.ppermute(fwd, 'tensor', TP_Z_FWD)]
    ppermute x7, waiting for transfers between devices: 0.02 us -> 9.38 us  [per_device(): got = lax.ppermute(bwd, 'tensor', TP_Z_BWD)]
    ppermute x1 -> x3, starting transfers between devices: 3.2 us -> 7.06 us  [the longest x1 3.22 us: per_device(): from_partner = lax.ppermute(to_partner, 'tensor', TP_L_SWAP)]
    ppermute x1 -> x3, waiting for transfers between devices: 3.65 us -> 7.48 us  [the longest x1 5.1 us: per_device(): fwd_diag = lax.ppermute(fwd[1], 'tensor', TP_DIAG_FWD)]
    ppermute x8 -> x7, starting transfers between devices: 15.5 us -> 13.6 us  [per_device(): got = lax.ppermute(fwd, 'tensor', TP_Z_FWD)]
  transfers between devices with their start and end apart: 39 -> 40, of which waited for: 20 -> 22; matrix products, arithmetic and copies ran while one was open for 6% -> 6% of each run, Pallas kernels for 0% -> 0%
where the time goes in v13:
time: 230 us; the launch traced here: 227 us
  starting transfers between devices  148 us (64%)
  waiting for transfers between devices  53.4 us (23%)
  matrix products  11.9 us (5%)
  local copies, waits for them, and re-layouts  7.88 us (3%)
  other arithmetic  3.64 us (2%)
    ppermute x7, starting transfers between devices, per_device(): bwd = lax.ppermute(bwd, 'tensor', TP_Z_BWD)  41 us
    ppermute x7, starting transfers between devices, per_device(): got = lax.ppermute(bwd, 'tensor', TP_Z_BWD)  38.1 us
    ppermute x7, starting transfers between devices, per_device(): got = lax.ppermute(fwd, 'tensor', TP_Z_FWD)  13.6 us
    ppermute x7, starting transfers between devices, per_device(): fwd = lax.ppermute(fwd, 'tensor', TP_Z_FWD)  13.4 us
    ppermute x7, waiting for transfers between devices, per_device(): got = lax.ppermute(fwd, 'tensor', TP_Z_FWD)  11.4 us
    ppermute x7, waiting for transfers between devices, per_device(): got = lax.ppermute(bwd, 'tensor', TP_Z_BWD)  9.38 us
    ppermute x7, waiting for transfers between devices, per_device(): bwd = lax.ppermute(bwd, 'tensor', TP_Z_BWD)  9.26 us
    dot_general x18, matrix products, ffn(): jnp.dot(rows[:, col:col + width], buf.reshape(width, 2 * ff_cols), prefer...  8.32 us
  transfers between devices with their start and end apart: 40, of which 22 were waited for; matrix products, arithmetic and copies ran while one was open for 6% of the time, Pallas kernels for 0%

profile of v13, /device:TPU:24, one launch (start us, length us, event | category | flops | bytes accessed | tf_op | source)
XLA Modules:
  0.0 226.9 jit_solution(2517893053261873539)
XLA Ops:
  2.0 7.5 %collective-permute-start.8 = (bf16[1,256,1024]{2,1,0:T(8,128)(2,1)S(1)}, bf16[1,256,1024]{2,1,0:T(8,128)(2,1)S(1)}, u32[]{:S(2)}, u32[]{:S(2)}) collective-permute-start(bf16[1,256,1024]{2,1,0:T(8,128)(2,1)S(1)} %bitcast.165), channel_id=1, source_target_pairs={{0,128},{32,160},{64,192},{96,224},{128,256},{160,288},{192,320},{... | collective-permute-start | bytes 1572872 | tf_op jit(solution)/shard_map/ppermute | solution.py:52
  14.4 6.6 %all-to-all-start = ((bf16[16,2,4224]{2,1,0:T(2,128)(2,1)}), bf16[16,2,4224]{2,1,0:T(2,128)(2,1)S(1)}, u32[]{:S(2)}, u32[]{:S(2)}) async-start(bf16[16,2,4224]{2,1,0:T(2,128)(2,1)} %reshape.947), calls=%async_computation | async-start | bytes 540672 | tf_op jit(solution)/shard_map/all_to_all | solution.py:96
  22.2 6.2 %all-to-all-done = bf16[16,2,4224]{2,1,0:T(2,128)(2,1)S(1)} async-done(((bf16[16,2,4224]{2,1,0:T(2,128)(2,1)}), bf16[16,2,4224]{2,1,0:T(2,128)(2,1)S(1)}, u32[]{:S(2)}, u32[]{:S(2)}) %all-to-all-start) | async-done | bytes 270368 | tf_op jit(solution)/shard_map/all_to_all | solution.py:96
  31.7 5.0 %collective-permute-done = bf16[16,4096]{1,0:T(8,128)(2,1)S(1)} collective-permute-done((bf16[16,4096]{1,0:T(8,128)(2,1)S(1)}, bf16[16,4096]{1,0:T(8,128)(2,1)S(1)}, u32[]{:S(2)}, u32[]{:S(2)}) %collective-permute-start) | collective-permute-done | bytes 131104 | tf_op jit(solution)/shard_map/ppermute | solution.py:127
  36.7 8.4 %collective-permute-start.1 = (bf16[2,16,4096]{2,1,0:T(8,128)(2,1)S(1)}, bf16[2,16,4096]{2,1,0:T(8,128)(2,1)S(1)}, u32[]{:S(2)}, u32[]{:S(2)}) collective-permute-start(bf16[2,16,4096]{2,1,0:T(8,128)(2,1)S(1)} %pad_maximum_fusion.4), channel_id=1, source_target_pairs={{0,15},{1,0},{2,1},{3,2},{4,3},{5,4},{6,5},{7,6},{8,7},{9,8},{10,9... | collective-permute-start | bytes 786440 | tf_op jit(solution)/shard_map/ppermute | solution.py:135
  47.1 4.0 %collective-permute-start.9 = (bf16[1,256,1024]{2,1,0:T(8,128)(2,1)S(1)}, bf16[1,256,1024]{2,1,0:T(8,128)(2,1)S(1)}, u32[]{:S(2)}, u32[]{:S(2)}) collective-permute-start(bf16[1,256,1024]{2,1,0:T(8,128)(2,1)S(1)} %collective-permute-done.8), channel_id=1, source_target_pairs={{0,128},{32,160},{64,192},{96,224},{128,256},{160,288},{192,320},{... | collective-permute-start | bytes 1572872 | tf_op jit(solution)/shard_map/ppermute | solution.py:53
  52.0 5.1 %collective-permute-start.2 = (bf16[2,16,4096]{2,1,0:T(8,128)(2,1)S(1)}, bf16[2,16,4096]{2,1,0:T(8,128)(2,1)S(1)}, u32[]{:S(2)}, u32[]{:S(2)}) collective-permute-start(bf16[2,16,4096]{2,1,0:T(8,128)(2,1)S(1)} %collective-permute-done.1), channel_id=1, source_target_pairs={{0,15},{1,0},{2,1},{3,2},{4,3},{5,4},{6,5},{7,6},{8,7},{9,8},{10,9... | collective-permute-start | bytes 786440 | tf_op jit(solution)/shard_map/ppermute | solution.py:135
  61.0 5.6 %collective-permute-start.3 = (bf16[2,16,4096]{2,1,0:T(8,128)(2,1)S(1)}, bf16[2,16,4096]{2,1,0:T(8,128)(2,1)S(1)}, u32[]{:S(2)}, u32[]{:S(2)}) collective-permute-start(bf16[2,16,4096]{2,1,0:T(8,128)(2,1)S(1)} %collective-permute-done.2), channel_id=1, source_target_pairs={{0,15},{1,0},{2,1},{3,2},{4,3},{5,4},{6,5},{7,6},{8,7},{9,8},{10,9... | collective-permute-start | bytes 786440 | tf_op jit(solution)/shard_map/ppermute | solution.py:135
  68.9 3.7 %collective-permute-start.11 = (bf16[4,256,1024]{2,1,0:T(8,128)(2,1)S(1)}, bf16[4,256,1024]{2,1,0:T(8,128)(2,1)S(1)}, u32[]{:S(2)}, u32[]{:S(2)}) collective-permute-start(bf16[4,256,1024]{2,1,0:T(8,128)(2,1)S(1)} %pad_maximum_fusion), channel_id=1, source_target_pairs={{0,64},{32,96},{64,0},{96,32},{128,192},{160,224},{192,128},{224,1... | collective-permute-start | bytes 6291464 | tf_op jit(solution)/shard_map/ppermute | solution.py:56
  72.7 5.1 %collective-permute-start.4 = (bf16[2,16,4096]{2,1,0:T(8,128)(2,1)S(1)}, bf16[2,16,4096]{2,1,0:T(8,128)(2,1)S(1)}, u32[]{:S(2)}, u32[]{:S(2)}) collective-permute-start(bf16[2,16,4096]{2,1,0:T(8,128)(2,1)S(1)} %collective-permute-done.3), channel_id=1, source_target_pairs={{0,15},{1,0},{2,1},{3,2},{4,3},{5,4},{6,5},{7,6},{8,7},{9,8},{10,9... | collective-permute-start | bytes 786440 | tf_op jit(solution)/shard_map/ppermute | solution.py:135
  81.7 5.6 %collective-permute-start.13 = (bf16[2,16,4096]{2,1,0:T(8,128)(2,1)S(1)}, bf16[2,16,4096]{2,1,0:T(8,128)(2,1)S(1)}, u32[]{:S(2)}, u32[]{:S(2)}) collective-permute-start(bf16[2,16,4096]{2,1,0:T(8,128)(2,1)S(1)} %collective-permute-done.4), channel_id=1, source_target_pairs={{0,15},{1,0},{2,1},{3,2},{4,3},{5,4},{6,5},{7,6},{8,7},{9,8},{10,9... | collective-permute-start | bytes 786440 | tf_op jit(solution)/shard_map/ppermute | solution.py:135
  91.2 5.6 %collective-permute-start.14 = (bf16[2,16,4096]{2,1,0:T(8,128)(2,1)S(1)}, bf16[2,16,4096]{2,1,0:T(8,128)(2,1)S(1)}, u32[]{:S(2)}, u32[]{:S(2)}) collective-permute-start(bf16[2,16,4096]{2,1,0:T(8,128)(2,1)S(1)} %collective-permute-done.13), channel_id=1, source_target_pairs={{0,15},{1,0},{2,1},{3,2},{4,3},{5,4},{6,5},{7,6},{8,7},{9,8},{10,9... | collective-permute-start | bytes 786440 | tf_op jit(solution)/shard_map/ppermute | solution.py:135
  100.8 5.6 %collective-permute-start.15 = (bf16[2,16,4096]{2,1,0:T(8,128)(2,1)S(1)}, bf16[2,16,4096]{2,1,0:T(8,128)(2,1)S(1)}, u32[]{:S(2)}, u32[]{:S(2)}) collective-permute-start(bf16[2,16,4096]{2,1,0:T(8,128)(2,1)S(1)} %collective-permute-done.14), channel_id=1, source_target_pairs={{0,15},{1,0},{2,1},{3,2},{4,3},{5,4},{6,5},{7,6},{8,7},{9,8},{10,9... | collective-permute-start | bytes 786440 | tf_op jit(solution)/shard_map/ppermute | solution.py:135
  111.2 5.6 %collective-permute-start.21 = (bf16[2,16,2048]{2,1,0:T(8,128)(2,1)S(1)}, bf16[2,16,2048]{2,1,0:T(8,128)(2,1)S(1)}, u32[]{:S(2)}, u32[]{:S(2)}) collective-permute-start(bf16[2,16,2048]{2,1,0:T(8,128)(2,1)S(1)} %slice.319), channel_id=1, source_target_pairs={{0,15},{1,0},{2,1},{3,2},{4,3},{5,4},{6,5},{7,6},{8,7},{9,8},{10,9... | collective-permute-start | bytes 393224 | tf_op jit(solution)/shard_map/ppermute | solution.py:141
  136.9 5.1 %collective-permute-start.31 = (bf16[2,16,4096]{2,1,0:T(8,128)(2,1)S(1)}, bf16[2,16,4096]{2,1,0:T(8,128)(2,1)S(1)}, u32[]{:S(2)}, u32[]{:S(2)}) collective-permute-start(bf16[2,16,4096]{2,1,0:T(8,128)(2,1)S(1)} %bitcast.212), channel_id=1, source_target_pairs={{0,15},{1,0},{2,1},{3,2},{4,3},{5,4},{6,5},{7,6},{8,7},{9,8},{10,9... | collective-permute-start | bytes 786440 | tf_op jit(solution)/shard_map/ppermute | solution.py:193
  142.7 3.9 %collective-permute-done.22 = bf16[2,16,4096]{2,1,0:T(8,128)(2,1)S(1)} collective-permute-done((bf16[2,16,4096]{2,1,0:T(8,128)(2,1)S(1)}, bf16[2,16,4096]{2,1,0:T(8,128)(2,1)S(1)}, u32[]{:S(2)}, u32[]{:S(2)}) %collective-permute-start.22) | collective-permute-done | bytes 262176 | tf_op jit(solution)/shard_map/ppermute | solution.py:186
  149.7 5.1 %collective-permute-start.32 = (bf16[2,16,4096]{2,1,0:T(8,128)(2,1)S(1)}, bf16[2,16,4096]{2,1,0:T(8,128)(2,1)S(1)}, u32[]{:S(2)}, u32[]{:S(2)}) collective-permute-start(bf16[2,16,4096]{2,1,0:T(8,128)(2,1)S(1)} %fusion.24), channel_id=1, source_target_pairs={{0,15},{1,0},{2,1},{3,2},{4,3},{5,4},{6,5},{7,6},{8,7},{9,8},{10,9... | collective-permute-start | bytes 786440 | tf_op jit(solution)/shard_map/ppermute | solution.py:193
  154.8 3.8 %collective-permute-done.23 = bf16[2,16,4096]{2,1,0:T(8,128)(2,1)S(1)} collective-permute-done((bf16[2,16,4096]{2,1,0:T(8,128)(2,1)S(1)}, bf16[2,16,4096]{2,1,0:T(8,128)(2,1)S(1)}, u32[]{:S(2)}, u32[]{:S(2)}) %collective-permute-start.23) | collective-permute-done | bytes 262176 | tf_op jit(solution)/shard_map/ppermute | solution.py:186
  160.1 5.4 %collective-permute-start.33 = (bf16[2,16,4096]{2,1,0:T(8,128)(2,1)S(1)}, bf16[2,16,4096]{2,1,0:T(8,128)(2,1)S(1)}, u32[]{:S(2)}, u32[]{:S(2)}) collective-permute-start(bf16[2,16,4096]{2,1,0:T(8,128)(2,1)S(1)} %fusion.23), channel_id=1, source_target_pairs={{0,15},{1,0},{2,1},{3,2},{4,3},{5,4},{6,5},{7,6},{8,7},{9,8},{10,9... | collective-permute-start | bytes 786440 | tf_op jit(solution)/shard_map/ppermute | solution.py:193
  169.8 5.6 %collective-permute-start.34 = (bf16[2,16,4096]{2,1,0:T(8,128)(2,1)S(1)}, bf16[2,16,4096]{2,1,0:T(8,128)(2,1)S(1)}, u32[]{:S(2)}, u32[]{:S(2)}) collective-permute-start(bf16[2,16,4096]{2,1,0:T(8,128)(2,1)S(1)} %fusion.22), channel_id=1, source_target_pairs={{0,15},{1,0},{2,1},{3,2},{4,3},{5,4},{6,5},{7,6},{8,7},{9,8},{10,9... | collective-permute-start | bytes 786440 | tf_op jit(solution)/shard_map/ppermute | solution.py:193
  179.3 5.6 %collective-permute-start.35 = (bf16[2,16,4096]{2,1,0:T(8,128)(2,1)S(1)}, bf16[2,16,4096]{2,1,0:T(8,128)(2,1)S(1)}, u32[]{:S(2)}, u32[]{:S(2)}) collective-permute-start(bf16[2,16,4096]{2,1,0:T(8,128)(2,1)S(1)} %fusion.21), channel_id=1, source_target_pairs={{0,15},{1,0},{2,1},{3,2},{4,3},{5,4},{6,5},{7,6},{8,7},{9,8},{10,9... | collective-permute-start | bytes 786440 | tf_op jit(solution)/shard_map/ppermute | solution.py:193
  188.9 5.6 %collective-permute-start.36 = (bf16[2,16,4096]{2,1,0:T(8,128)(2,1)S(1)}, bf16[2,16,4096]{2,1,0:T(8,128)(2,1)S(1)}, u32[]{:S(2)}, u32[]{:S(2)}) collective-permute-start(bf16[2,16,4096]{2,1,0:T(8,128)(2,1)S(1)} %fusion.20), channel_id=1, source_target_pairs={{0,15},{1,0},{2,1},{3,2},{4,3},{5,4},{6,5},{7,6},{8,7},{9,8},{10,9... | collective-permute-start | bytes 786440 | tf_op jit(solution)/shard_map/ppermute | solution.py:193
  198.5 5.6 %collective-permute-start.37 = (bf16[2,16,4096]{2,1,0:T(8,128)(2,1)S(1)}, bf16[2,16,4096]{2,1,0:T(8,128)(2,1)S(1)}, u32[]{:S(2)}, u32[]{:S(2)}) collective-permute-start(bf16[2,16,4096]{2,1,0:T(8,128)(2,1)S(1)} %fusion.19), channel_id=1, source_target_pairs={{0,15},{1,0},{2,1},{3,2},{4,3},{5,4},{6,5},{7,6},{8,7},{9,8},{10,9... | collective-permute-start | bytes 786440 | tf_op jit(solution)/shard_map/ppermute | solution.py:193
  218.6 5.1 %collective-permute-done.30 = bf16[16,4096]{1,0:T(8,128)(2,1)S(1)} collective-permute-done((bf16[16,4096]{1,0:T(8,128)(2,1)S(1)}, bf16[16,4096]{1,0:T(8,128)(2,1)S(1)}, u32[]{:S(2)}, u32[]{:S(2)}) %collective-permute-start.30) | collective-permute-done | bytes 131104 | tf_op jit(solution)/shard_map/ppermute | solution.py:184
  (161 shorter events, 94.7 us)
Async XLA Ops:
  2.0 45.1 %collective-permute-start.8 = (bf16[1,256,1024]{2,1,0:T(8,128)(2,1)S(1)}, bf16[1,256,1024]{2,1,0:T(8,128)(2,1)S(1)}, u32[]{:S(2)}, u32[]{:S(2)}) collective-permute-start(bf16[1,256,1024]{2,1,0:T(8,128)(2,1)S(1)} %bitcast.165), channel_id=1, source_target_pairs={{0,128},{32,160},{64,192},{96,224},{128,256},{160,288},{192,320},{... | collective-permute-start | bytes 1572872 | tf_op jit(solution)/shard_map/ppermute | solution.py:52
  9.5 59.1 %collective-permute-start.10 = (bf16[1,256,1024]{2,1,0:T(8,128)(2,1)S(1)}, bf16[1,256,1024]{2,1,0:T(8,128)(2,1)S(1)}, u32[]{:S(2)}, u32[]{:S(2)}) collective-permute-start(bf16[1,256,1024]{2,1,0:T(8,128)(2,1)S(1)} %bitcast.166), channel_id=1, source_target_pairs={{0,384},{32,416},{64,448},{96,480},{128,0},{160,32},{192,64},{224,... | collective-permute-start | bytes 1572872 | tf_op jit(solution)/shard_map/ppermute | solution.py:54
  14.4 14.0 %all-to-all-start = ((bf16[16,2,4224]{2,1,0:T(2,128)(2,1)}), bf16[16,2,4224]{2,1,0:T(2,128)(2,1)S(1)}, u32[]{:S(2)}, u32[]{:S(2)}) async-start(bf16[16,2,4224]{2,1,0:T(2,128)(2,1)} %reshape.947), calls=%async_computation | async-start | bytes 540672 | tf_op jit(solution)/shard_map/all_to_all | solution.py:96
  36.7 15.3 %collective-permute-start.1 = (bf16[2,16,4096]{2,1,0:T(8,128)(2,1)S(1)}, bf16[2,16,4096]{2,1,0:T(8,128)(2,1)S(1)}, u32[]{:S(2)}, u32[]{:S(2)}) collective-permute-start(bf16[2,16,4096]{2,1,0:T(8,128)(2,1)S(1)} %pad_maximum_fusion.4), channel_id=1, source_target_pairs={{0,15},{1,0},{2,1},{3,2},{4,3},{5,4},{6,5},{7,6},{8,7},{9,8},{10,9... | collective-permute-start | bytes 786440 | tf_op jit(solution)/shard_map/ppermute | solution.py:135
  45.1 12.0 %collective-permute-start.5 = (bf16[2,16,4096]{2,1,0:T(8,128)(2,1)S(1)}, bf16[2,16,4096]{2,1,0:T(8,128)(2,1)S(1)}, u32[]{:S(2)}, u32[]{:S(2)}) collective-permute-start(bf16[2,16,4096]{2,1,0:T(8,128)(2,1)S(1)} %pad_maximum_fusion.4), channel_id=1, source_target_pairs={{0,1},{1,2},{2,3},{3,4},{4,5},{5,6},{6,7},{7,8},{8,9},{9,10},{10,1... | collective-permute-start | bytes 786440 | tf_op jit(solution)/shard_map/ppermute | solution.py:131
  47.1 21.5 %collective-permute-start.9 = (bf16[1,256,1024]{2,1,0:T(8,128)(2,1)S(1)}, bf16[1,256,1024]{2,1,0:T(8,128)(2,1)S(1)}, u32[]{:S(2)}, u32[]{:S(2)}) collective-permute-start(bf16[1,256,1024]{2,1,0:T(8,128)(2,1)S(1)} %collective-permute-done.8), channel_id=1, source_target_pairs={{0,128},{32,160},{64,192},{96,224},{128,256},{160,288},{192,320},{... | collective-permute-start | bytes 1572872 | tf_op jit(solution)/shard_map/ppermute | solution.py:53
  61.0 11.7 %collective-permute-start.3 = (bf16[2,16,4096]{2,1,0:T(8,128)(2,1)S(1)}, bf16[2,16,4096]{2,1,0:T(8,128)(2,1)S(1)}, u32[]{:S(2)}, u32[]{:S(2)}) collective-permute-start(bf16[2,16,4096]{2,1,0:T(8,128)(2,1)S(1)} %collective-permute-done.2), channel_id=1, source_target_pairs={{0,15},{1,0},{2,1},{3,2},{4,3},{5,4},{6,5},{7,6},{8,7},{9,8},{10,9... | collective-permute-start | bytes 786440 | tf_op jit(solution)/shard_map/ppermute | solution.py:135
  66.6 11.2 %collective-permute-start.7 = (bf16[2,16,4096]{2,1,0:T(8,128)(2,1)S(1)}, bf16[2,16,4096]{2,1,0:T(8,128)(2,1)S(1)}, u32[]{:S(2)}, u32[]{:S(2)}) collective-permute-start(bf16[2,16,4096]{2,1,0:T(8,128)(2,1)S(1)} %collective-permute-done.6), channel_id=1, source_target_pairs={{0,1},{1,2},{2,3},{3,4},{4,5},{5,6},{6,7},{7,8},{8,9},{9,10},{10,1... | collective-permute-start | bytes 786440 | tf_op jit(solution)/shard_map/ppermute | solution.py:131
  68.9 50.5 %collective-permute-start.11 = (bf16[4,256,1024]{2,1,0:T(8,128)(2,1)S(1)}, bf16[4,256,1024]{2,1,0:T(8,128)(2,1)S(1)}, u32[]{:S(2)}, u32[]{:S(2)}) collective-permute-start(bf16[4,256,1024]{2,1,0:T(8,128)(2,1)S(1)} %pad_maximum_fusion), channel_id=1, source_target_pairs={{0,64},{32,96},{64,0},{96,32},{128,192},{160,224},{192,128},{224,1... | collective-permute-start | bytes 6291464 | tf_op jit(solution)/shard_map/ppermute | solution.py:56
  91.2 9.6 %collective-permute-start.14 = (bf16[2,16,4096]{2,1,0:T(8,128)(2,1)S(1)}, bf16[2,16,4096]{2,1,0:T(8,128)(2,1)S(1)}, u32[]{:S(2)}, u32[]{:S(2)}) collective-permute-start(bf16[2,16,4096]{2,1,0:T(8,128)(2,1)S(1)} %collective-permute-done.13), channel_id=1, source_target_pairs={{0,15},{1,0},{2,1},{3,2},{4,3},{5,4},{6,5},{7,6},{8,7},{9,8},{10,9... | collective-permute-start | bytes 786440 | tf_op jit(solution)/shard_map/ppermute | solution.py:135
  96.9 9.9 %collective-permute-start.18 = (bf16[2,16,4096]{2,1,0:T(8,128)(2,1)S(1)}, bf16[2,16,4096]{2,1,0:T(8,128)(2,1)S(1)}, u32[]{:S(2)}, u32[]{:S(2)}) collective-permute-start(bf16[2,16,4096]{2,1,0:T(8,128)(2,1)S(1)} %collective-permute-done.17), channel_id=1, source_target_pairs={{0,1},{1,2},{2,3},{3,4},{4,5},{5,6},{6,7},{7,8},{8,9},{9,10},{10,1... | collective-permute-start | bytes 786440 | tf_op jit(solution)/shard_map/ppermute | solution.py:131
  100.8 10.4 %collective-permute-start.15 = (bf16[2,16,4096]{2,1,0:T(8,128)(2,1)S(1)}, bf16[2,16,4096]{2,1,0:T(8,128)(2,1)S(1)}, u32[]{:S(2)}, u32[]{:S(2)}) collective-permute-start(bf16[2,16,4096]{2,1,0:T(8,128)(2,1)S(1)} %collective-permute-done.14), channel_id=1, source_target_pairs={{0,15},{1,0},{2,1},{3,2},{4,3},{5,4},{6,5},{7,6},{8,7},{9,8},{10,9... | collective-permute-start | bytes 786440 | tf_op jit(solution)/shard_map/ppermute | solution.py:135
  106.7 10.6 %collective-permute-start.19 = (bf16[2,16,4096]{2,1,0:T(8,128)(2,1)S(1)}, bf16[2,16,4096]{2,1,0:T(8,128)(2,1)S(1)}, u32[]{:S(2)}, u32[]{:S(2)}) collective-permute-start(bf16[2,16,4096]{2,1,0:T(8,128)(2,1)S(1)} %collective-permute-done.18), channel_id=1, source_target_pairs={{0,1},{1,2},{2,3},{3,4},{4,5},{5,6},{6,7},{7,8},{8,9},{9,10},{10,1... | collective-permute-start | bytes 786440 | tf_op jit(solution)/shard_map/ppermute | solution.py:131
  111.2 11.2 %collective-permute-start.21 = (bf16[2,16,2048]{2,1,0:T(8,128)(2,1)S(1)}, bf16[2,16,2048]{2,1,0:T(8,128)(2,1)S(1)}, u32[]{:S(2)}, u32[]{:S(2)}) collective-permute-start(bf16[2,16,2048]{2,1,0:T(8,128)(2,1)S(1)} %slice.319), channel_id=1, source_target_pairs={{0,15},{1,0},{2,1},{3,2},{4,3},{5,4},{6,5},{7,6},{8,7},{9,8},{10,9... | collective-permute-start | bytes 393224 | tf_op jit(solution)/shard_map/ppermute | solution.py:141
  134.8 11.7 %collective-permute-start.22 = (bf16[2,16,4096]{2,1,0:T(8,128)(2,1)S(1)}, bf16[2,16,4096]{2,1,0:T(8,128)(2,1)S(1)}, u32[]{:S(2)}, u32[]{:S(2)}) collective-permute-start(bf16[2,16,4096]{2,1,0:T(8,128)(2,1)S(1)} %bitcast.213), channel_id=1, source_target_pairs={{0,1},{1,2},{2,3},{3,4},{4,5},{5,6},{6,7},{7,8},{8,9},{9,10},{10,1... | collective-permute-start | bytes 786440 | tf_op jit(solution)/shard_map/ppermute | solution.py:186
  136.9 12.7 %collective-permute-start.31 = (bf16[2,16,4096]{2,1,0:T(8,128)(2,1)S(1)}, bf16[2,16,4096]{2,1,0:T(8,128)(2,1)S(1)}, u32[]{:S(2)}, u32[]{:S(2)}) collective-permute-start(bf16[2,16,4096]{2,1,0:T(8,128)(2,1)S(1)} %bitcast.212), channel_id=1, source_target_pairs={{0,15},{1,0},{2,1},{3,2},{4,3},{5,4},{6,5},{7,6},{8,7},{9,8},{10,9... | collective-permute-start | bytes 786440 | tf_op jit(solution)/shard_map/ppermute | solution.py:193
  147.7 10.9 %collective-permute-start.23 = (bf16[2,16,4096]{2,1,0:T(8,128)(2,1)S(1)}, bf16[2,16,4096]{2,1,0:T(8,128)(2,1)S(1)}, u32[]{:S(2)}, u32[]{:S(2)}) collective-permute-start(bf16[2,16,4096]{2,1,0:T(8,128)(2,1)S(1)} %fusion.31), channel_id=1, source_target_pairs={{0,1},{1,2},{2,3},{3,4},{4,5},{5,6},{6,7},{7,8},{8,9},{9,10},{10,1... | collective-permute-start | bytes 786440 | tf_op jit(solution)/shard_map/ppermute | solution.py:186
  149.7 10.3 %collective-permute-start.32 = (bf16[2,16,4096]{2,1,0:T(8,128)(2,1)S(1)}, bf16[2,16,4096]{2,1,0:T(8,128)(2,1)S(1)}, u32[]{:S(2)}, u32[]{:S(2)}) collective-permute-start(bf16[2,16,4096]{2,1,0:T(8,128)(2,1)S(1)} %fusion.24), channel_id=1, source_target_pairs={{0,15},{1,0},{2,1},{3,2},{4,3},{5,4},{6,5},{7,6},{8,7},{9,8},{10,9... | collective-permute-start | bytes 786440 | tf_op jit(solution)/shard_map/ppermute | solution.py:193
  160.1 9.6 %collective-permute-start.33 = (bf16[2,16,4096]{2,1,0:T(8,128)(2,1)S(1)}, bf16[2,16,4096]{2,1,0:T(8,128)(2,1)S(1)}, u32[]{:S(2)}, u32[]{:S(2)}) collective-permute-start(bf16[2,16,4096]{2,1,0:T(8,128)(2,1)S(1)} %fusion.23), channel_id=1, source_target_pairs={{0,15},{1,0},{2,1},{3,2},{4,3},{5,4},{6,5},{7,6},{8,7},{9,8},{10,9... | collective-permute-start | bytes 786440 | tf_op jit(solution)/shard_map/ppermute | solution.py:193
  165.6 9.7 %collective-permute-start.24 = (bf16[2,16,4096]{2,1,0:T(8,128)(2,1)S(1)}, bf16[2,16,4096]{2,1,0:T(8,128)(2,1)S(1)}, u32[]{:S(2)}, u32[]{:S(2)}) collective-permute-start(bf16[2,16,4096]{2,1,0:T(8,128)(2,1)S(1)} %fusion.30), channel_id=1, source_target_pairs={{0,1},{1,2},{2,3},{3,4},{4,5},{5,6},{6,7},{7,8},{8,9},{9,10},{10,1... | collective-permute-start | bytes 786440 | tf_op jit(solution)/shard_map/ppermute | solution.py:186
  188.9 9.6 %collective-permute-start.36 = (bf16[2,16,4096]{2,1,0:T(8,128)(2,1)S(1)}, bf16[2,16,4096]{2,1,0:T(8,128)(2,1)S(1)}, u32[]{:S(2)}, u32[]{:S(2)}) collective-permute-start(bf16[2,16,4096]{2,1,0:T(8,128)(2,1)S(1)} %fusion.20), channel_id=1, source_target_pairs={{0,15},{1,0},{2,1},{3,2},{4,3},{5,4},{6,5},{7,6},{8,7},{9,8},{10,9... | collective-permute-start | bytes 786440 | tf_op jit(solution)/shard_map/ppermute | solution.py:193
  194.5 9.9 %collective-permute-start.27 = (bf16[2,16,4096]{2,1,0:T(8,128)(2,1)S(1)}, bf16[2,16,4096]{2,1,0:T(8,128)(2,1)S(1)}, u32[]{:S(2)}, u32[]{:S(2)}) collective-permute-start(bf16[2,16,4096]{2,1,0:T(8,128)(2,1)S(1)} %fusion.27), channel_id=1, source_target_pairs={{0,1},{1,2},{2,3},{3,4},{4,5},{5,6},{6,7},{7,8},{8,9},{9,10},{10,1... | collective-permute-start | bytes 786440 | tf_op jit(solution)/shard_map/ppermute | solution.py:186
  204.5 10.2 %collective-permute-start.28 = (bf16[2,16,4096]{2,1,0:T(8,128)(2,1)S(1)}, bf16[2,16,4096]{2,1,0:T(8,128)(2,1)S(1)}, u32[]{:S(2)}, u32[]{:S(2)}) collective-permute-start(bf16[2,16,4096]{2,1,0:T(8,128)(2,1)S(1)} %fusion.26), channel_id=1, source_target_pairs={{0,1},{1,2},{2,3},{3,4},{4,5},{5,6},{6,7},{7,8},{8,9},{9,10},{10,1... | collective-permute-start | bytes 786440 | tf_op jit(solution)/shard_map/ppermute | solution.py:186
  208.0 10.6 %collective-permute-start.38 = (bf16[16,4096]{1,0:T(8,128)(2,1)S(1)}, bf16[16,4096]{1,0:T(8,128)(2,1)S(1)}, u32[]{:S(2)}, u32[]{:S(2)}) collective-permute-start(bf16[16,4096]{1,0:T(8,128)(2,1)S(1)} %fusion.55), channel_id=1, source_target_pairs={{0,16},{1,17},{2,18},{3,19},{4,20},{5,21},{6,22},{7,23},{8,24},{9,... | collective-permute-start | bytes 393224 | tf_op jit(solution)/shard_map/ppermute | solution.py:200
  (19 other events, 165.4 us)

commit v14 on v13

--- a/solution.py
+++ b/solution.py
@@ -37,6 +37,7 @@
 TP_Z_FWD = tp_perm(lambda l, z: (l, z + 1))
 TP_Z_BWD = tp_perm(lambda l, z: (l, z - 1))
 TP_DIAG_FWD = tp_perm(lambda l, z: (l + 1, z + 1))
+TP_DIAG_BWD = tp_perm(lambda l, z: (l + 1, z - 1))
 
 
 def normalize(row_block):
@@ -124,14 +125,19 @@
     travelling = jnp.take(
         travelling.reshape(shard_rows, dp_count, piece_rows), piece_index, axis=1
     ).reshape(shard_rows, feature_count)
-    pair = jnp.stack([travelling, lax.ppermute(travelling, "tensor", TP_L_SWAP)])
-    token_chunks = {0: pair}
-    fwd = pair
-    for s in range(nz // 2 - 1):
+    token_chunks = {0: jnp.stack([travelling, lax.ppermute(travelling, "tensor", TP_L_SWAP)])}
+    fwd = jnp.stack(
+        [lax.ppermute(travelling, "tensor", TP_Z_FWD), lax.ppermute(travelling, "tensor", TP_DIAG_FWD)]
+    )
+    token_chunks[nz - 1] = fwd
+    for s in range(1, nz // 2 - 1):
         fwd = lax.ppermute(fwd, "tensor", TP_Z_FWD)
         token_chunks[nz - 1 - s] = fwd
-    bwd = pair
-    for s in range(nz // 2 - 1):
+    bwd = jnp.stack(
+        [lax.ppermute(travelling, "tensor", TP_Z_BWD), lax.ppermute(travelling, "tensor", TP_DIAG_BWD)]
+    )
+    token_chunks[1] = bwd
+    for s in range(1, nz // 2 - 1):
         bwd = lax.ppermute(bwd, "tensor", TP_Z_BWD)
         token_chunks[s + 1] = bwd
     half = feature_count // 2

time: 230 us -> 236 us (1.026)
  starting transfers between devices: 148 us -> 155 us
    ppermute x0 -> x4, starting transfers between devices: none -> 17.6 us  [the longest x1 9.83 us: per_device(): lax.ppermute(travelling, 'tensor', TP_DIAG_BWD)]
    ppermute x7 -> x6, starting transfers between devices: 41 us -> 32.2 us  [per_device(): bwd = lax.ppermute(bwd, 'tensor', TP_Z_BWD)]
    ppermute x1, waiting for transfers between devices: 0.01 us -> 6.61 us  [gather_pieces(): lax.ppermute(jnp.concatenate([own, fwd1, fwd2, bwd1]), 'dp', DP_X_SWAP)]
    ppermute x1, waiting for transfers between devices: 5 us -> 0.01 us  [per_device(): lax.ppermute(travelling, 'tensor', TP_L_SWAP)]
    ppermute x1, waiting for transfers between devices: 3.07 us -> 0.01 us  [per_device(): lax.ppermute(fwd[..., :half], 'tensor', TP_Z_FWD)]
    ppermute x1, waiting for transfers between devices: 0.67 us -> 3.55 us  [gather_pieces(): other_core = lax.ppermute(chip, 'dp', DP_C_SWAP)]
    ppermute x7 -> x6, starting transfers between devices: 13.4 us -> 11.5 us  [per_device(): fwd = lax.ppermute(fwd, 'tensor', TP_Z_FWD)]
    ppermute x7 -> x6, waiting for transfers between devices: 9.26 us -> 7.67 us  [per_device(): bwd = lax.ppermute(bwd, 'tensor', TP_Z_BWD)]
  transfers between devices with their start and end apart: 40 -> 42, of which waited for: 22 -> 21; matrix products, arithmetic and copies ran while one was open for 6% -> 6% of each run, Pallas kernels for 0% -> 0%
where the time goes in v14:
time: 236 us; the launch traced here: 235 us
  starting transfers between devices  155 us (66%)
  waiting for transfers between devices  54.6 us (23%)
  matrix products  11.8 us (5%)
  local copies, waits for them, and re-layouts  7.94 us (3%)
  other arithmetic  3.69 us (2%)
    ppermute x7, starting transfers between devices, per_device(): got = lax.ppermute(bwd, 'tensor', TP_Z_BWD)  38.1 us
    ppermute x6, starting transfers between devices, per_device(): bwd = lax.ppermute(bwd, 'tensor', TP_Z_BWD)  32.2 us
    ppermute x7, starting transfers between devices, per_device(): got = lax.ppermute(fwd, 'tensor', TP_Z_FWD)  13.4 us
    ppermute x7, waiting for transfers between devices, per_device(): got = lax.ppermute(fwd, 'tensor', TP_Z_FWD)  12 us
    ppermute x6, starting transfers between devices, per_device(): fwd = lax.ppermute(fwd, 'tensor', TP_Z_FWD)  11.5 us
    ppermute x1, starting transfers between devices, per_device(): lax.ppermute(travelling, 'tensor', TP_DIAG_BWD)  9.83 us
    ppermute x7, waiting for transfers between devices, per_device(): got = lax.ppermute(bwd, 'tensor', TP_Z_BWD)  9.67 us
    dot_general x18, matrix products, ffn(): jnp.dot(rows[:, col:col + width], buf.reshape(width, 2 * ff_cols), prefer...  8.2 us
  transfers between devices with their start and end apart: 42, of which 21 were waited for; matrix products, arithmetic and copies ran while one was open for 6% of the time, Pallas kernels for 0%

profile of v14, /device:TPU:24, one launch (start us, length us, event | category | flops | bytes accessed | tf_op | source)
XLA Modules:
  0.0 234.8 jit_solution(8292788069203542309)
XLA Ops:
  2.0 7.5 %collective-permute-start.10 = (bf16[1,256,1024]{2,1,0:T(8,128)(2,1)S(1)}, bf16[1,256,1024]{2,1,0:T(8,128)(2,1)S(1)}, u32[]{:S(2)}, u32[]{:S(2)}) collective-permute-start(bf16[1,256,1024]{2,1,0:T(8,128)(2,1)S(1)} %bitcast.169), channel_id=1, source_target_pairs={{0,128},{32,160},{64,192},{96,224},{128,256},{160,288},{192,320},{... | collective-permute-start | bytes 1572872 | tf_op jit(solution)/shard_map/ppermute | solution.py:53
  14.4 6.6 %all-to-all-start = ((bf16[16,2,4224]{2,1,0:T(2,128)(2,1)}), bf16[16,2,4224]{2,1,0:T(2,128)(2,1)S(1)}, u32[]{:S(2)}, u32[]{:S(2)}) async-start(bf16[16,2,4224]{2,1,0:T(2,128)(2,1)} %reshape.947), calls=%async_computation | async-start | bytes 540672 | tf_op jit(solution)/shard_map/all_to_all | solution.py:97
  22.2 6.2 %all-to-all-done = bf16[16,2,4224]{2,1,0:T(2,128)(2,1)S(1)} async-done(((bf16[16,2,4224]{2,1,0:T(2,128)(2,1)}), bf16[16,2,4224]{2,1,0:T(2,128)(2,1)S(1)}, u32[]{:S(2)}, u32[]{:S(2)}) %all-to-all-start) | async-done | bytes 270368 | tf_op jit(solution)/shard_map/all_to_all | solution.py:97
  31.5 9.8 %collective-permute-start.2 = (bf16[16,4096]{1,0:T(8,128)(2,1)S(1)}, bf16[16,4096]{1,0:T(8,128)(2,1)S(1)}, u32[]{:S(2)}, u32[]{:S(2)}) collective-permute-start(bf16[16,4096]{1,0:T(8,128)(2,1)S(1)} %broadcast_select_fusion), channel_id=1, source_target_pairs={{0,31},{1,16},{2,17},{3,18},{4,19},{5,20},{6,21},{7,22},{8,23},{9,... | collective-permute-start | bytes 393224 | tf_op jit(solution)/shard_map/ppermute | solution.py:137
  49.5 5.1 %collective-permute-start.3 = (bf16[2,16,4096]{2,1,0:T(8,128)(2,1)S(1)}, bf16[2,16,4096]{2,1,0:T(8,128)(2,1)S(1)}, u32[]{:S(2)}, u32[]{:S(2)}) collective-permute-start(bf16[2,16,4096]{2,1,0:T(8,128)(2,1)S(1)} %pad_maximum_fusion.5), channel_id=1, source_target_pairs={{0,15},{1,0},{2,1},{3,2},{4,3},{5,4},{6,5},{7,6},{8,7},{9,8},{10,9... | collective-permute-start | bytes 786440 | tf_op jit(solution)/shard_map/ppermute | solution.py:141
  57.6 4.3 %collective-permute-start.11 = (bf16[1,256,1024]{2,1,0:T(8,128)(2,1)S(1)}, bf16[1,256,1024]{2,1,0:T(8,128)(2,1)S(1)}, u32[]{:S(2)}, u32[]{:S(2)}) collective-permute-start(bf16[1,256,1024]{2,1,0:T(8,128)(2,1)S(1)} %collective-permute-done.10), channel_id=1, source_target_pairs={{0,128},{32,160},{64,192},{96,224},{128,256},{160,288},{192,320},{... | collective-permute-start | bytes 1572872 | tf_op jit(solution)/shard_map/ppermute | solution.py:54
  62.7 5.1 %collective-permute-start.4 = (bf16[2,16,4096]{2,1,0:T(8,128)(2,1)S(1)}, bf16[2,16,4096]{2,1,0:T(8,128)(2,1)S(1)}, u32[]{:S(2)}, u32[]{:S(2)}) collective-permute-start(bf16[2,16,4096]{2,1,0:T(8,128)(2,1)S(1)} %collective-permute-done.3), channel_id=1, source_target_pairs={{0,15},{1,0},{2,1},{3,2},{4,3},{5,4},{6,5},{7,6},{8,7},{9,8},{10,9... | collective-permute-start | bytes 786440 | tf_op jit(solution)/shard_map/ppermute | solution.py:141
  71.7 5.6 %collective-permute-start.5 = (bf16[2,16,4096]{2,1,0:T(8,128)(2,1)S(1)}, bf16[2,16,4096]{2,1,0:T(8,128)(2,1)S(1)}, u32[]{:S(2)}, u32[]{:S(2)}) collective-permute-start(bf16[2,16,4096]{2,1,0:T(8,128)(2,1)S(1)} %collective-permute-done.4), channel_id=1, source_target_pairs={{0,15},{1,0},{2,1},{3,2},{4,3},{5,4},{6,5},{7,6},{8,7},{9,8},{10,9... | collective-permute-start | bytes 786440 | tf_op jit(solution)/shard_map/ppermute | solution.py:141
  83.2 5.1 %collective-permute-start.15 = (bf16[2,16,4096]{2,1,0:T(8,128)(2,1)S(1)}, bf16[2,16,4096]{2,1,0:T(8,128)(2,1)S(1)}, u32[]{:S(2)}, u32[]{:S(2)}) collective-permute-start(bf16[2,16,4096]{2,1,0:T(8,128)(2,1)S(1)} %collective-permute-done.5), channel_id=1, source_target_pairs={{0,15},{1,0},{2,1},{3,2},{4,3},{5,4},{6,5},{7,6},{8,7},{9,8},{10,9... | collective-permute-start | bytes 786440 | tf_op jit(solution)/shard_map/ppermute | solution.py:141
  92.2 5.6 %collective-permute-start.16 = (bf16[2,16,4096]{2,1,0:T(8,128)(2,1)S(1)}, bf16[2,16,4096]{2,1,0:T(8,128)(2,1)S(1)}, u32[]{:S(2)}, u32[]{:S(2)}) collective-permute-start(bf16[2,16,4096]{2,1,0:T(8,128)(2,1)S(1)} %collective-permute-done.15), channel_id=1, source_target_pairs={{0,15},{1,0},{2,1},{3,2},{4,3},{5,4},{6,5},{7,6},{8,7},{9,8},{10,9... | collective-permute-start | bytes 786440 | tf_op jit(solution)/shard_map/ppermute | solution.py:141
  102.0 5.6 %collective-permute-start.17 = (bf16[2,16,4096]{2,1,0:T(8,128)(2,1)S(1)}, bf16[2,16,4096]{2,1,0:T(8,128)(2,1)S(1)}, u32[]{:S(2)}, u32[]{:S(2)}) collective-permute-start(bf16[2,16,4096]{2,1,0:T(8,128)(2,1)S(1)} %collective-permute-done.16), channel_id=1, source_target_pairs={{0,15},{1,0},{2,1},{3,2},{4,3},{5,4},{6,5},{7,6},{8,7},{9,8},{10,9... | collective-permute-start | bytes 786440 | tf_op jit(solution)/shard_map/ppermute | solution.py:141
  112.5 5.6 %collective-permute-start.23 = (bf16[2,16,2048]{2,1,0:T(8,128)(2,1)S(1)}, bf16[2,16,2048]{2,1,0:T(8,128)(2,1)S(1)}, u32[]{:S(2)}, u32[]{:S(2)}) collective-permute-start(bf16[2,16,2048]{2,1,0:T(8,128)(2,1)S(1)} %slice.321), channel_id=1, source_target_pairs={{0,15},{1,0},{2,1},{3,2},{4,3},{5,4},{6,5},{7,6},{8,7},{9,8},{10,9... | collective-permute-start | bytes 393224 | tf_op jit(solution)/shard_map/ppermute | solution.py:147
  120.7 6.6 %collective-permute-done.13 = bf16[4,256,1024]{2,1,0:T(8,128)(2,1)S(1)} collective-permute-done((bf16[4,256,1024]{2,1,0:T(8,128)(2,1)S(1)}, bf16[4,256,1024]{2,1,0:T(8,128)(2,1)S(1)}, u32[]{:S(2)}, u32[]{:S(2)}) %collective-permute-start.13) | collective-permute-done | bytes 2097184 | tf_op jit(solution)/shard_map/ppermute | solution.py:57
  133.0 3.5 %collective-permute-done.14 = bf16[8,256,1024]{2,1,0:T(8,128)(2,1)S(1)} collective-permute-done((bf16[8,256,1024]{2,1,0:T(8,128)(2,1)S(1)}, bf16[8,256,1024]{2,1,0:T(8,128)(2,1)S(1)}, u32[]{:S(2)}, u32[]{:S(2)}) %collective-permute-start.14) | collective-permute-done | bytes 4194336 | tf_op jit(solution)/shard_map/ppermute | solution.py:60
  144.6 5.1 %collective-permute-start.33 = (bf16[2,16,4096]{2,1,0:T(8,128)(2,1)S(1)}, bf16[2,16,4096]{2,1,0:T(8,128)(2,1)S(1)}, u32[]{:S(2)}, u32[]{:S(2)}) collective-permute-start(bf16[2,16,4096]{2,1,0:T(8,128)(2,1)S(1)} %bitcast.216), channel_id=1, source_target_pairs={{0,15},{1,0},{2,1},{3,2},{4,3},{5,4},{6,5},{7,6},{8,7},{9,8},{10,9... | collective-permute-start | bytes 786440 | tf_op jit(solution)/shard_map/ppermute | solution.py:199
  150.3 3.9 %collective-permute-done.24 = bf16[2,16,4096]{2,1,0:T(8,128)(2,1)S(1)} collective-permute-done((bf16[2,16,4096]{2,1,0:T(8,128)(2,1)S(1)}, bf16[2,16,4096]{2,1,0:T(8,128)(2,1)S(1)}, u32[]{:S(2)}, u32[]{:S(2)}) %collective-permute-start.24) | collective-permute-done | bytes 262176 | tf_op jit(solution)/shard_map/ppermute | solution.py:192
  157.4 5.1 %collective-permute-start.34 = (bf16[2,16,4096]{2,1,0:T(8,128)(2,1)S(1)}, bf16[2,16,4096]{2,1,0:T(8,128)(2,1)S(1)}, u32[]{:S(2)}, u32[]{:S(2)}) collective-permute-start(bf16[2,16,4096]{2,1,0:T(8,128)(2,1)S(1)} %fusion.24), channel_id=1, source_target_pairs={{0,15},{1,0},{2,1},{3,2},{4,3},{5,4},{6,5},{7,6},{8,7},{9,8},{10,9... | collective-permute-start | bytes 786440 | tf_op jit(solution)/shard_map/ppermute | solution.py:199
  167.5 5.4 %collective-permute-start.35 = (bf16[2,16,4096]{2,1,0:T(8,128)(2,1)S(1)}, bf16[2,16,4096]{2,1,0:T(8,128)(2,1)S(1)}, u32[]{:S(2)}, u32[]{:S(2)}) collective-permute-start(bf16[2,16,4096]{2,1,0:T(8,128)(2,1)S(1)} %fusion.23), channel_id=1, source_target_pairs={{0,15},{1,0},{2,1},{3,2},{4,3},{5,4},{6,5},{7,6},{8,7},{9,8},{10,9... | collective-permute-start | bytes 786440 | tf_op jit(solution)/shard_map/ppermute | solution.py:199
  176.9 5.6 %collective-permute-start.36 = (bf16[2,16,4096]{2,1,0:T(8,128)(2,1)S(1)}, bf16[2,16,4096]{2,1,0:T(8,128)(2,1)S(1)}, u32[]{:S(2)}, u32[]{:S(2)}) collective-permute-start(bf16[2,16,4096]{2,1,0:T(8,128)(2,1)S(1)} %fusion.22), channel_id=1, source_target_pairs={{0,15},{1,0},{2,1},{3,2},{4,3},{5,4},{6,5},{7,6},{8,7},{9,8},{10,9... | collective-permute-start | bytes 786440 | tf_op jit(solution)/shard_map/ppermute | solution.py:199
  186.4 5.6 %collective-permute-start.37 = (bf16[2,16,4096]{2,1,0:T(8,128)(2,1)S(1)}, bf16[2,16,4096]{2,1,0:T(8,128)(2,1)S(1)}, u32[]{:S(2)}, u32[]{:S(2)}) collective-permute-start(bf16[2,16,4096]{2,1,0:T(8,128)(2,1)S(1)} %fusion.21), channel_id=1, source_target_pairs={{0,15},{1,0},{2,1},{3,2},{4,3},{5,4},{6,5},{7,6},{8,7},{9,8},{10,9... | collective-permute-start | bytes 786440 | tf_op jit(solution)/shard_map/ppermute | solution.py:199
  196.0 5.6 %collective-permute-start.38 = (bf16[2,16,4096]{2,1,0:T(8,128)(2,1)S(1)}, bf16[2,16,4096]{2,1,0:T(8,128)(2,1)S(1)}, u32[]{:S(2)}, u32[]{:S(2)}) collective-permute-start(bf16[2,16,4096]{2,1,0:T(8,128)(2,1)S(1)} %fusion.20), channel_id=1, source_target_pairs={{0,15},{1,0},{2,1},{3,2},{4,3},{5,4},{6,5},{7,6},{8,7},{9,8},{10,9... | collective-permute-start | bytes 786440 | tf_op jit(solution)/shard_map/ppermute | solution.py:199
  206.2 5.6 %collective-permute-start.39 = (bf16[2,16,4096]{2,1,0:T(8,128)(2,1)S(1)}, bf16[2,16,4096]{2,1,0:T(8,128)(2,1)S(1)}, u32[]{:S(2)}, u32[]{:S(2)}) collective-permute-start(bf16[2,16,4096]{2,1,0:T(8,128)(2,1)S(1)} %fusion.19), channel_id=1, source_target_pairs={{0,15},{1,0},{2,1},{3,2},{4,3},{5,4},{6,5},{7,6},{8,7},{9,8},{10,9... | collective-permute-start | bytes 786440 | tf_op jit(solution)/shard_map/ppermute | solution.py:199
  218.8 4.3 %collective-permute-done.30 = bf16[2,16,4096]{2,1,0:T(8,128)(2,1)S(1)} collective-permute-done((bf16[2,16,4096]{2,1,0:T(8,128)(2,1)S(1)}, bf16[2,16,4096]{2,1,0:T(8,128)(2,1)S(1)}, u32[]{:S(2)}, u32[]{:S(2)}) %collective-permute-start.30) | collective-permute-done | bytes 262176 | tf_op jit(solution)/shard_map/ppermute | solution.py:192
  227.0 5.1 %collective-permute-done.32 = bf16[16,4096]{1,0:T(8,128)(2,1)S(1)} collective-permute-done((bf16[16,4096]{1,0:T(8,128)(2,1)S(1)}, bf16[16,4096]{1,0:T(8,128)(2,1)S(1)}, u32[]{:S(2)}, u32[]{:S(2)}) %collective-permute-start.32) | collective-permute-done | bytes 131104 | tf_op jit(solution)/shard_map/ppermute | solution.py:190
  (167 shorter events, 99.4 us)
Async XLA Ops:
  2.0 55.5 %collective-permute-start.10 = (bf16[1,256,1024]{2,1,0:T(8,128)(2,1)S(1)}, bf16[1,256,1024]{2,1,0:T(8,128)(2,1)S(1)}, u32[]{:S(2)}, u32[]{:S(2)}) collective-permute-start(bf16[1,256,1024]{2,1,0:T(8,128)(2,1)S(1)} %bitcast.169), channel_id=1, source_target_pairs={{0,128},{32,160},{64,192},{96,224},{128,256},{160,288},{192,320},{... | collective-permute-start | bytes 1572872 | tf_op jit(solution)/shard_map/ppermute | solution.py:53
  9.5 69.8 %collective-permute-start.12 = (bf16[1,256,1024]{2,1,0:T(8,128)(2,1)S(1)}, bf16[1,256,1024]{2,1,0:T(8,128)(2,1)S(1)}, u32[]{:S(2)}, u32[]{:S(2)}) collective-permute-start(bf16[1,256,1024]{2,1,0:T(8,128)(2,1)S(1)} %bitcast.170), channel_id=1, source_target_pairs={{0,384},{32,416},{64,448},{96,480},{128,0},{160,32},{192,64},{224,... | collective-permute-start | bytes 1572872 | tf_op jit(solution)/shard_map/ppermute | solution.py:55
  14.4 14.0 %all-to-all-start = ((bf16[16,2,4224]{2,1,0:T(2,128)(2,1)}), bf16[16,2,4224]{2,1,0:T(2,128)(2,1)S(1)}, u32[]{:S(2)}, u32[]{:S(2)}) async-start(bf16[16,2,4224]{2,1,0:T(2,128)(2,1)} %reshape.947), calls=%async_computation | async-start | bytes 540672 | tf_op jit(solution)/shard_map/all_to_all | solution.py:97
  29.6 14.9 %collective-permute-start = (bf16[16,4096]{1,0:T(8,128)(2,1)S(1)}, bf16[16,4096]{1,0:T(8,128)(2,1)S(1)}, u32[]{:S(2)}, u32[]{:S(2)}) collective-permute-start(bf16[16,4096]{1,0:T(8,128)(2,1)S(1)} %broadcast_select_fusion), channel_id=1, source_target_pairs={{0,16},{1,17},{2,18},{3,19},{4,20},{5,21},{6,22},{7,23},{8,24},{9,... | collective-permute-start | bytes 393224 | tf_op jit(solution)/shard_map/ppermute | solution.py:128
  31.5 16.0 %collective-permute-start.2 = (bf16[16,4096]{1,0:T(8,128)(2,1)S(1)}, bf16[16,4096]{1,0:T(8,128)(2,1)S(1)}, u32[]{:S(2)}, u32[]{:S(2)}) collective-permute-start(bf16[16,4096]{1,0:T(8,128)(2,1)S(1)} %broadcast_select_fusion), channel_id=1, source_target_pairs={{0,31},{1,16},{2,17},{3,18},{4,19},{5,20},{6,21},{7,22},{8,23},{9,... | collective-permute-start | bytes 393224 | tf_op jit(solution)/shard_map/ppermute | solution.py:137
  44.5 10.2 %collective-permute-start.7 = (bf16[16,4096]{1,0:T(8,128)(2,1)S(1)}, bf16[16,4096]{1,0:T(8,128)(2,1)S(1)}, u32[]{:S(2)}, u32[]{:S(2)}) collective-permute-start(bf16[16,4096]{1,0:T(8,128)(2,1)S(1)} %broadcast_select_fusion), channel_id=1, source_target_pairs={{0,17},{1,18},{2,19},{3,20},{4,21},{5,22},{6,23},{7,24},{8,25},{9,... | collective-permute-start | bytes 393224 | tf_op jit(solution)/shard_map/ppermute | solution.py:130
  49.5 13.2 %collective-permute-start.3 = (bf16[2,16,4096]{2,1,0:T(8,128)(2,1)S(1)}, bf16[2,16,4096]{2,1,0:T(8,128)(2,1)S(1)}, u32[]{:S(2)}, u32[]{:S(2)}) collective-permute-start(bf16[2,16,4096]{2,1,0:T(8,128)(2,1)S(1)} %pad_maximum_fusion.5), channel_id=1, source_target_pairs={{0,15},{1,0},{2,1},{3,2},{4,3},{5,4},{6,5},{7,6},{8,7},{9,8},{10,9... | collective-permute-start | bytes 786440 | tf_op jit(solution)/shard_map/ppermute | solution.py:141
  55.6 12.2 %collective-permute-start.8 = (bf16[2,16,4096]{2,1,0:T(8,128)(2,1)S(1)}, bf16[2,16,4096]{2,1,0:T(8,128)(2,1)S(1)}, u32[]{:S(2)}, u32[]{:S(2)}) collective-permute-start(bf16[2,16,4096]{2,1,0:T(8,128)(2,1)S(1)} %pad_maximum_fusion.6), channel_id=1, source_target_pairs={{0,1},{1,2},{2,3},{3,4},{4,5},{5,6},{6,7},{7,8},{8,9},{9,10},{10,1... | collective-permute-start | bytes 786440 | tf_op jit(solution)/shard_map/ppermute | solution.py:134
  57.6 21.7 %collective-permute-start.11 = (bf16[1,256,1024]{2,1,0:T(8,128)(2,1)S(1)}, bf16[1,256,1024]{2,1,0:T(8,128)(2,1)S(1)}, u32[]{:S(2)}, u32[]{:S(2)}) collective-permute-start(bf16[1,256,1024]{2,1,0:T(8,128)(2,1)S(1)} %collective-permute-done.10), channel_id=1, source_target_pairs={{0,128},{32,160},{64,192},{96,224},{128,256},{160,288},{192,320},{... | collective-permute-start | bytes 1572872 | tf_op jit(solution)/shard_map/ppermute | solution.py:54
  71.7 11.4 %collective-permute-start.5 = (bf16[2,16,4096]{2,1,0:T(8,128)(2,1)S(1)}, bf16[2,16,4096]{2,1,0:T(8,128)(2,1)S(1)}, u32[]{:S(2)}, u32[]{:S(2)}) collective-permute-start(bf16[2,16,4096]{2,1,0:T(8,128)(2,1)S(1)} %collective-permute-done.4), channel_id=1, source_target_pairs={{0,15},{1,0},{2,1},{3,2},{4,3},{5,4},{6,5},{7,6},{8,7},{9,8},{10,9... | collective-permute-start | bytes 786440 | tf_op jit(solution)/shard_map/ppermute | solution.py:141
  77.3 11.1 %collective-permute-start.18 = (bf16[2,16,4096]{2,1,0:T(8,128)(2,1)S(1)}, bf16[2,16,4096]{2,1,0:T(8,128)(2,1)S(1)}, u32[]{:S(2)}, u32[]{:S(2)}) collective-permute-start(bf16[2,16,4096]{2,1,0:T(8,128)(2,1)S(1)} %collective-permute-done.9), channel_id=1, source_target_pairs={{0,1},{1,2},{2,3},{3,4},{4,5},{5,6},{6,7},{7,8},{8,9},{9,10},{10,1... | collective-permute-start | bytes 786440 | tf_op jit(solution)/shard_map/ppermute | solution.py:134
  79.6 47.7 %collective-permute-start.13 = (bf16[4,256,1024]{2,1,0:T(8,128)(2,1)S(1)}, bf16[4,256,1024]{2,1,0:T(8,128)(2,1)S(1)}, u32[]{:S(2)}, u32[]{:S(2)}) collective-permute-start(bf16[4,256,1024]{2,1,0:T(8,128)(2,1)S(1)} %pad_maximum_fusion), channel_id=1, source_target_pairs={{0,64},{32,96},{64,0},{96,32},{128,192},{160,224},{192,128},{224,1... | collective-permute-start | bytes 6291464 | tf_op jit(solution)/shard_map/ppermute | solution.py:57
  97.9 10.0 %collective-permute-start.20 = (bf16[2,16,4096]{2,1,0:T(8,128)(2,1)S(1)}, bf16[2,16,4096]{2,1,0:T(8,128)(2,1)S(1)}, u32[]{:S(2)}, u32[]{:S(2)}) collective-permute-start(bf16[2,16,4096]{2,1,0:T(8,128)(2,1)S(1)} %collective-permute-done.19), channel_id=1, source_target_pairs={{0,1},{1,2},{2,3},{3,4},{4,5},{5,6},{6,7},{7,8},{8,9},{9,10},{10,1... | collective-permute-start | bytes 786440 | tf_op jit(solution)/shard_map/ppermute | solution.py:134
  102.0 10.5 %collective-permute-start.17 = (bf16[2,16,4096]{2,1,0:T(8,128)(2,1)S(1)}, bf16[2,16,4096]{2,1,0:T(8,128)(2,1)S(1)}, u32[]{:S(2)}, u32[]{:S(2)}) collective-permute-start(bf16[2,16,4096]{2,1,0:T(8,128)(2,1)S(1)} %collective-permute-done.16), channel_id=1, source_target_pairs={{0,15},{1,0},{2,1},{3,2},{4,3},{5,4},{6,5},{7,6},{8,7},{9,8},{10,9... | collective-permute-start | bytes 786440 | tf_op jit(solution)/shard_map/ppermute | solution.py:141
  107.9 10.8 %collective-permute-start.21 = (bf16[2,16,4096]{2,1,0:T(8,128)(2,1)S(1)}, bf16[2,16,4096]{2,1,0:T(8,128)(2,1)S(1)}, u32[]{:S(2)}, u32[]{:S(2)}) collective-permute-start(bf16[2,16,4096]{2,1,0:T(8,128)(2,1)S(1)} %collective-permute-done.20), channel_id=1, source_target_pairs={{0,1},{1,2},{2,3},{3,4},{4,5},{5,6},{6,7},{7,8},{8,9},{9,10},{10,1... | collective-permute-start | bytes 786440 | tf_op jit(solution)/shard_map/ppermute | solution.py:134
  112.5 18.0 %collective-permute-start.23 = (bf16[2,16,2048]{2,1,0:T(8,128)(2,1)S(1)}, bf16[2,16,2048]{2,1,0:T(8,128)(2,1)S(1)}, u32[]{:S(2)}, u32[]{:S(2)}) collective-permute-start(bf16[2,16,2048]{2,1,0:T(8,128)(2,1)S(1)} %slice.321), channel_id=1, source_target_pairs={{0,15},{1,0},{2,1},{3,2},{4,3},{5,4},{6,5},{7,6},{8,7},{9,8},{10,9... | collective-permute-start | bytes 393224 | tf_op jit(solution)/shard_map/ppermute | solution.py:147
  118.7 11.8 %collective-permute-start.22 = (bf16[2,16,2048]{2,1,0:T(8,128)(2,1)S(1)}, bf16[2,16,2048]{2,1,0:T(8,128)(2,1)S(1)}, u32[]{:S(2)}, u32[]{:S(2)}) collective-permute-start(bf16[2,16,2048]{2,1,0:T(8,128)(2,1)S(1)} %slice.320), channel_id=1, source_target_pairs={{0,1},{1,2},{2,3},{3,4},{4,5},{5,6},{6,7},{7,8},{8,9},{9,10},{10,1... | collective-permute-start | bytes 393224 | tf_op jit(solution)/shard_map/ppermute | solution.py:146
  142.7 11.5 %collective-permute-start.24 = (bf16[2,16,4096]{2,1,0:T(8,128)(2,1)S(1)}, bf16[2,16,4096]{2,1,0:T(8,128)(2,1)S(1)}, u32[]{:S(2)}, u32[]{:S(2)}) collective-permute-start(bf16[2,16,4096]{2,1,0:T(8,128)(2,1)S(1)} %bitcast.217), channel_id=1, source_target_pairs={{0,1},{1,2},{2,3},{3,4},{4,5},{5,6},{6,7},{7,8},{8,9},{9,10},{10,1... | collective-permute-start | bytes 786440 | tf_op jit(solution)/shard_map/ppermute | solution.py:192
  144.6 12.7 %collective-permute-start.33 = (bf16[2,16,4096]{2,1,0:T(8,128)(2,1)S(1)}, bf16[2,16,4096]{2,1,0:T(8,128)(2,1)S(1)}, u32[]{:S(2)}, u32[]{:S(2)}) collective-permute-start(bf16[2,16,4096]{2,1,0:T(8,128)(2,1)S(1)} %bitcast.216), channel_id=1, source_target_pairs={{0,15},{1,0},{2,1},{3,2},{4,3},{5,4},{6,5},{7,6},{8,7},{9,8},{10,9... | collective-permute-start | bytes 786440 | tf_op jit(solution)/shard_map/ppermute | solution.py:199
  155.4 10.6 %collective-permute-start.25 = (bf16[2,16,4096]{2,1,0:T(8,128)(2,1)S(1)}, bf16[2,16,4096]{2,1,0:T(8,128)(2,1)S(1)}, u32[]{:S(2)}, u32[]{:S(2)}) collective-permute-start(bf16[2,16,4096]{2,1,0:T(8,128)(2,1)S(1)} %fusion.31), channel_id=1, source_target_pairs={{0,1},{1,2},{2,3},{3,4},{4,5},{5,6},{6,7},{7,8},{8,9},{9,10},{10,1... | collective-permute-start | bytes 786440 | tf_op jit(solution)/shard_map/ppermute | solution.py:192
  196.0 10.1 %collective-permute-start.38 = (bf16[2,16,4096]{2,1,0:T(8,128)(2,1)S(1)}, bf16[2,16,4096]{2,1,0:T(8,128)(2,1)S(1)}, u32[]{:S(2)}, u32[]{:S(2)}) collective-permute-start(bf16[2,16,4096]{2,1,0:T(8,128)(2,1)S(1)} %fusion.20), channel_id=1, source_target_pairs={{0,15},{1,0},{2,1},{3,2},{4,3},{5,4},{6,5},{7,6},{8,7},{9,8},{10,9... | collective-permute-start | bytes 786440 | tf_op jit(solution)/shard_map/ppermute | solution.py:199
  201.7 10.4 %collective-permute-start.29 = (bf16[2,16,4096]{2,1,0:T(8,128)(2,1)S(1)}, bf16[2,16,4096]{2,1,0:T(8,128)(2,1)S(1)}, u32[]{:S(2)}, u32[]{:S(2)}) collective-permute-start(bf16[2,16,4096]{2,1,0:T(8,128)(2,1)S(1)} %fusion.27), channel_id=1, source_target_pairs={{0,1},{1,2},{2,3},{3,4},{4,5},{5,6},{6,7},{7,8},{8,9},{9,10},{10,1... | collective-permute-start | bytes 786440 | tf_op jit(solution)/shard_map/ppermute | solution.py:192
  212.2 10.9 %collective-permute-start.30 = (bf16[2,16,4096]{2,1,0:T(8,128)(2,1)S(1)}, bf16[2,16,4096]{2,1,0:T(8,128)(2,1)S(1)}, u32[]{:S(2)}, u32[]{:S(2)}) collective-permute-start(bf16[2,16,4096]{2,1,0:T(8,128)(2,1)S(1)} %fusion.26), channel_id=1, source_target_pairs={{0,1},{1,2},{2,3},{3,4},{4,5},{5,6},{6,7},{7,8},{8,9},{9,10},{10,1... | collective-permute-start | bytes 786440 | tf_op jit(solution)/shard_map/ppermute | solution.py:192
  215.7 11.3 %collective-permute-start.40 = (bf16[16,4096]{1,0:T(8,128)(2,1)S(1)}, bf16[16,4096]{1,0:T(8,128)(2,1)S(1)}, u32[]{:S(2)}, u32[]{:S(2)}) collective-permute-start(bf16[16,4096]{1,0:T(8,128)(2,1)S(1)} %fusion.55), channel_id=1, source_target_pairs={{0,16},{1,17},{2,18},{3,19},{4,20},{5,21},{6,22},{7,23},{8,24},{9,... | collective-permute-start | bytes 393224 | tf_op jit(solution)/shard_map/ppermute | solution.py:206
  (21 other events, 185.2 us)

commit v15 on v13

--- a/solution.py
+++ b/solution.py
@@ -165,7 +165,7 @@
 
     chunk = nl * shard_rows
     blocks = {}
-    groups = ([8, 9], [5, 6, 7, 10, 11, 12], [0, 1, 2, 3, 4, 13, 14, 15])
+    groups = ([8, 9], [0, 1, 2, 3, 4, 5, 6, 7, 10, 11, 12, 13, 14, 15])
     hiddens = [
         ffn(jnp.concatenate([normed[k * chunk : (k + 1) * chunk] for k in group], axis=0)) for group in groups
     ]

time: 230 us -> 222 us (0.965)
  starting transfers between devices: 148 us -> 145 us
    ppermute x7, waiting for transfers between devices: 0.99 us -> 12.4 us  [per_device(): fwd = lax.ppermute(fwd, 'tensor', TP_Z_FWD)]
    ppermute x7, waiting for transfers between devices: 9.38 us -> 0.02 us  [per_device(): got = lax.ppermute(bwd, 'tensor', TP_Z_BWD)]
    ppermute x7, waiting for transfers between devices: 9.26 us -> 0.02 us  [per_device(): bwd = lax.ppermute(bwd, 'tensor', TP_Z_BWD)]
    ppermute x7, waiting for transfers between devices: 11.4 us -> 19.6 us  [per_device(): got = lax.ppermute(fwd, 'tensor', TP_Z_FWD)]
    ppermute x1, waiting for transfers between devices: 3.07 us -> 0.01 us  [per_device(): lax.ppermute(fwd[..., :half], 'tensor', TP_Z_FWD)]
    ppermute x1, waiting for transfers between devices: 0.67 us -> 3.46 us  [gather_pieces(): other_core = lax.ppermute(chip, 'dp', DP_C_SWAP)]
    dot_general x18 -> x12, matrix products: 8.32 us -> 7.25 us  [ffn(): jnp.dot(rows[:, col:col + width], buf.reshape(width, 2 * ff_cols), prefer...]
  transfers between devices with their start and end apart: 40 -> 40, of which waited for: 22 -> 18; matrix products, arithmetic and copies ran while one was open for 6% -> 6% of each run, Pallas kernels for 0% -> 0%
where the time goes in v15:
time: 222 us; the launch traced here: 219 us
  starting transfers between devices  145 us (65%)
  waiting for transfers between devices  51.6 us (23%)
  matrix products  10.6 us (5%)
  local copies, waits for them, and re-layouts  6.6 us (3%)
  other arithmetic  3.66 us (2%)
    ppermute x7, starting transfers between devices, per_device(): bwd = lax.ppermute(bwd, 'tensor', TP_Z_BWD)  39.3 us
    ppermute x7, starting transfers between devices, per_device(): got = lax.ppermute(bwd, 'tensor', TP_Z_BWD)  36.4 us
    ppermute x7, waiting for transfers between devices, per_device(): got = lax.ppermute(fwd, 'tensor', TP_Z_FWD)  19.6 us
    ppermute x7, starting transfers between devices, per_device(): fwd = lax.ppermute(fwd, 'tensor', TP_Z_FWD)  13.6 us
    ppermute x7, starting transfers between devices, per_device(): got = lax.ppermute(fwd, 'tensor', TP_Z_FWD)  13.4 us
    ppermute x7, waiting for transfers between devices, per_device(): fwd = lax.ppermute(fwd, 'tensor', TP_Z_FWD)  12.4 us
    ppermute x1, starting transfers between devices, gather_pieces(): fwd1 = lax.ppermute(own, 'dp', DP_Y_FWD)  7.5 us
    dot_general x12, matrix products, ffn(): jnp.dot(rows[:, col:col + width], buf.reshape(width, 2 * ff_cols), prefer...  7.25 us
  transfers between devices with their start and end apart: 40, of which 18 were waited for; matrix products, arithmetic and copies ran while one was open for 6% of the time, Pallas kernels for 0%

profile of v15, /device:TPU:24, one launch (start us, length us, event | category | flops | bytes accessed | tf_op | source)
XLA Modules:
  0.0 219.4 jit_solution(9426215271295438768)
XLA Ops:
  2.0 7.5 %collective-permute-start.14 = (bf16[1,256,1024]{2,1,0:T(8,128)(2,1)S(1)}, bf16[1,256,1024]{2,1,0:T(8,128)(2,1)S(1)}, u32[]{:S(2)}, u32[]{:S(2)}) collective-permute-start(bf16[1,256,1024]{2,1,0:T(8,128)(2,1)S(1)} %bitcast.160), channel_id=1, source_target_pairs={{0,128},{32,160},{64,192},{96,224},{128,256},{160,288},{192,320},{... | collective-permute-start | bytes 1572872 | tf_op jit(solution)/shard_map/ppermute | solution.py:52
  14.4 6.6 %all-to-all-start = ((bf16[16,2,4224]{2,1,0:T(2,128)(2,1)}), bf16[16,2,4224]{2,1,0:T(2,128)(2,1)S(1)}, u32[]{:S(2)}, u32[]{:S(2)}) async-start(bf16[16,2,4224]{2,1,0:T(2,128)(2,1)} %reshape.941), calls=%async_computation | async-start | bytes 540672 | tf_op jit(solution)/shard_map/all_to_all | solution.py:96
  22.2 6.2 %all-to-all-done = bf16[16,2,4224]{2,1,0:T(2,128)(2,1)S(1)} async-done(((bf16[16,2,4224]{2,1,0:T(2,128)(2,1)}), bf16[16,2,4224]{2,1,0:T(2,128)(2,1)S(1)}, u32[]{:S(2)}, u32[]{:S(2)}) %all-to-all-start) | async-done | bytes 270368 | tf_op jit(solution)/shard_map/all_to_all | solution.py:96
  31.7 5.1 %collective-permute-done = bf16[16,4096]{1,0:T(8,128)(2,1)S(1)} collective-permute-done((bf16[16,4096]{1,0:T(8,128)(2,1)S(1)}, bf16[16,4096]{1,0:T(8,128)(2,1)S(1)}, u32[]{:S(2)}, u32[]{:S(2)}) %collective-permute-start) | collective-permute-done | bytes 131104 | tf_op jit(solution)/shard_map/ppermute | solution.py:127
  38.8 8.4 %collective-permute-start.1 = (bf16[2,16,4096]{2,1,0:T(8,128)(2,1)S(1)}, bf16[2,16,4096]{2,1,0:T(8,128)(2,1)S(1)}, u32[]{:S(2)}, u32[]{:S(2)}) collective-permute-start(bf16[2,16,4096]{2,1,0:T(8,128)(2,1)S(1)} %pad_maximum_fusion.4), channel_id=1, source_target_pairs={{0,15},{1,0},{2,1},{3,2},{4,3},{5,4},{6,5},{7,6},{8,7},{9,8},{10,9... | collective-permute-start | bytes 786440 | tf_op jit(solution)/shard_map/ppermute | solution.py:135
  47.2 4.0 %collective-permute-start.15 = (bf16[1,256,1024]{2,1,0:T(8,128)(2,1)S(1)}, bf16[1,256,1024]{2,1,0:T(8,128)(2,1)S(1)}, u32[]{:S(2)}, u32[]{:S(2)}) collective-permute-start(bf16[1,256,1024]{2,1,0:T(8,128)(2,1)S(1)} %collective-permute-done.14), channel_id=1, source_target_pairs={{0,128},{32,160},{64,192},{96,224},{128,256},{160,288},{192,320},{... | collective-permute-start | bytes 1572872 | tf_op jit(solution)/shard_map/ppermute | solution.py:53
  54.3 5.1 %collective-permute-start.2 = (bf16[2,16,4096]{2,1,0:T(8,128)(2,1)S(1)}, bf16[2,16,4096]{2,1,0:T(8,128)(2,1)S(1)}, u32[]{:S(2)}, u32[]{:S(2)}) collective-permute-start(bf16[2,16,4096]{2,1,0:T(8,128)(2,1)S(1)} %collective-permute-done.1), channel_id=1, source_target_pairs={{0,15},{1,0},{2,1},{3,2},{4,3},{5,4},{6,5},{7,6},{8,7},{9,8},{10,9... | collective-permute-start | bytes 786440 | tf_op jit(solution)/shard_map/ppermute | solution.py:135
  63.8 5.1 %collective-permute-start.3 = (bf16[2,16,4096]{2,1,0:T(8,128)(2,1)S(1)}, bf16[2,16,4096]{2,1,0:T(8,128)(2,1)S(1)}, u32[]{:S(2)}, u32[]{:S(2)}) collective-permute-start(bf16[2,16,4096]{2,1,0:T(8,128)(2,1)S(1)} %collective-permute-done.2), channel_id=1, source_target_pairs={{0,15},{1,0},{2,1},{3,2},{4,3},{5,4},{6,5},{7,6},{8,7},{9,8},{10,9... | collective-permute-start | bytes 786440 | tf_op jit(solution)/shard_map/ppermute | solution.py:135
  69.2 3.7 %collective-permute-start.17 = (bf16[4,256,1024]{2,1,0:T(8,128)(2,1)S(1)}, bf16[4,256,1024]{2,1,0:T(8,128)(2,1)S(1)}, u32[]{:S(2)}, u32[]{:S(2)}) collective-permute-start(bf16[4,256,1024]{2,1,0:T(8,128)(2,1)S(1)} %pad_maximum_fusion), channel_id=1, source_target_pairs={{0,64},{32,96},{64,0},{96,32},{128,192},{160,224},{192,128},{224,1... | collective-permute-start | bytes 6291464 | tf_op jit(solution)/shard_map/ppermute | solution.py:56
  75.0 5.1 %collective-permute-start.4 = (bf16[2,16,4096]{2,1,0:T(8,128)(2,1)S(1)}, bf16[2,16,4096]{2,1,0:T(8,128)(2,1)S(1)}, u32[]{:S(2)}, u32[]{:S(2)}) collective-permute-start(bf16[2,16,4096]{2,1,0:T(8,128)(2,1)S(1)} %collective-permute-done.3), channel_id=1, source_target_pairs={{0,15},{1,0},{2,1},{3,2},{4,3},{5,4},{6,5},{7,6},{8,7},{9,8},{10,9... | collective-permute-start | bytes 786440 | tf_op jit(solution)/shard_map/ppermute | solution.py:135
  84.4 5.1 %collective-permute-start.5 = (bf16[2,16,4096]{2,1,0:T(8,128)(2,1)S(1)}, bf16[2,16,4096]{2,1,0:T(8,128)(2,1)S(1)}, u32[]{:S(2)}, u32[]{:S(2)}) collective-permute-start(bf16[2,16,4096]{2,1,0:T(8,128)(2,1)S(1)} %collective-permute-done.4), channel_id=1, source_target_pairs={{0,15},{1,0},{2,1},{3,2},{4,3},{5,4},{6,5},{7,6},{8,7},{9,8},{10,9... | collective-permute-start | bytes 786440 | tf_op jit(solution)/shard_map/ppermute | solution.py:135
  93.9 5.1 %collective-permute-start.6 = (bf16[2,16,4096]{2,1,0:T(8,128)(2,1)S(1)}, bf16[2,16,4096]{2,1,0:T(8,128)(2,1)S(1)}, u32[]{:S(2)}, u32[]{:S(2)}) collective-permute-start(bf16[2,16,4096]{2,1,0:T(8,128)(2,1)S(1)} %collective-permute-done.5), channel_id=1, source_target_pairs={{0,15},{1,0},{2,1},{3,2},{4,3},{5,4},{6,5},{7,6},{8,7},{9,8},{10,9... | collective-permute-start | bytes 786440 | tf_op jit(solution)/shard_map/ppermute | solution.py:135
  103.4 5.3 %collective-permute-start.7 = (bf16[2,16,4096]{2,1,0:T(8,128)(2,1)S(1)}, bf16[2,16,4096]{2,1,0:T(8,128)(2,1)S(1)}, u32[]{:S(2)}, u32[]{:S(2)}) collective-permute-start(bf16[2,16,4096]{2,1,0:T(8,128)(2,1)S(1)} %collective-permute-done.6), channel_id=1, source_target_pairs={{0,15},{1,0},{2,1},{3,2},{4,3},{5,4},{6,5},{7,6},{8,7},{9,8},{10,9... | collective-permute-start | bytes 786440 | tf_op jit(solution)/shard_map/ppermute | solution.py:135
  113.6 5.5 %collective-permute-start.21 = (bf16[2,16,2048]{2,1,0:T(8,128)(2,1)S(1)}, bf16[2,16,2048]{2,1,0:T(8,128)(2,1)S(1)}, u32[]{:S(2)}, u32[]{:S(2)}) collective-permute-start(bf16[2,16,2048]{2,1,0:T(8,128)(2,1)S(1)} %slice.279), channel_id=1, source_target_pairs={{0,15},{1,0},{2,1},{3,2},{4,3},{5,4},{6,5},{7,6},{8,7},{9,8},{10,9... | collective-permute-start | bytes 393224 | tf_op jit(solution)/shard_map/ppermute | solution.py:141
  124.9 3.5 %collective-permute-done.18 = bf16[8,256,1024]{2,1,0:T(8,128)(2,1)S(1)} collective-permute-done((bf16[8,256,1024]{2,1,0:T(8,128)(2,1)S(1)}, bf16[8,256,1024]{2,1,0:T(8,128)(2,1)S(1)}, u32[]{:S(2)}, u32[]{:S(2)}) %collective-permute-start.18) | collective-permute-done | bytes 4194336 | tf_op jit(solution)/shard_map/ppermute | solution.py:59
  134.4 5.3 %collective-permute-start.31 = (bf16[2,16,4096]{2,1,0:T(8,128)(2,1)S(1)}, bf16[2,16,4096]{2,1,0:T(8,128)(2,1)S(1)}, u32[]{:S(2)}, u32[]{:S(2)}) collective-permute-start(bf16[2,16,4096]{2,1,0:T(8,128)(2,1)S(1)} %bitcast.199), channel_id=1, source_target_pairs={{0,15},{1,0},{2,1},{3,2},{4,3},{5,4},{6,5},{7,6},{8,7},{9,8},{10,9... | collective-permute-start | bytes 786440 | tf_op jit(solution)/shard_map/ppermute | solution.py:193
  148.4 5.1 %collective-permute-start.32 = (bf16[2,16,4096]{2,1,0:T(8,128)(2,1)S(1)}, bf16[2,16,4096]{2,1,0:T(8,128)(2,1)S(1)}, u32[]{:S(2)}, u32[]{:S(2)}) collective-permute-start(bf16[2,16,4096]{2,1,0:T(8,128)(2,1)S(1)} %fusion.15), channel_id=1, source_target_pairs={{0,15},{1,0},{2,1},{3,2},{4,3},{5,4},{6,5},{7,6},{8,7},{9,8},{10,9... | collective-permute-start | bytes 786440 | tf_op jit(solution)/shard_map/ppermute | solution.py:193
  153.6 3.5 %collective-permute-done.23 = bf16[2,16,4096]{2,1,0:T(8,128)(2,1)S(1)} collective-permute-done((bf16[2,16,4096]{2,1,0:T(8,128)(2,1)S(1)}, bf16[2,16,4096]{2,1,0:T(8,128)(2,1)S(1)}, u32[]{:S(2)}, u32[]{:S(2)}) %collective-permute-start.23) | collective-permute-done | bytes 262176 | tf_op jit(solution)/shard_map/ppermute | solution.py:186
  159.1 5.1 %collective-permute-start.33 = (bf16[2,16,4096]{2,1,0:T(8,128)(2,1)S(1)}, bf16[2,16,4096]{2,1,0:T(8,128)(2,1)S(1)}, u32[]{:S(2)}, u32[]{:S(2)}) collective-permute-start(bf16[2,16,4096]{2,1,0:T(8,128)(2,1)S(1)} %fusion.14), channel_id=1, source_target_pairs={{0,15},{1,0},{2,1},{3,2},{4,3},{5,4},{6,5},{7,6},{8,7},{9,8},{10,9... | collective-permute-start | bytes 786440 | tf_op jit(solution)/shard_map/ppermute | solution.py:193
  168.9 5.1 %collective-permute-start.34 = (bf16[2,16,4096]{2,1,0:T(8,128)(2,1)S(1)}, bf16[2,16,4096]{2,1,0:T(8,128)(2,1)S(1)}, u32[]{:S(2)}, u32[]{:S(2)}) collective-permute-start(bf16[2,16,4096]{2,1,0:T(8,128)(2,1)S(1)} %fusion.13), channel_id=1, source_target_pairs={{0,15},{1,0},{2,1},{3,2},{4,3},{5,4},{6,5},{7,6},{8,7},{9,8},{10,9... | collective-permute-start | bytes 786440 | tf_op jit(solution)/shard_map/ppermute | solution.py:193
  178.4 5.1 %collective-permute-start.35 = (bf16[2,16,4096]{2,1,0:T(8,128)(2,1)S(1)}, bf16[2,16,4096]{2,1,0:T(8,128)(2,1)S(1)}, u32[]{:S(2)}, u32[]{:S(2)}) collective-permute-start(bf16[2,16,4096]{2,1,0:T(8,128)(2,1)S(1)} %fusion.12), channel_id=1, source_target_pairs={{0,15},{1,0},{2,1},{3,2},{4,3},{5,4},{6,5},{7,6},{8,7},{9,8},{10,9... | collective-permute-start | bytes 786440 | tf_op jit(solution)/shard_map/ppermute | solution.py:193
  188.0 5.1 %collective-permute-start.36 = (bf16[2,16,4096]{2,1,0:T(8,128)(2,1)S(1)}, bf16[2,16,4096]{2,1,0:T(8,128)(2,1)S(1)}, u32[]{:S(2)}, u32[]{:S(2)}) collective-permute-start(bf16[2,16,4096]{2,1,0:T(8,128)(2,1)S(1)} %fusion.11), channel_id=1, source_target_pairs={{0,15},{1,0},{2,1},{3,2},{4,3},{5,4},{6,5},{7,6},{8,7},{9,8},{10,9... | collective-permute-start | bytes 786440 | tf_op jit(solution)/shard_map/ppermute | solution.py:193
  197.7 5.4 %collective-permute-start.37 = (bf16[2,16,4096]{2,1,0:T(8,128)(2,1)S(1)}, bf16[2,16,4096]{2,1,0:T(8,128)(2,1)S(1)}, u32[]{:S(2)}, u32[]{:S(2)}) collective-permute-start(bf16[2,16,4096]{2,1,0:T(8,128)(2,1)S(1)} %fusion.10), channel_id=1, source_target_pairs={{0,15},{1,0},{2,1},{3,2},{4,3},{5,4},{6,5},{7,6},{8,7},{9,8},{10,9... | collective-permute-start | bytes 786440 | tf_op jit(solution)/shard_map/ppermute | solution.py:193
  210.3 3.5 %collective-permute-start.38 = (bf16[16,4096]{1,0:T(8,128)(2,1)S(1)}, bf16[16,4096]{1,0:T(8,128)(2,1)S(1)}, u32[]{:S(2)}, u32[]{:S(2)}) collective-permute-start(bf16[16,4096]{1,0:T(8,128)(2,1)S(1)} %fusion.37), channel_id=1, source_target_pairs={{0,16},{1,17},{2,18},{3,19},{4,20},{5,21},{6,22},{7,23},{8,24},{9,... | collective-permute-start | bytes 393224 | tf_op jit(solution)/shard_map/ppermute | solution.py:200
  (152 shorter events, 92.9 us)
Async XLA Ops:
  2.0 45.2 %collective-permute-start.14 = (bf16[1,256,1024]{2,1,0:T(8,128)(2,1)S(1)}, bf16[1,256,1024]{2,1,0:T(8,128)(2,1)S(1)}, u32[]{:S(2)}, u32[]{:S(2)}) collective-permute-start(bf16[1,256,1024]{2,1,0:T(8,128)(2,1)S(1)} %bitcast.160), channel_id=1, source_target_pairs={{0,128},{32,160},{64,192},{96,224},{128,256},{160,288},{192,320},{... | collective-permute-start | bytes 1572872 | tf_op jit(solution)/shard_map/ppermute | solution.py:52
  9.5 59.4 %collective-permute-start.16 = (bf16[1,256,1024]{2,1,0:T(8,128)(2,1)S(1)}, bf16[1,256,1024]{2,1,0:T(8,128)(2,1)S(1)}, u32[]{:S(2)}, u32[]{:S(2)}) collective-permute-start(bf16[1,256,1024]{2,1,0:T(8,128)(2,1)S(1)} %bitcast.161), channel_id=1, source_target_pairs={{0,384},{32,416},{64,448},{96,480},{128,0},{160,32},{192,64},{224,... | collective-permute-start | bytes 1572872 | tf_op jit(solution)/shard_map/ppermute | solution.py:54
  14.4 14.0 %all-to-all-start = ((bf16[16,2,4224]{2,1,0:T(2,128)(2,1)}), bf16[16,2,4224]{2,1,0:T(2,128)(2,1)S(1)}, u32[]{:S(2)}, u32[]{:S(2)}) async-start(bf16[16,2,4224]{2,1,0:T(2,128)(2,1)} %reshape.941), calls=%async_computation | async-start | bytes 540672 | tf_op jit(solution)/shard_map/all_to_all | solution.py:96
  36.8 15.3 %collective-permute-start.8 = (bf16[2,16,4096]{2,1,0:T(8,128)(2,1)S(1)}, bf16[2,16,4096]{2,1,0:T(8,128)(2,1)S(1)}, u32[]{:S(2)}, u32[]{:S(2)}) collective-permute-start(bf16[2,16,4096]{2,1,0:T(8,128)(2,1)S(1)} %pad_maximum_fusion.4), channel_id=1, source_target_pairs={{0,1},{1,2},{2,3},{3,4},{4,5},{5,6},{6,7},{7,8},{8,9},{9,10},{10,1... | collective-permute-start | bytes 786440 | tf_op jit(solution)/shard_map/ppermute | solution.py:131
  38.8 15.5 %collective-permute-start.1 = (bf16[2,16,4096]{2,1,0:T(8,128)(2,1)S(1)}, bf16[2,16,4096]{2,1,0:T(8,128)(2,1)S(1)}, u32[]{:S(2)}, u32[]{:S(2)}) collective-permute-start(bf16[2,16,4096]{2,1,0:T(8,128)(2,1)S(1)} %pad_maximum_fusion.4), channel_id=1, source_target_pairs={{0,15},{1,0},{2,1},{3,2},{4,3},{5,4},{6,5},{7,6},{8,7},{9,8},{10,9... | collective-permute-start | bytes 786440 | tf_op jit(solution)/shard_map/ppermute | solution.py:135
  47.2 21.7 %collective-permute-start.15 = (bf16[1,256,1024]{2,1,0:T(8,128)(2,1)S(1)}, bf16[1,256,1024]{2,1,0:T(8,128)(2,1)S(1)}, u32[]{:S(2)}, u32[]{:S(2)}) collective-permute-start(bf16[1,256,1024]{2,1,0:T(8,128)(2,1)S(1)} %collective-permute-done.14), channel_id=1, source_target_pairs={{0,128},{32,160},{64,192},{96,224},{128,256},{160,288},{192,320},{... | collective-permute-start | bytes 1572872 | tf_op jit(solution)/shard_map/ppermute | solution.py:53
  52.1 9.7 %collective-permute-start.9 = (bf16[2,16,4096]{2,1,0:T(8,128)(2,1)S(1)}, bf16[2,16,4096]{2,1,0:T(8,128)(2,1)S(1)}, u32[]{:S(2)}, u32[]{:S(2)}) collective-permute-start(bf16[2,16,4096]{2,1,0:T(8,128)(2,1)S(1)} %collective-permute-done.8), channel_id=1, source_target_pairs={{0,1},{1,2},{2,3},{3,4},{4,5},{5,6},{6,7},{7,8},{8,9},{9,10},{10,1... | collective-permute-start | bytes 786440 | tf_op jit(solution)/shard_map/ppermute | solution.py:131
  61.8 11.2 %collective-permute-start.10 = (bf16[2,16,4096]{2,1,0:T(8,128)(2,1)S(1)}, bf16[2,16,4096]{2,1,0:T(8,128)(2,1)S(1)}, u32[]{:S(2)}, u32[]{:S(2)}) collective-permute-start(bf16[2,16,4096]{2,1,0:T(8,128)(2,1)S(1)} %collective-permute-done.9), channel_id=1, source_target_pairs={{0,1},{1,2},{2,3},{3,4},{4,5},{5,6},{6,7},{7,8},{8,9},{9,10},{10,1... | collective-permute-start | bytes 786440 | tf_op jit(solution)/shard_map/ppermute | solution.py:131
  63.8 11.2 %collective-permute-start.3 = (bf16[2,16,4096]{2,1,0:T(8,128)(2,1)S(1)}, bf16[2,16,4096]{2,1,0:T(8,128)(2,1)S(1)}, u32[]{:S(2)}, u32[]{:S(2)}) collective-permute-start(bf16[2,16,4096]{2,1,0:T(8,128)(2,1)S(1)} %collective-permute-done.2), channel_id=1, source_target_pairs={{0,15},{1,0},{2,1},{3,2},{4,3},{5,4},{6,5},{7,6},{8,7},{9,8},{10,9... | collective-permute-start | bytes 786440 | tf_op jit(solution)/shard_map/ppermute | solution.py:135
  69.2 49.9 %collective-permute-start.17 = (bf16[4,256,1024]{2,1,0:T(8,128)(2,1)S(1)}, bf16[4,256,1024]{2,1,0:T(8,128)(2,1)S(1)}, u32[]{:S(2)}, u32[]{:S(2)}) collective-permute-start(bf16[4,256,1024]{2,1,0:T(8,128)(2,1)S(1)} %pad_maximum_fusion), channel_id=1, source_target_pairs={{0,64},{32,96},{64,0},{96,32},{128,192},{160,224},{192,128},{224,1... | collective-permute-start | bytes 6291464 | tf_op jit(solution)/shard_map/ppermute | solution.py:56
  73.0 9.5 %collective-permute-start.11 = (bf16[2,16,4096]{2,1,0:T(8,128)(2,1)S(1)}, bf16[2,16,4096]{2,1,0:T(8,128)(2,1)S(1)}, u32[]{:S(2)}, u32[]{:S(2)}) collective-permute-start(bf16[2,16,4096]{2,1,0:T(8,128)(2,1)S(1)} %collective-permute-done.10), channel_id=1, source_target_pairs={{0,1},{1,2},{2,3},{3,4},{4,5},{5,6},{6,7},{7,8},{8,9},{9,10},{10,1... | collective-permute-start | bytes 786440 | tf_op jit(solution)/shard_map/ppermute | solution.py:131
  101.4 10.1 %collective-permute-start.19 = (bf16[2,16,4096]{2,1,0:T(8,128)(2,1)S(1)}, bf16[2,16,4096]{2,1,0:T(8,128)(2,1)S(1)}, u32[]{:S(2)}, u32[]{:S(2)}) collective-permute-start(bf16[2,16,4096]{2,1,0:T(8,128)(2,1)S(1)} %collective-permute-done.13), channel_id=1, source_target_pairs={{0,1},{1,2},{2,3},{3,4},{4,5},{5,6},{6,7},{7,8},{8,9},{9,10},{10,1... | collective-permute-start | bytes 786440 | tf_op jit(solution)/shard_map/ppermute | solution.py:131
  103.4 10.2 %collective-permute-start.7 = (bf16[2,16,4096]{2,1,0:T(8,128)(2,1)S(1)}, bf16[2,16,4096]{2,1,0:T(8,128)(2,1)S(1)}, u32[]{:S(2)}, u32[]{:S(2)}) collective-permute-start(bf16[2,16,4096]{2,1,0:T(8,128)(2,1)S(1)} %collective-permute-done.6), channel_id=1, source_target_pairs={{0,15},{1,0},{2,1},{3,2},{4,3},{5,4},{6,5},{7,6},{8,7},{9,8},{10,9... | collective-permute-start | bytes 786440 | tf_op jit(solution)/shard_map/ppermute | solution.py:135
  111.6 11.0 %collective-permute-start.20 = (bf16[2,16,2048]{2,1,0:T(8,128)(2,1)S(1)}, bf16[2,16,2048]{2,1,0:T(8,128)(2,1)S(1)}, u32[]{:S(2)}, u32[]{:S(2)}) collective-permute-start(bf16[2,16,2048]{2,1,0:T(8,128)(2,1)S(1)} %slice.278), channel_id=1, source_target_pairs={{0,1},{1,2},{2,3},{3,4},{4,5},{5,6},{6,7},{7,8},{8,9},{9,10},{10,1... | collective-permute-start | bytes 393224 | tf_op jit(solution)/shard_map/ppermute | solution.py:140
  132.4 11.4 %collective-permute-start.22 = (bf16[2,16,4096]{2,1,0:T(8,128)(2,1)S(1)}, bf16[2,16,4096]{2,1,0:T(8,128)(2,1)S(1)}, u32[]{:S(2)}, u32[]{:S(2)}) collective-permute-start(bf16[2,16,4096]{2,1,0:T(8,128)(2,1)S(1)} %bitcast.200), channel_id=1, source_target_pairs={{0,1},{1,2},{2,3},{3,4},{4,5},{5,6},{6,7},{7,8},{8,9},{9,10},{10,1... | collective-permute-start | bytes 786440 | tf_op jit(solution)/shard_map/ppermute | solution.py:186
  134.4 14.0 %collective-permute-start.31 = (bf16[2,16,4096]{2,1,0:T(8,128)(2,1)S(1)}, bf16[2,16,4096]{2,1,0:T(8,128)(2,1)S(1)}, u32[]{:S(2)}, u32[]{:S(2)}) collective-permute-start(bf16[2,16,4096]{2,1,0:T(8,128)(2,1)S(1)} %bitcast.199), channel_id=1, source_target_pairs={{0,15},{1,0},{2,1},{3,2},{4,3},{5,4},{6,5},{7,6},{8,7},{9,8},{10,9... | collective-permute-start | bytes 786440 | tf_op jit(solution)/shard_map/ppermute | solution.py:193
  146.4 10.6 %collective-permute-start.23 = (bf16[2,16,4096]{2,1,0:T(8,128)(2,1)S(1)}, bf16[2,16,4096]{2,1,0:T(8,128)(2,1)S(1)}, u32[]{:S(2)}, u32[]{:S(2)}) collective-permute-start(bf16[2,16,4096]{2,1,0:T(8,128)(2,1)S(1)} %fusion.22), channel_id=1, source_target_pairs={{0,1},{1,2},{2,3},{3,4},{4,5},{5,6},{6,7},{7,8},{8,9},{9,10},{10,1... | collective-permute-start | bytes 786440 | tf_op jit(solution)/shard_map/ppermute | solution.py:186
  148.4 10.6 %collective-permute-start.32 = (bf16[2,16,4096]{2,1,0:T(8,128)(2,1)S(1)}, bf16[2,16,4096]{2,1,0:T(8,128)(2,1)S(1)}, u32[]{:S(2)}, u32[]{:S(2)}) collective-permute-start(bf16[2,16,4096]{2,1,0:T(8,128)(2,1)S(1)} %fusion.15), channel_id=1, source_target_pairs={{0,15},{1,0},{2,1},{3,2},{4,3},{5,4},{6,5},{7,6},{8,7},{9,8},{10,9... | collective-permute-start | bytes 786440 | tf_op jit(solution)/shard_map/ppermute | solution.py:193
  157.1 9.7 %collective-permute-start.24 = (bf16[2,16,4096]{2,1,0:T(8,128)(2,1)S(1)}, bf16[2,16,4096]{2,1,0:T(8,128)(2,1)S(1)}, u32[]{:S(2)}, u32[]{:S(2)}) collective-permute-start(bf16[2,16,4096]{2,1,0:T(8,128)(2,1)S(1)} %fusion.21), channel_id=1, source_target_pairs={{0,1},{1,2},{2,3},{3,4},{4,5},{5,6},{6,7},{7,8},{8,9},{9,10},{10,1... | collective-permute-start | bytes 786440 | tf_op jit(solution)/shard_map/ppermute | solution.py:186
  159.1 9.7 %collective-permute-start.33 = (bf16[2,16,4096]{2,1,0:T(8,128)(2,1)S(1)}, bf16[2,16,4096]{2,1,0:T(8,128)(2,1)S(1)}, u32[]{:S(2)}, u32[]{:S(2)}) collective-permute-start(bf16[2,16,4096]{2,1,0:T(8,128)(2,1)S(1)} %fusion.14), channel_id=1, source_target_pairs={{0,15},{1,0},{2,1},{3,2},{4,3},{5,4},{6,5},{7,6},{8,7},{9,8},{10,9... | collective-permute-start | bytes 786440 | tf_op jit(solution)/shard_map/ppermute | solution.py:193
  185.9 9.6 %collective-permute-start.27 = (bf16[2,16,4096]{2,1,0:T(8,128)(2,1)S(1)}, bf16[2,16,4096]{2,1,0:T(8,128)(2,1)S(1)}, u32[]{:S(2)}, u32[]{:S(2)}) collective-permute-start(bf16[2,16,4096]{2,1,0:T(8,128)(2,1)S(1)} %fusion.18), channel_id=1, source_target_pairs={{0,1},{1,2},{2,3},{3,4},{4,5},{5,6},{6,7},{7,8},{8,9},{9,10},{10,1... | collective-permute-start | bytes 786440 | tf_op jit(solution)/shard_map/ppermute | solution.py:186
  188.0 9.6 %collective-permute-start.36 = (bf16[2,16,4096]{2,1,0:T(8,128)(2,1)S(1)}, bf16[2,16,4096]{2,1,0:T(8,128)(2,1)S(1)}, u32[]{:S(2)}, u32[]{:S(2)}) collective-permute-start(bf16[2,16,4096]{2,1,0:T(8,128)(2,1)S(1)} %fusion.11), channel_id=1, source_target_pairs={{0,15},{1,0},{2,1},{3,2},{4,3},{5,4},{6,5},{7,6},{8,7},{9,8},{10,9... | collective-permute-start | bytes 786440 | tf_op jit(solution)/shard_map/ppermute | solution.py:193
  195.6 10.7 %collective-permute-start.28 = (bf16[2,16,4096]{2,1,0:T(8,128)(2,1)S(1)}, bf16[2,16,4096]{2,1,0:T(8,128)(2,1)S(1)}, u32[]{:S(2)}, u32[]{:S(2)}) collective-permute-start(bf16[2,16,4096]{2,1,0:T(8,128)(2,1)S(1)} %fusion.17), channel_id=1, source_target_pairs={{0,1},{1,2},{2,3},{3,4},{4,5},{5,6},{6,7},{7,8},{8,9},{9,10},{10,1... | collective-permute-start | bytes 786440 | tf_op jit(solution)/shard_map/ppermute | solution.py:186
  197.7 12.6 %collective-permute-start.37 = (bf16[2,16,4096]{2,1,0:T(8,128)(2,1)S(1)}, bf16[2,16,4096]{2,1,0:T(8,128)(2,1)S(1)}, u32[]{:S(2)}, u32[]{:S(2)}) collective-permute-start(bf16[2,16,4096]{2,1,0:T(8,128)(2,1)S(1)} %fusion.10), channel_id=1, source_target_pairs={{0,15},{1,0},{2,1},{3,2},{4,3},{5,4},{6,5},{7,6},{8,7},{9,8},{10,9... | collective-permute-start | bytes 786440 | tf_op jit(solution)/shard_map/ppermute | solution.py:193
  (19 other events, 181.8 us)

commit v16 on v15

--- a/solution.py
+++ b/solution.py
@@ -165,7 +165,7 @@
 
     chunk = nl * shard_rows
     blocks = {}
-    groups = ([8, 9], [0, 1, 2, 3, 4, 5, 6, 7, 10, 11, 12, 13, 14, 15])
+    groups = ([8, 9, 0, 1, 2, 3, 4, 5, 6, 7, 10, 11, 12, 13, 14, 15],)
     hiddens = [
         ffn(jnp.concatenate([normed[k * chunk : (k + 1) * chunk] for k in group], axis=0)) for group in groups
     ]

time: 222 us -> 255 us (1.15)
  waiting for transfers between devices: 51.6 us -> 85.1 us
  starting transfers between devices: 145 us -> 149 us
    ppermute x1, waiting for transfers between devices: 0.01 us -> 26.1 us  [gather_pieces(): lax.ppermute(jnp.concatenate([own, fwd1, fwd2, bwd1]), 'dp', DP_X_SWAP)]
    ppermute x7, waiting for transfers between devices: 0.02 us -> 16.2 us  [per_device(): got = lax.ppermute(bwd, 'tensor', TP_Z_BWD)]
    ppermute x7, waiting for transfers between devices: 19.6 us -> 5.15 us  [per_device(): got = lax.ppermute(fwd, 'tensor', TP_Z_FWD)]
    ppermute x7, waiting for transfers between devices: 12.4 us -> 0.59 us  [per_device(): fwd = lax.ppermute(fwd, 'tensor', TP_Z_FWD)]
    ppermute x7, waiting for transfers between devices: 0.02 us -> 8.65 us  [per_device(): bwd = lax.ppermute(bwd, 'tensor', TP_Z_BWD)]
    ppermute x1, waiting for transfers between devices: 0.01 us -> 5.6 us  [per_device(): lax.ppermute(fwd[..., :half], 'tensor', TP_Z_FWD)]
    ppermute x1, starting transfers between devices: 7.5 us -> 3.46 us  [gather_pieces(): fwd1 = lax.ppermute(own, 'dp', DP_Y_FWD)]
    ppermute x7, starting transfers between devices: 39.3 us -> 42.2 us  [per_device(): bwd = lax.ppermute(bwd, 'tensor', TP_Z_BWD)]
  transfers between devices with their start and end apart: 40 -> 40, of which waited for: 18 -> 23; matrix products, arithmetic and copies ran while one was open for 6% -> 2% of each run, Pallas kernels for 0% -> 0%
where the time goes in v16:
time: 255 us; the launch traced here: 252 us
  starting transfers between devices  149 us (58%)
  waiting for transfers between devices  85.1 us (33%)
  matrix products  8.53 us (3%)
  local copies, waits for them, and re-layouts  4.57 us (2%)
  other arithmetic  3.43 us (1%)
    ppermute x7, starting transfers between devices, per_device(): bwd = lax.ppermute(bwd, 'tensor', TP_Z_BWD)  42.2 us
    ppermute x7, starting transfers between devices, per_device(): got = lax.ppermute(bwd, 'tensor', TP_Z_BWD)  38.5 us
    ppermute x1, waiting for transfers between devices, gather_pieces(): lax.ppermute(jnp.concatenate([own, fwd1, fwd2, bwd1]), 'dp', DP_X_SWAP)  26.1 us
    ppermute x7, waiting for transfers between devices, per_device(): got = lax.ppermute(bwd, 'tensor', TP_Z_BWD)  16.2 us
    ppermute x7, starting transfers between devices, per_device(): got = lax.ppermute(fwd, 'tensor', TP_Z_FWD)  13.4 us
    ppermute x7, starting transfers between devices, per_device(): fwd = lax.ppermute(fwd, 'tensor', TP_Z_FWD)  13.4 us
    all_to_all x1, starting transfers between devices, per_device(): lax.all_to_all(jnp.concatenate([outgoing, place_cols], axis=1).reshape(dp...  8.99 us
    ppermute x7, waiting for transfers between devices, per_device(): bwd = lax.ppermute(bwd, 'tensor', TP_Z_BWD)  8.65 us
  transfers between devices with their start and end apart: 40, of which 23 were waited for; matrix products, arithmetic and copies ran while one was open for 2% of the time, Pallas kernels for 0%

profile of v16, /device:TPU:24, one launch (start us, length us, event | category | flops | bytes accessed | tf_op | source)
XLA Modules:
  0.0 252.3 jit_solution(9294383449576792508)
XLA Ops:
  3.0 9.0 %all-to-all-start = ((bf16[16,2,4224]{2,1,0:T(2,128)(2,1)}), bf16[16,2,4224]{2,1,0:T(2,128)(2,1)S(1)}, u32[]{:S(2)}, u32[]{:S(2)}) async-start(bf16[16,2,4224]{2,1,0:T(2,128)(2,1)} %reshape.935), calls=%async_computation | async-start | bytes 540672 | tf_op jit(solution)/shard_map/all_to_all | solution.py:96
  12.3 7.0 %all-to-all-done = bf16[16,2,4224]{2,1,0:T(2,128)(2,1)S(1)} async-done(((bf16[16,2,4224]{2,1,0:T(2,128)(2,1)}), bf16[16,2,4224]{2,1,0:T(2,128)(2,1)S(1)}, u32[]{:S(2)}, u32[]{:S(2)}) %all-to-all-start) | async-done | bytes 270368 | tf_op jit(solution)/shard_map/all_to_all | solution.py:96
  22.7 5.0 %collective-permute-done = bf16[16,4096]{1,0:T(8,128)(2,1)S(1)} collective-permute-done((bf16[16,4096]{1,0:T(8,128)(2,1)S(1)}, bf16[16,4096]{1,0:T(8,128)(2,1)S(1)}, u32[]{:S(2)}, u32[]{:S(2)}) %collective-permute-start) | collective-permute-done | bytes 131104 | tf_op jit(solution)/shard_map/ppermute | solution.py:127
  27.7 9.6 %collective-permute-start.9 = (bf16[2,16,4096]{2,1,0:T(8,128)(2,1)S(1)}, bf16[2,16,4096]{2,1,0:T(8,128)(2,1)S(1)}, u32[]{:S(2)}, u32[]{:S(2)}) collective-permute-start(bf16[2,16,4096]{2,1,0:T(8,128)(2,1)S(1)} %pad_maximum_fusion.2), channel_id=1, source_target_pairs={{0,15},{1,0},{2,1},{3,2},{4,3},{5,4},{6,5},{7,6},{8,7},{9,8},{10,9... | collective-permute-start | bytes 786440 | tf_op jit(solution)/shard_map/ppermute | solution.py:135
  42.0 5.6 %collective-permute-start.10 = (bf16[2,16,4096]{2,1,0:T(8,128)(2,1)S(1)}, bf16[2,16,4096]{2,1,0:T(8,128)(2,1)S(1)}, u32[]{:S(2)}, u32[]{:S(2)}) collective-permute-start(bf16[2,16,4096]{2,1,0:T(8,128)(2,1)S(1)} %collective-permute-done.9), channel_id=1, source_target_pairs={{0,15},{1,0},{2,1},{3,2},{4,3},{5,4},{6,5},{7,6},{8,7},{9,8},{10,9... | collective-permute-start | bytes 786440 | tf_op jit(solution)/shard_map/ppermute | solution.py:135
  51.4 5.6 %collective-permute-start.11 = (bf16[2,16,4096]{2,1,0:T(8,128)(2,1)S(1)}, bf16[2,16,4096]{2,1,0:T(8,128)(2,1)S(1)}, u32[]{:S(2)}, u32[]{:S(2)}) collective-permute-start(bf16[2,16,4096]{2,1,0:T(8,128)(2,1)S(1)} %collective-permute-done.10), channel_id=1, source_target_pairs={{0,15},{1,0},{2,1},{3,2},{4,3},{5,4},{6,5},{7,6},{8,7},{9,8},{10,9... | collective-permute-start | bytes 786440 | tf_op jit(solution)/shard_map/ppermute | solution.py:135
  62.5 5.1 %collective-permute-start.12 = (bf16[2,16,4096]{2,1,0:T(8,128)(2,1)S(1)}, bf16[2,16,4096]{2,1,0:T(8,128)(2,1)S(1)}, u32[]{:S(2)}, u32[]{:S(2)}) collective-permute-start(bf16[2,16,4096]{2,1,0:T(8,128)(2,1)S(1)} %collective-permute-done.11), channel_id=1, source_target_pairs={{0,15},{1,0},{2,1},{3,2},{4,3},{5,4},{6,5},{7,6},{8,7},{9,8},{10,9... | collective-permute-start | bytes 786440 | tf_op jit(solution)/shard_map/ppermute | solution.py:135
  71.5 5.6 %collective-permute-start.13 = (bf16[2,16,4096]{2,1,0:T(8,128)(2,1)S(1)}, bf16[2,16,4096]{2,1,0:T(8,128)(2,1)S(1)}, u32[]{:S(2)}, u32[]{:S(2)}) collective-permute-start(bf16[2,16,4096]{2,1,0:T(8,128)(2,1)S(1)} %collective-permute-done.12), channel_id=1, source_target_pairs={{0,15},{1,0},{2,1},{3,2},{4,3},{5,4},{6,5},{7,6},{8,7},{9,8},{10,9... | collective-permute-start | bytes 786440 | tf_op jit(solution)/shard_map/ppermute | solution.py:135
  81.5 4.9 %collective-permute-start.18 = (bf16[1,256,1024]{2,1,0:T(8,128)(2,1)S(1)}, bf16[1,256,1024]{2,1,0:T(8,128)(2,1)S(1)}, u32[]{:S(2)}, u32[]{:S(2)}) collective-permute-start(bf16[1,256,1024]{2,1,0:T(8,128)(2,1)S(1)} %collective-permute-done.17), channel_id=1, source_target_pairs={{0,128},{32,160},{64,192},{96,224},{128,256},{160,288},{192,320},{... | collective-permute-start | bytes 1572872 | tf_op jit(solution)/shard_map/ppermute | solution.py:53
  86.4 5.1 %collective-permute-start.14 = (bf16[2,16,4096]{2,1,0:T(8,128)(2,1)S(1)}, bf16[2,16,4096]{2,1,0:T(8,128)(2,1)S(1)}, u32[]{:S(2)}, u32[]{:S(2)}) collective-permute-start(bf16[2,16,4096]{2,1,0:T(8,128)(2,1)S(1)} %collective-permute-done.13), channel_id=1, source_target_pairs={{0,15},{1,0},{2,1},{3,2},{4,3},{5,4},{6,5},{7,6},{8,7},{9,8},{10,9... | collective-permute-start | bytes 786440 | tf_op jit(solution)/shard_map/ppermute | solution.py:135
  95.6 5.6 %collective-permute-start.15 = (bf16[2,16,4096]{2,1,0:T(8,128)(2,1)S(1)}, bf16[2,16,4096]{2,1,0:T(8,128)(2,1)S(1)}, u32[]{:S(2)}, u32[]{:S(2)}) collective-permute-start(bf16[2,16,4096]{2,1,0:T(8,128)(2,1)S(1)} %collective-permute-done.14), channel_id=1, source_target_pairs={{0,15},{1,0},{2,1},{3,2},{4,3},{5,4},{6,5},{7,6},{8,7},{9,8},{10,9... | collective-permute-start | bytes 786440 | tf_op jit(solution)/shard_map/ppermute | solution.py:135
  103.7 4.6 %collective-permute-start.20 = (bf16[4,256,1024]{2,1,0:T(8,128)(2,1)S(1)}, bf16[4,256,1024]{2,1,0:T(8,128)(2,1)S(1)}, u32[]{:S(2)}, u32[]{:S(2)}) collective-permute-start(bf16[4,256,1024]{2,1,0:T(8,128)(2,1)S(1)} %pad_maximum_fusion), channel_id=1, source_target_pairs={{0,64},{32,96},{64,0},{96,32},{128,192},{160,224},{192,128},{224,1... | collective-permute-start | bytes 6291464 | tf_op jit(solution)/shard_map/ppermute | solution.py:56
  108.4 5.1 %collective-permute-start.16 = (bf16[2,16,2048]{2,1,0:T(8,128)(2,1)S(1)}, bf16[2,16,2048]{2,1,0:T(8,128)(2,1)S(1)}, u32[]{:S(2)}, u32[]{:S(2)}) collective-permute-start(bf16[2,16,2048]{2,1,0:T(8,128)(2,1)S(1)} %slice.239), channel_id=1, source_target_pairs={{0,15},{1,0},{2,1},{3,2},{4,3},{5,4},{6,5},{7,6},{8,7},{9,8},{10,9... | collective-permute-start | bytes 393224 | tf_op jit(solution)/shard_map/ppermute | solution.py:141
  116.0 5.6 %collective-permute-done.8 = bf16[2,16,2048]{2,1,0:T(8,128)(2,1)S(1)} collective-permute-done((bf16[2,16,2048]{2,1,0:T(8,128)(2,1)S(1)}, bf16[2,16,2048]{2,1,0:T(8,128)(2,1)S(1)}, u32[]{:S(2)}, u32[]{:S(2)}) %collective-permute-start.8) | collective-permute-done | bytes 131104 | tf_op jit(solution)/shard_map/ppermute | solution.py:140
  121.9 26.1 %collective-permute-done.20 = bf16[4,256,1024]{2,1,0:T(8,128)(2,1)S(1)} collective-permute-done((bf16[4,256,1024]{2,1,0:T(8,128)(2,1)S(1)}, bf16[4,256,1024]{2,1,0:T(8,128)(2,1)S(1)}, u32[]{:S(2)}, u32[]{:S(2)}) %collective-permute-start.20) | collective-permute-done | bytes 2097184 | tf_op jit(solution)/shard_map/ppermute | solution.py:56
  164.6 4.9 %collective-permute-start.31 = (bf16[2,16,4096]{2,1,0:T(8,128)(2,1)S(1)}, bf16[2,16,4096]{2,1,0:T(8,128)(2,1)S(1)}, u32[]{:S(2)}, u32[]{:S(2)}) collective-permute-start(bf16[2,16,4096]{2,1,0:T(8,128)(2,1)S(1)} %bitcast.164), channel_id=1, source_target_pairs={{0,15},{1,0},{2,1},{3,2},{4,3},{5,4},{6,5},{7,6},{8,7},{9,8},{10,9... | collective-permute-start | bytes 786440 | tf_op jit(solution)/shard_map/ppermute | solution.py:193
  175.4 5.6 %collective-permute-start.32 = (bf16[2,16,4096]{2,1,0:T(8,128)(2,1)S(1)}, bf16[2,16,4096]{2,1,0:T(8,128)(2,1)S(1)}, u32[]{:S(2)}, u32[]{:S(2)}) collective-permute-start(bf16[2,16,4096]{2,1,0:T(8,128)(2,1)S(1)} %fusion.12), channel_id=1, source_target_pairs={{0,15},{1,0},{2,1},{3,2},{4,3},{5,4},{6,5},{7,6},{8,7},{9,8},{10,9... | collective-permute-start | bytes 786440 | tf_op jit(solution)/shard_map/ppermute | solution.py:193
  186.0 5.6 %collective-permute-start.33 = (bf16[2,16,4096]{2,1,0:T(8,128)(2,1)S(1)}, bf16[2,16,4096]{2,1,0:T(8,128)(2,1)S(1)}, u32[]{:S(2)}, u32[]{:S(2)}) collective-permute-start(bf16[2,16,4096]{2,1,0:T(8,128)(2,1)S(1)} %fusion.11), channel_id=1, source_target_pairs={{0,15},{1,0},{2,1},{3,2},{4,3},{5,4},{6,5},{7,6},{8,7},{9,8},{10,9... | collective-permute-start | bytes 786440 | tf_op jit(solution)/shard_map/ppermute | solution.py:193
  195.8 5.6 %collective-permute-start.34 = (bf16[2,16,4096]{2,1,0:T(8,128)(2,1)S(1)}, bf16[2,16,4096]{2,1,0:T(8,128)(2,1)S(1)}, u32[]{:S(2)}, u32[]{:S(2)}) collective-permute-start(bf16[2,16,4096]{2,1,0:T(8,128)(2,1)S(1)} %fusion.10), channel_id=1, source_target_pairs={{0,15},{1,0},{2,1},{3,2},{4,3},{5,4},{6,5},{7,6},{8,7},{9,8},{10,9... | collective-permute-start | bytes 786440 | tf_op jit(solution)/shard_map/ppermute | solution.py:193
  205.3 5.6 %collective-permute-start.35 = (bf16[2,16,4096]{2,1,0:T(8,128)(2,1)S(1)}, bf16[2,16,4096]{2,1,0:T(8,128)(2,1)S(1)}, u32[]{:S(2)}, u32[]{:S(2)}) collective-permute-start(bf16[2,16,4096]{2,1,0:T(8,128)(2,1)S(1)} %fusion.9), channel_id=1, source_target_pairs={{0,15},{1,0},{2,1},{3,2},{4,3},{5,4},{6,5},{7,6},{8,7},{9,8},{10,9... | collective-permute-start | bytes 786440 | tf_op jit(solution)/shard_map/ppermute | solution.py:193
  214.9 5.6 %collective-permute-start.36 = (bf16[2,16,4096]{2,1,0:T(8,128)(2,1)S(1)}, bf16[2,16,4096]{2,1,0:T(8,128)(2,1)S(1)}, u32[]{:S(2)}, u32[]{:S(2)}) collective-permute-start(bf16[2,16,4096]{2,1,0:T(8,128)(2,1)S(1)} %fusion.8), channel_id=1, source_target_pairs={{0,15},{1,0},{2,1},{3,2},{4,3},{5,4},{6,5},{7,6},{8,7},{9,8},{10,9... | collective-permute-start | bytes 786440 | tf_op jit(solution)/shard_map/ppermute | solution.py:193
  224.6 5.6 %collective-permute-start.37 = (bf16[2,16,4096]{2,1,0:T(8,128)(2,1)S(1)}, bf16[2,16,4096]{2,1,0:T(8,128)(2,1)S(1)}, u32[]{:S(2)}, u32[]{:S(2)}) collective-permute-start(bf16[2,16,4096]{2,1,0:T(8,128)(2,1)S(1)} %fusion.7), channel_id=1, source_target_pairs={{0,15},{1,0},{2,1},{3,2},{4,3},{5,4},{6,5},{7,6},{8,7},{9,8},{10,9... | collective-permute-start | bytes 786440 | tf_op jit(solution)/shard_map/ppermute | solution.py:193
  236.6 4.8 %collective-permute-done.28 = bf16[2,16,4096]{2,1,0:T(8,128)(2,1)S(1)} collective-permute-done((bf16[2,16,4096]{2,1,0:T(8,128)(2,1)S(1)}, bf16[2,16,4096]{2,1,0:T(8,128)(2,1)S(1)}, u32[]{:S(2)}, u32[]{:S(2)}) %collective-permute-start.28) | collective-permute-done | bytes 262176 | tf_op jit(solution)/shard_map/ppermute | solution.py:186
  245.4 5.1 %collective-permute-done.30 = bf16[16,4096]{1,0:T(8,128)(2,1)S(1)} collective-permute-done((bf16[16,4096]{1,0:T(8,128)(2,1)S(1)}, bf16[16,4096]{1,0:T(8,128)(2,1)S(1)}, u32[]{:S(2)}, u32[]{:S(2)}) %collective-permute-start.30) | collective-permute-done | bytes 131104 | tf_op jit(solution)/shard_map/ppermute | solution.py:184
  (147 shorter events, 92.8 us)
Async XLA Ops:
  3.0 16.3 %all-to-all-start = ((bf16[16,2,4224]{2,1,0:T(2,128)(2,1)}), bf16[16,2,4224]{2,1,0:T(2,128)(2,1)S(1)}, u32[]{:S(2)}, u32[]{:S(2)}) async-start(bf16[16,2,4224]{2,1,0:T(2,128)(2,1)} %reshape.935), calls=%async_computation | async-start | bytes 540672 | tf_op jit(solution)/shard_map/all_to_all | solution.py:96
  27.7 14.3 %collective-permute-start.9 = (bf16[2,16,4096]{2,1,0:T(8,128)(2,1)S(1)}, bf16[2,16,4096]{2,1,0:T(8,128)(2,1)S(1)}, u32[]{:S(2)}, u32[]{:S(2)}) collective-permute-start(bf16[2,16,4096]{2,1,0:T(8,128)(2,1)S(1)} %pad_maximum_fusion.2), channel_id=1, source_target_pairs={{0,15},{1,0},{2,1},{3,2},{4,3},{5,4},{6,5},{7,6},{8,7},{9,8},{10,9... | collective-permute-start | bytes 786440 | tf_op jit(solution)/shard_map/ppermute | solution.py:135
  37.3 10.2 %collective-permute-start.1 = (bf16[2,16,4096]{2,1,0:T(8,128)(2,1)S(1)}, bf16[2,16,4096]{2,1,0:T(8,128)(2,1)S(1)}, u32[]{:S(2)}, u32[]{:S(2)}) collective-permute-start(bf16[2,16,4096]{2,1,0:T(8,128)(2,1)S(1)} %pad_maximum_fusion.2), channel_id=1, source_target_pairs={{0,1},{1,2},{2,3},{3,4},{4,5},{5,6},{6,7},{7,8},{8,9},{9,10},{10,1... | collective-permute-start | bytes 786440 | tf_op jit(solution)/shard_map/ppermute | solution.py:131
  51.4 11.1 %collective-permute-start.11 = (bf16[2,16,4096]{2,1,0:T(8,128)(2,1)S(1)}, bf16[2,16,4096]{2,1,0:T(8,128)(2,1)S(1)}, u32[]{:S(2)}, u32[]{:S(2)}) collective-permute-start(bf16[2,16,4096]{2,1,0:T(8,128)(2,1)S(1)} %collective-permute-done.10), channel_id=1, source_target_pairs={{0,15},{1,0},{2,1},{3,2},{4,3},{5,4},{6,5},{7,6},{8,7},{9,8},{10,9... | collective-permute-start | bytes 786440 | tf_op jit(solution)/shard_map/ppermute | solution.py:135
  57.0 10.6 %collective-permute-start.3 = (bf16[2,16,4096]{2,1,0:T(8,128)(2,1)S(1)}, bf16[2,16,4096]{2,1,0:T(8,128)(2,1)S(1)}, u32[]{:S(2)}, u32[]{:S(2)}) collective-permute-start(bf16[2,16,4096]{2,1,0:T(8,128)(2,1)S(1)} %collective-permute-done.2), channel_id=1, source_target_pairs={{0,1},{1,2},{2,3},{3,4},{4,5},{5,6},{6,7},{7,8},{8,9},{9,10},{10,1... | collective-permute-start | bytes 786440 | tf_op jit(solution)/shard_map/ppermute | solution.py:131
  59.0 22.4 %collective-permute-start.17 = (bf16[1,256,1024]{2,1,0:T(8,128)(2,1)S(1)}, bf16[1,256,1024]{2,1,0:T(8,128)(2,1)S(1)}, u32[]{:S(2)}, u32[]{:S(2)}) collective-permute-start(bf16[1,256,1024]{2,1,0:T(8,128)(2,1)S(1)} %bitcast.137), channel_id=1, source_target_pairs={{0,128},{32,160},{64,192},{96,224},{128,256},{160,288},{192,320},{... | collective-permute-start | bytes 1572872 | tf_op jit(solution)/shard_map/ppermute | solution.py:52
  67.7 9.7 %collective-permute-start.4 = (bf16[2,16,4096]{2,1,0:T(8,128)(2,1)S(1)}, bf16[2,16,4096]{2,1,0:T(8,128)(2,1)S(1)}, u32[]{:S(2)}, u32[]{:S(2)}) collective-permute-start(bf16[2,16,4096]{2,1,0:T(8,128)(2,1)S(1)} %collective-permute-done.3), channel_id=1, source_target_pairs={{0,1},{1,2},{2,3},{3,4},{4,5},{5,6},{6,7},{7,8},{8,9},{9,10},{10,1... | collective-permute-start | bytes 786440 | tf_op jit(solution)/shard_map/ppermute | solution.py:131
  71.5 14.9 %collective-permute-start.13 = (bf16[2,16,4096]{2,1,0:T(8,128)(2,1)S(1)}, bf16[2,16,4096]{2,1,0:T(8,128)(2,1)S(1)}, u32[]{:S(2)}, u32[]{:S(2)}) collective-permute-start(bf16[2,16,4096]{2,1,0:T(8,128)(2,1)S(1)} %collective-permute-done.12), channel_id=1, source_target_pairs={{0,15},{1,0},{2,1},{3,2},{4,3},{5,4},{6,5},{7,6},{8,7},{9,8},{10,9... | collective-permute-start | bytes 786440 | tf_op jit(solution)/shard_map/ppermute | solution.py:135
  77.4 14.2 %collective-permute-start.5 = (bf16[2,16,4096]{2,1,0:T(8,128)(2,1)S(1)}, bf16[2,16,4096]{2,1,0:T(8,128)(2,1)S(1)}, u32[]{:S(2)}, u32[]{:S(2)}) collective-permute-start(bf16[2,16,4096]{2,1,0:T(8,128)(2,1)S(1)} %collective-permute-done.4), channel_id=1, source_target_pairs={{0,1},{1,2},{2,3},{3,4},{4,5},{5,6},{6,7},{7,8},{8,9},{9,10},{10,1... | collective-permute-start | bytes 786440 | tf_op jit(solution)/shard_map/ppermute | solution.py:131
  79.3 24.2 %collective-permute-start.19 = (bf16[1,256,1024]{2,1,0:T(8,128)(2,1)S(1)}, bf16[1,256,1024]{2,1,0:T(8,128)(2,1)S(1)}, u32[]{:S(2)}, u32[]{:S(2)}) collective-permute-start(bf16[1,256,1024]{2,1,0:T(8,128)(2,1)S(1)} %bitcast.138), channel_id=1, source_target_pairs={{0,384},{32,416},{64,448},{96,480},{128,0},{160,32},{192,64},{224,... | collective-permute-start | bytes 1572872 | tf_op jit(solution)/shard_map/ppermute | solution.py:54
  81.5 22.0 %collective-permute-start.18 = (bf16[1,256,1024]{2,1,0:T(8,128)(2,1)S(1)}, bf16[1,256,1024]{2,1,0:T(8,128)(2,1)S(1)}, u32[]{:S(2)}, u32[]{:S(2)}) collective-permute-start(bf16[1,256,1024]{2,1,0:T(8,128)(2,1)S(1)} %collective-permute-done.17), channel_id=1, source_target_pairs={{0,128},{32,160},{64,192},{96,224},{128,256},{160,288},{192,320},{... | collective-permute-start | bytes 1572872 | tf_op jit(solution)/shard_map/ppermute | solution.py:53
  91.5 9.9 %collective-permute-start.6 = (bf16[2,16,4096]{2,1,0:T(8,128)(2,1)S(1)}, bf16[2,16,4096]{2,1,0:T(8,128)(2,1)S(1)}, u32[]{:S(2)}, u32[]{:S(2)}) collective-permute-start(bf16[2,16,4096]{2,1,0:T(8,128)(2,1)S(1)} %collective-permute-done.5), channel_id=1, source_target_pairs={{0,1},{1,2},{2,3},{3,4},{4,5},{5,6},{6,7},{7,8},{8,9},{9,10},{10,1... | collective-permute-start | bytes 786440 | tf_op jit(solution)/shard_map/ppermute | solution.py:131
  95.6 12.8 %collective-permute-start.15 = (bf16[2,16,4096]{2,1,0:T(8,128)(2,1)S(1)}, bf16[2,16,4096]{2,1,0:T(8,128)(2,1)S(1)}, u32[]{:S(2)}, u32[]{:S(2)}) collective-permute-start(bf16[2,16,4096]{2,1,0:T(8,128)(2,1)S(1)} %collective-permute-done.14), channel_id=1, source_target_pairs={{0,15},{1,0},{2,1},{3,2},{4,3},{5,4},{6,5},{7,6},{8,7},{9,8},{10,9... | collective-permute-start | bytes 786440 | tf_op jit(solution)/shard_map/ppermute | solution.py:135
  101.5 12.0 %collective-permute-start.7 = (bf16[2,16,4096]{2,1,0:T(8,128)(2,1)S(1)}, bf16[2,16,4096]{2,1,0:T(8,128)(2,1)S(1)}, u32[]{:S(2)}, u32[]{:S(2)}) collective-permute-start(bf16[2,16,4096]{2,1,0:T(8,128)(2,1)S(1)} %collective-permute-done.6), channel_id=1, source_target_pairs={{0,1},{1,2},{2,3},{3,4},{4,5},{5,6},{6,7},{7,8},{8,9},{9,10},{10,1... | collective-permute-start | bytes 786440 | tf_op jit(solution)/shard_map/ppermute | solution.py:131
  103.7 44.2 %collective-permute-start.20 = (bf16[4,256,1024]{2,1,0:T(8,128)(2,1)S(1)}, bf16[4,256,1024]{2,1,0:T(8,128)(2,1)S(1)}, u32[]{:S(2)}, u32[]{:S(2)}) collective-permute-start(bf16[4,256,1024]{2,1,0:T(8,128)(2,1)S(1)} %pad_maximum_fusion), channel_id=1, source_target_pairs={{0,64},{32,96},{64,0},{96,32},{128,192},{160,224},{192,128},{224,1... | collective-permute-start | bytes 6291464 | tf_op jit(solution)/shard_map/ppermute | solution.py:56
  164.6 10.7 %collective-permute-start.31 = (bf16[2,16,4096]{2,1,0:T(8,128)(2,1)S(1)}, bf16[2,16,4096]{2,1,0:T(8,128)(2,1)S(1)}, u32[]{:S(2)}, u32[]{:S(2)}) collective-permute-start(bf16[2,16,4096]{2,1,0:T(8,128)(2,1)S(1)} %bitcast.164), channel_id=1, source_target_pairs={{0,15},{1,0},{2,1},{3,2},{4,3},{5,4},{6,5},{7,6},{8,7},{9,8},{10,9... | collective-permute-start | bytes 786440 | tf_op jit(solution)/shard_map/ppermute | solution.py:193
  169.5 11.5 %collective-permute-start.22 = (bf16[2,16,4096]{2,1,0:T(8,128)(2,1)S(1)}, bf16[2,16,4096]{2,1,0:T(8,128)(2,1)S(1)}, u32[]{:S(2)}, u32[]{:S(2)}) collective-permute-start(bf16[2,16,4096]{2,1,0:T(8,128)(2,1)S(1)} %bitcast.163), channel_id=1, source_target_pairs={{0,1},{1,2},{2,3},{3,4},{4,5},{5,6},{6,7},{7,8},{8,9},{9,10},{10,1... | collective-permute-start | bytes 786440 | tf_op jit(solution)/shard_map/ppermute | solution.py:186
  175.4 10.6 %collective-permute-start.32 = (bf16[2,16,4096]{2,1,0:T(8,128)(2,1)S(1)}, bf16[2,16,4096]{2,1,0:T(8,128)(2,1)S(1)}, u32[]{:S(2)}, u32[]{:S(2)}) collective-permute-start(bf16[2,16,4096]{2,1,0:T(8,128)(2,1)S(1)} %fusion.12), channel_id=1, source_target_pairs={{0,15},{1,0},{2,1},{3,2},{4,3},{5,4},{6,5},{7,6},{8,7},{9,8},{10,9... | collective-permute-start | bytes 786440 | tf_op jit(solution)/shard_map/ppermute | solution.py:193
  181.1 10.6 %collective-permute-start.23 = (bf16[2,16,4096]{2,1,0:T(8,128)(2,1)S(1)}, bf16[2,16,4096]{2,1,0:T(8,128)(2,1)S(1)}, u32[]{:S(2)}, u32[]{:S(2)}) collective-permute-start(bf16[2,16,4096]{2,1,0:T(8,128)(2,1)S(1)} %fusion.19), channel_id=1, source_target_pairs={{0,1},{1,2},{2,3},{3,4},{4,5},{5,6},{6,7},{7,8},{8,9},{9,10},{10,1... | collective-permute-start | bytes 786440 | tf_op jit(solution)/shard_map/ppermute | solution.py:186
  186.0 9.7 %collective-permute-start.33 = (bf16[2,16,4096]{2,1,0:T(8,128)(2,1)S(1)}, bf16[2,16,4096]{2,1,0:T(8,128)(2,1)S(1)}, u32[]{:S(2)}, u32[]{:S(2)}) collective-permute-start(bf16[2,16,4096]{2,1,0:T(8,128)(2,1)S(1)} %fusion.11), channel_id=1, source_target_pairs={{0,15},{1,0},{2,1},{3,2},{4,3},{5,4},{6,5},{7,6},{8,7},{9,8},{10,9... | collective-permute-start | bytes 786440 | tf_op jit(solution)/shard_map/ppermute | solution.py:193
  191.7 9.7 %collective-permute-start.24 = (bf16[2,16,4096]{2,1,0:T(8,128)(2,1)S(1)}, bf16[2,16,4096]{2,1,0:T(8,128)(2,1)S(1)}, u32[]{:S(2)}, u32[]{:S(2)}) collective-permute-start(bf16[2,16,4096]{2,1,0:T(8,128)(2,1)S(1)} %fusion.18), channel_id=1, source_target_pairs={{0,1},{1,2},{2,3},{3,4},{4,5},{5,6},{6,7},{7,8},{8,9},{9,10},{10,1... | collective-permute-start | bytes 786440 | tf_op jit(solution)/shard_map/ppermute | solution.py:186
  220.6 9.9 %collective-permute-start.27 = (bf16[2,16,4096]{2,1,0:T(8,128)(2,1)S(1)}, bf16[2,16,4096]{2,1,0:T(8,128)(2,1)S(1)}, u32[]{:S(2)}, u32[]{:S(2)}) collective-permute-start(bf16[2,16,4096]{2,1,0:T(8,128)(2,1)S(1)} %fusion.15), channel_id=1, source_target_pairs={{0,1},{1,2},{2,3},{3,4},{4,5},{5,6},{6,7},{7,8},{8,9},{9,10},{10,1... | collective-permute-start | bytes 786440 | tf_op jit(solution)/shard_map/ppermute | solution.py:186
  230.5 10.9 %collective-permute-start.28 = (bf16[2,16,4096]{2,1,0:T(8,128)(2,1)S(1)}, bf16[2,16,4096]{2,1,0:T(8,128)(2,1)S(1)}, u32[]{:S(2)}, u32[]{:S(2)}) collective-permute-start(bf16[2,16,4096]{2,1,0:T(8,128)(2,1)S(1)} %fusion.14), channel_id=1, source_target_pairs={{0,1},{1,2},{2,3},{3,4},{4,5},{5,6},{6,7},{7,8},{8,9},{9,10},{10,1... | collective-permute-start | bytes 786440 | tf_op jit(solution)/shard_map/ppermute | solution.py:186
  234.1 11.3 %collective-permute-start.38 = (bf16[16,4096]{1,0:T(8,128)(2,1)S(1)}, bf16[16,4096]{1,0:T(8,128)(2,1)S(1)}, u32[]{:S(2)}, u32[]{:S(2)}) collective-permute-start(bf16[16,4096]{1,0:T(8,128)(2,1)S(1)} %fusion.32), channel_id=1, source_target_pairs={{0,16},{1,17},{2,18},{3,19},{4,20},{5,21},{6,22},{7,23},{8,24},{9,... | collective-permute-start | bytes 393224 | tf_op jit(solution)/shard_map/ppermute | solution.py:200
  (20 other events, 265.1 us)

commit v17 on v16

--- a/solution.py
+++ b/solution.py
@@ -165,7 +165,7 @@
 
     chunk = nl * shard_rows
     blocks = {}
-    groups = ([8, 9, 0, 1, 2, 3, 4, 5, 6, 7, 10, 11, 12, 13, 14, 15],)
+    groups = ([8, 9, 7, 10], [0, 1, 2, 3, 4, 5, 6, 11, 12, 13, 14, 15])
     hiddens = [
         ffn(jnp.concatenate([normed[k * chunk : (k + 1) * chunk] for k in group], axis=0)) for group in groups
     ]

time: 255 us -> 239 us (0.937)
  waiting for transfers between devices: 85.1 us -> 67 us
  starting transfers between devices: 149 us -> 145 us
  local copies, waits for them, and re-layouts: 4.57 us -> 8.37 us
    ppermute x7, waiting for transfers between devices: 0.59 us -> 14.2 us  [per_device(): fwd = lax.ppermute(fwd, 'tensor', TP_Z_FWD)]
    ppermute x1, waiting for transfers between devices: 26.1 us -> 13.3 us  [gather_pieces(): lax.ppermute(jnp.concatenate([own, fwd1, fwd2, bwd1]), 'dp', DP_X_SWAP)]
    ppermute x7, starting transfers between devices: 42.2 us -> 36.3 us  [per_device(): bwd = lax.ppermute(bwd, 'tensor', TP_Z_BWD)]
    ppermute x1, waiting for transfers between devices: 5.6 us -> 0.58 us  [per_device(): lax.ppermute(fwd[..., :half], 'tensor', TP_Z_FWD)]
    ppermute x7, waiting for transfers between devices: 8.65 us -> 3.86 us  [per_device(): bwd = lax.ppermute(bwd, 'tensor', TP_Z_BWD)]
    ppermute x1, waiting for transfers between devices: 4.14 us -> 0.01 us  [gather_pieces(): other_core = lax.ppermute(chip, 'dp', DP_C_SWAP)]
    ppermute x1, starting transfers between devices: 3.46 us -> 7.5 us  [gather_pieces(): fwd1 = lax.ppermute(own, 'dp', DP_Y_FWD)]
    ppermute x7, waiting for transfers between devices: 16.2 us -> 13.2 us  [per_device(): got = lax.ppermute(bwd, 'tensor', TP_Z_BWD)]
  transfers between devices with their start and end apart: 40 -> 40, of which waited for: 23 -> 22; matrix products, arithmetic and copies ran while one was open for 2% -> 6% of each run, Pallas kernels for 0% -> 0%
where the time goes in v17:
time: 239 us; the launch traced here: 235 us
  starting transfers between devices  145 us (61%)
  waiting for transfers between devices  67 us (28%)
  matrix products  9.72 us (4%)
  local copies, waits for them, and re-layouts  8.37 us (4%)
  other arithmetic  3.6 us (2%)
    ppermute x7, starting transfers between devices, per_device(): got = lax.ppermute(bwd, 'tensor', TP_Z_BWD)  38.7 us
    ppermute x7, starting transfers between devices, per_device(): bwd = lax.ppermute(bwd, 'tensor', TP_Z_BWD)  36.3 us
    ppermute x7, starting transfers between devices, per_device(): fwd = lax.ppermute(fwd, 'tensor', TP_Z_FWD)  15.4 us
    ppermute x7, waiting for transfers between devices, per_device(): fwd = lax.ppermute(fwd, 'tensor', TP_Z_FWD)  14.2 us
    ppermute x7, starting transfers between devices, per_device(): got = lax.ppermute(fwd, 'tensor', TP_Z_FWD)  13.6 us
    ppermute x1, waiting for transfers between devices, gather_pieces(): lax.ppermute(jnp.concatenate([own, fwd1, fwd2, bwd1]), 'dp', DP_X_SWAP)  13.3 us
    ppermute x7, waiting for transfers between devices, per_device(): got = lax.ppermute(bwd, 'tensor', TP_Z_BWD)  13.2 us
    ppermute x1, starting transfers between devices, gather_pieces(): fwd1 = lax.ppermute(own, 'dp', DP_Y_FWD)  7.5 us
  transfers between devices with their start and end apart: 40, of which 22 were waited for; matrix products, arithmetic and copies ran while one was open for 6% of the time, Pallas kernels for 0%

profile of v17, /device:TPU:24, one launch (start us, length us, event | category | flops | bytes accessed | tf_op | source)
XLA Modules:
  0.0 235.2 jit_solution(2565599630699803289)
XLA Ops:
  2.0 7.5 %collective-permute-start.12 = (bf16[1,256,1024]{2,1,0:T(8,128)(2,1)S(1)}, bf16[1,256,1024]{2,1,0:T(8,128)(2,1)S(1)}, u32[]{:S(2)}, u32[]{:S(2)}) collective-permute-start(bf16[1,256,1024]{2,1,0:T(8,128)(2,1)S(1)} %bitcast.166), channel_id=1, source_target_pairs={{0,128},{32,160},{64,192},{96,224},{128,256},{160,288},{192,320},{... | collective-permute-start | bytes 1572872 | tf_op jit(solution)/shard_map/ppermute | solution.py:52
  14.4 6.6 %all-to-all-start = ((bf16[16,2,4224]{2,1,0:T(2,128)(2,1)}), bf16[16,2,4224]{2,1,0:T(2,128)(2,1)S(1)}, u32[]{:S(2)}, u32[]{:S(2)}) async-start(bf16[16,2,4224]{2,1,0:T(2,128)(2,1)} %reshape.941), calls=%async_computation | async-start | bytes 540672 | tf_op jit(solution)/shard_map/all_to_all | solution.py:96
  22.2 6.2 %all-to-all-done = bf16[16,2,4224]{2,1,0:T(2,128)(2,1)S(1)} async-done(((bf16[16,2,4224]{2,1,0:T(2,128)(2,1)}), bf16[16,2,4224]{2,1,0:T(2,128)(2,1)S(1)}, u32[]{:S(2)}, u32[]{:S(2)}) %all-to-all-start) | async-done | bytes 270368 | tf_op jit(solution)/shard_map/all_to_all | solution.py:96
  31.7 5.1 %collective-permute-done = bf16[16,4096]{1,0:T(8,128)(2,1)S(1)} collective-permute-done((bf16[16,4096]{1,0:T(8,128)(2,1)S(1)}, bf16[16,4096]{1,0:T(8,128)(2,1)S(1)}, u32[]{:S(2)}, u32[]{:S(2)}) %collective-permute-start) | collective-permute-done | bytes 131104 | tf_op jit(solution)/shard_map/ppermute | solution.py:127
  38.8 8.4 %collective-permute-start.1 = (bf16[2,16,4096]{2,1,0:T(8,128)(2,1)S(1)}, bf16[2,16,4096]{2,1,0:T(8,128)(2,1)S(1)}, u32[]{:S(2)}, u32[]{:S(2)}) collective-permute-start(bf16[2,16,4096]{2,1,0:T(8,128)(2,1)S(1)} %pad_maximum_fusion.8), channel_id=1, source_target_pairs={{0,15},{1,0},{2,1},{3,2},{4,3},{5,4},{6,5},{7,6},{8,7},{9,8},{10,9... | collective-permute-start | bytes 786440 | tf_op jit(solution)/shard_map/ppermute | solution.py:135
  47.2 4.0 %collective-permute-start.13 = (bf16[1,256,1024]{2,1,0:T(8,128)(2,1)S(1)}, bf16[1,256,1024]{2,1,0:T(8,128)(2,1)S(1)}, u32[]{:S(2)}, u32[]{:S(2)}) collective-permute-start(bf16[1,256,1024]{2,1,0:T(8,128)(2,1)S(1)} %collective-permute-done.12), channel_id=1, source_target_pairs={{0,128},{32,160},{64,192},{96,224},{128,256},{160,288},{192,320},{... | collective-permute-start | bytes 1572872 | tf_op jit(solution)/shard_map/ppermute | solution.py:53
  54.3 5.1 %collective-permute-start.2 = (bf16[2,16,4096]{2,1,0:T(8,128)(2,1)S(1)}, bf16[2,16,4096]{2,1,0:T(8,128)(2,1)S(1)}, u32[]{:S(2)}, u32[]{:S(2)}) collective-permute-start(bf16[2,16,4096]{2,1,0:T(8,128)(2,1)S(1)} %collective-permute-done.1), channel_id=1, source_target_pairs={{0,15},{1,0},{2,1},{3,2},{4,3},{5,4},{6,5},{7,6},{8,7},{9,8},{10,9... | collective-permute-start | bytes 786440 | tf_op jit(solution)/shard_map/ppermute | solution.py:135
  63.8 5.1 %collective-permute-start.3 = (bf16[2,16,4096]{2,1,0:T(8,128)(2,1)S(1)}, bf16[2,16,4096]{2,1,0:T(8,128)(2,1)S(1)}, u32[]{:S(2)}, u32[]{:S(2)}) collective-permute-start(bf16[2,16,4096]{2,1,0:T(8,128)(2,1)S(1)} %collective-permute-done.2), channel_id=1, source_target_pairs={{0,15},{1,0},{2,1},{3,2},{4,3},{5,4},{6,5},{7,6},{8,7},{9,8},{10,9... | collective-permute-start | bytes 786440 | tf_op jit(solution)/shard_map/ppermute | solution.py:135
  69.2 3.7 %collective-permute-start.15 = (bf16[4,256,1024]{2,1,0:T(8,128)(2,1)S(1)}, bf16[4,256,1024]{2,1,0:T(8,128)(2,1)S(1)}, u32[]{:S(2)}, u32[]{:S(2)}) collective-permute-start(bf16[4,256,1024]{2,1,0:T(8,128)(2,1)S(1)} %pad_maximum_fusion), channel_id=1, source_target_pairs={{0,64},{32,96},{64,0},{96,32},{128,192},{160,224},{192,128},{224,1... | collective-permute-start | bytes 6291464 | tf_op jit(solution)/shard_map/ppermute | solution.py:56
  75.0 5.1 %collective-permute-start.4 = (bf16[2,16,4096]{2,1,0:T(8,128)(2,1)S(1)}, bf16[2,16,4096]{2,1,0:T(8,128)(2,1)S(1)}, u32[]{:S(2)}, u32[]{:S(2)}) collective-permute-start(bf16[2,16,4096]{2,1,0:T(8,128)(2,1)S(1)} %collective-permute-done.3), channel_id=1, source_target_pairs={{0,15},{1,0},{2,1},{3,2},{4,3},{5,4},{6,5},{7,6},{8,7},{9,8},{10,9... | collective-permute-start | bytes 786440 | tf_op jit(solution)/shard_map/ppermute | solution.py:135
  84.4 5.1 %collective-permute-start.5 = (bf16[2,16,4096]{2,1,0:T(8,128)(2,1)S(1)}, bf16[2,16,4096]{2,1,0:T(8,128)(2,1)S(1)}, u32[]{:S(2)}, u32[]{:S(2)}) collective-permute-start(bf16[2,16,4096]{2,1,0:T(8,128)(2,1)S(1)} %collective-permute-done.4), channel_id=1, source_target_pairs={{0,15},{1,0},{2,1},{3,2},{4,3},{5,4},{6,5},{7,6},{8,7},{9,8},{10,9... | collective-permute-start | bytes 786440 | tf_op jit(solution)/shard_map/ppermute | solution.py:135
  93.9 5.1 %collective-permute-start.6 = (bf16[2,16,4096]{2,1,0:T(8,128)(2,1)S(1)}, bf16[2,16,4096]{2,1,0:T(8,128)(2,1)S(1)}, u32[]{:S(2)}, u32[]{:S(2)}) collective-permute-start(bf16[2,16,4096]{2,1,0:T(8,128)(2,1)S(1)} %collective-permute-done.5), channel_id=1, source_target_pairs={{0,15},{1,0},{2,1},{3,2},{4,3},{5,4},{6,5},{7,6},{8,7},{9,8},{10,9... | collective-permute-start | bytes 786440 | tf_op jit(solution)/shard_map/ppermute | solution.py:135
  99.1 3.8 %collective-permute-done.6 = bf16[2,16,4096]{2,1,0:T(8,128)(2,1)S(1)} collective-permute-done((bf16[2,16,4096]{2,1,0:T(8,128)(2,1)S(1)}, bf16[2,16,4096]{2,1,0:T(8,128)(2,1)S(1)}, u32[]{:S(2)}, u32[]{:S(2)}) %collective-permute-start.6) | collective-permute-done | bytes 262176 | tf_op jit(solution)/shard_map/ppermute | solution.py:135
  103.0 13.3 %collective-permute-done.15 = bf16[4,256,1024]{2,1,0:T(8,128)(2,1)S(1)} collective-permute-done((bf16[4,256,1024]{2,1,0:T(8,128)(2,1)S(1)}, bf16[4,256,1024]{2,1,0:T(8,128)(2,1)S(1)}, u32[]{:S(2)}, u32[]{:S(2)}) %collective-permute-start.15) | collective-permute-done | bytes 2097184 | tf_op jit(solution)/shard_map/ppermute | solution.py:56
  125.1 7.0 %collective-permute-done.18 = bf16[2,16,4096]{2,1,0:T(8,128)(2,1)S(1)} collective-permute-done((bf16[2,16,4096]{2,1,0:T(8,128)(2,1)S(1)}, bf16[2,16,4096]{2,1,0:T(8,128)(2,1)S(1)}, u32[]{:S(2)}, u32[]{:S(2)}) %collective-permute-start.18) | collective-permute-done | bytes 262176 | tf_op jit(solution)/shard_map/ppermute | solution.py:131
  134.6 4.6 %collective-permute-start.21 = (bf16[2,16,2048]{2,1,0:T(8,128)(2,1)S(1)}, bf16[2,16,2048]{2,1,0:T(8,128)(2,1)S(1)}, u32[]{:S(2)}, u32[]{:S(2)}) collective-permute-start(bf16[2,16,2048]{2,1,0:T(8,128)(2,1)S(1)} %slice.279), channel_id=1, source_target_pairs={{0,15},{1,0},{2,1},{3,2},{4,3},{5,4},{6,5},{7,6},{8,7},{9,8},{10,9... | collective-permute-start | bytes 393224 | tf_op jit(solution)/shard_map/ppermute | solution.py:141
  151.4 5.6 %collective-permute-start.31 = (bf16[2,16,4096]{2,1,0:T(8,128)(2,1)S(1)}, bf16[2,16,4096]{2,1,0:T(8,128)(2,1)S(1)}, u32[]{:S(2)}, u32[]{:S(2)}) collective-permute-start(bf16[2,16,4096]{2,1,0:T(8,128)(2,1)S(1)} %bitcast.209), channel_id=1, source_target_pairs={{0,15},{1,0},{2,1},{3,2},{4,3},{5,4},{6,5},{7,6},{8,7},{9,8},{10,9... | collective-permute-start | bytes 786440 | tf_op jit(solution)/shard_map/ppermute | solution.py:193
  163.9 5.1 %collective-permute-start.32 = (bf16[2,16,4096]{2,1,0:T(8,128)(2,1)S(1)}, bf16[2,16,4096]{2,1,0:T(8,128)(2,1)S(1)}, u32[]{:S(2)}, u32[]{:S(2)}) collective-permute-start(bf16[2,16,4096]{2,1,0:T(8,128)(2,1)S(1)} %fusion.17), channel_id=1, source_target_pairs={{0,15},{1,0},{2,1},{3,2},{4,3},{5,4},{6,5},{7,6},{8,7},{9,8},{10,9... | collective-permute-start | bytes 786440 | tf_op jit(solution)/shard_map/ppermute | solution.py:193
  172.9 5.6 %collective-permute-start.33 = (bf16[2,16,4096]{2,1,0:T(8,128)(2,1)S(1)}, bf16[2,16,4096]{2,1,0:T(8,128)(2,1)S(1)}, u32[]{:S(2)}, u32[]{:S(2)}) collective-permute-start(bf16[2,16,4096]{2,1,0:T(8,128)(2,1)S(1)} %fusion.16), channel_id=1, source_target_pairs={{0,15},{1,0},{2,1},{3,2},{4,3},{5,4},{6,5},{7,6},{8,7},{9,8},{10,9... | collective-permute-start | bytes 786440 | tf_op jit(solution)/shard_map/ppermute | solution.py:193
  182.5 5.6 %collective-permute-start.34 = (bf16[2,16,4096]{2,1,0:T(8,128)(2,1)S(1)}, bf16[2,16,4096]{2,1,0:T(8,128)(2,1)S(1)}, u32[]{:S(2)}, u32[]{:S(2)}) collective-permute-start(bf16[2,16,4096]{2,1,0:T(8,128)(2,1)S(1)} %fusion.15), channel_id=1, source_target_pairs={{0,15},{1,0},{2,1},{3,2},{4,3},{5,4},{6,5},{7,6},{8,7},{9,8},{10,9... | collective-permute-start | bytes 786440 | tf_op jit(solution)/shard_map/ppermute | solution.py:193
  192.6 5.6 %collective-permute-start.35 = (bf16[2,16,4096]{2,1,0:T(8,128)(2,1)S(1)}, bf16[2,16,4096]{2,1,0:T(8,128)(2,1)S(1)}, u32[]{:S(2)}, u32[]{:S(2)}) collective-permute-start(bf16[2,16,4096]{2,1,0:T(8,128)(2,1)S(1)} %fusion.14), channel_id=1, source_target_pairs={{0,15},{1,0},{2,1},{3,2},{4,3},{5,4},{6,5},{7,6},{8,7},{9,8},{10,9... | collective-permute-start | bytes 786440 | tf_op jit(solution)/shard_map/ppermute | solution.py:193
  203.8 5.6 %collective-permute-start.36 = (bf16[2,16,4096]{2,1,0:T(8,128)(2,1)S(1)}, bf16[2,16,4096]{2,1,0:T(8,128)(2,1)S(1)}, u32[]{:S(2)}, u32[]{:S(2)}) collective-permute-start(bf16[2,16,4096]{2,1,0:T(8,128)(2,1)S(1)} %fusion.13), channel_id=1, source_target_pairs={{0,15},{1,0},{2,1},{3,2},{4,3},{5,4},{6,5},{7,6},{8,7},{9,8},{10,9... | collective-permute-start | bytes 786440 | tf_op jit(solution)/shard_map/ppermute | solution.py:193
  212.2 3.9 %collective-permute-done.36 = bf16[2,16,4096]{2,1,0:T(8,128)(2,1)S(1)} collective-permute-done((bf16[2,16,4096]{2,1,0:T(8,128)(2,1)S(1)}, bf16[2,16,4096]{2,1,0:T(8,128)(2,1)S(1)}, u32[]{:S(2)}, u32[]{:S(2)}) %collective-permute-start.36) | collective-permute-done | bytes 262176 | tf_op jit(solution)/shard_map/ppermute | solution.py:193
  216.2 5.6 %collective-permute-start.37 = (bf16[2,16,4096]{2,1,0:T(8,128)(2,1)S(1)}, bf16[2,16,4096]{2,1,0:T(8,128)(2,1)S(1)}, u32[]{:S(2)}, u32[]{:S(2)}) collective-permute-start(bf16[2,16,4096]{2,1,0:T(8,128)(2,1)S(1)} %fusion.12), channel_id=1, source_target_pairs={{0,15},{1,0},{2,1},{3,2},{4,3},{5,4},{6,5},{7,6},{8,7},{9,8},{10,9... | collective-permute-start | bytes 786440 | tf_op jit(solution)/shard_map/ppermute | solution.py:193
  (150 shorter events, 95.0 us)
Async XLA Ops:
  2.0 45.2 %collective-permute-start.12 = (bf16[1,256,1024]{2,1,0:T(8,128)(2,1)S(1)}, bf16[1,256,1024]{2,1,0:T(8,128)(2,1)S(1)}, u32[]{:S(2)}, u32[]{:S(2)}) collective-permute-start(bf16[1,256,1024]{2,1,0:T(8,128)(2,1)S(1)} %bitcast.166), channel_id=1, source_target_pairs={{0,128},{32,160},{64,192},{96,224},{128,256},{160,288},{192,320},{... | collective-permute-start | bytes 1572872 | tf_op jit(solution)/shard_map/ppermute | solution.py:52
  9.5 59.4 %collective-permute-start.14 = (bf16[1,256,1024]{2,1,0:T(8,128)(2,1)S(1)}, bf16[1,256,1024]{2,1,0:T(8,128)(2,1)S(1)}, u32[]{:S(2)}, u32[]{:S(2)}) collective-permute-start(bf16[1,256,1024]{2,1,0:T(8,128)(2,1)S(1)} %bitcast.167), channel_id=1, source_target_pairs={{0,384},{32,416},{64,448},{96,480},{128,0},{160,32},{192,64},{224,... | collective-permute-start | bytes 1572872 | tf_op jit(solution)/shard_map/ppermute | solution.py:54
  14.4 14.0 %all-to-all-start = ((bf16[16,2,4224]{2,1,0:T(2,128)(2,1)}), bf16[16,2,4224]{2,1,0:T(2,128)(2,1)S(1)}, u32[]{:S(2)}, u32[]{:S(2)}) async-start(bf16[16,2,4224]{2,1,0:T(2,128)(2,1)} %reshape.941), calls=%async_computation | async-start | bytes 540672 | tf_op jit(solution)/shard_map/all_to_all | solution.py:96
  36.8 15.3 %collective-permute-start.7 = (bf16[2,16,4096]{2,1,0:T(8,128)(2,1)S(1)}, bf16[2,16,4096]{2,1,0:T(8,128)(2,1)S(1)}, u32[]{:S(2)}, u32[]{:S(2)}) collective-permute-start(bf16[2,16,4096]{2,1,0:T(8,128)(2,1)S(1)} %pad_maximum_fusion.8), channel_id=1, source_target_pairs={{0,1},{1,2},{2,3},{3,4},{4,5},{5,6},{6,7},{7,8},{8,9},{9,10},{10,1... | collective-permute-start | bytes 786440 | tf_op jit(solution)/shard_map/ppermute | solution.py:131
  38.8 15.5 %collective-permute-start.1 = (bf16[2,16,4096]{2,1,0:T(8,128)(2,1)S(1)}, bf16[2,16,4096]{2,1,0:T(8,128)(2,1)S(1)}, u32[]{:S(2)}, u32[]{:S(2)}) collective-permute-start(bf16[2,16,4096]{2,1,0:T(8,128)(2,1)S(1)} %pad_maximum_fusion.8), channel_id=1, source_target_pairs={{0,15},{1,0},{2,1},{3,2},{4,3},{5,4},{6,5},{7,6},{8,7},{9,8},{10,9... | collective-permute-start | bytes 786440 | tf_op jit(solution)/shard_map/ppermute | solution.py:135
  47.2 21.7 %collective-permute-start.13 = (bf16[1,256,1024]{2,1,0:T(8,128)(2,1)S(1)}, bf16[1,256,1024]{2,1,0:T(8,128)(2,1)S(1)}, u32[]{:S(2)}, u32[]{:S(2)}) collective-permute-start(bf16[1,256,1024]{2,1,0:T(8,128)(2,1)S(1)} %collective-permute-done.12), channel_id=1, source_target_pairs={{0,128},{32,160},{64,192},{96,224},{128,256},{160,288},{192,320},{... | collective-permute-start | bytes 1572872 | tf_op jit(solution)/shard_map/ppermute | solution.py:53
  52.1 9.7 %collective-permute-start.8 = (bf16[2,16,4096]{2,1,0:T(8,128)(2,1)S(1)}, bf16[2,16,4096]{2,1,0:T(8,128)(2,1)S(1)}, u32[]{:S(2)}, u32[]{:S(2)}) collective-permute-start(bf16[2,16,4096]{2,1,0:T(8,128)(2,1)S(1)} %collective-permute-done.7), channel_id=1, source_target_pairs={{0,1},{1,2},{2,3},{3,4},{4,5},{5,6},{6,7},{7,8},{8,9},{9,10},{10,1... | collective-permute-start | bytes 786440 | tf_op jit(solution)/shard_map/ppermute | solution.py:131
  61.8 11.2 %collective-permute-start.9 = (bf16[2,16,4096]{2,1,0:T(8,128)(2,1)S(1)}, bf16[2,16,4096]{2,1,0:T(8,128)(2,1)S(1)}, u32[]{:S(2)}, u32[]{:S(2)}) collective-permute-start(bf16[2,16,4096]{2,1,0:T(8,128)(2,1)S(1)} %collective-permute-done.8), channel_id=1, source_target_pairs={{0,1},{1,2},{2,3},{3,4},{4,5},{5,6},{6,7},{7,8},{8,9},{9,10},{10,1... | collective-permute-start | bytes 786440 | tf_op jit(solution)/shard_map/ppermute | solution.py:131
  63.8 11.2 %collective-permute-start.3 = (bf16[2,16,4096]{2,1,0:T(8,128)(2,1)S(1)}, bf16[2,16,4096]{2,1,0:T(8,128)(2,1)S(1)}, u32[]{:S(2)}, u32[]{:S(2)}) collective-permute-start(bf16[2,16,4096]{2,1,0:T(8,128)(2,1)S(1)} %collective-permute-done.2), channel_id=1, source_target_pairs={{0,15},{1,0},{2,1},{3,2},{4,3},{5,4},{6,5},{7,6},{8,7},{9,8},{10,9... | collective-permute-start | bytes 786440 | tf_op jit(solution)/shard_map/ppermute | solution.py:135
  69.2 47.0 %collective-permute-start.15 = (bf16[4,256,1024]{2,1,0:T(8,128)(2,1)S(1)}, bf16[4,256,1024]{2,1,0:T(8,128)(2,1)S(1)}, u32[]{:S(2)}, u32[]{:S(2)}) collective-permute-start(bf16[4,256,1024]{2,1,0:T(8,128)(2,1)S(1)} %pad_maximum_fusion), channel_id=1, source_target_pairs={{0,64},{32,96},{64,0},{96,32},{128,192},{160,224},{192,128},{224,1... | collective-permute-start | bytes 6291464 | tf_op jit(solution)/shard_map/ppermute | solution.py:56
  92.0 28.6 %collective-permute-start.17 = (bf16[2,16,4096]{2,1,0:T(8,128)(2,1)S(1)}, bf16[2,16,4096]{2,1,0:T(8,128)(2,1)S(1)}, u32[]{:S(2)}, u32[]{:S(2)}) collective-permute-start(bf16[2,16,4096]{2,1,0:T(8,128)(2,1)S(1)} %collective-permute-done.11), channel_id=1, source_target_pairs={{0,1},{1,2},{2,3},{3,4},{4,5},{5,6},{6,7},{7,8},{8,9},{9,10},{10,1... | collective-permute-start | bytes 786440 | tf_op jit(solution)/shard_map/ppermute | solution.py:131
  116.4 27.5 %collective-permute-start.16 = (bf16[8,256,1024]{2,1,0:T(8,128)(2,1)S(1)}, bf16[8,256,1024]{2,1,0:T(8,128)(2,1)S(1)}, u32[]{:S(2)}, u32[]{:S(2)}) collective-permute-start(bf16[8,256,1024]{2,1,0:T(8,128)(2,1)S(1)} %constant_dynamic-update-slice_fusion.14), channel_id=1, source_target_pairs={{0,32},{32,0},{64,96},{96,64},{128,160},{160,128},{192,224},{224,1... | collective-permute-start | bytes 12582920 | tf_op jit(solution)/shard_map/ppermute | solution.py:59
  118.4 16.2 %collective-permute-start.20 = (bf16[2,16,4096]{2,1,0:T(8,128)(2,1)S(1)}, bf16[2,16,4096]{2,1,0:T(8,128)(2,1)S(1)}, u32[]{:S(2)}, u32[]{:S(2)}) collective-permute-start(bf16[2,16,4096]{2,1,0:T(8,128)(2,1)S(1)} %collective-permute-done.6), channel_id=1, source_target_pairs={{0,15},{1,0},{2,1},{3,2},{4,3},{5,4},{6,5},{7,6},{8,7},{9,8},{10,9... | collective-permute-start | bytes 786440 | tf_op jit(solution)/shard_map/ppermute | solution.py:135
  120.6 11.5 %collective-permute-start.18 = (bf16[2,16,4096]{2,1,0:T(8,128)(2,1)S(1)}, bf16[2,16,4096]{2,1,0:T(8,128)(2,1)S(1)}, u32[]{:S(2)}, u32[]{:S(2)}) collective-permute-start(bf16[2,16,4096]{2,1,0:T(8,128)(2,1)S(1)} %collective-permute-done.17), channel_id=1, source_target_pairs={{0,1},{1,2},{2,3},{3,4},{4,5},{5,6},{6,7},{7,8},{8,9},{9,10},{10,1... | collective-permute-start | bytes 786440 | tf_op jit(solution)/shard_map/ppermute | solution.py:131
  149.5 10.0 %collective-permute-start.22 = (bf16[2,16,4096]{2,1,0:T(8,128)(2,1)S(1)}, bf16[2,16,4096]{2,1,0:T(8,128)(2,1)S(1)}, u32[]{:S(2)}, u32[]{:S(2)}) collective-permute-start(bf16[2,16,4096]{2,1,0:T(8,128)(2,1)S(1)} %bitcast.210), channel_id=1, source_target_pairs={{0,1},{1,2},{2,3},{3,4},{4,5},{5,6},{6,7},{7,8},{8,9},{9,10},{10,1... | collective-permute-start | bytes 786440 | tf_op jit(solution)/shard_map/ppermute | solution.py:186
  151.4 12.3 %collective-permute-start.31 = (bf16[2,16,4096]{2,1,0:T(8,128)(2,1)S(1)}, bf16[2,16,4096]{2,1,0:T(8,128)(2,1)S(1)}, u32[]{:S(2)}, u32[]{:S(2)}) collective-permute-start(bf16[2,16,4096]{2,1,0:T(8,128)(2,1)S(1)} %bitcast.209), channel_id=1, source_target_pairs={{0,15},{1,0},{2,1},{3,2},{4,3},{5,4},{6,5},{7,6},{8,7},{9,8},{10,9... | collective-permute-start | bytes 786440 | tf_op jit(solution)/shard_map/ppermute | solution.py:193
  172.9 9.5 %collective-permute-start.33 = (bf16[2,16,4096]{2,1,0:T(8,128)(2,1)S(1)}, bf16[2,16,4096]{2,1,0:T(8,128)(2,1)S(1)}, u32[]{:S(2)}, u32[]{:S(2)}) collective-permute-start(bf16[2,16,4096]{2,1,0:T(8,128)(2,1)S(1)} %fusion.16), channel_id=1, source_target_pairs={{0,15},{1,0},{2,1},{3,2},{4,3},{5,4},{6,5},{7,6},{8,7},{9,8},{10,9... | collective-permute-start | bytes 786440 | tf_op jit(solution)/shard_map/ppermute | solution.py:193
  182.5 10.0 %collective-permute-start.34 = (bf16[2,16,4096]{2,1,0:T(8,128)(2,1)S(1)}, bf16[2,16,4096]{2,1,0:T(8,128)(2,1)S(1)}, u32[]{:S(2)}, u32[]{:S(2)}) collective-permute-start(bf16[2,16,4096]{2,1,0:T(8,128)(2,1)S(1)} %fusion.15), channel_id=1, source_target_pairs={{0,15},{1,0},{2,1},{3,2},{4,3},{5,4},{6,5},{7,6},{8,7},{9,8},{10,9... | collective-permute-start | bytes 786440 | tf_op jit(solution)/shard_map/ppermute | solution.py:193
  188.2 10.4 %collective-permute-start.26 = (bf16[2,16,4096]{2,1,0:T(8,128)(2,1)S(1)}, bf16[2,16,4096]{2,1,0:T(8,128)(2,1)S(1)}, u32[]{:S(2)}, u32[]{:S(2)}) collective-permute-start(bf16[2,16,4096]{2,1,0:T(8,128)(2,1)S(1)} %fusion.21), channel_id=1, source_target_pairs={{0,1},{1,2},{2,3},{3,4},{4,5},{5,6},{6,7},{7,8},{8,9},{9,10},{10,1... | collective-permute-start | bytes 786440 | tf_op jit(solution)/shard_map/ppermute | solution.py:186
  192.6 11.2 %collective-permute-start.35 = (bf16[2,16,4096]{2,1,0:T(8,128)(2,1)S(1)}, bf16[2,16,4096]{2,1,0:T(8,128)(2,1)S(1)}, u32[]{:S(2)}, u32[]{:S(2)}) collective-permute-start(bf16[2,16,4096]{2,1,0:T(8,128)(2,1)S(1)} %fusion.14), channel_id=1, source_target_pairs={{0,15},{1,0},{2,1},{3,2},{4,3},{5,4},{6,5},{7,6},{8,7},{9,8},{10,9... | collective-permute-start | bytes 786440 | tf_op jit(solution)/shard_map/ppermute | solution.py:193
  198.6 11.5 %collective-permute-start.27 = (bf16[2,16,4096]{2,1,0:T(8,128)(2,1)S(1)}, bf16[2,16,4096]{2,1,0:T(8,128)(2,1)S(1)}, u32[]{:S(2)}, u32[]{:S(2)}) collective-permute-start(bf16[2,16,4096]{2,1,0:T(8,128)(2,1)S(1)} %fusion.20), channel_id=1, source_target_pairs={{0,1},{1,2},{2,3},{3,4},{4,5},{5,6},{6,7},{7,8},{8,9},{9,10},{10,1... | collective-permute-start | bytes 786440 | tf_op jit(solution)/shard_map/ppermute | solution.py:186
  203.8 12.3 %collective-permute-start.36 = (bf16[2,16,4096]{2,1,0:T(8,128)(2,1)S(1)}, bf16[2,16,4096]{2,1,0:T(8,128)(2,1)S(1)}, u32[]{:S(2)}, u32[]{:S(2)}) collective-permute-start(bf16[2,16,4096]{2,1,0:T(8,128)(2,1)S(1)} %fusion.13), channel_id=1, source_target_pairs={{0,15},{1,0},{2,1},{3,2},{4,3},{5,4},{6,5},{7,6},{8,7},{9,8},{10,9... | collective-permute-start | bytes 786440 | tf_op jit(solution)/shard_map/ppermute | solution.py:193
  210.2 11.9 %collective-permute-start.28 = (bf16[2,16,4096]{2,1,0:T(8,128)(2,1)S(1)}, bf16[2,16,4096]{2,1,0:T(8,128)(2,1)S(1)}, u32[]{:S(2)}, u32[]{:S(2)}) collective-permute-start(bf16[2,16,4096]{2,1,0:T(8,128)(2,1)S(1)} %fusion.19), channel_id=1, source_target_pairs={{0,1},{1,2},{2,3},{3,4},{4,5},{5,6},{6,7},{7,8},{8,9},{9,10},{10,1... | collective-permute-start | bytes 786440 | tf_op jit(solution)/shard_map/ppermute | solution.py:186
  216.2 9.9 %collective-permute-start.37 = (bf16[2,16,4096]{2,1,0:T(8,128)(2,1)S(1)}, bf16[2,16,4096]{2,1,0:T(8,128)(2,1)S(1)}, u32[]{:S(2)}, u32[]{:S(2)}) collective-permute-start(bf16[2,16,4096]{2,1,0:T(8,128)(2,1)S(1)} %fusion.12), channel_id=1, source_target_pairs={{0,15},{1,0},{2,1},{3,2},{4,3},{5,4},{6,5},{7,6},{8,7},{9,8},{10,9... | collective-permute-start | bytes 786440 | tf_op jit(solution)/shard_map/ppermute | solution.py:193
  (19 other events, 177.7 us)
